TPU v7x, 32 devices: a whole 2x2x4 slice. The times are simulated.
32 devices in a mesh: col: 8 (over z, y), row: 4 (over x, core).
Axes of the slice: x: 2, y: 2, z: 4, core: 2. Of those that a mesh axis runs over, the one named last changes fastest.
Arguments:
- tiles: bfloat16 [2, 4096, 8192], P(None, 'row', 'col')
- extents: int32 [2, 4, 8], replicated, may hold values from 32 to 128
- offsets: int32 [2, 4, 8], replicated, may hold values from 0 to 127, as said below
- bands: int32 [2, 4, 8], replicated, may hold values from 0 to 8, as said below
Outputs:
- blended: float32 [2, 4096, 8192], P(None, 'row', 'col')
- weight_total: float32 [4096, 8192], P('row', 'col')
Inputs may be any that keep to these rules, and one draw needn't show every extreme that they name: Some tile has both offsets equal to 127 and some tile has both equal to 0. `bands`: entry 0 of a tile is smaller than entry 1; some tile has the band 0 to 8.
All inputs are finite; a program needn't handle non-finite values.
Results may differ from a plain program's by a relative error of at most 0.0003.
Values may be sent and summed in bfloat16 or wider, within the bound.
No kernel may reach another device: no remote copies, remote signals or barrier semaphores. Data moves between devices by JAX's collectives and lax.ppermute only.
A program may use at most 128 MiB of HBM per device.

v0:
```python
import jax
import jax.numpy as jnp
from jax import lax
from jax.sharding import PartitionSpec as P

STRIP = 128
SPILL = 128
BLOCK = 128


eps = 1e-06


def extended(cells, sides, width):
    for axis, dim in sides:
        count = lax.axis_size(axis)
        ends = count - 1
        head = lax.slice_in_dim(cells, 0, width, axis=dim)
        tail = lax.slice_in_dim(cells, cells.shape[dim] - width, cells.shape[dim], axis=dim)
        cells = jnp.concatenate(
            [
                lax.ppermute(tail, axis, [(i, (i + 1) % count) for i in range(ends)]),
                cells,
                lax.ppermute(head, axis, [((i + 1) % count, i) for i in range(ends)]),
            ],
            axis=dim,
        )
    return cells


def from_behind(block, axis, distance):
    devices = range(lax.axis_size(axis))
    route = [(i - distance, i) for i in devices if i - distance in devices]
    return lax.ppermute(block, axis, route)


def pair_terms(former, latter, window):
    full_window = jnp.broadcast_to(window, former.shape)
    number = jnp.sum(full_window, axis=(-2, -1), keepdims=True)
    mean_former = jnp.sum(former * full_window, axis=(-2, -1), keepdims=True) / number
    mean_latter = jnp.sum(latter * full_window, axis=(-2, -1), keepdims=True) / number
    dev_former = (former - mean_former) * full_window
    dev_latter = (latter - mean_latter) * full_window
    flat_number = number[..., 0, 0]
    var_former = jnp.sum(dev_former * dev_former, axis=(-2, -1)) / flat_number
    var_latter = jnp.sum(dev_latter * dev_latter, axis=(-2, -1)) / flat_number
    covariance = jnp.sum(dev_former * dev_latter, axis=(-2, -1)) / flat_number
    weight = covariance * covariance / ((var_former + eps) * (var_latter + eps))
    log_ratio = 0.25 * (jnp.log(var_latter + eps) - jnp.log(var_former + eps))
    shift_term = 0.5 * (mean_latter - mean_former)[..., 0, 0]
    return (weight, weight * log_ratio, weight * shift_term)


def combine(right_pair, down_pair, left_pair, upper_pair):
    denominator = 1.0 + right_pair[0] + down_pair[0] + left_pair[0] + upper_pair[0]
    log_gain = (right_pair[1] + down_pair[1] - left_pair[1] - upper_pair[1]) / denominator
    offset = (right_pair[2] + down_pair[2] - left_pair[2] - upper_pair[2]) / denominator
    return (log_gain, offset)


def apply_terms(strips, log_gain, offset):
    return jnp.exp(log_gain)[:, None, None] * strips + offset[:, None, None]


def blend_weight(row_ids, col_ids, band_low, band_high, tile_px):
    half = tile_px / 2.0
    row_fade = (jnp.minimum(row_ids, tile_px - 1 - row_ids) + 1).astype(jnp.float32) / half
    col_fade = (jnp.minimum(col_ids, tile_px - 1 - col_ids) + 1).astype(jnp.float32) / half
    live = ((row_ids >= band_low * BLOCK) & (row_ids < band_high * BLOCK)).astype(jnp.float32)
    return (live * row_fade)[:, None] * col_fade[None, :]


def place_piece(
    raw_data,
    log_gain,
    offset,
    top_shift,
    left_shift,
    band_low,
    band_high,
    out_rows,
    out_cols,
    tile_px,
):
    reach = STRIP + SPILL
    planes = raw_data.shape[0]
    padded = jnp.pad(raw_data, ((0, 0), (reach, reach), (reach, reach)))
    zero = jnp.zeros((), jnp.int32)
    top_shift = jnp.asarray(top_shift, jnp.int32)
    left_shift = jnp.asarray(left_shift, jnp.int32)
    window = lax.dynamic_slice(
        padded, (zero, reach - top_shift, reach - left_shift), (planes, out_rows, out_cols)
    )
    src_rows = jnp.arange(out_rows, dtype=jnp.int32) - top_shift
    src_cols = jnp.arange(out_cols, dtype=jnp.int32) - left_shift
    row_valid = ((src_rows >= 0) & (src_rows < raw_data.shape[1])).astype(jnp.float32)
    col_valid = ((src_cols >= 0) & (src_cols < raw_data.shape[2])).astype(jnp.float32)
    weight = blend_weight(src_rows, src_cols, band_low, band_high, tile_px)
    weight = weight * row_valid[:, None] * col_valid[None, :]
    values = apply_terms(window.astype(jnp.float32), log_gain, offset) * weight[None]
    return jnp.concatenate([values, weight[None]], axis=0)


def four_pairs(own_strips, far_strips, windows):
    right_pair = pair_terms(own_strips[0], far_strips[0], windows[0])
    down_pair = pair_terms(own_strips[1], far_strips[1], windows[1])
    left_pair = pair_terms(far_strips[2], own_strips[2], windows[2])
    upper_pair = pair_terms(far_strips[3], own_strips[3], windows[3])
    return combine(right_pair, down_pair, left_pair, upper_pair)


def local(tiles, extents, offsets, bands):
    planes, tile_px, _ = tiles.shape
    row_index = lax.axis_index("row")
    col_index = lax.axis_index("col")
    padded = extended(tiles, (("col", 2), ("row", 1)), STRIP)
    width = STRIP
    own_right = tiles[:, :, tile_px - width :].astype(jnp.float32)
    own_down = tiles[:, tile_px - width :, :].astype(jnp.float32)
    own_left = tiles[:, :, :width].astype(jnp.float32)
    own_up = tiles[:, :width, :].astype(jnp.float32)
    far_right = padded[:, width : width + tile_px, width + tile_px :].astype(jnp.float32)
    far_down = padded[:, width + tile_px :, width : width + tile_px].astype(jnp.float32)
    far_left = padded[:, width : width + tile_px, :width].astype(jnp.float32)
    far_up = padded[:, :width, width : width + tile_px].astype(jnp.float32)
    left_col = jnp.maximum(col_index - 1, 0)
    upper_row = jnp.maximum(row_index - 1, 0)
    strip_ids = jnp.arange(width, dtype=jnp.int32)
    windows = (
        (strip_ids < extents[0, row_index, col_index]).astype(jnp.float32)[None, None, :],
        (strip_ids < extents[1, row_index, col_index]).astype(jnp.float32)[None, :, None],
        (strip_ids < extents[0, row_index, left_col]).astype(jnp.float32)[None, None, :],
        (strip_ids < extents[1, upper_row, col_index]).astype(jnp.float32)[None, :, None],
    )
    own_strips = (own_right, own_down, own_left, own_up)
    far_strips = (far_right, far_down, far_left, far_up)
    gain_one, level_one = four_pairs(own_strips, far_strips, windows)
    gain_terms = jnp.concatenate([gain_one, level_one])[:, None, None]
    near_terms = extended(gain_terms, (("col", 2), ("row", 1)), 1)
    places = ((1, 2), (2, 1), (1, 0), (0, 1))
    own_fixed = tuple((apply_terms(item, gain_one, level_one) for item in own_strips))
    far_fixed = tuple(
        (
            apply_terms(
                item, near_terms[:planes, spot[0], spot[1]], near_terms[planes:, spot[0], spot[1]]
            )
            for item, spot in zip(far_strips, places)
        )
    )
    gain_two, level_two = four_pairs(own_fixed, far_fixed, windows)
    log_gain = gain_one + gain_two
    level = jnp.exp(gain_two) * level_one + level_two
    own_low = bands[0, row_index, col_index]
    own_high = bands[1, row_index, col_index]
    canvas = place_piece(
        tiles,
        log_gain,
        level,
        offsets[0, row_index, col_index],
        offsets[1, row_index, col_index],
        own_low,
        own_high,
        tile_px + SPILL,
        tile_px + SPILL,
        tile_px,
    )
    section = canvas[:, :tile_px, :tile_px]
    band_in = from_behind(canvas[:, :, tile_px:], "col", 1)
    section = section.at[:, :, :SPILL].add(band_in[:, :tile_px])
    lower_part = canvas[:, tile_px:, :tile_px].at[:, :, :SPILL].add(band_in[:, tile_px:])
    lower_in = from_behind(lower_part, "row", 1)
    section = section.at[:, :SPILL, :].add(lower_in)
    return (section[:planes], section[planes])


def solution(mesh):
    return jax.shard_map(
        local,
        mesh=mesh,
        in_specs=(P(None, "row", "col"), P(), P(), P()),
        out_specs=(P(None, "row", "col"), P("row", "col")),
        check_vma=False,
    )
```

profile of v0, /device:TPU:10, one launch (start us, length us, event | category | flops | bytes accessed | tf_op | source)
XLA Modules:
  0.0 153.0 jit_solution(15024654875804194639)
XLA Ops:
  1.9 3.4 %collective-permute-start.1 = (bf16[2,1024,128]{2,1,0:T(8,128)(2,1)S(1)}, bf16[2,1024,128]{2,1,0:T(8,128)(2,1)S(1)}, u32[]{:S(2)}, u32[]{:S(2)}) collective-permute-start(bf16[2,1024,128]{2,1,0:T(8,128)(2,1)S(1)} %get-tuple-element.99), channel_id=1, source_target_pairs={{0,4},{4,8},{8,12},{12,16},{16,20},{20,24},{24,28},{1,5},{5,9},{9,... | collective-permute-start | bytes 1572872 | tf_op jit(solution)/shard_map/ppermute | solution.py:22
  5.4 3.3 %collective-permute-start = (bf16[2,1024,128]{2,1,0:T(8,128)(2,1)S(1)}, bf16[2,1024,128]{2,1,0:T(8,128)(2,1)S(1)}, u32[]{:S(2)}, u32[]{:S(2)}) collective-permute-start(bf16[2,1024,128]{2,1,0:T(8,128)(2,1)S(1)} %get-tuple-element.98), channel_id=1, source_target_pairs={{4,0},{8,4},{12,8},{16,12},{20,16},{24,20},{28,24},{5,1},{9,5},{13... | collective-permute-start | bytes 1572872 | tf_op jit(solution)/shard_map/ppermute | solution.py:24
  12.1 1.4 constant_dynamic-slice_fusion
  15.5 3.1 %multiply_multiply_fusion.1 = f32[1152,1152]{1,0:T(8,128)} fusion(f32[1152]{0:T(1024)S(1)} %get-tuple-element.137, f32[1152]{0:T(1024)S(1)} %get-tuple-element.136, f32[1152]{0:T(1024)S(1)} %fusion.118, f32[1152]{0:T(1024)S(1)} %fusion.115), kind=kLoop, calls=%fused_computation.12 | loop fusion | flops 3981312 | bytes 5326848 | tf_op jit(solution)/shard_map/mul | solution.py:99
  18.6 3.1 %multiply_multiply_fusion = f32[1,1152,1152]{2,1,0:T(8,128)} fusion(f32[1152]{0:T(1024)S(1)} %get-tuple-element.137, f32[1152]{0:T(1024)S(1)} %get-tuple-element.136, f32[1152]{0:T(1024)S(1)} %fusion.118, f32[1152]{0:T(1024)S(1)} %fusion.115), kind=kLoop, calls=%fused_computation.11 | loop fusion | flops 3981312 | bytes 5326848 | tf_op jit(solution)/shard_map/mul | solution.py:99
  27.9 2.8 %constant_dynamic-update-slice_fusion.1 = bf16[2,1024,1280]{2,1,0:T(8,128)(2,1)S(1)} fusion(bf16[2,1024,1280]{2,1,0:T(8,128)(2,1)S(1)} %constant_dynamic-update-slice_fusion.2, bf16[2,1024,1024]{2,1,0:T(8,128)(2,1)} %param.10), kind=kLoop, calls=%fused_computation.166 | loop fusion | bytes 8388608
  30.9 1.9 %collective-permute-start.3 = (bf16[2,128,1280]{2,1,0:T(8,128)(2,1)S(1)}, bf16[2,128,1280]{2,1,0:T(8,128)(2,1)S(1)}, u32[]{:S(2)}, u32[]{:S(2)}) collective-permute-start(bf16[2,128,1280]{2,1,0:T(8,128)(2,1)S(1)} %get-tuple-element.97), channel_id=1, source_target_pairs={{0,1},{1,2},{2,3},{4,5},{5,6},{6,7},{8,9},{9,10},{10,11},{12,13},{... | collective-permute-start | bytes 1966088 | tf_op jit(solution)/shard_map/ppermute | solution.py:22
  32.8 3.6 %collective-permute-start.2 = (bf16[2,128,1280]{2,1,0:T(8,128)(2,1)S(1)}, bf16[2,128,1280]{2,1,0:T(8,128)(2,1)S(1)}, u32[]{:S(2)}, u32[]{:S(2)}) collective-permute-start(bf16[2,128,1280]{2,1,0:T(8,128)(2,1)S(1)} %get-tuple-element.96), channel_id=1, source_target_pairs={{1,0},{2,1},{3,2},{5,4},{6,5},{7,6},{9,8},{10,9},{11,10},{13,12},{... | collective-permute-start | bytes 1966088 | tf_op jit(solution)/shard_map/ppermute | solution.py:24
  38.6 4.2 %collective-permute-done.3 = bf16[2,128,1280]{2,1,0:T(8,128)(2,1)S(1)} collective-permute-done((bf16[2,128,1280]{2,1,0:T(8,128)(2,1)S(1)}, bf16[2,128,1280]{2,1,0:T(8,128)(2,1)S(1)}, u32[]{:S(2)}, u32[]{:S(2)}) %collective-permute-start.3) | collective-permute-done | bytes 655392 | tf_op jit(solution)/shard_map/ppermute | solution.py:22
  42.8 1.8 %collective-permute-done.2 = bf16[2,128,1280]{2,1,0:T(8,128)(2,1)S(1)} collective-permute-done((bf16[2,128,1280]{2,1,0:T(8,128)(2,1)S(1)}, bf16[2,128,1280]{2,1,0:T(8,128)(2,1)S(1)}, u32[]{:S(2)}, u32[]{:S(2)}) %collective-permute-start.2) | collective-permute-done | bytes 655392 | tf_op jit(solution)/shard_map/ppermute | solution.py:24
  46.9 4.3 %collective-permute-start.4 = (f32[4,1,1]{0,2,1:T(1,128)S(1)}, f32[4,1,1]{0,2,1:T(1,128)S(1)}, u32[]{:S(2)}, u32[]{:S(2)}) collective-permute-start(f32[4,1,1]{0,2,1:T(1,128)S(1)} %maximum_bitcast_fusion), channel_id=1, source_target_pairs={{4,0},{8,4},{12,8},{16,12},{20,16},{24,20},{28,24},{5,1},{9,5},{13... | collective-permute-start | bytes 56 | tf_op jit(solution)/shard_map/ppermute | solution.py:24
  51.1 2.0 %collective-permute-start.5 = (f32[4,1,1]{0,2,1:T(1,128)S(1)}, f32[4,1,1]{0,2,1:T(1,128)S(1)}, u32[]{:S(2)}, u32[]{:S(2)}) collective-permute-start(f32[4,1,1]{0,2,1:T(1,128)S(1)} %maximum_bitcast_fusion), channel_id=1, source_target_pairs={{0,4},{4,8},{8,12},{12,16},{16,20},{20,24},{24,28},{1,5},{5,9},{9,... | collective-permute-start | bytes 56 | tf_op jit(solution)/shard_map/ppermute | solution.py:22
  53.2 4.3 %collective-permute-done.5 = f32[4,1,1]{0,2,1:T(1,128)S(1)} collective-permute-done((f32[4,1,1]{0,2,1:T(1,128)S(1)}, f32[4,1,1]{0,2,1:T(1,128)S(1)}, u32[]{:S(2)}, u32[]{:S(2)}) %collective-permute-start.5) | collective-permute-done | bytes 48 | tf_op jit(solution)/shard_map/ppermute | solution.py:22
  57.5 2.7 %collective-permute-start.6 = (f32[4,1,3]{0,2,1:T(4,128)S(1)}, f32[4,1,3]{0,2,1:T(4,128)S(1)}, u32[]{:S(2)}, u32[]{:S(2)}) collective-permute-start(f32[4,1,3]{0,2,1:T(4,128)S(1)} %pad_maximum_fusion.1), channel_id=1, source_target_pairs={{1,0},{2,1},{3,2},{5,4},{6,5},{7,6},{9,8},{10,9},{11,10},{13,12},{... | collective-permute-start | bytes 152 | tf_op jit(solution)/shard_map/ppermute | solution.py:24
  60.2 2.1 %collective-permute-start.7 = (f32[4,1,3]{0,2,1:T(4,128)S(1)}, f32[4,1,3]{0,2,1:T(4,128)S(1)}, u32[]{:S(2)}, u32[]{:S(2)}) collective-permute-start(f32[4,1,3]{0,2,1:T(4,128)S(1)} %pad_maximum_fusion.1), channel_id=1, source_target_pairs={{0,1},{1,2},{2,3},{4,5},{5,6},{6,7},{8,9},{9,10},{10,11},{12,13},{... | collective-permute-start | bytes 152 | tf_op jit(solution)/shard_map/ppermute | solution.py:22
  67.9 12.2 %add_multiply_fusion = f32[2,1152,1152]{2,1,0:T(8,128)} fusion(s32[]{:T(128)S(6)} %select_n.10, s32[]{:T(128)S(6)} %select_n.11, bf16[2,1024,1024]{2,1,0:T(8,128)(2,1)} %param.10, f32[1152,1152]{1,0:T(8,128)} %multiply_multiply_fusion.1, f32[2]{0:T(128)S(1)} %divide_add_fusion, f32[2]{0:T(128)S(1)} %get-tuple-element.84), kind=kLoop, calls=%fused_computation.9 | loop fusion | flops 10616832 | bytes 20119576 | tf_op jit(solution)/shard_map/mul | solution.py:100
  80.1 1.5 %fusion.1 = f32[3,1152,128]{2,1,0:T(8,128)S(1)} fusion(f32[2,1152,1152]{2,1,0:T(8,128)} %add_multiply_fusion, f32[1,1152,1152]{2,1,0:T(8,128)S(1)} %bitcast.29), kind=kLoop, calls=%fused_computation.14 | loop fusion | flops 442368 | bytes 17694720 | tf_op jit(solution)/shard_map/concatenate | solution.py:101
  81.6 2.5 %collective-permute-start.8 = (f32[3,1152,128]{2,1,0:T(8,128)S(1)}, f32[3,1152,128]{2,1,0:T(8,128)S(1)}, u32[]{:S(2)}, u32[]{:S(2)}) collective-permute-start(f32[3,1152,128]{2,1,0:T(8,128)S(1)} %fusion.1), channel_id=1, source_target_pairs={{0,4},{4,8},{8,12},{12,16},{16,20},{20,24},{24,28},{1,5},{5,9},{9,... | collective-permute-start | bytes 5308424 | tf_op jit(solution)/shard_map/ppermute | solution.py:34
  84.6 39.6 %collective-permute-done.8 = f32[3,1152,128]{2,1,0:T(8,128)S(1)} collective-permute-done((f32[3,1152,128]{2,1,0:T(8,128)S(1)}, f32[3,1152,128]{2,1,0:T(8,128)S(1)}, u32[]{:S(2)}, u32[]{:S(2)}) %collective-permute-start.8) | collective-permute-done | bytes 1769504 | tf_op jit(solution)/shard_map/ppermute | solution.py:34
  124.3 1.9 %collective-permute-start.9 = (f32[3,128,1024]{2,1,0:T(8,128)S(1)}, f32[3,128,1024]{2,1,0:T(8,128)S(1)}, u32[]{:S(2)}, u32[]{:S(2)}) collective-permute-start(f32[3,128,1024]{2,1,0:T(8,128)S(1)} %fusion.111), channel_id=1, source_target_pairs={{0,1},{1,2},{2,3},{4,5},{5,6},{6,7},{8,9},{9,10},{10,11},{12,13},{... | collective-permute-start | bytes 4718600 | tf_op jit(solution)/shard_map/ppermute | solution.py:34
  126.2 1.8 %fusion = f32[3,1024,1024]{2,1,0:T(8,128)S(1)} fusion(f32[2,1152,1152]{2,1,0:T(8,128)S(1)} %copy-done, f32[1,1152,1152]{2,1,0:T(8,128)S(1)} %bitcast.29), kind=kLoop, calls=%fused_computation.8 | loop fusion | flops 3145728 | bytes 28508160 | tf_op jit(solution)/shard_map/concatenate | solution.py:101
  128.3 17.8 %collective-permute-done.9 = f32[3,128,1024]{2,1,0:T(8,128)S(1)} collective-permute-done((f32[3,128,1024]{2,1,0:T(8,128)S(1)}, f32[3,128,1024]{2,1,0:T(8,128)S(1)}, u32[]{:S(2)}, u32[]{:S(2)}) %collective-permute-start.9) | collective-permute-done | bytes 1572896 | tf_op jit(solution)/shard_map/ppermute | solution.py:34
  146.5 4.2 %slice.186 = f32[2,1024,1024]{2,1,0:T(8,128)} slice(f32[3,1024,1024]{2,1,0:T(8,128)S(1)} %fusion.6), slice={[0:2], [0:1024], [0:1024]} | slice | bytes 16777216 | tf_op jit(solution)/shard_map/slice | solution.py:173
  150.7 2.3 %slice_bitcast_fusion = f32[1024,1024]{1,0:T(8,128)} fusion(f32[3,1024,1024]{2,1,0:T(8,128)S(1)} %fusion.6), kind=kLoop, calls=%fused_computation.13 | loop fusion | bytes 8388608 | tf_op jit(solution)/shard_map/squeeze | solution.py:173
  (59 shorter events, 20.1 us)
Async XLA Ops:
  1.9 25.8 %collective-permute-start.1 = (bf16[2,1024,128]{2,1,0:T(8,128)(2,1)S(1)}, bf16[2,1024,128]{2,1,0:T(8,128)(2,1)S(1)}, u32[]{:S(2)}, u32[]{:S(2)}) collective-permute-start(bf16[2,1024,128]{2,1,0:T(8,128)(2,1)S(1)} %get-tuple-element.99), channel_id=1, source_target_pairs={{0,4},{4,8},{8,12},{12,16},{16,20},{20,24},{24,28},{1,5},{5,9},{9,... | collective-permute-start | bytes 1572872 | tf_op jit(solution)/shard_map/ppermute | solution.py:22
  5.4 25.3 %collective-permute-start = (bf16[2,1024,128]{2,1,0:T(8,128)(2,1)S(1)}, bf16[2,1024,128]{2,1,0:T(8,128)(2,1)S(1)}, u32[]{:S(2)}, u32[]{:S(2)}) collective-permute-start(bf16[2,1024,128]{2,1,0:T(8,128)(2,1)S(1)} %get-tuple-element.98), channel_id=1, source_target_pairs={{4,0},{8,4},{12,8},{16,12},{20,16},{24,20},{28,24},{5,1},{9,5},{13... | collective-permute-start | bytes 1572872 | tf_op jit(solution)/shard_map/ppermute | solution.py:24
  27.9 8.6 %copy-start.1 = (bf16[2,1024,1024]{2,1,0:T(8,128)(2,1)S(1)}, bf16[2,1024,1024]{2,1,0:T(8,128)(2,1)}, u32[]{:S(2)}) copy-start(bf16[2,1024,1024]{2,1,0:T(8,128)(2,1)} %param.10) | copy-start | bytes 12582916
  30.9 11.9 %collective-permute-start.3 = (bf16[2,128,1280]{2,1,0:T(8,128)(2,1)S(1)}, bf16[2,128,1280]{2,1,0:T(8,128)(2,1)S(1)}, u32[]{:S(2)}, u32[]{:S(2)}) collective-permute-start(bf16[2,128,1280]{2,1,0:T(8,128)(2,1)S(1)} %get-tuple-element.97), channel_id=1, source_target_pairs={{0,1},{1,2},{2,3},{4,5},{5,6},{6,7},{8,9},{9,10},{10,11},{12,13},{... | collective-permute-start | bytes 1966088 | tf_op jit(solution)/shard_map/ppermute | solution.py:22
  32.8 11.7 %collective-permute-start.2 = (bf16[2,128,1280]{2,1,0:T(8,128)(2,1)S(1)}, bf16[2,128,1280]{2,1,0:T(8,128)(2,1)S(1)}, u32[]{:S(2)}, u32[]{:S(2)}) collective-permute-start(bf16[2,128,1280]{2,1,0:T(8,128)(2,1)S(1)} %get-tuple-element.96), channel_id=1, source_target_pairs={{1,0},{2,1},{3,2},{5,4},{6,5},{7,6},{9,8},{10,9},{11,10},{13,12},{... | collective-permute-start | bytes 1966088 | tf_op jit(solution)/shard_map/ppermute | solution.py:24
  46.9 6.3 %collective-permute-start.4 = (f32[4,1,1]{0,2,1:T(1,128)S(1)}, f32[4,1,1]{0,2,1:T(1,128)S(1)}, u32[]{:S(2)}, u32[]{:S(2)}) collective-permute-start(f32[4,1,1]{0,2,1:T(1,128)S(1)} %maximum_bitcast_fusion), channel_id=1, source_target_pairs={{4,0},{8,4},{12,8},{16,12},{20,16},{24,20},{28,24},{5,1},{9,5},{13... | collective-permute-start | bytes 56 | tf_op jit(solution)/shard_map/ppermute | solution.py:24
  51.1 6.4 %collective-permute-start.5 = (f32[4,1,1]{0,2,1:T(1,128)S(1)}, f32[4,1,1]{0,2,1:T(1,128)S(1)}, u32[]{:S(2)}, u32[]{:S(2)}) collective-permute-start(f32[4,1,1]{0,2,1:T(1,128)S(1)} %maximum_bitcast_fusion), channel_id=1, source_target_pairs={{0,4},{4,8},{8,12},{12,16},{16,20},{20,24},{24,28},{1,5},{5,9},{9,... | collective-permute-start | bytes 56 | tf_op jit(solution)/shard_map/ppermute | solution.py:22
  57.5 7.5 %collective-permute-start.6 = (f32[4,1,3]{0,2,1:T(4,128)S(1)}, f32[4,1,3]{0,2,1:T(4,128)S(1)}, u32[]{:S(2)}, u32[]{:S(2)}) collective-permute-start(f32[4,1,3]{0,2,1:T(4,128)S(1)} %pad_maximum_fusion.1), channel_id=1, source_target_pairs={{1,0},{2,1},{3,2},{5,4},{6,5},{7,6},{9,8},{10,9},{11,10},{13,12},{... | collective-permute-start | bytes 152 | tf_op jit(solution)/shard_map/ppermute | solution.py:24
  60.2 5.5 %collective-permute-start.7 = (f32[4,1,3]{0,2,1:T(4,128)S(1)}, f32[4,1,3]{0,2,1:T(4,128)S(1)}, u32[]{:S(2)}, u32[]{:S(2)}) collective-permute-start(f32[4,1,3]{0,2,1:T(4,128)S(1)} %pad_maximum_fusion.1), channel_id=1, source_target_pairs={{0,1},{1,2},{2,3},{4,5},{5,6},{6,7},{8,9},{9,10},{10,11},{12,13},{... | collective-permute-start | bytes 152 | tf_op jit(solution)/shard_map/ppermute | solution.py:22
  67.0 13.1 %slice-start = ((s8[5308416]{0:T(1024)(128)(4,1)}), s8[4194304]{0:T(1024)(128)(4,1)S(1)}, s32[]{:S(2)}) async-start(s8[5308416]{0:T(1024)(128)(4,1)} %bitcast.28), calls=%async_computation | async-start | bytes 8388608
  67.9 12.2 %slice-start.1 = ((s8[5308416]{0:T(1024)(128)(4,1)}), s8[1114112]{0:T(1024)(128)(4,1)S(1)}, s32[]{:S(2)}) async-start(s8[5308416]{0:T(1024)(128)(4,1)} %bitcast.28), calls=%async_computation.1 | async-start | bytes 2228224
  80.1 4.4 %copy-start = (f32[2,1152,1152]{2,1,0:T(8,128)S(1)}, f32[2,1152,1152]{2,1,0:T(8,128)}, u32[]{:S(2)}) copy-start(f32[2,1152,1152]{2,1,0:T(8,128)} %add_multiply_fusion) | copy-start | bytes 31850500
  81.6 42.7 %collective-permute-start.8 = (f32[3,1152,128]{2,1,0:T(8,128)S(1)}, f32[3,1152,128]{2,1,0:T(8,128)S(1)}, u32[]{:S(2)}, u32[]{:S(2)}) collective-permute-start(f32[3,1152,128]{2,1,0:T(8,128)S(1)} %fusion.1), channel_id=1, source_target_pairs={{0,4},{4,8},{8,12},{12,16},{16,20},{20,24},{24,28},{1,5},{5,9},{9,... | collective-permute-start | bytes 5308424 | tf_op jit(solution)/shard_map/ppermute | solution.py:34
  124.3 21.7 %collective-permute-start.9 = (f32[3,128,1024]{2,1,0:T(8,128)S(1)}, f32[3,128,1024]{2,1,0:T(8,128)S(1)}, u32[]{:S(2)}, u32[]{:S(2)}) collective-permute-start(f32[3,128,1024]{2,1,0:T(8,128)S(1)} %fusion.111), channel_id=1, source_target_pairs={{0,1},{1,2},{2,3},{4,5},{5,6},{6,7},{8,9},{9,10},{10,11},{12,13},{... | collective-permute-start | bytes 4718600 | tf_op jit(solution)/shard_map/ppermute | solution.py:34
where the time goes:
time: 154 us; the launch traced here: 153 us
  waiting for transfers between devices  68.5 us (44%)
  other arithmetic  37.4 us (24%)
  starting transfers between devices  27.8 us (18%)
  local copies, waits for them, and re-layouts  14.4 us (9%)
  between operations  4.9 us (3%)
    ppermute x2, waiting for transfers between devices, from_behind(): return lax.ppermute(block, axis, route)  57.4 us
    ppermute x4, starting transfers between devices, extended(): lax.ppermute(head, axis, [((i + 1) % count, i) for i in range(ends)])  13.9 us
    mul x1, other arithmetic, place_piece(): apply_terms(window.astype(jnp.float32), log_gain, offset) * weight[None]  12.2 us
    ppermute x4, starting transfers between devices, extended(): lax.ppermute(tail, axis, [(i, (i + 1) % count) for i in range(ends)])  9.48 us
    ppermute x4, waiting for transfers between devices, extended(): lax.ppermute(tail, axis, [(i, (i + 1) % count) for i in range(ends)])  9.36 us
    mul x2, other arithmetic, place_piece(): weight = weight * row_valid[:, None] * col_valid[None, :]  6.27 us
    reduce_sum x4, other arithmetic, pair_terms(): var_former = jnp.sum(dev_former * dev_former, axis=(-2, -1)) / flat_number  4.59 us
    ppermute x2, starting transfers between devices, from_behind(): return lax.ppermute(block, axis, route)  4.38 us
  transfers between devices with their start and end apart: 10, of which 6 were waited for; matrix products, arithmetic and copies ran while one was open for 16% of the time, Pallas kernels for 0%

commit v1 on v0

v1 whole, which is shorter than its diff:
```python
import jax
import jax.numpy as jnp
from jax import lax
from jax.sharding import PartitionSpec as P

STRIP = 128
SPILL = 128
BLOCK = 128


eps = 1e-06


def from_behind(block, axis, count):
    return lax.ppermute(block, axis, [(i, i + 1) for i in range(count - 1)])


def strip_stats(former, latter, window):
    full = jnp.broadcast_to(window, former.shape)
    number = jnp.sum(full, axis=(-2, -1))
    mean_former = jnp.sum(former * full, axis=(-2, -1)) / number
    mean_latter = jnp.sum(latter * full, axis=(-2, -1)) / number
    dev_former = (former - mean_former[:, None, None]) * full
    dev_latter = (latter - mean_latter[:, None, None]) * full
    var_former = jnp.sum(dev_former * dev_former, axis=(-2, -1)) / number
    var_latter = jnp.sum(dev_latter * dev_latter, axis=(-2, -1)) / number
    covariance = jnp.sum(dev_former * dev_latter, axis=(-2, -1)) / number
    return jnp.stack([mean_former, mean_latter, var_former, var_latter, covariance])


def pair_terms(stats):
    mean_former, mean_latter, var_former, var_latter, covariance = stats
    weight = covariance * covariance / ((var_former + eps) * (var_latter + eps))
    log_ratio = 0.25 * (jnp.log(var_latter + eps) - jnp.log(var_former + eps))
    shift_term = 0.5 * (mean_latter - mean_former)
    return (weight, weight * log_ratio, weight * shift_term)


def corrected_stats(stats, gain_a, level_a, gain_b, level_b):
    mean_former, mean_latter, var_former, var_latter, covariance = stats
    return (
        gain_a * mean_former + level_a,
        gain_b * mean_latter + level_b,
        gain_a * gain_a * var_former,
        gain_b * gain_b * var_latter,
        gain_a * gain_b * covariance,
    )


def tile_terms(horiz_terms, vert_terms):
    first_h = tuple(jnp.pad(item, ((0, 0), (0, 1), (0, 0))) for item in horiz_terms)
    second_h = tuple(jnp.pad(item, ((0, 0), (1, 0), (0, 0))) for item in horiz_terms)
    first_v = tuple(jnp.pad(item, ((0, 1), (0, 0), (0, 0))) for item in vert_terms)
    second_v = tuple(jnp.pad(item, ((1, 0), (0, 0), (0, 0))) for item in vert_terms)
    denominator = 1.0 + first_h[0] + first_v[0] + second_h[0] + second_v[0]
    log_gain = (first_h[1] + first_v[1] - second_h[1] - second_v[1]) / denominator
    offset = (first_h[2] + first_v[2] - second_h[2] - second_v[2]) / denominator
    return log_gain, offset


def grid_solve(horiz_stats, vert_stats):
    gain_one, level_one = tile_terms(pair_terms(horiz_stats), pair_terms(vert_stats))
    scale = jnp.exp(gain_one)
    horiz_two = corrected_stats(
        horiz_stats, scale[:, :-1], level_one[:, :-1], scale[:, 1:], level_one[:, 1:]
    )
    vert_two = corrected_stats(
        vert_stats, scale[:-1], level_one[:-1], scale[1:], level_one[1:]
    )
    gain_two, level_two = tile_terms(pair_terms(horiz_two), pair_terms(vert_two))
    log_gain = gain_one + gain_two
    level = jnp.exp(gain_two) * level_one + level_two
    return log_gain, level


def fade(ids, tile_px):
    return (jnp.minimum(ids, tile_px - 1 - ids) + 1).astype(jnp.float32) / (tile_px / 2.0)


def row_weight(ids, band_low, band_high, tile_px, present):
    live = (ids >= band_low * BLOCK) & (ids < band_high * BLOCK) & (ids >= 0) & (ids < tile_px)
    return live.astype(jnp.float32) * present * fade(ids, tile_px)


def col_weight(ids, tile_px, present):
    live = (ids >= 0) & (ids < tile_px)
    return live.astype(jnp.float32) * present * fade(ids, tile_px)


def piece(source, pads, start, size, rows_w, cols_w, log_gain, level):
    padded = jnp.pad(source, pads)
    zero = jnp.zeros((), jnp.int32)
    window = lax.dynamic_slice(padded, (zero, start[0], start[1]), size)
    weight = rows_w[:, None] * cols_w[None, :]
    values = (
        jnp.exp(log_gain)[:, None, None] * window.astype(jnp.float32) + level[:, None, None]
    ) * weight[None]
    return values, weight


def local(tiles, extents, offsets, bands):
    planes, tile_px, _ = tiles.shape
    n_row = lax.axis_size("row")
    n_col = lax.axis_size("col")
    row_index = lax.axis_index("row")
    col_index = lax.axis_index("col")
    width = STRIP

    right_strip = tiles[:, :, tile_px - width :]
    down_strip = tiles[:, tile_px - width :, :]
    corner = tiles[:, tile_px - width :, tile_px - width :]
    from_left = from_behind(right_strip, "col", n_col)
    from_up = from_behind(down_strip, "row", n_row)
    diagonal = [
        (j * n_row + i, (j + 1) * n_row + i + 1) for i in range(n_row - 1) for j in range(n_col - 1)
    ]
    from_corner = lax.ppermute(corner, ("col", "row"), diagonal)

    left_col = jnp.maximum(col_index - 1, 0)
    upper_row = jnp.maximum(row_index - 1, 0)
    strip_ids = jnp.arange(width, dtype=jnp.int32)
    horiz_window = (strip_ids < extents[0, row_index, left_col]).astype(jnp.float32)[None, None, :]
    vert_window = (strip_ids < extents[1, upper_row, col_index]).astype(jnp.float32)[None, :, None]
    horiz = strip_stats(
        from_left.astype(jnp.float32), tiles[:, :, :width].astype(jnp.float32), horiz_window
    )
    vert = strip_stats(
        from_up.astype(jnp.float32), tiles[:, :width, :].astype(jnp.float32), vert_window
    )
    gathered = lax.all_gather(jnp.stack([horiz, vert]), ("col", "row"))
    gathered = gathered.reshape((n_col, n_row) + gathered.shape[1:]).swapaxes(0, 1)
    horiz_stats = tuple(gathered[:, 1:, 0, k] for k in range(5))
    vert_stats = tuple(gathered[1:, :, 1, k] for k in range(5))
    log_gain, level = grid_solve(horiz_stats, vert_stats)

    def terms_at(r, c):
        return log_gain[r, c], level[r, c]

    has_left = (col_index > 0).astype(jnp.float32)
    has_up = (row_index > 0).astype(jnp.float32)
    ids = jnp.arange(tile_px, dtype=jnp.int32)
    edge = jnp.arange(width, dtype=jnp.int32)

    def weights_of(r, c, row_ids, col_ids, present):
        rows_w = row_weight(row_ids, bands[0, r, c], bands[1, r, c], tile_px, present)
        cols_w = col_weight(col_ids, tile_px, jnp.float32(1.0))
        return rows_w, cols_w

    top, left = offsets[0, row_index, col_index], offsets[1, row_index, col_index]
    rows_w, cols_w = weights_of(row_index, col_index, ids - top, ids - left, jnp.float32(1.0))
    own_vals, own_w = piece(
        tiles, ((0, 0), (SPILL, 0), (SPILL, 0)), (SPILL - top, SPILL - left),
        (planes, tile_px, tile_px), rows_w, cols_w, *terms_at(row_index, col_index),
    )
    top_l, left_l = offsets[0, row_index, left_col], offsets[1, row_index, left_col]
    rows_w, cols_w = weights_of(
        row_index, left_col, ids - top_l, edge + tile_px - left_l, has_left
    )
    left_vals, left_w = piece(
        from_left, ((0, 0), (SPILL, 0), (0, width)), (SPILL - top_l, width - left_l),
        (planes, tile_px, width), rows_w, cols_w, *terms_at(row_index, left_col),
    )
    top_u, left_u = offsets[0, upper_row, col_index], offsets[1, upper_row, col_index]
    rows_w, cols_w = weights_of(
        upper_row, col_index, edge + tile_px - top_u, ids - left_u, has_up
    )
    up_vals, up_w = piece(
        from_up, ((0, 0), (0, width), (SPILL, 0)), (width - top_u, SPILL - left_u),
        (planes, width, tile_px), rows_w, cols_w, *terms_at(upper_row, col_index),
    )
    top_c, left_c = offsets[0, upper_row, left_col], offsets[1, upper_row, left_col]
    rows_w, cols_w = weights_of(
        upper_row, left_col, edge + tile_px - top_c, edge + tile_px - left_c, has_up * has_left
    )
    corner_vals, corner_w = piece(
        from_corner, ((0, 0), (0, width), (0, width)), (width - top_c, width - left_c),
        (planes, width, width), rows_w, cols_w, *terms_at(upper_row, left_col),
    )

    blended = own_vals.at[:, :, :width].add(left_vals)
    blended = blended.at[:, :width, :].add(up_vals)
    blended = blended.at[:, :width, :width].add(corner_vals)
    weight = own_w.at[:, :width].add(left_w)
    weight = weight.at[:width, :].add(up_w)
    weight = weight.at[:width, :width].add(corner_w)
    return blended, weight


def solution(mesh):
    return jax.shard_map(
        local,
        mesh=mesh,
        in_specs=(P(None, "row", "col"), P(), P(), P()),
        out_specs=(P(None, "row", "col"), P("row", "col")),
        check_vma=False,
    )
```

time: 154 us -> 105 us (0.68)
  the two profiles are of different devices: /device:TPU:10 before, /device:TPU:0 now
where the time goes in v1:
time: 105 us; the launch traced here: 104 us
  blocking collectives  36.9 us (35%)
  other arithmetic  28.3 us (27%)
  between operations  15.7 us (15%)
  local copies, waits for them, and re-layouts  12.4 us (12%)
  starting transfers between devices  11 us (10%)
    all_gather x1, blocking collectives, local(): gathered = lax.all_gather(jnp.stack([horiz, vert]), ('col', 'row'))  36.9 us
    ppermute x2, starting transfers between devices, from_behind(): return lax.ppermute(block, axis, [(i, i + 1) for i in range(count - 1)])  6.72 us
    mul x1, other arithmetic, piece(): (jnp.exp(log_gain)[:, None, None] * window.astype(jnp.float32) + level[:,...  5.23 us
    ppermute x1, starting transfers between devices, local(): from_corner = lax.ppermute(corner, ('col', 'row'), diagonal)  4.33 us
    mul x3, other arithmetic, row_weight(): return live.astype(jnp.float32) * present * fade(ids, tile_px)  3.65 us
    reduce_sum x2, other arithmetic, strip_stats(): covariance = jnp.sum(dev_former * dev_latter, axis=(-2, -1)) / number  3.52 us
    unnamed x2, local copies, waits for them, and re-layouts  3.4 us
    reduce_sum x2, other arithmetic, strip_stats(): mean_latter = jnp.sum(latter * full, axis=(-2, -1)) / number  2.93 us
  transfers between devices with their start and end apart: 3, of which 0 were waited for; matrix products, arithmetic and copies ran while one was open for 35% of the time, Pallas kernels for 0%

profile of v1, /device:TPU:0, one launch (start us, length us, event | category | flops | bytes accessed | tf_op | source)
XLA Modules:
  0.0 104.3 jit_solution(5995284832800290218)
XLA Ops:
  0.6 0.9 slice.233
  1.5 4.3 %collective-permute-start.2 = (bf16[2,128,128]{2,1,0:T(8,128)(2,1)S(1)}, bf16[2,128,128]{2,1,0:T(8,128)(2,1)S(1)}, u32[]{:S(2)}, u32[]{:S(2)}) collective-permute-start(bf16[2,128,128]{2,1,0:T(8,128)(2,1)S(1)} %slice.233), channel_id=1, source_target_pairs={{0,5},{4,9},{8,13},{12,17},{16,21},{20,25},{24,29},{1,6},{5,10},{9... | collective-permute-start | bytes 196616 | tf_op jit(solution)/shard_map/ppermute | solution.py:117
  5.8 1.1 %slice.208 = bf16[2,1024,128]{2,1,0:T(8,128)(2,1)S(1)} slice(bf16[2,1024,1024]{2,1,0:T(8,128)(2,1)} %param.16), slice={[0:2], [0:1024], [896:1024]} | slice | bytes 1048576 | tf_op jit(solution)/shard_map/slice | solution.py:109
  6.9 3.5 %collective-permute-start = (bf16[2,1024,128]{2,1,0:T(8,128)(2,1)S(1)}, bf16[2,1024,128]{2,1,0:T(8,128)(2,1)S(1)}, u32[]{:S(2)}, u32[]{:S(2)}) collective-permute-start(bf16[2,1024,128]{2,1,0:T(8,128)(2,1)S(1)} %slice.208), channel_id=1, source_target_pairs={{0,4},{4,8},{8,12},{12,16},{16,20},{20,24},{24,28},{1,5},{5,9},{9,... | collective-permute-start | bytes 1572872 | tf_op jit(solution)/shard_map/ppermute | solution.py:15
  10.4 1.1 %slice.210 = bf16[2,128,1024]{2,1,0:T(8,128)(2,1)S(1)} slice(bf16[2,1024,1024]{2,1,0:T(8,128)(2,1)} %param.16), slice={[0:2], [896:1024], [0:1024]} | slice | bytes 1048576 | tf_op jit(solution)/shard_map/slice | solution.py:110
  11.5 3.3 %collective-permute-start.1 = (bf16[2,128,1024]{2,1,0:T(8,128)(2,1)S(1)}, bf16[2,128,1024]{2,1,0:T(8,128)(2,1)S(1)}, u32[]{:S(2)}, u32[]{:S(2)}) collective-permute-start(bf16[2,128,1024]{2,1,0:T(8,128)(2,1)S(1)} %slice.210), channel_id=1, source_target_pairs={{0,1},{1,2},{2,3},{4,5},{5,6},{6,7},{8,9},{9,10},{10,11},{12,13},{... | collective-permute-start | bytes 1572872 | tf_op jit(solution)/shard_map/ppermute | solution.py:15
  14.7 0.7 compare_reduce_fusion
  15.4 1.5 %constant_dynamic-slice_fusion.18 = (s32[1,1,1]{2,1,0:T(1,128)}, s32[1,1,1]{2,1,0:T(1,128)}, s32[1,1,1]{2,1,0:T(1,128)}, s32[1,1,1]{2,1,0:T(1,128)}, s32[1,1,1]{...) fusion(s32[2,4,8]{2,1,0:T(4,128)} %param.18, s32[]{:T(128)S(6)} %max.7, s32[]{:T(128)S(6)} %max.6, ...), kind=kLoop, calls=%fused_computation.170 | loop fusion | bytes 80 | tf_op jit(solution)/shard_map/dynamic_slice | solution.py:171
  26.8 1.3 %and_select_fusion = (f32[128]{0:T(128)S(1)}, f32[128]{0:T(128)S(1)}) fusion(s32[]{:T(128)} %bitcast.39, s32[]{:T(128)} %bitcast.31), kind=kLoop, calls=%fused_computation.180 | loop fusion | flops 2688 | bytes 1032 | tf_op jit(solution)/shard_map/mul | solution.py:87
  28.1 1.3 %constant_dynamic-slice_fusion.16 = (s32[1,1,1]{2,1,0:T(1,128)}, s32[1,1,1]{2,1,0:T(1,128)}) fusion(s32[2,4,8]{2,1,0:T(4,128)} %param.17, s32[]{:T(128)S(6)} %select_n.20, s32[]{:T(128)S(6)} %max.6, s32[]{:T(128)S(6)} %max.7, s32[]{:T(128)S(6)} %select_n.21), kind=kLoop, calls=%fused_computation.67 | loop fusion | bytes 32 | tf_op jit(solution)/shard_map/dynamic_slice | solution.py:122
  30.1 1.6 %constant_dynamic-slice_fusion = (s32[1,1,1]{2,1,0:T(1,128)}, s32[1,1,1]{2,1,0:T(1,128)}, s32[1,1,1]{2,1,0:T(1,128)}, s32[1,1,1]{2,1,0:T(1,128)}, s32[1,1,1]{2,1...) fusion(s32[2,4,8]{2,1,0:T(4,128)} %param.19, s32[]{:T(128)S(6)} %max.7, s32[]{:T(128)S(6)} %max.6, ...), kind=kLoop, calls=%fused_computation.49 | loop fusion | bytes 80 | tf_op jit(solution)/shard_map/dynamic_slice | solution.py:145
  36.7 1.2 %fusion.39 = (f32[1024]{0:T(1024)S(1)}, f32[1024]{0:T(1024)S(1)}) fusion(s32[]{:T(128)} %bitcast.29, s32[]{:T(128)} %bitcast.28, s32[]{:T(128)} %bitcast.22, s32[]{:T(128)} %bitcast.23), kind=kLoop, calls=%fused_computation.96 | loop fusion | flops 24576 | bytes 8208 | tf_op jit(solution)/shard_map/mul | solution.py:82
  37.9 1.2 %fusion.94 = (f32[128]{0:T(128)S(1)}, f32[128]{0:T(128)S(1)}) fusion(f32[]{:T(128)S(6)} %convert_element_type.158, s32[]{:T(128)} %bitcast.37, s32[]{:T(128)} %bitcast.36, s32[]{:T(128)} %bitcast.34, f32[]{:T(128)S(6)} %mul.506, s32[]{:T(128)} %bitcast.41, s32[]{:T(128)} %bitcast.40, s32[]{:T(128)} %bitcast.38), kind=kLoop, calls=%fused_computation.202 | loop fusion | flops 3968 | bytes 1056 | tf_op jit(solution)/shard_map/mul | solution.py:82
  39.8 1.2 %fusion.47 = (f32[1024]{0:T(1024)S(1)}, f32[1024]{0:T(1024)S(1)}) fusion(f32[]{:T(128)S(6)} %convert_element_type.154, s32[]{:T(128)} %bitcast.33, s32[]{:T(128)} %bitcast.32, s32[]{:T(128)} %bitcast.30, s32[]{:T(128)} %bitcast.35), kind=kLoop, calls=%fused_computation.104 | loop fusion | flops 25600 | bytes 8212 | tf_op jit(solution)/shard_map/mul | solution.py:82
  41.0 2.4 %broadcast_multiply_fusion = f32[1024,1024]{1,0:T(8,128)} fusion(f32[1024]{0:T(1024)S(1)} %get-tuple-element.155, f32[1024]{0:T(1024)S(1)} %get-tuple-element.154), kind=kLoop, calls=%fused_computation.2 | loop fusion | flops 1048576 | bytes 4202496 | tf_op jit(solution)/shard_map/mul | solution.py:94
  43.3 1.4 %fusion.6 = (f32[2]{0:T(128)S(1)}, f32[2]{0:T(128)S(1)}, f32[2]{0:T(128)S(1)}) fusion(f32[128]{0:T(128)S(1)} %compare_convert_fusion.1, bf16[2,1024,1024]{2,1,0:T(8,128)(2,1)} %param.16, bf16[2,1024,128]{2,1,0:T(8,128)(2,1)S(1)} %collective-permute-done), kind=kLoop, calls=%fused_computation.19 | loop fusion | flops 1835002 | bytes 1049112 | tf_op jit(solution)/shard_map/reduce_sum | solution.py:22
  45.0 1.7 %fusion.5 = (f32[2]{0:T(128)S(1)}, f32[2]{0:T(128)S(1)}, f32[2]{0:T(128)S(1)}) fusion(bf16[2,1024,128]{2,1,0:T(8,128)(2,1)S(1)} %collective-permute-done, f32[2]{0:T(128)S(1)} %get-tuple-element.147, f32[2]{0:T(128)S(1)} %get-tuple-element.148, f32[128]{0:T(128)S(1)} %compare_convert_fusion.1, bf16[2,1024,1024]{2,1,0:T(8,128)(2,1)} %param.16), kind=kLoop, calls=%fused_computation.18 | loop fusion | flops 3145722 | bytes 1049128 | tf_op jit(solution)/shard_map/reduce_sum | solution.py:27
  47.0 1.5 %fusion.16 = (f32[2]{0:T(128)S(1)}, f32[2]{0:T(128)S(1)}, f32[2]{0:T(128)S(1)}) fusion(f32[128]{0:T(128)S(1)} %compare_convert_fusion, bf16[2,1024,1024]{2,1,0:T(8,128)(2,1)} %param.16, bf16[2,128,1024]{2,1,0:T(8,128)(2,1)S(1)} %collective-permute-done.1), kind=kLoop, calls=%fused_computation.29 | loop fusion | flops 1835002 | bytes 1049112 | tf_op jit(solution)/shard_map/reduce_sum | solution.py:22
  48.7 1.8 %fusion.15 = (f32[2]{0:T(128)S(1)}, f32[2]{0:T(128)S(1)}, f32[2]{0:T(128)S(1)}) fusion(bf16[2,128,1024]{2,1,0:T(8,128)(2,1)S(1)} %collective-permute-done.1, f32[2]{0:T(128)S(1)} %get-tuple-element.152, f32[2]{0:T(128)S(1)} %get-tuple-element.153, f32[128]{0:T(128)S(1)} %compare_convert_fusion, bf16[2,1024,1024]{2,1,0:T(8,128)(2,1)} %param.16), kind=kLoop, calls=%fused_computation.28 | loop fusion | flops 3145722 | bytes 1049128 | tf_op jit(solution)/shard_map/reduce_sum | solution.py:27
  51.0 36.9 %all-gather = f32[64,5,2]{1,2,0:T(2,128)S(1)} all-gather(f32[2,5,2]{1,2,0:T(2,128)S(1)} %pad_maximum_fusion), channel_id=2, replica_groups=mesh['col'=8,'row'=4] {'col','row'}, dimensions={0}, use_global_device_ids=true | all-gather | bytes 2640 | tf_op jit(solution)/shard_map/all_gather | solution.py:130
  88.9 5.2 %add_multiply_fusion = f32[2,1024,1024]{2,1,0:T(8,128)S(1)} fusion(s32[]{:T(128)S(6)} %select_n.22, s32[]{:T(128)S(6)} %select_n.23, bf16[2,1024,1024]{2,1,0:T(8,128)(2,1)} %param.16, f32[1024,1024]{1,0:T(8,128)} %broadcast_multiply_fusion, f32[2]{0:T(128)S(1)} %get-tuple-element.87, f32[2]{0:T(128)S(1)} %get-tuple-element.162), kind=kLoop, calls=%fused_computation | loop fusion | flops 8388608 | bytes 16777240 | tf_op jit(solution)/shard_map/mul | solution.py:95
  94.1 2.7 %fusion.21 = (f32[1024,1024]{1,0:T(8,128)}, f32[1024,128]{1,0:T(8,128)S(1)}) fusion(f32[1024,1024]{1,0:T(8,128)} %broadcast_multiply_fusion, pred[]{:T(512)} %compare_reduce_fusion, f32[128]{0:T(128)S(1)} %get-tuple-element.159, f32[1024]{0:T(1024)S(1)} %get-tuple-element.156), kind=kLoop, calls=%fused_computation.37 | loop fusion | flops 393216 | bytes 1577984 | tf_op jit(solution)/shard_map/scatter-add | solution.py:183
  96.8 2.0 %constant_dynamic-update-slice_fusion = (f32[1024,1024]{1,0:T(8,128)}, f32[128,1024]{1,0:T(8,128)S(1)}, f32[128,1024]{1,0:T(8,128)S(1)}) fusion(f32[1024,1024]{1,0:T(8,128)} %get-tuple-element.122, f32[1024]{0:T(1024)S(1)} %get-tuple-element.157, f32[128]{0:T(128)S(1)} %get-tuple-element.160), kind=kLoop, calls=%fused_computation.51 | loop fusion | flops 262144 | bytes 2101760 | tf_op jit(solution)/shard_map/scatter-add | solution.py:184
  101.0 3.4 %copy-done = f32[2,1024,1024]{2,1,0:T(8,128)} copy-done((f32[2,1024,1024]{2,1,0:T(8,128)}, f32[2,1024,1024]{2,1,0:T(8,128)S(1)}, u32[]{:S(2)}) %copy-start) | copy-done | bytes 8388632
  (42 shorter events, 5.5 us)
Async XLA Ops:
  1.5 99.3 %collective-permute-start.2 = (bf16[2,128,128]{2,1,0:T(8,128)(2,1)S(1)}, bf16[2,128,128]{2,1,0:T(8,128)(2,1)S(1)}, u32[]{:S(2)}, u32[]{:S(2)}) collective-permute-start(bf16[2,128,128]{2,1,0:T(8,128)(2,1)S(1)} %slice.233), channel_id=1, source_target_pairs={{0,5},{4,9},{8,13},{12,17},{16,21},{20,25},{24,29},{1,6},{5,10},{9... | collective-permute-start | bytes 196616 | tf_op jit(solution)/shard_map/ppermute | solution.py:117
  6.9 36.4 %collective-permute-start = (bf16[2,1024,128]{2,1,0:T(8,128)(2,1)S(1)}, bf16[2,1024,128]{2,1,0:T(8,128)(2,1)S(1)}, u32[]{:S(2)}, u32[]{:S(2)}) collective-permute-start(bf16[2,1024,128]{2,1,0:T(8,128)(2,1)S(1)} %slice.208), channel_id=1, source_target_pairs={{0,4},{4,8},{8,12},{12,16},{16,20},{20,24},{24,28},{1,5},{5,9},{9,... | collective-permute-start | bytes 1572872 | tf_op jit(solution)/shard_map/ppermute | solution.py:15
  11.5 35.5 %collective-permute-start.1 = (bf16[2,128,1024]{2,1,0:T(8,128)(2,1)S(1)}, bf16[2,128,1024]{2,1,0:T(8,128)(2,1)S(1)}, u32[]{:S(2)}, u32[]{:S(2)}) collective-permute-start(bf16[2,128,1024]{2,1,0:T(8,128)(2,1)S(1)} %slice.210), channel_id=1, source_target_pairs={{0,1},{1,2},{2,3},{4,5},{5,6},{6,7},{8,9},{9,10},{10,11},{12,13},{... | collective-permute-start | bytes 1572872 | tf_op jit(solution)/shard_map/ppermute | solution.py:15
  100.9 3.4 %copy-start = (f32[2,1024,1024]{2,1,0:T(8,128)}, f32[2,1024,1024]{2,1,0:T(8,128)S(1)}, u32[]{:S(2)}) copy-start(f32[2,1024,1024]{2,1,0:T(8,128)S(1)} %fusion.22) | copy-start | bytes 25165828

commit v2 on v1

--- a/solution.py
+++ b/solution.py
@@ -127,8 +127,11 @@
     vert = strip_stats(
         from_up.astype(jnp.float32), tiles[:, :width, :].astype(jnp.float32), vert_window
     )
-    gathered = lax.all_gather(jnp.stack([horiz, vert]), ("col", "row"))
-    gathered = gathered.reshape((n_col, n_row) + gathered.shape[1:]).swapaxes(0, 1)
+    own_stats = jnp.stack([horiz, vert])
+    slot = (
+        (jnp.arange(n_row)[:, None] == row_index) & (jnp.arange(n_col)[None, :] == col_index)
+    ).astype(jnp.float32)
+    gathered = lax.psum(slot[:, :, None, None, None] * own_stats[None, None], ("col", "row"))
     horiz_stats = tuple(gathered[:, 1:, 0, k] for k in range(5))
     vert_stats = tuple(gathered[1:, :, 1, k] for k in range(5))
     log_gain, level = grid_solve(horiz_stats, vert_stats)

time: 105 us -> 109 us (1.038)
  blocking collectives: 36.9 us -> 39.8 us
    psum x0 -> x1, blocking collectives: none -> 39.8 us  [local(): lax.psum(slot[:, :, None, None, None] * own_stats[None, None], ('col', 'r...]
    all_gather x1 -> x0, blocking collectives: 36.9 us -> none  [local(): gathered = lax.all_gather(jnp.stack([horiz, vert]), ('col', 'row'))]
  transfers between devices with their start and end apart: 3 -> 3, of which waited for: 0 -> 0; matrix products, arithmetic and copies ran while one was open for 35% -> 34% of each run, Pallas kernels for 0% -> 0%
where the time goes in v2:
time: 109 us; the launch traced here: 108 us
  blocking collectives  39.8 us (37%)
  other arithmetic  28.5 us (26%)
  between operations  15.9 us (15%)
  local copies, waits for them, and re-layouts  12.3 us (11%)
  starting transfers between devices  11 us (10%)
    psum x1, blocking collectives, local(): lax.psum(slot[:, :, None, None, None] * own_stats[None, None], ('col', 'r...  39.8 us
    ppermute x2, starting transfers between devices, from_behind(): return lax.ppermute(block, axis, [(i, i + 1) for i in range(count - 1)])  6.72 us
    mul x1, other arithmetic, piece(): (jnp.exp(log_gain)[:, None, None] * window.astype(jnp.float32) + level[:,...  5.32 us
    ppermute x1, starting transfers between devices, local(): from_corner = lax.ppermute(corner, ('col', 'row'), diagonal)  4.33 us
    mul x3, other arithmetic, row_weight(): return live.astype(jnp.float32) * present * fade(ids, tile_px)  3.72 us
    reduce_sum x2, other arithmetic, strip_stats(): covariance = jnp.sum(dev_former * dev_latter, axis=(-2, -1)) / number  3.52 us
    unnamed x2, local copies, waits for them, and re-layouts  3.4 us
    reduce_sum x2, other arithmetic, strip_stats(): mean_latter = jnp.sum(latter * full, axis=(-2, -1)) / number  2.93 us
  transfers between devices with their start and end apart: 3, of which 0 were waited for; matrix products, arithmetic and copies ran while one was open for 34% of the time, Pallas kernels for 0%

profile of v2, /device:TPU:0, one launch (start us, length us, event | category | flops | bytes accessed | tf_op | source)
XLA Modules:
  0.0 107.5 jit_solution(3838218047312337407)
XLA Ops:
  0.6 0.9 slice.233
  1.5 4.3 %collective-permute-start.2 = (bf16[2,128,128]{2,1,0:T(8,128)(2,1)S(1)}, bf16[2,128,128]{2,1,0:T(8,128)(2,1)S(1)}, u32[]{:S(2)}, u32[]{:S(2)}) collective-permute-start(bf16[2,128,128]{2,1,0:T(8,128)(2,1)S(1)} %slice.233), channel_id=1, source_target_pairs={{0,5},{4,9},{8,13},{12,17},{16,21},{20,25},{24,29},{1,6},{5,10},{9... | collective-permute-start | bytes 196616 | tf_op jit(solution)/shard_map/ppermute | solution.py:117
  5.8 1.1 %slice.208 = bf16[2,1024,128]{2,1,0:T(8,128)(2,1)S(1)} slice(bf16[2,1024,1024]{2,1,0:T(8,128)(2,1)} %param.16), slice={[0:2], [0:1024], [896:1024]} | slice | bytes 1048576 | tf_op jit(solution)/shard_map/slice | solution.py:109
  6.9 3.5 %collective-permute-start = (bf16[2,1024,128]{2,1,0:T(8,128)(2,1)S(1)}, bf16[2,1024,128]{2,1,0:T(8,128)(2,1)S(1)}, u32[]{:S(2)}, u32[]{:S(2)}) collective-permute-start(bf16[2,1024,128]{2,1,0:T(8,128)(2,1)S(1)} %slice.208), channel_id=1, source_target_pairs={{0,4},{4,8},{8,12},{12,16},{16,20},{20,24},{24,28},{1,5},{5,9},{9,... | collective-permute-start | bytes 1572872 | tf_op jit(solution)/shard_map/ppermute | solution.py:15
  10.4 1.1 %slice.210 = bf16[2,128,1024]{2,1,0:T(8,128)(2,1)S(1)} slice(bf16[2,1024,1024]{2,1,0:T(8,128)(2,1)} %param.16), slice={[0:2], [896:1024], [0:1024]} | slice | bytes 1048576 | tf_op jit(solution)/shard_map/slice | solution.py:110
  11.5 3.3 %collective-permute-start.1 = (bf16[2,128,1024]{2,1,0:T(8,128)(2,1)S(1)}, bf16[2,128,1024]{2,1,0:T(8,128)(2,1)S(1)}, u32[]{:S(2)}, u32[]{:S(2)}) collective-permute-start(bf16[2,128,1024]{2,1,0:T(8,128)(2,1)S(1)} %slice.210), channel_id=1, source_target_pairs={{0,1},{1,2},{2,3},{4,5},{5,6},{6,7},{8,9},{9,10},{10,11},{12,13},{... | collective-permute-start | bytes 1572872 | tf_op jit(solution)/shard_map/ppermute | solution.py:15
  15.5 1.5 %constant_dynamic-slice_fusion.18 = (s32[1,1,1]{2,1,0:T(1,128)}, s32[1,1,1]{2,1,0:T(1,128)}, s32[1,1,1]{2,1,0:T(1,128)}, s32[1,1,1]{2,1,0:T(1,128)}, s32[1,1,1]{...) fusion(s32[2,4,8]{2,1,0:T(4,128)} %param.18, s32[]{:T(128)S(6)} %max.7, s32[]{:T(128)S(6)} %max.6, ...), kind=kLoop, calls=%fused_computation.171 | loop fusion | bytes 80 | tf_op jit(solution)/shard_map/dynamic_slice | solution.py:174
  26.8 1.2 %and_select_fusion = (f32[128]{0:T(128)S(1)}, f32[128]{0:T(128)S(1)}) fusion(s32[]{:T(128)} %bitcast.37, s32[]{:T(128)} %bitcast.29), kind=kLoop, calls=%fused_computation.181 | loop fusion | flops 2688 | bytes 1032 | tf_op jit(solution)/shard_map/mul | solution.py:87
  28.0 1.3 %constant_dynamic-slice_fusion.16 = (s32[1,1,1]{2,1,0:T(1,128)}, s32[1,1,1]{2,1,0:T(1,128)}) fusion(s32[2,4,8]{2,1,0:T(4,128)} %param.17, s32[]{:T(128)S(6)} %select_n.20, s32[]{:T(128)S(6)} %max.6, s32[]{:T(128)S(6)} %max.7, s32[]{:T(128)S(6)} %select_n.21), kind=kLoop, calls=%fused_computation.68 | loop fusion | bytes 32 | tf_op jit(solution)/shard_map/dynamic_slice | solution.py:122
  30.6 1.6 %constant_dynamic-slice_fusion = (s32[1,1,1]{2,1,0:T(1,128)}, s32[1,1,1]{2,1,0:T(1,128)}, s32[1,1,1]{2,1,0:T(1,128)}, s32[1,1,1]{2,1,0:T(1,128)}, s32[1,1,1]{2,1...) fusion(s32[2,4,8]{2,1,0:T(4,128)} %param.19, s32[]{:T(128)S(6)} %max.7, s32[]{:T(128)S(6)} %max.6, ...), kind=kLoop, calls=%fused_computation.50 | loop fusion | bytes 80 | tf_op jit(solution)/shard_map/dynamic_slice | solution.py:148
  37.3 1.2 %fusion.39 = (f32[1024]{0:T(1024)S(1)}, f32[1024]{0:T(1024)S(1)}) fusion(s32[]{:T(128)} %bitcast.27, s32[]{:T(128)} %bitcast.26, s32[]{:T(128)} %bitcast.20, s32[]{:T(128)} %bitcast.21), kind=kLoop, calls=%fused_computation.97 | loop fusion | flops 24576 | bytes 8208 | tf_op jit(solution)/shard_map/mul | solution.py:82
  38.5 1.3 %fusion.47 = (f32[1024]{0:T(1024)S(1)}, f32[1024]{0:T(1024)S(1)}) fusion(f32[]{:T(128)S(6)} %convert_element_type.162, s32[]{:T(128)} %bitcast.31, s32[]{:T(128)} %bitcast.30, s32[]{:T(128)} %bitcast.28, s32[]{:T(128)} %bitcast.33), kind=kLoop, calls=%fused_computation.105 | loop fusion | flops 25600 | bytes 8212 | tf_op jit(solution)/shard_map/mul | solution.py:82
  39.8 1.2 %fusion.94 = (f32[128]{0:T(128)S(1)}, f32[128]{0:T(128)S(1)}) fusion(f32[]{:T(128)S(6)} %convert_element_type.166, s32[]{:T(128)} %bitcast.35, s32[]{:T(128)} %bitcast.34, s32[]{:T(128)} %bitcast.32, f32[]{:T(128)S(6)} %mul.522, s32[]{:T(128)} %bitcast.39, s32[]{:T(128)} %bitcast.38, s32[]{:T(128)} %bitcast.36), kind=kLoop, calls=%fused_computation.204 | loop fusion | flops 3968 | bytes 1056 | tf_op jit(solution)/shard_map/mul | solution.py:82
  41.1 2.4 %broadcast_multiply_fusion = f32[1024,1024]{1,0:T(8,128)} fusion(f32[1024]{0:T(1024)S(1)} %get-tuple-element.155, f32[1024]{0:T(1024)S(1)} %get-tuple-element.154), kind=kLoop, calls=%fused_computation.2 | loop fusion | flops 1048576 | bytes 4202496 | tf_op jit(solution)/shard_map/mul | solution.py:94
  43.5 1.4 %fusion.6 = (f32[2]{0:T(128)S(1)}, f32[2]{0:T(128)S(1)}, f32[2]{0:T(128)S(1)}) fusion(f32[128]{0:T(128)S(1)} %compare_convert_fusion.1, bf16[2,1024,1024]{2,1,0:T(8,128)(2,1)} %param.16, bf16[2,1024,128]{2,1,0:T(8,128)(2,1)S(1)} %collective-permute-done), kind=kLoop, calls=%fused_computation.19 | loop fusion | flops 1835002 | bytes 1049112 | tf_op jit(solution)/shard_map/reduce_sum | solution.py:22
  45.1 1.7 %fusion.5 = (f32[2]{0:T(128)S(1)}, f32[2]{0:T(128)S(1)}, f32[2]{0:T(128)S(1)}) fusion(bf16[2,1024,128]{2,1,0:T(8,128)(2,1)S(1)} %collective-permute-done, f32[2]{0:T(128)S(1)} %get-tuple-element.147, f32[2]{0:T(128)S(1)} %get-tuple-element.148, f32[128]{0:T(128)S(1)} %compare_convert_fusion.1, bf16[2,1024,1024]{2,1,0:T(8,128)(2,1)} %param.16), kind=kLoop, calls=%fused_computation.18 | loop fusion | flops 3145722 | bytes 1049128 | tf_op jit(solution)/shard_map/reduce_sum | solution.py:27
  47.1 1.5 %fusion.16 = (f32[2]{0:T(128)S(1)}, f32[2]{0:T(128)S(1)}, f32[2]{0:T(128)S(1)}) fusion(f32[128]{0:T(128)S(1)} %compare_convert_fusion, bf16[2,1024,1024]{2,1,0:T(8,128)(2,1)} %param.16, bf16[2,128,1024]{2,1,0:T(8,128)(2,1)S(1)} %collective-permute-done.1), kind=kLoop, calls=%fused_computation.29 | loop fusion | flops 1835002 | bytes 1049112 | tf_op jit(solution)/shard_map/reduce_sum | solution.py:22
  48.8 1.8 %fusion.15 = (f32[2]{0:T(128)S(1)}, f32[2]{0:T(128)S(1)}, f32[2]{0:T(128)S(1)}) fusion(bf16[2,128,1024]{2,1,0:T(8,128)(2,1)S(1)} %collective-permute-done.1, f32[2]{0:T(128)S(1)} %get-tuple-element.152, f32[2]{0:T(128)S(1)} %get-tuple-element.153, f32[128]{0:T(128)S(1)} %compare_convert_fusion, bf16[2,1024,1024]{2,1,0:T(8,128)(2,1)} %param.16), kind=kLoop, calls=%fused_computation.28 | loop fusion | flops 3145722 | bytes 1049128 | tf_op jit(solution)/shard_map/reduce_sum | solution.py:27
  51.3 39.8 %psum.7 = f32[4,8,2,5,2]{1,4,0,3,2:T(2,128)S(1)} all-reduce(f32[4,8,2,5,2]{1,4,0,3,2:T(2,128)S(1)} %broadcast_multiply_fusion.4), channel_id=1, replica_groups=mesh['col'=8,'row'=4] {'col','row'}, use_global_device_ids=true, to_apply=%region_12.0 | all-reduce | flops 640 | bytes 5120 | tf_op jit(solution)/shard_map/psum | solution.py:134
  91.9 5.3 %add_multiply_fusion = f32[2,1024,1024]{2,1,0:T(8,128)S(1)} fusion(s32[]{:T(128)S(6)} %select_n.22, s32[]{:T(128)S(6)} %select_n.23, bf16[2,1024,1024]{2,1,0:T(8,128)(2,1)} %param.16, f32[1024,1024]{1,0:T(8,128)} %broadcast_multiply_fusion, f32[2]{0:T(128)S(1)} %get-tuple-element.87, f32[2]{0:T(128)S(1)} %get-tuple-element.162), kind=kLoop, calls=%fused_computation | loop fusion | flops 8388608 | bytes 16777240 | tf_op jit(solution)/shard_map/mul | solution.py:95
  97.3 2.7 %fusion.21 = (f32[1024,1024]{1,0:T(8,128)}, f32[1024,128]{1,0:T(8,128)S(1)}) fusion(f32[1024,1024]{1,0:T(8,128)} %broadcast_multiply_fusion, pred[]{:T(512)} %compare_reduce_fusion, f32[128]{0:T(128)S(1)} %get-tuple-element.159, f32[1024]{0:T(1024)S(1)} %get-tuple-element.156), kind=kLoop, calls=%fused_computation.37 | loop fusion | flops 393216 | bytes 1577984 | tf_op jit(solution)/shard_map/scatter-add | solution.py:186
  100.0 2.0 %constant_dynamic-update-slice_fusion = (f32[1024,1024]{1,0:T(8,128)}, f32[128,1024]{1,0:T(8,128)S(1)}, f32[128,1024]{1,0:T(8,128)S(1)}) fusion(f32[1024,1024]{1,0:T(8,128)} %get-tuple-element.122, f32[1024]{0:T(1024)S(1)} %get-tuple-element.157, f32[128]{0:T(128)S(1)} %get-tuple-element.160), kind=kLoop, calls=%fused_computation.52 | loop fusion | flops 262144 | bytes 2101760 | tf_op jit(solution)/shard_map/scatter-add | solution.py:187
  103.2 0.7 fusion.23
  104.1 3.4 %copy-done = f32[2,1024,1024]{2,1,0:T(8,128)} copy-done((f32[2,1024,1024]{2,1,0:T(8,128)}, f32[2,1024,1024]{2,1,0:T(8,128)S(1)}, u32[]{:S(2)}) %copy-start) | copy-done | bytes 8388632
  (46 shorter events, 5.5 us)
Async XLA Ops:
  1.5 102.4 %collective-permute-start.2 = (bf16[2,128,128]{2,1,0:T(8,128)(2,1)S(1)}, bf16[2,128,128]{2,1,0:T(8,128)(2,1)S(1)}, u32[]{:S(2)}, u32[]{:S(2)}) collective-permute-start(bf16[2,128,128]{2,1,0:T(8,128)(2,1)S(1)} %slice.233), channel_id=1, source_target_pairs={{0,5},{4,9},{8,13},{12,17},{16,21},{20,25},{24,29},{1,6},{5,10},{9... | collective-permute-start | bytes 196616 | tf_op jit(solution)/shard_map/ppermute | solution.py:117
  6.9 36.6 %collective-permute-start = (bf16[2,1024,128]{2,1,0:T(8,128)(2,1)S(1)}, bf16[2,1024,128]{2,1,0:T(8,128)(2,1)S(1)}, u32[]{:S(2)}, u32[]{:S(2)}) collective-permute-start(bf16[2,1024,128]{2,1,0:T(8,128)(2,1)S(1)} %slice.208), channel_id=1, source_target_pairs={{0,4},{4,8},{8,12},{12,16},{16,20},{20,24},{24,28},{1,5},{5,9},{9,... | collective-permute-start | bytes 1572872 | tf_op jit(solution)/shard_map/ppermute | solution.py:15
  11.5 35.7 %collective-permute-start.1 = (bf16[2,128,1024]{2,1,0:T(8,128)(2,1)S(1)}, bf16[2,128,1024]{2,1,0:T(8,128)(2,1)S(1)}, u32[]{:S(2)}, u32[]{:S(2)}) collective-permute-start(bf16[2,128,1024]{2,1,0:T(8,128)(2,1)S(1)} %slice.210), channel_id=1, source_target_pairs={{0,1},{1,2},{2,3},{4,5},{5,6},{6,7},{8,9},{9,10},{10,11},{12,13},{... | collective-permute-start | bytes 1572872 | tf_op jit(solution)/shard_map/ppermute | solution.py:15
  104.1 3.4 %copy-start = (f32[2,1024,1024]{2,1,0:T(8,128)}, f32[2,1024,1024]{2,1,0:T(8,128)S(1)}, u32[]{:S(2)}) copy-start(f32[2,1024,1024]{2,1,0:T(8,128)S(1)} %fusion.22) | copy-start | bytes 25165828

commit v3 on v1

--- a/solution.py
+++ b/solution.py
@@ -9,10 +9,6 @@
 
 
 eps = 1e-06
-
-
-def from_behind(block, axis, count):
-    return lax.ppermute(block, axis, [(i, i + 1) for i in range(count - 1)])
 
 
 def strip_stats(former, latter, window):
@@ -47,32 +43,6 @@
     )
 
 
-def tile_terms(horiz_terms, vert_terms):
-    first_h = tuple(jnp.pad(item, ((0, 0), (0, 1), (0, 0))) for item in horiz_terms)
-    second_h = tuple(jnp.pad(item, ((0, 0), (1, 0), (0, 0))) for item in horiz_terms)
-    first_v = tuple(jnp.pad(item, ((0, 1), (0, 0), (0, 0))) for item in vert_terms)
-    second_v = tuple(jnp.pad(item, ((1, 0), (0, 0), (0, 0))) for item in vert_terms)
-    denominator = 1.0 + first_h[0] + first_v[0] + second_h[0] + second_v[0]
-    log_gain = (first_h[1] + first_v[1] - second_h[1] - second_v[1]) / denominator
-    offset = (first_h[2] + first_v[2] - second_h[2] - second_v[2]) / denominator
-    return log_gain, offset
-
-
-def grid_solve(horiz_stats, vert_stats):
-    gain_one, level_one = tile_terms(pair_terms(horiz_stats), pair_terms(vert_stats))
-    scale = jnp.exp(gain_one)
-    horiz_two = corrected_stats(
-        horiz_stats, scale[:, :-1], level_one[:, :-1], scale[:, 1:], level_one[:, 1:]
-    )
-    vert_two = corrected_stats(
-        vert_stats, scale[:-1], level_one[:-1], scale[1:], level_one[1:]
-    )
-    gain_two, level_two = tile_terms(pair_terms(horiz_two), pair_terms(vert_two))
-    log_gain = gain_one + gain_two
-    level = jnp.exp(gain_two) * level_one + level_two
-    return log_gain, level
-
-
 def fade(ids, tile_px):
     return (jnp.minimum(ids, tile_px - 1 - ids) + 1).astype(jnp.float32) / (tile_px / 2.0)
 
@@ -98,6 +68,25 @@
     return values, weight
 
 
+def shifted(block, axis, count, step):
+    if step > 0:
+        route = [(i, i + 1) for i in range(count - 1)]
+    else:
+        route = [(i + 1, i) for i in range(count - 1)]
+    return lax.ppermute(block, axis, route)
+
+
+def combine(right_pair, down_pair, left_pair, upper_pair):
+    denominator = 1.0 + right_pair[0] + down_pair[0] + left_pair[0] + upper_pair[0]
+    log_gain = (right_pair[1] + down_pair[1] - left_pair[1] - upper_pair[1]) / denominator
+    offset = (right_pair[2] + down_pair[2] - left_pair[2] - upper_pair[2]) / denominator
+    return log_gain, offset
+
+
+def masked_terms(stats, present):
+    return tuple(jnp.where(present, item, 0.0) for item in pair_terms(stats))
+
+
 def local(tiles, extents, offsets, bands):
     planes, tile_px, _ = tiles.shape
     n_row = lax.axis_size("row")
@@ -108,9 +97,13 @@
 
     right_strip = tiles[:, :, tile_px - width :]
     down_strip = tiles[:, tile_px - width :, :]
+    left_strip = tiles[:, :, :width]
+    up_strip = tiles[:, :width, :]
     corner = tiles[:, tile_px - width :, tile_px - width :]
-    from_left = from_behind(right_strip, "col", n_col)
-    from_up = from_behind(down_strip, "row", n_row)
+    from_left = shifted(right_strip, "col", n_col, 1)
+    from_up = shifted(down_strip, "row", n_row, 1)
+    from_right = shifted(left_strip, "col", n_col, -1)
+    from_down = shifted(up_strip, "row", n_row, -1)
     diagonal = [
         (j * n_row + i, (j + 1) * n_row + i + 1) for i in range(n_row - 1) for j in range(n_col - 1)
     ]
@@ -119,22 +112,71 @@
     left_col = jnp.maximum(col_index - 1, 0)
     upper_row = jnp.maximum(row_index - 1, 0)
     strip_ids = jnp.arange(width, dtype=jnp.int32)
-    horiz_window = (strip_ids < extents[0, row_index, left_col]).astype(jnp.float32)[None, None, :]
-    vert_window = (strip_ids < extents[1, upper_row, col_index]).astype(jnp.float32)[None, :, None]
-    horiz = strip_stats(
-        from_left.astype(jnp.float32), tiles[:, :, :width].astype(jnp.float32), horiz_window
-    )
-    vert = strip_stats(
-        from_up.astype(jnp.float32), tiles[:, :width, :].astype(jnp.float32), vert_window
-    )
-    gathered = lax.all_gather(jnp.stack([horiz, vert]), ("col", "row"))
-    gathered = gathered.reshape((n_col, n_row) + gathered.shape[1:]).swapaxes(0, 1)
-    horiz_stats = tuple(gathered[:, 1:, 0, k] for k in range(5))
-    vert_stats = tuple(gathered[1:, :, 1, k] for k in range(5))
-    log_gain, level = grid_solve(horiz_stats, vert_stats)
-
-    def terms_at(r, c):
-        return log_gain[r, c], level[r, c]
+
+    def across(extent):
+        return (strip_ids < extent).astype(jnp.float32)[None, None, :]
+
+    def along(extent):
+        return (strip_ids < extent).astype(jnp.float32)[None, :, None]
+
+    f32 = jnp.float32
+    right_stats = strip_stats(
+        right_strip.astype(f32), from_right.astype(f32), across(extents[0, row_index, col_index])
+    )
+    down_stats = strip_stats(
+        down_strip.astype(f32), from_down.astype(f32), along(extents[1, row_index, col_index])
+    )
+    left_stats = strip_stats(
+        from_left.astype(f32), left_strip.astype(f32), across(extents[0, row_index, left_col])
+    )
+    up_stats = strip_stats(
+        from_up.astype(f32), up_strip.astype(f32), along(extents[1, upper_row, col_index])
+    )
+    has_right = col_index < n_col - 1
+    has_down = row_index < n_row - 1
+    has_left_pair = col_index > 0
+    has_up_pair = row_index > 0
+    gain_one, level_one = combine(
+        masked_terms(right_stats, has_right),
+        masked_terms(down_stats, has_down),
+        masked_terms(left_stats, has_left_pair),
+        masked_terms(up_stats, has_up_pair),
+    )
+    first = jnp.concatenate([gain_one, level_one])
+    near = [
+        shifted(first, "col", n_col, -1),
+        shifted(first, "row", n_row, -1),
+        shifted(first, "col", n_col, 1),
+        shifted(first, "row", n_row, 1),
+    ]
+    scale = jnp.exp(gain_one)
+    near_scale = [jnp.exp(item[:planes]) for item in near]
+    near_level = [item[planes:] for item in near]
+    right_two = corrected_stats(right_stats, scale, level_one, near_scale[0], near_level[0])
+    down_two = corrected_stats(down_stats, scale, level_one, near_scale[1], near_level[1])
+    left_two = corrected_stats(left_stats, near_scale[2], near_level[2], scale, level_one)
+    up_two = corrected_stats(up_stats, near_scale[3], near_level[3], scale, level_one)
+    gain_two, level_two = combine(
+        masked_terms(right_two, has_right),
+        masked_terms(down_two, has_down),
+        masked_terms(left_two, has_left_pair),
+        masked_terms(up_two, has_up_pair),
+    )
+    own_gain = gain_one + gain_two
+    own_level = jnp.exp(gain_two) * level_one + level_two
+    final = jnp.concatenate([own_gain, own_level])
+    final_left = shifted(final, "col", n_col, 1)
+    final_up = shifted(final, "row", n_row, 1)
+    final_corner = lax.ppermute(final, ("col", "row"), diagonal)
+    found = {
+        "own": (own_gain, own_level),
+        "left": (final_left[:planes], final_left[planes:]),
+        "up": (final_up[:planes], final_up[planes:]),
+        "corner": (final_corner[:planes], final_corner[planes:]),
+    }
+
+    def terms_at(which):
+        return found[which]
 
     has_left = (col_index > 0).astype(jnp.float32)
     has_up = (row_index > 0).astype(jnp.float32)
@@ -150,7 +192,7 @@
     rows_w, cols_w = weights_of(row_index, col_index, ids - top, ids - left, jnp.float32(1.0))
     own_vals, own_w = piece(
         tiles, ((0, 0), (SPILL, 0), (SPILL, 0)), (SPILL - top, SPILL - left),
-        (planes, tile_px, tile_px), rows_w, cols_w, *terms_at(row_index, col_index),
+        (planes, tile_px, tile_px), rows_w, cols_w, *terms_at("own"),
     )
     top_l, left_l = offsets[0, row_index, left_col], offsets[1, row_index, left_col]
     rows_w, cols_w = weights_of(
@@ -158,7 +200,7 @@
     )
     left_vals, left_w = piece(
         from_left, ((0, 0), (SPILL, 0), (0, width)), (SPILL - top_l, width - left_l),
-        (planes, tile_px, width), rows_w, cols_w, *terms_at(row_index, left_col),
+        (planes, tile_px, width), rows_w, cols_w, *terms_at("left"),
     )
     top_u, left_u = offsets[0, upper_row, col_index], offsets[1, upper_row, col_index]
     rows_w, cols_w = weights_of(
@@ -166,7 +208,7 @@
     )
     up_vals, up_w = piece(
         from_up, ((0, 0), (0, width), (SPILL, 0)), (width - top_u, SPILL - left_u),
-        (planes, width, tile_px), rows_w, cols_w, *terms_at(upper_row, col_index),
+        (planes, width, tile_px), rows_w, cols_w, *terms_at("up"),
     )
     top_c, left_c = offsets[0, upper_row, left_col], offsets[1, upper_row, left_col]
     rows_w, cols_w = weights_of(
@@ -174,7 +216,7 @@
     )
     corner_vals, corner_w = piece(
         from_corner, ((0, 0), (0, width), (0, width)), (width - top_c, width - left_c),
-        (planes, width, width), rows_w, cols_w, *terms_at(upper_row, left_col),
+        (planes, width, width), rows_w, cols_w, *terms_at("corner"),
     )
 
     blended = own_vals.at[:, :, :width].add(left_vals)

time: 105 us -> 86.5 us (0.82)
  blocking collectives: 36.9 us -> 0 us
  starting transfers between devices: 11 us -> 36.4 us
  other arithmetic: 28.3 us -> 19.4 us
  waiting for transfers between devices: 0.01 us -> 4.17 us
  local copies, waits for them, and re-layouts: 12.4 us -> 10 us
    all_gather x1 -> x0, blocking collectives: 36.9 us -> none  [local(): gathered = lax.all_gather(jnp.stack([horiz, vert]), ('col', 'row'))]
    ppermute x2 -> x11, starting transfers between devices: 6.72 us -> 32.1 us  [the longest x10 29.1 us: shifted(): return lax.ppermute(block, axis, route)]
    ppermute x2 -> x11, waiting for transfers between devices: 0.01 us -> 4.16 us  [the longest x10 4.16 us: shifted(): return lax.ppermute(block, axis, route)]
    mul x1, other arithmetic: 2.35 us -> 0.34 us  [piece(): weight = rows_w[:, None] * cols_w[None, :]]
    reduce_sum x2, other arithmetic: 2.93 us -> 0.95 us  [strip_stats(): mean_former = jnp.sum(former * full, axis=(-2, -1)) / number]
    mul x1, other arithmetic: 5.23 us -> 3.35 us  [piece(): (jnp.exp(log_gain)[:, None, None] * window.astype(jnp.float32) + level[:,...]
    scatter-add x1, other arithmetic: 2 us -> 0.19 us  [local(): weight = weight.at[:width, :].add(up_w)]
    scatter-add x1, other arithmetic: 2.73 us -> 1.02 us  [local(): weight = own_w.at[:, :width].add(left_w)]
  transfers between devices with their start and end apart: 3 -> 12, of which waited for: 0 -> 2; matrix products, arithmetic and copies ran while one was open for 35% -> 29% of each run, Pallas kernels for 0% -> 0%
where the time goes in v3:
time: 86.5 us; the launch traced here: 85.7 us
  starting transfers between devices  36.4 us (42%)
  other arithmetic  19.4 us (22%)
  between operations  15.7 us (18%)
  local copies, waits for them, and re-layouts  10 us (12%)
  waiting for transfers between devices  4.17 us (5%)
    ppermute x10, starting transfers between devices, shifted(): return lax.ppermute(block, axis, route)  29.1 us
    ppermute x1, starting transfers between devices, local(): from_corner = lax.ppermute(corner, ('col', 'row'), diagonal)  4.33 us
    ppermute x10, waiting for transfers between devices, shifted(): return lax.ppermute(block, axis, route)  4.16 us
    unnamed x12, local copies, waits for them, and re-layouts  3.42 us
    mul x3, other arithmetic, row_weight(): return live.astype(jnp.float32) * present * fade(ids, tile_px)  3.39 us
    mul x1, other arithmetic, piece(): (jnp.exp(log_gain)[:, None, None] * window.astype(jnp.float32) + level[:,...  3.35 us
    reduce_sum x4, other arithmetic, strip_stats(): covariance = jnp.sum(dev_former * dev_latter, axis=(-2, -1)) / number  3.28 us
    ppermute x1, starting transfers between devices, local(): final_corner = lax.ppermute(final, ('col', 'row'), diagonal)  3 us
  transfers between devices with their start and end apart: 12, of which 2 were waited for; matrix products, arithmetic and copies ran while one was open for 29% of the time, Pallas kernels for 0%

profile of v3, /device:TPU:0, one launch (start us, length us, event | category | flops | bytes accessed | tf_op | source)
XLA Modules:
  0.0 85.7 jit_solution(12261818205397092871)
XLA Ops:
  1.5 4.3 %collective-permute-start.11 = (bf16[2,128,128]{2,1,0:T(8,128)(2,1)S(1)}, bf16[2,128,128]{2,1,0:T(8,128)(2,1)S(1)}, u32[]{:S(2)}, u32[]{:S(2)}) collective-permute-start(bf16[2,128,128]{2,1,0:T(8,128)(2,1)S(1)} %slice.216), channel_id=1, source_target_pairs={{0,5},{4,9},{8,13},{12,17},{16,21},{20,25},{24,29},{1,6},{5,10},{9... | collective-permute-start | bytes 196616 | tf_op jit(solution)/shard_map/ppermute | solution.py:110
  5.9 2.2 %fusion.120 = (bf16[2,128,1024]{2,1,0:T(8,128)(2,1)}, bf16[2,128,1024]{2,1,0:T(8,128)(2,1)}) fusion(bf16[2,1024,1024]{2,1,0:T(8,128)(2,1)} %param.16), kind=kLoop, calls=%fused_computation.248 | loop fusion | bytes 2097152 | tf_op jit(solution)/shard_map/slice | solution.py:101
  8.1 1.3 %collective-permute-start.1 = (bf16[2,128,1024]{2,1,0:T(8,128)(2,1)}, bf16[2,128,1024]{2,1,0:T(8,128)(2,1)S(1)}, u32[]{:S(2)}, u32[]{:S(2)}) collective-permute-start(bf16[2,128,1024]{2,1,0:T(8,128)(2,1)} %get-tuple-element.120), channel_id=1, source_target_pairs={{1,0},{2,1},{3,2},{5,4},{6,5},{7,6},{9,8},{10,9},{11,10},{13,12},{... | collective-permute-start | bytes 1572872 | tf_op jit(solution)/shard_map/ppermute | solution.py:76
  9.4 4.2 %collective-permute-start.3 = (bf16[2,128,1024]{2,1,0:T(8,128)(2,1)}, bf16[2,128,1024]{2,1,0:T(8,128)(2,1)S(1)}, u32[]{:S(2)}, u32[]{:S(2)}) collective-permute-start(bf16[2,128,1024]{2,1,0:T(8,128)(2,1)} %get-tuple-element.121), channel_id=1, source_target_pairs={{0,1},{1,2},{2,3},{4,5},{5,6},{6,7},{8,9},{9,10},{10,11},{12,13},{... | collective-permute-start | bytes 1572872 | tf_op jit(solution)/shard_map/ppermute | solution.py:76
  13.6 1.3 %fusion.119 = (bf16[2,1024,128]{2,1,0:T(8,128)(2,1)S(1)}, bf16[2,1024,128]{2,1,0:T(8,128)(2,1)S(1)}) fusion(bf16[2,1024,1024]{2,1,0:T(8,128)(2,1)} %param.16), kind=kLoop, calls=%fused_computation.247 | loop fusion | bytes 2097152 | tf_op jit(solution)/shard_map/slice | solution.py:100
  14.9 1.3 %collective-permute-start = (bf16[2,1024,128]{2,1,0:T(8,128)(2,1)S(1)}, bf16[2,1024,128]{2,1,0:T(8,128)(2,1)S(1)}, u32[]{:S(2)}, u32[]{:S(2)}) collective-permute-start(bf16[2,1024,128]{2,1,0:T(8,128)(2,1)S(1)} %get-tuple-element.118), channel_id=1, source_target_pairs={{4,0},{8,4},{12,8},{16,12},{20,16},{24,20},{28,24},{5,1},{9,5},{13... | collective-permute-start | bytes 1572872 | tf_op jit(solution)/shard_map/ppermute | solution.py:76
  16.2 4.6 %collective-permute-start.2 = (bf16[2,1024,128]{2,1,0:T(8,128)(2,1)S(1)}, bf16[2,1024,128]{2,1,0:T(8,128)(2,1)S(1)}, u32[]{:S(2)}, u32[]{:S(2)}) collective-permute-start(bf16[2,1024,128]{2,1,0:T(8,128)(2,1)S(1)} %get-tuple-element.119), channel_id=1, source_target_pairs={{0,4},{4,8},{8,12},{12,16},{16,20},{20,24},{24,28},{1,5},{5,9},{9,... | collective-permute-start | bytes 1572872 | tf_op jit(solution)/shard_map/ppermute | solution.py:76
  31.9 1.1 %and_select_fusion = (f32[128]{0:T(128)S(1)}, f32[128]{0:T(128)S(1)}) fusion(s32[]{:T(128)} %bitcast.17, s32[]{:T(128)} %bitcast.9), kind=kLoop, calls=%fused_computation.146 | loop fusion | flops 2688 | bytes 1032 | tf_op jit(solution)/shard_map/mul | solution.py:57
  40.0 1.3 %compare_convert_fusion.1 = (f32[128]{0:T(128)S(1)}, f32[128]{0:T(128)S(1)}) fusion(s32[]{:T(128)} %bitcast.2, s32[]{:T(128)} %bitcast), kind=kLoop, calls=%fused_computation.151 | loop fusion | flops 512 | bytes 1032 | tf_op jit(solution)/shard_map/convert_element_type | solution.py:117
  41.4 1.5 %fusion.47 = (f32[1024]{0:T(1024)S(1)}, f32[1024]{0:T(1024)S(1)}) fusion(s32[]{:T(128)} %bitcast.7, s32[]{:T(128)} %bitcast.6, s32[]{:T(128)} %bitcast.4, s32[]{:T(128)} %bitcast.5), kind=kLoop, calls=%fused_computation.98 | loop fusion | flops 24576 | bytes 8208 | tf_op jit(solution)/shard_map/mul | solution.py:52
  43.6 1.2 %compare_convert_fusion = (f32[128]{0:T(128)S(1)}, f32[128]{0:T(128)S(1)}) fusion(s32[]{:T(128)} %bitcast.3, s32[]{:T(128)} %bitcast.1), kind=kLoop, calls=%fused_computation.150 | loop fusion | flops 512 | bytes 1032 | tf_op jit(solution)/shard_map/convert_element_type | solution.py:120
  45.2 1.2 %fusion.80 = (f32[128]{0:T(128)S(1)}, f32[128]{0:T(128)S(1)}) fusion(f32[]{:T(128)S(6)} %convert_element_type.162, s32[]{:T(128)} %bitcast.15, s32[]{:T(128)} %bitcast.14, s32[]{:T(128)} %bitcast.12, f32[]{:T(128)S(6)} %mul.713, s32[]{:T(128)} %bitcast.19, s32[]{:T(128)} %bitcast.18, s32[]{:T(128)} %bitcast.16), kind=kLoop, calls=%fused_computation.182 | loop fusion | flops 3968 | bytes 1056 | tf_op jit(solution)/shard_map/mul | solution.py:52
  47.0 1.0 %fusion.34 = (f32[2]{0:T(128)S(1)}, f32[2]{0:T(128)S(1)}, f32[2]{0:T(128)S(1)}, f32[2]{0:T(128)S(1)}, f32[2]{0:T(128)S(1)}, /*index=5*/f32[2]{0:T(128)S(1)}) fusion(bf16[2,128,1024]{2,1,0:T(8,128)(2,1)S(1)} %collective-permute-done.3, f32[2]{0:T(128)S(1)} %get-tuple-element.160, f32[2]{0:T(128)S(1)} %get-tuple-element.159, f32[128]{0:T(128)S(1)} %get-tuple-element.167, ...), kind=kLoop, calls=%fused_computation.55 | loop fusion | flops 4980724 | bytes 2098240 | tf_op jit(solution)/shard_map/reduce_sum | solution.py:23
  50.8 3.0 %collective-permute-start.7 = (f32[4]{0:T(128)S(1)}, f32[4]{0:T(128)S(1)}, u32[]{:S(2)}, u32[]{:S(2)}) collective-permute-start(f32[4]{0:T(128)S(1)} %pad_maximum_fusion), channel_id=1, source_target_pairs={{0,1},{1,2},{2,3},{4,5},{5,6},{6,7},{8,9},{9,10},{10,11},{12,13},{... | collective-permute-start | bytes 56 | tf_op jit(solution)/shard_map/ppermute | solution.py:76
  53.9 4.3 %collective-permute-start.6 = (f32[4]{0:T(128)S(1)}, f32[4]{0:T(128)S(1)}, u32[]{:S(2)}, u32[]{:S(2)}) collective-permute-start(f32[4]{0:T(128)S(1)} %pad_maximum_fusion), channel_id=1, source_target_pairs={{0,4},{4,8},{8,12},{12,16},{16,20},{20,24},{24,28},{1,5},{5,9},{9,... | collective-permute-start | bytes 56 | tf_op jit(solution)/shard_map/ppermute | solution.py:76
  58.2 1.3 %collective-permute-start.5 = (f32[4]{0:T(128)S(1)}, f32[4]{0:T(128)S(1)}, u32[]{:S(2)}, u32[]{:S(2)}) collective-permute-start(f32[4]{0:T(128)S(1)} %pad_maximum_fusion), channel_id=1, source_target_pairs={{1,0},{2,1},{3,2},{5,4},{6,5},{7,6},{9,8},{10,9},{11,10},{13,12},{... | collective-permute-start | bytes 56 | tf_op jit(solution)/shard_map/ppermute | solution.py:76
  59.5 1.3 %collective-permute-start.4 = (f32[4]{0:T(128)S(1)}, f32[4]{0:T(128)S(1)}, u32[]{:S(2)}, u32[]{:S(2)}) collective-permute-start(f32[4]{0:T(128)S(1)} %pad_maximum_fusion), channel_id=1, source_target_pairs={{4,0},{8,4},{12,8},{16,12},{20,16},{24,20},{28,24},{5,1},{9,5},{13... | collective-permute-start | bytes 56 | tf_op jit(solution)/shard_map/ppermute | solution.py:76
  61.2 3.7 %collective-permute-done.4 = f32[4]{0:T(128)S(1)} collective-permute-done((f32[4]{0:T(128)S(1)}, f32[4]{0:T(128)S(1)}, u32[]{:S(2)}, u32[]{:S(2)}) %collective-permute-start.4) | collective-permute-done | bytes 48 | tf_op jit(solution)/shard_map/ppermute | solution.py:76
  65.1 3.0 %collective-permute-start.10 = (f32[4]{0:T(128)S(1)}, f32[4]{0:T(128)S(1)}, u32[]{:S(2)}, u32[]{:S(2)}) collective-permute-start(f32[4]{0:T(128)S(1)} %pad_maximum_fusion.1), channel_id=1, source_target_pairs={{0,5},{4,9},{8,13},{12,17},{16,21},{20,25},{24,29},{1,6},{5,10},{9... | collective-permute-start | bytes 56 | tf_op jit(solution)/shard_map/ppermute | solution.py:170
  68.1 4.4 %collective-permute-start.9 = (f32[4]{0:T(128)S(1)}, f32[4]{0:T(128)S(1)}, u32[]{:S(2)}, u32[]{:S(2)}) collective-permute-start(f32[4]{0:T(128)S(1)} %pad_maximum_fusion.1), channel_id=1, source_target_pairs={{0,1},{1,2},{2,3},{4,5},{5,6},{6,7},{8,9},{9,10},{10,11},{12,13},{... | collective-permute-start | bytes 56 | tf_op jit(solution)/shard_map/ppermute | solution.py:76
  72.6 3.4 %collective-permute-start.8 = (f32[4]{0:T(128)S(1)}, f32[4]{0:T(128)S(1)}, u32[]{:S(2)}, u32[]{:S(2)}) collective-permute-start(f32[4]{0:T(128)S(1)} %pad_maximum_fusion.1), channel_id=1, source_target_pairs={{0,4},{4,8},{8,12},{12,16},{16,20},{20,24},{24,28},{1,5},{5,9},{9,... | collective-permute-start | bytes 56 | tf_op jit(solution)/shard_map/ppermute | solution.py:76
  76.0 3.3 %add_multiply_fusion = f32[2,1024,1024]{2,1,0:T(8,128)S(1)} fusion(s32[]{:T(128)S(6)} %select_n.200, s32[]{:T(128)S(6)} %select_n.201, bf16[2,1024,1024]{2,1,0:T(8,128)(2,1)S(1)} %copy-done, f32[1024,1024]{1,0:T(8,128)S(1)} %broadcast_multiply_fusion, f32[2]{0:T(128)S(1)} %divide_add_fusion, f32[2]{0:T(128)S(1)} %get-tuple-element.102), kind=kLoop, calls=%fused_computation | loop fusion | flops 8388608 | bytes 16777240 | tf_op jit(solution)/shard_map/mul | solution.py:65
  79.4 1.0 %fusion.41 = (f32[1024,1024]{1,0:T(8,128)S(1)}, f32[1024,128]{1,0:T(8,128)S(1)}) fusion(f32[1024,1024]{1,0:T(8,128)S(1)} %broadcast_multiply_fusion, pred[]{:T(512)} %compare_reduce_fusion, f32[128]{0:T(128)S(1)} %get-tuple-element.164, f32[1024]{0:T(1024)S(1)} %fusion.55), kind=kLoop, calls=%fused_computation.65 | loop fusion | flops 393216 | bytes 1577473 | tf_op jit(solution)/shard_map/scatter-add | solution.py:225
  82.7 3.0 %copy-done.2 = f32[2,1024,1024]{2,1,0:T(8,128)} copy-done((f32[2,1024,1024]{2,1,0:T(8,128)}, f32[2,1024,1024]{2,1,0:T(8,128)S(1)}, u32[]{:S(2)}) %copy-start.2) | copy-done | bytes 8388632
  (53 shorter events, 11.6 us)
Async XLA Ops:
  0.6 20.8 %copy-start.3 = (s32[2,4,8]{2,1,0:T(4,128)S(1)}, s32[2,4,8]{2,1,0:T(4,128)}, u32[]{:S(2)}) copy-start(s32[2,4,8]{2,1,0:T(4,128)} %param.18) | copy-start | bytes 772
  0.6 33.1 %copy-start.5 = (s32[2,4,8]{2,1,0:T(4,128)S(1)}, s32[2,4,8]{2,1,0:T(4,128)}, u32[]{:S(2)}) copy-start(s32[2,4,8]{2,1,0:T(4,128)} %param.17) | copy-start | bytes 772
  0.7 33.8 %copy-start.4 = (s32[2,4,8]{2,1,0:T(4,128)S(1)}, s32[2,4,8]{2,1,0:T(4,128)}, u32[]{:S(2)}) copy-start(s32[2,4,8]{2,1,0:T(4,128)} %param.19) | copy-start | bytes 772
  1.5 80.6 %collective-permute-start.11 = (bf16[2,128,128]{2,1,0:T(8,128)(2,1)S(1)}, bf16[2,128,128]{2,1,0:T(8,128)(2,1)S(1)}, u32[]{:S(2)}, u32[]{:S(2)}) collective-permute-start(bf16[2,128,128]{2,1,0:T(8,128)(2,1)S(1)} %slice.216), channel_id=1, source_target_pairs={{0,5},{4,9},{8,13},{12,17},{16,21},{20,25},{24,29},{1,6},{5,10},{9... | collective-permute-start | bytes 196616 | tf_op jit(solution)/shard_map/ppermute | solution.py:110
  8.1 38.9 %collective-permute-start.1 = (bf16[2,128,1024]{2,1,0:T(8,128)(2,1)}, bf16[2,128,1024]{2,1,0:T(8,128)(2,1)S(1)}, u32[]{:S(2)}, u32[]{:S(2)}) collective-permute-start(bf16[2,128,1024]{2,1,0:T(8,128)(2,1)} %get-tuple-element.120), channel_id=1, source_target_pairs={{1,0},{2,1},{3,2},{5,4},{6,5},{7,6},{9,8},{10,9},{11,10},{13,12},{... | collective-permute-start | bytes 1572872 | tf_op jit(solution)/shard_map/ppermute | solution.py:76
  9.4 37.0 %collective-permute-start.3 = (bf16[2,128,1024]{2,1,0:T(8,128)(2,1)}, bf16[2,128,1024]{2,1,0:T(8,128)(2,1)S(1)}, u32[]{:S(2)}, u32[]{:S(2)}) collective-permute-start(bf16[2,128,1024]{2,1,0:T(8,128)(2,1)} %get-tuple-element.121), channel_id=1, source_target_pairs={{0,1},{1,2},{2,3},{4,5},{5,6},{6,7},{8,9},{9,10},{10,11},{12,13},{... | collective-permute-start | bytes 1572872 | tf_op jit(solution)/shard_map/ppermute | solution.py:76
  14.9 33.5 %collective-permute-start = (bf16[2,1024,128]{2,1,0:T(8,128)(2,1)S(1)}, bf16[2,1024,128]{2,1,0:T(8,128)(2,1)S(1)}, u32[]{:S(2)}, u32[]{:S(2)}) collective-permute-start(bf16[2,1024,128]{2,1,0:T(8,128)(2,1)S(1)} %get-tuple-element.118), channel_id=1, source_target_pairs={{4,0},{8,4},{12,8},{16,12},{20,16},{24,20},{28,24},{5,1},{9,5},{13... | collective-permute-start | bytes 1572872 | tf_op jit(solution)/shard_map/ppermute | solution.py:76
  16.2 31.8 %collective-permute-start.2 = (bf16[2,1024,128]{2,1,0:T(8,128)(2,1)S(1)}, bf16[2,1024,128]{2,1,0:T(8,128)(2,1)S(1)}, u32[]{:S(2)}, u32[]{:S(2)}) collective-permute-start(bf16[2,1024,128]{2,1,0:T(8,128)(2,1)S(1)} %get-tuple-element.119), channel_id=1, source_target_pairs={{0,4},{4,8},{8,12},{12,16},{16,20},{20,24},{24,28},{1,5},{5,9},{9,... | collective-permute-start | bytes 1572872 | tf_op jit(solution)/shard_map/ppermute | solution.py:76
  41.4 5.0 %copy-start = (bf16[2,1024,1024]{2,1,0:T(8,128)(2,1)S(1)}, bf16[2,1024,1024]{2,1,0:T(8,128)(2,1)}, u32[]{:S(2)}) copy-start(bf16[2,1024,1024]{2,1,0:T(8,128)(2,1)} %param.16) | copy-start | bytes 12582916
  50.8 10.0 %collective-permute-start.7 = (f32[4]{0:T(128)S(1)}, f32[4]{0:T(128)S(1)}, u32[]{:S(2)}, u32[]{:S(2)}) collective-permute-start(f32[4]{0:T(128)S(1)} %pad_maximum_fusion), channel_id=1, source_target_pairs={{0,1},{1,2},{2,3},{4,5},{5,6},{6,7},{8,9},{9,10},{10,11},{12,13},{... | collective-permute-start | bytes 56 | tf_op jit(solution)/shard_map/ppermute | solution.py:76
  53.9 6.9 %collective-permute-start.6 = (f32[4]{0:T(128)S(1)}, f32[4]{0:T(128)S(1)}, u32[]{:S(2)}, u32[]{:S(2)}) collective-permute-start(f32[4]{0:T(128)S(1)} %pad_maximum_fusion), channel_id=1, source_target_pairs={{0,4},{4,8},{8,12},{12,16},{16,20},{20,24},{24,28},{1,5},{5,9},{9,... | collective-permute-start | bytes 56 | tf_op jit(solution)/shard_map/ppermute | solution.py:76
  58.2 3.1 %collective-permute-start.5 = (f32[4]{0:T(128)S(1)}, f32[4]{0:T(128)S(1)}, u32[]{:S(2)}, u32[]{:S(2)}) collective-permute-start(f32[4]{0:T(128)S(1)} %pad_maximum_fusion), channel_id=1, source_target_pairs={{1,0},{2,1},{3,2},{5,4},{6,5},{7,6},{9,8},{10,9},{11,10},{13,12},{... | collective-permute-start | bytes 56 | tf_op jit(solution)/shard_map/ppermute | solution.py:76
  59.5 5.5 %collective-permute-start.4 = (f32[4]{0:T(128)S(1)}, f32[4]{0:T(128)S(1)}, u32[]{:S(2)}, u32[]{:S(2)}) collective-permute-start(f32[4]{0:T(128)S(1)} %pad_maximum_fusion), channel_id=1, source_target_pairs={{4,0},{8,4},{12,8},{16,12},{20,16},{24,20},{28,24},{5,1},{9,5},{13... | collective-permute-start | bytes 56 | tf_op jit(solution)/shard_map/ppermute | solution.py:76
  65.1 16.9 %collective-permute-start.10 = (f32[4]{0:T(128)S(1)}, f32[4]{0:T(128)S(1)}, u32[]{:S(2)}, u32[]{:S(2)}) collective-permute-start(f32[4]{0:T(128)S(1)} %pad_maximum_fusion.1), channel_id=1, source_target_pairs={{0,5},{4,9},{8,13},{12,17},{16,21},{20,25},{24,29},{1,6},{5,10},{9... | collective-permute-start | bytes 56 | tf_op jit(solution)/shard_map/ppermute | solution.py:170
  68.1 12.5 %collective-permute-start.9 = (f32[4]{0:T(128)S(1)}, f32[4]{0:T(128)S(1)}, u32[]{:S(2)}, u32[]{:S(2)}) collective-permute-start(f32[4]{0:T(128)S(1)} %pad_maximum_fusion.1), channel_id=1, source_target_pairs={{0,1},{1,2},{2,3},{4,5},{5,6},{6,7},{8,9},{9,10},{10,11},{12,13},{... | collective-permute-start | bytes 56 | tf_op jit(solution)/shard_map/ppermute | solution.py:76
  72.6 8.2 %collective-permute-start.8 = (f32[4]{0:T(128)S(1)}, f32[4]{0:T(128)S(1)}, u32[]{:S(2)}, u32[]{:S(2)}) collective-permute-start(f32[4]{0:T(128)S(1)} %pad_maximum_fusion.1), channel_id=1, source_target_pairs={{0,4},{4,8},{8,12},{12,16},{16,20},{20,24},{24,28},{1,5},{5,9},{9,... | collective-permute-start | bytes 56 | tf_op jit(solution)/shard_map/ppermute | solution.py:76
  80.7 2.0 %copy-start.1 = (f32[1024,1024]{1,0:T(8,128)}, f32[1024,1024]{1,0:T(8,128)S(1)}, u32[]{:S(2)}) copy-start(f32[1024,1024]{1,0:T(8,128)S(1)} %get-tuple-element.145) | copy-start | bytes 12582916
  82.3 3.4 %copy-start.2 = (f32[2,1024,1024]{2,1,0:T(8,128)}, f32[2,1024,1024]{2,1,0:T(8,128)S(1)}, u32[]{:S(2)}) copy-start(f32[2,1024,1024]{2,1,0:T(8,128)S(1)} %fusion.42) | copy-start | bytes 25165828

commit v4 on v3

--- a/solution.py
+++ b/solution.py
@@ -1,11 +1,16 @@
+import functools
+
 import jax
 import jax.numpy as jnp
 from jax import lax
 from jax.sharding import PartitionSpec as P
+from jax.experimental import pallas as pl
+from jax.experimental.pallas import tpu as pltpu
 
 STRIP = 128
 SPILL = 128
 BLOCK = 128
+ROWS = 256
 
 
 eps = 1e-06
@@ -43,29 +48,134 @@
     )
 
 
-def fade(ids, tile_px):
-    return (jnp.minimum(ids, tile_px - 1 - ids) + 1).astype(jnp.float32) / (tile_px / 2.0)
-
-
-def row_weight(ids, band_low, band_high, tile_px, present):
-    live = (ids >= band_low * BLOCK) & (ids < band_high * BLOCK) & (ids >= 0) & (ids < tile_px)
-    return live.astype(jnp.float32) * present * fade(ids, tile_px)
-
-
-def col_weight(ids, tile_px, present):
-    live = (ids >= 0) & (ids < tile_px)
-    return live.astype(jnp.float32) * present * fade(ids, tile_px)
-
-
-def piece(source, pads, start, size, rows_w, cols_w, log_gain, level):
-    padded = jnp.pad(source, pads)
-    zero = jnp.zeros((), jnp.int32)
-    window = lax.dynamic_slice(padded, (zero, start[0], start[1]), size)
-    weight = rows_w[:, None] * cols_w[None, :]
-    values = (
-        jnp.exp(log_gain)[:, None, None] * window.astype(jnp.float32) + level[:, None, None]
-    ) * weight[None]
-    return values, weight
+def blend_kernel(idx_ref, off_ref, band_ref, terms_ref, cur_ref, prev_ref, lcur_ref, lprev_ref,
+                 up_ref, corner_ref, out_ref, w_ref, *, n_row, n_col):
+    f32 = jnp.float32
+    step = pl.program_id(0)
+    planes, rows, tile_px = cur_ref.shape
+    width = lcur_ref.shape[2]
+    cells = n_row * n_col
+    r = idx_ref[0]
+    c = idx_ref[1]
+    lc = jnp.maximum(c - 1, 0)
+    ur = jnp.maximum(r - 1, 0)
+    has_left = c > 0
+    has_up = r > 0
+
+    def table(ref, k, rr, cc):
+        return ref[k * cells + rr * n_col + cc]
+
+    def fade(ids):
+        return (jnp.minimum(ids, tile_px - 1 - ids) + 1).astype(f32) / (tile_px / 2.0)
+
+    def band_rows(ids, rr, cc, extra):
+        live = (ids >= table(band_ref, 0, rr, cc) * BLOCK) & (ids < table(band_ref, 1, rr, cc) * BLOCK)
+        live = live & (ids >= 0) & (ids < tile_px) & extra
+        return jnp.where(live, fade(ids), 0.0)
+
+    def gain(k, p):
+        return terms_ref[k * 2 * planes + p], terms_ref[k * 2 * planes + planes + p]
+
+    t = lax.broadcasted_iota(jnp.int32, (rows, 1), 0)
+    x = lax.broadcasted_iota(jnp.int32, (1, tile_px), 1)
+    xs = lax.broadcasted_iota(jnp.int32, (1, width), 1)
+    y = step * rows + t
+    top = table(off_ref, 0, r, c)
+    left = table(off_ref, 1, r, c)
+    top_l = table(off_ref, 0, r, lc)
+    left_l = table(off_ref, 1, r, lc)
+    j = x - left
+    w_own = band_rows(y - top, r, c, True) * jnp.where(j >= 0, fade(j), 0.0)
+    j_l = xs + tile_px - left_l
+    w_left = band_rows(y - top_l, r, lc, has_left) * jnp.where(j_l < tile_px, fade(j_l), 0.0)
+    w_ref[...] = w_own
+    w_ref[:, :width] += w_left
+    for p in range(planes):
+        cur = cur_ref[p].astype(f32)
+        prev = prev_ref[p].astype(f32)
+        shifted_rows = jnp.where(t >= top, pltpu.roll(cur, top, 0), pltpu.roll(prev, top, 0))
+        window = pltpu.roll(shifted_rows, left, 1)
+        scale, level = gain(0, p)
+        out_ref[p] = (scale * window + level) * w_own
+        lcur = lcur_ref[p].astype(f32)
+        lprev = lprev_ref[p].astype(f32)
+        shifted_rows = jnp.where(t >= top_l, pltpu.roll(lcur, top_l, 0), pltpu.roll(lprev, top_l, 0))
+        window = pltpu.roll(shifted_rows, left_l, 1)
+        scale, level = gain(1, p)
+        out_ref[p, :, :width] += (scale * window + level) * w_left
+
+    @pl.when(step == 0)
+    def _():
+        te = lax.broadcasted_iota(jnp.int32, (width, 1), 0)
+        top_u = table(off_ref, 0, ur, c)
+        left_u = table(off_ref, 1, ur, c)
+        top_c = table(off_ref, 0, ur, lc)
+        left_c = table(off_ref, 1, ur, lc)
+        j_u = x - left_u
+        w_up = band_rows(te + tile_px - top_u, ur, c, has_up) * jnp.where(j_u >= 0, fade(j_u), 0.0)
+        j_c = xs + tile_px - left_c
+        w_corner = band_rows(te + tile_px - top_c, ur, lc, has_up & has_left) * jnp.where(
+            j_c < tile_px, fade(j_c), 0.0
+        )
+        w_ref[:width, :] += w_up
+        w_ref[:width, :width] += w_corner
+        for p in range(planes):
+            window = pltpu.roll(pltpu.roll(up_ref[p].astype(f32), top_u, 0), left_u, 1)
+            scale, level = gain(2, p)
+            out_ref[p, :width, :] += (scale * window + level) * w_up
+            window = pltpu.roll(pltpu.roll(corner_ref[p].astype(f32), top_c, 0), left_c, 1)
+            scale, level = gain(3, p)
+            out_ref[p, :width, :width] += (scale * window + level) * w_corner
+
+
+def blend(idx, offsets, bands, terms, tiles, from_left, from_up, from_corner, n_row, n_col):
+    planes, tile_px, _ = tiles.shape
+    width = from_left.shape[2]
+    rows = min(ROWS, tile_px)
+    steps = tile_px // rows
+
+    def cur(b, *_):
+        return (0, b, 0)
+
+    def prev(b, *_):
+        return (0, jnp.maximum(b - 1, 0), 0)
+
+    def fixed(b, *_):
+        return (0, 0, 0)
+
+    grid_spec = pltpu.PrefetchScalarGridSpec(
+        num_scalar_prefetch=3,
+        grid=(steps,),
+        in_specs=[
+            pl.BlockSpec(memory_space=pltpu.SMEM),
+            pl.BlockSpec((planes, rows, tile_px), cur),
+            pl.BlockSpec((planes, rows, tile_px), prev),
+            pl.BlockSpec((planes, rows, width), cur),
+            pl.BlockSpec((planes, rows, width), prev),
+            pl.BlockSpec((planes, width, tile_px), fixed),
+            pl.BlockSpec((planes, width, width), fixed),
+        ],
+        out_specs=[
+            pl.BlockSpec((planes, rows, tile_px), cur),
+            pl.BlockSpec((rows, tile_px), lambda b, *_: (b, 0)),
+        ],
+    )
+    out_bytes = 4 * (planes + 1) * tile_px * tile_px
+    in_bytes = 2 * 2 * planes * tile_px * (tile_px + width)
+    return pl.pallas_call(
+        functools.partial(blend_kernel, n_row=n_row, n_col=n_col),
+        grid_spec=grid_spec,
+        out_shape=[
+            jax.ShapeDtypeStruct((planes, tile_px, tile_px), jnp.float32),
+            jax.ShapeDtypeStruct((tile_px, tile_px), jnp.float32),
+        ],
+        compiler_params=pltpu.CompilerParams(dimension_semantics=("arbitrary",)),
+        cost_estimate=pl.CostEstimate(
+            flops=12 * planes * tile_px * tile_px, transcendentals=0,
+            bytes_accessed=out_bytes + in_bytes,
+        ),
+    )(idx, offsets.reshape(-1), bands.reshape(-1), terms, tiles, tiles, from_left, from_left,
+      from_up, from_corner)
 
 
 def shifted(block, axis, count, step):
@@ -168,64 +278,14 @@
     final_left = shifted(final, "col", n_col, 1)
     final_up = shifted(final, "row", n_row, 1)
     final_corner = lax.ppermute(final, ("col", "row"), diagonal)
-    found = {
-        "own": (own_gain, own_level),
-        "left": (final_left[:planes], final_left[planes:]),
-        "up": (final_up[:planes], final_up[planes:]),
-        "corner": (final_corner[:planes], final_corner[planes:]),
-    }
-
-    def terms_at(which):
-        return found[which]
-
-    has_left = (col_index > 0).astype(jnp.float32)
-    has_up = (row_index > 0).astype(jnp.float32)
-    ids = jnp.arange(tile_px, dtype=jnp.int32)
-    edge = jnp.arange(width, dtype=jnp.int32)
-
-    def weights_of(r, c, row_ids, col_ids, present):
-        rows_w = row_weight(row_ids, bands[0, r, c], bands[1, r, c], tile_px, present)
-        cols_w = col_weight(col_ids, tile_px, jnp.float32(1.0))
-        return rows_w, cols_w
-
-    top, left = offsets[0, row_index, col_index], offsets[1, row_index, col_index]
-    rows_w, cols_w = weights_of(row_index, col_index, ids - top, ids - left, jnp.float32(1.0))
-    own_vals, own_w = piece(
-        tiles, ((0, 0), (SPILL, 0), (SPILL, 0)), (SPILL - top, SPILL - left),
-        (planes, tile_px, tile_px), rows_w, cols_w, *terms_at("own"),
-    )
-    top_l, left_l = offsets[0, row_index, left_col], offsets[1, row_index, left_col]
-    rows_w, cols_w = weights_of(
-        row_index, left_col, ids - top_l, edge + tile_px - left_l, has_left
-    )
-    left_vals, left_w = piece(
-        from_left, ((0, 0), (SPILL, 0), (0, width)), (SPILL - top_l, width - left_l),
-        (planes, tile_px, width), rows_w, cols_w, *terms_at("left"),
-    )
-    top_u, left_u = offsets[0, upper_row, col_index], offsets[1, upper_row, col_index]
-    rows_w, cols_w = weights_of(
-        upper_row, col_index, edge + tile_px - top_u, ids - left_u, has_up
-    )
-    up_vals, up_w = piece(
-        from_up, ((0, 0), (0, width), (SPILL, 0)), (width - top_u, SPILL - left_u),
-        (planes, width, tile_px), rows_w, cols_w, *terms_at("up"),
-    )
-    top_c, left_c = offsets[0, upper_row, left_col], offsets[1, upper_row, left_col]
-    rows_w, cols_w = weights_of(
-        upper_row, left_col, edge + tile_px - top_c, edge + tile_px - left_c, has_up * has_left
-    )
-    corner_vals, corner_w = piece(
-        from_corner, ((0, 0), (0, width), (0, width)), (width - top_c, width - left_c),
-        (planes, width, width), rows_w, cols_w, *terms_at("corner"),
-    )
-
-    blended = own_vals.at[:, :, :width].add(left_vals)
-    blended = blended.at[:, :width, :].add(up_vals)
-    blended = blended.at[:, :width, :width].add(corner_vals)
-    weight = own_w.at[:, :width].add(left_w)
-    weight = weight.at[:width, :].add(up_w)
-    weight = weight.at[:width, :width].add(corner_w)
-    return blended, weight
+    terms = jnp.concatenate([
+        jnp.exp(own_gain), own_level,
+        jnp.exp(final_left[:planes]), final_left[planes:],
+        jnp.exp(final_up[:planes]), final_up[planes:],
+        jnp.exp(final_corner[:planes]), final_corner[planes:],
+    ])
+    idx = jnp.stack([row_index, col_index]).astype(jnp.int32)
+    return blend(idx, offsets, bands, terms, tiles, from_left, from_up, from_corner, n_row, n_col)
 
 
 def solution(mesh):

time: 86.5 us -> 96 us (1.11)
  the two profiles are of different devices: /device:TPU:0 before, /device:TPU:16 now
where the time goes in v4:
time: 96 us; the launch traced here: 95 us
  starting transfers between devices  32.7 us (34%)
  Pallas kernels  22.2 us (23%)
  waiting for transfers between devices  20 us (21%)
  other arithmetic  11.5 us (12%)
  local copies, waits for them, and re-layouts  7.76 us (8%)
    ppermute x10, starting transfers between devices, shifted(): return lax.ppermute(block, axis, route)  27.5 us
    pallas_call x1, Pallas kernels, blend(): pl.pallas_call(functools.partial(blend_kernel, n_row=n_row, n_col=n_col),...  22.2 us
    ppermute x10, waiting for transfers between devices, shifted(): return lax.ppermute(block, axis, route)  20 us
    reduce_sum x4, other arithmetic, strip_stats(): covariance = jnp.sum(dev_former * dev_latter, axis=(-2, -1)) / number  4.43 us
    reduce_sum x2, other arithmetic, strip_stats(): mean_former = jnp.sum(former * full, axis=(-2, -1)) / number  3.3 us
    ppermute x1, starting transfers between devices, local(): from_corner = lax.ppermute(corner, ('col', 'row'), diagonal)  2.85 us
    ppermute x1, starting transfers between devices, local(): final_corner = lax.ppermute(final, ('col', 'row'), diagonal)  2.39 us
    slice x1, local copies, waits for them, and re-layouts, local(): up_strip = tiles[:, :width, :]  2.24 us
  transfers between devices with their start and end apart: 12, of which 3 were waited for; matrix products, arithmetic and copies ran while one was open for 19% of the time, Pallas kernels for 0%

profile of v4, /device:TPU:16, one launch (start us, length us, event | category | flops | bytes accessed | tf_op | source)
XLA Modules:
  0.0 95.0 jit_solution(11576900589099164246)
XLA Ops:
  0.7 0.9 slice.75
  1.5 2.9 %collective-permute-start.11 = (bf16[2,128,128]{2,1,0:T(8,128)(2,1)S(1)}, bf16[2,128,128]{2,1,0:T(8,128)(2,1)S(1)}, u32[]{:S(2)}, u32[]{:S(2)}) collective-permute-start(bf16[2,128,128]{2,1,0:T(8,128)(2,1)S(1)} %slice.75), channel_id=1, source_target_pairs={{0,5},{4,9},{8,13},{12,17},{16,21},{20,25},{24,29},{1,6},{5,10},{9... | collective-permute-start | bytes 196616 | tf_op jit(solution)/shard_map/ppermute | solution.py:220
  4.4 2.2 %fusion.66 = (bf16[2,128,1024]{2,1,0:T(8,128)(2,1)}, bf16[2,128,1024]{2,1,0:T(8,128)(2,1)}) fusion(bf16[2,1024,1024]{2,1,0:T(8,128)(2,1)} %prev_ref.1), kind=kLoop, calls=%fused_computation.144 | loop fusion | bytes 2097152 | tf_op jit(solution)/shard_map/slice | solution.py:211
  6.6 1.3 %collective-permute-start.1 = (bf16[2,128,1024]{2,1,0:T(8,128)(2,1)}, bf16[2,128,1024]{2,1,0:T(8,128)(2,1)S(1)}, u32[]{:S(2)}, u32[]{:S(2)}) collective-permute-start(bf16[2,128,1024]{2,1,0:T(8,128)(2,1)} %get-tuple-element.45), channel_id=1, source_target_pairs={{1,0},{2,1},{3,2},{5,4},{6,5},{7,6},{9,8},{10,9},{11,10},{13,12},{... | collective-permute-start | bytes 1572872 | tf_op jit(solution)/shard_map/ppermute | solution.py:186
  7.9 4.2 %collective-permute-start.3 = (bf16[2,128,1024]{2,1,0:T(8,128)(2,1)}, bf16[2,128,1024]{2,1,0:T(8,128)(2,1)S(1)}, u32[]{:S(2)}, u32[]{:S(2)}) collective-permute-start(bf16[2,128,1024]{2,1,0:T(8,128)(2,1)} %get-tuple-element.46), channel_id=1, source_target_pairs={{0,1},{1,2},{2,3},{4,5},{5,6},{6,7},{8,9},{9,10},{10,11},{12,13},{... | collective-permute-start | bytes 1572872 | tf_op jit(solution)/shard_map/ppermute | solution.py:186
  12.1 1.3 %fusion.65 = (bf16[2,1024,128]{2,1,0:T(8,128)(2,1)S(1)}, bf16[2,1024,128]{2,1,0:T(8,128)(2,1)S(1)}) fusion(bf16[2,1024,1024]{2,1,0:T(8,128)(2,1)} %prev_ref.1), kind=kLoop, calls=%fused_computation.143 | loop fusion | bytes 2097152 | tf_op jit(solution)/shard_map/slice | solution.py:210
  13.4 3.3 %collective-permute-start = (bf16[2,1024,128]{2,1,0:T(8,128)(2,1)S(1)}, bf16[2,1024,128]{2,1,0:T(8,128)(2,1)S(1)}, u32[]{:S(2)}, u32[]{:S(2)}) collective-permute-start(bf16[2,1024,128]{2,1,0:T(8,128)(2,1)S(1)} %get-tuple-element.43), channel_id=1, source_target_pairs={{4,0},{8,4},{12,8},{16,12},{20,16},{24,20},{28,24},{5,1},{9,5},{13... | collective-permute-start | bytes 1572872 | tf_op jit(solution)/shard_map/ppermute | solution.py:186
  16.7 2.5 %collective-permute-start.2 = (bf16[2,1024,128]{2,1,0:T(8,128)(2,1)S(1)}, bf16[2,1024,128]{2,1,0:T(8,128)(2,1)S(1)}, u32[]{:S(2)}, u32[]{:S(2)}) collective-permute-start(bf16[2,1024,128]{2,1,0:T(8,128)(2,1)S(1)} %get-tuple-element.44), channel_id=1, source_target_pairs={{0,4},{4,8},{8,12},{12,16},{16,20},{20,24},{24,28},{1,5},{5,9},{9,... | collective-permute-start | bytes 1572872 | tf_op jit(solution)/shard_map/ppermute | solution.py:186
  21.2 1.6 %compare_convert_fusion.1 = (f32[128]{0:T(128)S(1)}, f32[128]{0:T(128)S(1)}) fusion(s32[]{:T(128)} %bitcast.4, s32[]{:T(128)} %bitcast.2), kind=kLoop, calls=%fused_computation.61 | loop fusion | flops 512 | bytes 1032 | tf_op jit(solution)/shard_map/convert_element_type | solution.py:227
  22.8 1.2 %compare_convert_fusion = (f32[128]{0:T(128)S(1)}, f32[128]{0:T(128)S(1)}) fusion(s32[]{:T(128)} %bitcast.5, s32[]{:T(128)} %bitcast.3), kind=kLoop, calls=%fused_computation.60 | loop fusion | flops 512 | bytes 1032 | tf_op jit(solution)/shard_map/convert_element_type | solution.py:230
  24.7 1.7 %fusion.30 = (f32[2]{0:T(128)S(1)}, f32[2]{0:T(128)S(1)}, f32[2]{0:T(128)S(1)}) fusion(bf16[2,128,1024]{2,1,0:T(8,128)(2,1)S(1)} %collective-permute-done.3.up_ref, f32[128]{0:T(128)S(1)} %get-tuple-element.67, bf16[2,1024,1024]{2,1,0:T(8,128)(2,1)} %prev_ref.1), kind=kLoop, calls=%fused_computation.46 | loop fusion | flops 1835002 | bytes 1049112 | tf_op jit(solution)/shard_map/reduce_sum | solution.py:22
  26.4 2.2 %fusion.34 = (f32[2]{0:T(128)S(1)}, f32[2]{0:T(128)S(1)}, f32[2]{0:T(128)S(1)}, f32[2]{0:T(128)S(1)}, f32[2]{0:T(128)S(1)}, /*index=5*/f32[2]{0:T(128)S(1)}) fusion(bf16[2,128,1024]{2,1,0:T(8,128)(2,1)S(1)} %collective-permute-done.3.up_ref, f32[2]{0:T(128)S(1)} %get-tuple-element.64, f32[2]{0:T(128)S(1)} %get-tuple-element.63, ...), kind=kLoop, calls=%fused_computation.50 | loop fusion | flops 4980724 | bytes 2098240 | tf_op jit(solution)/shard_map/reduce_sum | solution.py:28
  28.5 12.7 %collective-permute-done.2.lcur_ref.lprev_ref = bf16[2,1024,128]{2,1,0:T(8,128)(2,1)S(1)} collective-permute-done((bf16[2,1024,128]{2,1,0:T(8,128)(2,1)S(1)}, bf16[2,1024,128]{2,1,0:T(8,128)(2,1)S(1)}, u32[]{:S(2)}, u32[]{:S(2)}) %collective-permute-start.2) | collective-permute-done | bytes 524320 | tf_op jit(solution)/shard_map/ppermute | solution.py:186
  41.2 1.6 %fusion.20 = (f32[2]{0:T(128)S(1)}, f32[2]{0:T(128)S(1)}, f32[2]{0:T(128)S(1)}) fusion(bf16[2,1024,128]{2,1,0:T(8,128)(2,1)S(1)} %collective-permute-done.2.lcur_ref.lprev_ref, f32[128]{0:T(128)S(1)} %get-tuple-element.65, bf16[2,1024,1024]{2,1,0:T(8,128)(2,1)} %prev_ref.1), kind=kLoop, calls=%fused_computation.36 | loop fusion | flops 1835002 | bytes 1049112 | tf_op jit(solution)/shard_map/reduce_sum | solution.py:22
  45.3 2.1 %collective-permute-start.7 = (f32[4]{0:T(128)S(1)}, f32[4]{0:T(128)S(1)}, u32[]{:S(2)}, u32[]{:S(2)}) collective-permute-start(f32[4]{0:T(128)S(1)} %pad_maximum_fusion), channel_id=1, source_target_pairs={{0,1},{1,2},{2,3},{4,5},{5,6},{6,7},{8,9},{9,10},{10,11},{12,13},{... | collective-permute-start | bytes 56 | tf_op jit(solution)/shard_map/ppermute | solution.py:186
  47.4 4.3 %collective-permute-start.6 = (f32[4]{0:T(128)S(1)}, f32[4]{0:T(128)S(1)}, u32[]{:S(2)}, u32[]{:S(2)}) collective-permute-start(f32[4]{0:T(128)S(1)} %pad_maximum_fusion), channel_id=1, source_target_pairs={{0,4},{4,8},{8,12},{12,16},{16,20},{20,24},{24,28},{1,5},{5,9},{9,... | collective-permute-start | bytes 56 | tf_op jit(solution)/shard_map/ppermute | solution.py:186
  51.7 1.3 %collective-permute-start.5 = (f32[4]{0:T(128)S(1)}, f32[4]{0:T(128)S(1)}, u32[]{:S(2)}, u32[]{:S(2)}) collective-permute-start(f32[4]{0:T(128)S(1)} %pad_maximum_fusion), channel_id=1, source_target_pairs={{1,0},{2,1},{3,2},{5,4},{6,5},{7,6},{9,8},{10,9},{11,10},{13,12},{... | collective-permute-start | bytes 56 | tf_op jit(solution)/shard_map/ppermute | solution.py:186
  53.0 2.4 %collective-permute-start.4 = (f32[4]{0:T(128)S(1)}, f32[4]{0:T(128)S(1)}, u32[]{:S(2)}, u32[]{:S(2)}) collective-permute-start(f32[4]{0:T(128)S(1)} %pad_maximum_fusion), channel_id=1, source_target_pairs={{4,0},{8,4},{12,8},{16,12},{20,16},{24,20},{28,24},{5,1},{9,5},{13... | collective-permute-start | bytes 56 | tf_op jit(solution)/shard_map/ppermute | solution.py:186
  55.5 3.0 %collective-permute-done.4 = f32[4]{0:T(128)S(1)} collective-permute-done((f32[4]{0:T(128)S(1)}, f32[4]{0:T(128)S(1)}, u32[]{:S(2)}, u32[]{:S(2)}) %collective-permute-start.4) | collective-permute-done | bytes 48 | tf_op jit(solution)/shard_map/ppermute | solution.py:186
  58.6 2.4 %collective-permute-start.10 = (f32[4]{0:T(128)S(1)}, f32[4]{0:T(128)S(1)}, u32[]{:S(2)}, u32[]{:S(2)}) collective-permute-start(f32[4]{0:T(128)S(1)} %pad_maximum_fusion.1), channel_id=1, source_target_pairs={{0,5},{4,9},{8,13},{12,17},{16,21},{20,25},{24,29},{1,6},{5,10},{9... | collective-permute-start | bytes 56 | tf_op jit(solution)/shard_map/ppermute | solution.py:280
  61.0 4.1 %collective-permute-start.9 = (f32[4]{0:T(128)S(1)}, f32[4]{0:T(128)S(1)}, u32[]{:S(2)}, u32[]{:S(2)}) collective-permute-start(f32[4]{0:T(128)S(1)} %pad_maximum_fusion.1), channel_id=1, source_target_pairs={{0,1},{1,2},{2,3},{4,5},{5,6},{6,7},{8,9},{9,10},{10,11},{12,13},{... | collective-permute-start | bytes 56 | tf_op jit(solution)/shard_map/ppermute | solution.py:186
  65.2 1.9 %collective-permute-start.8 = (f32[4]{0:T(128)S(1)}, f32[4]{0:T(128)S(1)}, u32[]{:S(2)}, u32[]{:S(2)}) collective-permute-start(f32[4]{0:T(128)S(1)} %pad_maximum_fusion.1), channel_id=1, source_target_pairs={{0,4},{4,8},{8,12},{12,16},{16,20},{20,24},{24,28},{1,5},{5,9},{9,... | collective-permute-start | bytes 56 | tf_op jit(solution)/shard_map/ppermute | solution.py:186
  67.3 4.3 %collective-permute-done.8 = f32[4]{0:T(128)S(1)} collective-permute-done((f32[4]{0:T(128)S(1)}, f32[4]{0:T(128)S(1)}, u32[]{:S(2)}, u32[]{:S(2)}) %collective-permute-start.8) | collective-permute-done | bytes 48 | tf_op jit(solution)/shard_map/ppermute | solution.py:186
  72.9 22.2 %shard_map.59 = (f32[2,1024,1024]{2,1,0:T(8,128)}, f32[1024,1024]{1,0:T(8,128)}) custom-call(s32[2]{0:T(128)} %pad_add_fusion.idx_ref, s32[64]{0:T(128)} %reshape.70.off_ref, s32[64]{0:T(128)} %reshape.71.band_ref, f32[16]{0:T(128)} %concatenate.11.terms_ref, bf16[2,1024,1024]{2,1,0:T(8,128)(2,1)} %prev_ref.1, bf16[2,1024,1024]{2,1,0:T(8,128)(2,1)} %prev_ref.1, ...), custom_call_target="tpu_custom_call" | custom-call | flops 25165824 | bytes 22020096 | tf_op jit(solution)/shard_map/pallas_call | solution.py:165
  (44 shorter events, 6.6 us)
Async XLA Ops:
  0.6 18.6 %copy-start.4 = (s32[2,4,8]{2,1,0:T(4,128)S(1)}, s32[2,4,8]{2,1,0:T(4,128)}, u32[]{:S(2)}) copy-start(s32[2,4,8]{2,1,0:T(4,128)} %param.6) | copy-start | bytes 772
  0.6 19.2 %copy-start.5 = (s32[2,4,8]{2,1,0:T(4,128)S(1)}, s32[2,4,8]{2,1,0:T(4,128)}, u32[]{:S(2)}) copy-start(s32[2,4,8]{2,1,0:T(4,128)} %param.7) | copy-start | bytes 772
  0.7 19.9 %copy-start.6 = (s32[2,4,8]{2,1,0:T(4,128)S(1)}, s32[2,4,8]{2,1,0:T(4,128)}, u32[]{:S(2)}) copy-start(s32[2,4,8]{2,1,0:T(4,128)} %param.5) | copy-start | bytes 772
  1.5 70.7 %collective-permute-start.11 = (bf16[2,128,128]{2,1,0:T(8,128)(2,1)S(1)}, bf16[2,128,128]{2,1,0:T(8,128)(2,1)S(1)}, u32[]{:S(2)}, u32[]{:S(2)}) collective-permute-start(bf16[2,128,128]{2,1,0:T(8,128)(2,1)S(1)} %slice.75), channel_id=1, source_target_pairs={{0,5},{4,9},{8,13},{12,17},{16,21},{20,25},{24,29},{1,6},{5,10},{9... | collective-permute-start | bytes 196616 | tf_op jit(solution)/shard_map/ppermute | solution.py:220
  6.6 19.7 %collective-permute-start.1 = (bf16[2,128,1024]{2,1,0:T(8,128)(2,1)}, bf16[2,128,1024]{2,1,0:T(8,128)(2,1)S(1)}, u32[]{:S(2)}, u32[]{:S(2)}) collective-permute-start(bf16[2,128,1024]{2,1,0:T(8,128)(2,1)} %get-tuple-element.45), channel_id=1, source_target_pairs={{1,0},{2,1},{3,2},{5,4},{6,5},{7,6},{9,8},{10,9},{11,10},{13,12},{... | collective-permute-start | bytes 1572872 | tf_op jit(solution)/shard_map/ppermute | solution.py:186
  7.9 16.7 %collective-permute-start.3 = (bf16[2,128,1024]{2,1,0:T(8,128)(2,1)}, bf16[2,128,1024]{2,1,0:T(8,128)(2,1)S(1)}, u32[]{:S(2)}, u32[]{:S(2)}) collective-permute-start(bf16[2,128,1024]{2,1,0:T(8,128)(2,1)} %get-tuple-element.46), channel_id=1, source_target_pairs={{0,1},{1,2},{2,3},{4,5},{5,6},{6,7},{8,9},{9,10},{10,11},{12,13},{... | collective-permute-start | bytes 1572872 | tf_op jit(solution)/shard_map/ppermute | solution.py:186
  13.4 29.4 %collective-permute-start = (bf16[2,1024,128]{2,1,0:T(8,128)(2,1)S(1)}, bf16[2,1024,128]{2,1,0:T(8,128)(2,1)S(1)}, u32[]{:S(2)}, u32[]{:S(2)}) collective-permute-start(bf16[2,1024,128]{2,1,0:T(8,128)(2,1)S(1)} %get-tuple-element.43), channel_id=1, source_target_pairs={{4,0},{8,4},{12,8},{16,12},{20,16},{24,20},{28,24},{5,1},{9,5},{13... | collective-permute-start | bytes 1572872 | tf_op jit(solution)/shard_map/ppermute | solution.py:186
  16.7 24.5 %collective-permute-start.2 = (bf16[2,1024,128]{2,1,0:T(8,128)(2,1)S(1)}, bf16[2,1024,128]{2,1,0:T(8,128)(2,1)S(1)}, u32[]{:S(2)}, u32[]{:S(2)}) collective-permute-start(bf16[2,1024,128]{2,1,0:T(8,128)(2,1)S(1)} %get-tuple-element.44), channel_id=1, source_target_pairs={{0,4},{4,8},{8,12},{12,16},{16,20},{20,24},{24,28},{1,5},{5,9},{9,... | collective-permute-start | bytes 1572872 | tf_op jit(solution)/shard_map/ppermute | solution.py:186
  20.5 22.3 %copy-start = (bf16[2,1024,1024]{2,1,0:T(8,128)(2,1)S(1)}, bf16[2,1024,1024]{2,1,0:T(8,128)(2,1)}, u32[]{:S(2)}) copy-start(bf16[2,1024,1024]{2,1,0:T(8,128)(2,1)} %prev_ref.1) | copy-start | bytes 12582916
  24.7 20.5 %copy-start.2 = (bf16[2,128,1024]{2,1,0:T(8,128)(2,1)}, bf16[2,128,1024]{2,1,0:T(8,128)(2,1)S(1)}, u32[]{:S(2)}) copy-start(bf16[2,128,1024]{2,1,0:T(8,128)(2,1)S(1)} %collective-permute-done.3.up_ref) | copy-start | bytes 1572868
  41.2 31.0 %copy-start.1 = (bf16[2,1024,128]{2,1,0:T(8,128)(2,1)}, bf16[2,1024,128]{2,1,0:T(8,128)(2,1)S(1)}, u32[]{:S(2)}) copy-start(bf16[2,1024,128]{2,1,0:T(8,128)(2,1)S(1)} %collective-permute-done.2.lcur_ref.lprev_ref) | copy-start | bytes 1572868
  45.3 10.2 %collective-permute-start.7 = (f32[4]{0:T(128)S(1)}, f32[4]{0:T(128)S(1)}, u32[]{:S(2)}, u32[]{:S(2)}) collective-permute-start(f32[4]{0:T(128)S(1)} %pad_maximum_fusion), channel_id=1, source_target_pairs={{0,1},{1,2},{2,3},{4,5},{5,6},{6,7},{8,9},{9,10},{10,11},{12,13},{... | collective-permute-start | bytes 56 | tf_op jit(solution)/shard_map/ppermute | solution.py:186
  47.4 8.1 %collective-permute-start.6 = (f32[4]{0:T(128)S(1)}, f32[4]{0:T(128)S(1)}, u32[]{:S(2)}, u32[]{:S(2)}) collective-permute-start(f32[4]{0:T(128)S(1)} %pad_maximum_fusion), channel_id=1, source_target_pairs={{0,4},{4,8},{8,12},{12,16},{16,20},{20,24},{24,28},{1,5},{5,9},{9,... | collective-permute-start | bytes 56 | tf_op jit(solution)/shard_map/ppermute | solution.py:186
  51.7 3.8 %collective-permute-start.5 = (f32[4]{0:T(128)S(1)}, f32[4]{0:T(128)S(1)}, u32[]{:S(2)}, u32[]{:S(2)}) collective-permute-start(f32[4]{0:T(128)S(1)} %pad_maximum_fusion), channel_id=1, source_target_pairs={{1,0},{2,1},{3,2},{5,4},{6,5},{7,6},{9,8},{10,9},{11,10},{13,12},{... | collective-permute-start | bytes 56 | tf_op jit(solution)/shard_map/ppermute | solution.py:186
  53.0 5.5 %collective-permute-start.4 = (f32[4]{0:T(128)S(1)}, f32[4]{0:T(128)S(1)}, u32[]{:S(2)}, u32[]{:S(2)}) collective-permute-start(f32[4]{0:T(128)S(1)} %pad_maximum_fusion), channel_id=1, source_target_pairs={{4,0},{8,4},{12,8},{16,12},{20,16},{24,20},{28,24},{5,1},{9,5},{13... | collective-permute-start | bytes 56 | tf_op jit(solution)/shard_map/ppermute | solution.py:186
  58.6 8.5 %collective-permute-start.10 = (f32[4]{0:T(128)S(1)}, f32[4]{0:T(128)S(1)}, u32[]{:S(2)}, u32[]{:S(2)}) collective-permute-start(f32[4]{0:T(128)S(1)} %pad_maximum_fusion.1), channel_id=1, source_target_pairs={{0,5},{4,9},{8,13},{12,17},{16,21},{20,25},{24,29},{1,6},{5,10},{9... | collective-permute-start | bytes 56 | tf_op jit(solution)/shard_map/ppermute | solution.py:280
  61.0 6.2 %collective-permute-start.9 = (f32[4]{0:T(128)S(1)}, f32[4]{0:T(128)S(1)}, u32[]{:S(2)}, u32[]{:S(2)}) collective-permute-start(f32[4]{0:T(128)S(1)} %pad_maximum_fusion.1), channel_id=1, source_target_pairs={{0,1},{1,2},{2,3},{4,5},{5,6},{6,7},{8,9},{9,10},{10,11},{12,13},{... | collective-permute-start | bytes 56 | tf_op jit(solution)/shard_map/ppermute | solution.py:186
  65.2 6.4 %collective-permute-start.8 = (f32[4]{0:T(128)S(1)}, f32[4]{0:T(128)S(1)}, u32[]{:S(2)}, u32[]{:S(2)}) collective-permute-start(f32[4]{0:T(128)S(1)} %pad_maximum_fusion.1), channel_id=1, source_target_pairs={{0,4},{4,8},{8,12},{12,16},{16,20},{20,24},{24,28},{1,5},{5,9},{9,... | collective-permute-start | bytes 56 | tf_op jit(solution)/shard_map/ppermute | solution.py:186
  72.2 0.6 copy-start.3

commit v5 on v3

--- a/solution.py
+++ b/solution.py
@@ -102,8 +102,6 @@
     corner = tiles[:, tile_px - width :, tile_px - width :]
     from_left = shifted(right_strip, "col", n_col, 1)
     from_up = shifted(down_strip, "row", n_row, 1)
-    from_right = shifted(left_strip, "col", n_col, -1)
-    from_down = shifted(up_strip, "row", n_row, -1)
     diagonal = [
         (j * n_row + i, (j + 1) * n_row + i + 1) for i in range(n_row - 1) for j in range(n_col - 1)
     ]
@@ -120,18 +118,14 @@
         return (strip_ids < extent).astype(jnp.float32)[None, :, None]
 
     f32 = jnp.float32
-    right_stats = strip_stats(
-        right_strip.astype(f32), from_right.astype(f32), across(extents[0, row_index, col_index])
-    )
-    down_stats = strip_stats(
-        down_strip.astype(f32), from_down.astype(f32), along(extents[1, row_index, col_index])
-    )
     left_stats = strip_stats(
         from_left.astype(f32), left_strip.astype(f32), across(extents[0, row_index, left_col])
     )
     up_stats = strip_stats(
         from_up.astype(f32), up_strip.astype(f32), along(extents[1, upper_row, col_index])
     )
+    right_stats = shifted(left_stats, "col", n_col, -1)
+    down_stats = shifted(up_stats, "row", n_row, -1)
     has_right = col_index < n_col - 1
     has_down = row_index < n_row - 1
     has_left_pair = col_index > 0

time: 86.5 us -> 98.8 us (1.14)
  other arithmetic: 19.4 us -> 28.2 us
  local copies, waits for them, and re-layouts: 10 us -> 12.6 us
  waiting for transfers between devices: 4.17 us -> 6.04 us
  starting transfers between devices: 36.4 us -> 34.8 us
    ppermute x10, starting transfers between devices: 29.1 us -> 26 us  [shifted(): return lax.ppermute(block, axis, route)]
    mul x1, other arithmetic: 0.34 us -> 2.35 us  [piece(): weight = rows_w[:, None] * cols_w[None, :]]
    reduce_sum x2, other arithmetic: 0.95 us -> 2.93 us  [strip_stats(): mean_former = jnp.sum(former * full, axis=(-2, -1)) / number]
    mul x1, other arithmetic: 3.35 us -> 5.31 us  [piece(): (jnp.exp(log_gain)[:, None, None] * window.astype(jnp.float32) + level[:,...]
    ppermute x10, waiting for transfers between devices: 4.16 us -> 6.03 us  [shifted(): return lax.ppermute(block, axis, route)]
    scatter-add x1, other arithmetic: 0.19 us -> 2 us  [local(): weight = weight.at[:width, :].add(up_w)]
    scatter-add x1, other arithmetic: 1.02 us -> 2.73 us  [local(): weight = own_w.at[:, :width].add(left_w)]
    ppermute x1, starting transfers between devices: 3 us -> 4.39 us  [local(): final_corner = lax.ppermute(final, ('col', 'row'), diagonal)]
  transfers between devices with their start and end apart: 12 -> 12, of which waited for: 2 -> 3; matrix products, arithmetic and copies ran while one was open for 29% -> 37% of each run, Pallas kernels for 0% -> 0%
where the time goes in v5:
time: 98.8 us; the launch traced here: 97.6 us
  starting transfers between devices  34.8 us (35%)
  other arithmetic  28.2 us (29%)
  between operations  15.9 us (16%)
  local copies, waits for them, and re-layouts  12.6 us (13%)
  waiting for transfers between devices  6.04 us (6%)
    ppermute x10, starting transfers between devices, shifted(): return lax.ppermute(block, axis, route)  26 us
    ppermute x10, waiting for transfers between devices, shifted(): return lax.ppermute(block, axis, route)  6.03 us
    mul x1, other arithmetic, piece(): (jnp.exp(log_gain)[:, None, None] * window.astype(jnp.float32) + level[:,...  5.31 us
    ppermute x1, starting transfers between devices, local(): final_corner = lax.ppermute(final, ('col', 'row'), diagonal)  4.39 us
    ppermute x1, starting transfers between devices, local(): from_corner = lax.ppermute(corner, ('col', 'row'), diagonal)  4.33 us
    reduce_sum x2, other arithmetic, strip_stats(): covariance = jnp.sum(dev_former * dev_latter, axis=(-2, -1)) / number  3.52 us
    unnamed x2, local copies, waits for them, and re-layouts  3.4 us
    mul x3, other arithmetic, row_weight(): return live.astype(jnp.float32) * present * fade(ids, tile_px)  3.02 us
  transfers between devices with their start and end apart: 12, of which 3 were waited for; matrix products, arithmetic and copies ran while one was open for 37% of the time, Pallas kernels for 0%

profile of v5, /device:TPU:0, one launch (start us, length us, event | category | flops | bytes accessed | tf_op | source)
XLA Modules:
  0.0 97.6 jit_solution(6017997561787808673)
XLA Ops:
  1.5 4.3 %collective-permute-start.11 = (bf16[2,128,128]{2,1,0:T(8,128)(2,1)S(1)}, bf16[2,128,128]{2,1,0:T(8,128)(2,1)S(1)}, u32[]{:S(2)}, u32[]{:S(2)}) collective-permute-start(bf16[2,128,128]{2,1,0:T(8,128)(2,1)S(1)} %slice.216), channel_id=1, source_target_pairs={{0,5},{4,9},{8,13},{12,17},{16,21},{20,25},{24,29},{1,6},{5,10},{9... | collective-permute-start | bytes 196616 | tf_op jit(solution)/shard_map/ppermute | solution.py:108
  6.9 3.5 %collective-permute-start = (bf16[2,1024,128]{2,1,0:T(8,128)(2,1)S(1)}, bf16[2,1024,128]{2,1,0:T(8,128)(2,1)S(1)}, u32[]{:S(2)}, u32[]{:S(2)}) collective-permute-start(bf16[2,1024,128]{2,1,0:T(8,128)(2,1)S(1)} %slice.196), channel_id=1, source_target_pairs={{0,4},{4,8},{8,12},{12,16},{16,20},{20,24},{24,28},{1,5},{5,9},{9,... | collective-permute-start | bytes 1572872 | tf_op jit(solution)/shard_map/ppermute | solution.py:76
  11.5 3.3 %collective-permute-start.2 = (bf16[2,128,1024]{2,1,0:T(8,128)(2,1)S(1)}, bf16[2,128,1024]{2,1,0:T(8,128)(2,1)S(1)}, u32[]{:S(2)}, u32[]{:S(2)}) collective-permute-start(bf16[2,128,1024]{2,1,0:T(8,128)(2,1)S(1)} %slice.198), channel_id=1, source_target_pairs={{0,1},{1,2},{2,3},{4,5},{5,6},{6,7},{8,9},{9,10},{10,11},{12,13},{... | collective-permute-start | bytes 1572872 | tf_op jit(solution)/shard_map/ppermute | solution.py:76
  15.4 1.5 %constant_dynamic-slice_fusion.10 = (s32[1,1,1]{2,1,0:T(1,128)}, s32[1,1,1]{2,1,0:T(1,128)}, s32[1,1,1]{2,1,0:T(1,128)}, s32[1,1,1]{2,1,0:T(1,128)}, s32[1,1,1]{...) fusion(s32[2,4,8]{2,1,0:T(4,128)} %param.18, s32[]{:T(128)S(6)} %max.7, s32[]{:T(128)S(6)} %max.6, ...), kind=kLoop, calls=%fused_computation.105 | loop fusion | bytes 80 | tf_op jit(solution)/shard_map/dynamic_slice | solution.py:207
  28.7 1.3 %constant_dynamic-slice_fusion.8 = (s32[1,1,1]{2,1,0:T(1,128)}, s32[1,1,1]{2,1,0:T(1,128)}) fusion(s32[2,4,8]{2,1,0:T(4,128)} %param.17, s32[]{:T(128)S(6)} %select_n.171, s32[]{:T(128)S(6)} %max.6, s32[]{:T(128)S(6)} %max.7, s32[]{:T(128)S(6)} %select_n.174), kind=kLoop, calls=%fused_computation.63 | loop fusion | bytes 32 | tf_op jit(solution)/shard_map/dynamic_slice | solution.py:122
  30.7 1.6 %constant_dynamic-slice_fusion = (s32[1,1,1]{2,1,0:T(1,128)}, s32[1,1,1]{2,1,0:T(1,128)}, s32[1,1,1]{2,1,0:T(1,128)}, s32[1,1,1]{2,1,0:T(1,128)}, s32[1,1,1]{2,1...) fusion(s32[2,4,8]{2,1,0:T(4,128)} %param.19, s32[]{:T(128)S(6)} %max.7, s32[]{:T(128)S(6)} %max.6, ...), kind=kLoop, calls=%fused_computation.53 | loop fusion | bytes 80 | tf_op jit(solution)/shard_map/dynamic_slice | solution.py:181
  41.1 2.4 %broadcast_multiply_fusion = f32[1024,1024]{1,0:T(8,128)} fusion(f32[1024]{0:T(1024)S(1)} %get-tuple-element.143, f32[1024]{0:T(1024)S(1)} %get-tuple-element.142), kind=kLoop, calls=%fused_computation.2 | loop fusion | flops 1048576 | bytes 4202496 | tf_op jit(solution)/shard_map/mul | solution.py:64
  43.4 1.4 %fusion = (f32[2]{0:T(128)S(1)}, f32[2]{0:T(128)S(1)}, f32[2]{0:T(128)S(1)}) fusion(bf16[2,1024,128]{2,1,0:T(8,128)(2,1)S(1)} %collective-permute-done, f32[128]{0:T(128)S(1)} %compare_convert_fusion.1, bf16[2,1024,1024]{2,1,0:T(8,128)(2,1)} %param.16), kind=kLoop, calls=%fused_computation.13 | loop fusion | flops 1835002 | bytes 1049112 | tf_op jit(solution)/shard_map/reduce_sum | solution.py:17
  45.1 1.7 %fusion.5 = (f32[2]{0:T(128)S(1)}, f32[2]{0:T(128)S(1)}, f32[2]{0:T(128)S(1)}) fusion(bf16[2,1024,128]{2,1,0:T(8,128)(2,1)S(1)} %collective-permute-done, f32[2]{0:T(128)S(1)} %get-tuple-element.139, f32[2]{0:T(128)S(1)} %get-tuple-element.138, f32[128]{0:T(128)S(1)} %compare_convert_fusion.1, bf16[2,1024,1024]{2,1,0:T(8,128)(2,1)} %param.16), kind=kLoop, calls=%fused_computation.18 | loop fusion | flops 3145722 | bytes 1049128 | tf_op jit(solution)/shard_map/reduce_sum | solution.py:23
  48.5 1.5 %fusion.10 = (f32[2]{0:T(128)S(1)}, f32[2]{0:T(128)S(1)}, f32[2]{0:T(128)S(1)}) fusion(bf16[2,128,1024]{2,1,0:T(8,128)(2,1)S(1)} %collective-permute-done.2, f32[128]{0:T(128)S(1)} %compare_convert_fusion, bf16[2,1024,1024]{2,1,0:T(8,128)(2,1)} %param.16), kind=kLoop, calls=%fused_computation.23 | loop fusion | flops 1835002 | bytes 1049112 | tf_op jit(solution)/shard_map/reduce_sum | solution.py:17
  50.2 1.8 %fusion.15 = (f32[2]{0:T(128)S(1)}, f32[2]{0:T(128)S(1)}, f32[2]{0:T(128)S(1)}) fusion(bf16[2,128,1024]{2,1,0:T(8,128)(2,1)S(1)} %collective-permute-done.2, f32[2]{0:T(128)S(1)} %get-tuple-element.141, f32[2]{0:T(128)S(1)} %get-tuple-element.140, f32[128]{0:T(128)S(1)} %compare_convert_fusion, bf16[2,1024,1024]{2,1,0:T(8,128)(2,1)} %param.16), kind=kLoop, calls=%fused_computation.28 | loop fusion | flops 3145722 | bytes 1049128 | tf_op jit(solution)/shard_map/reduce_sum | solution.py:23
  53.9 1.5 %collective-permute-done.3 = f32[5,2]{0,1:T(2,128)S(1)} collective-permute-done((f32[5,2]{0,1:T(2,128)S(1)}, f32[5,2]{0,1:T(2,128)S(1)}, u32[]{:S(2)}, u32[]{:S(2)}) %collective-permute-start.3) | collective-permute-done | bytes 72 | tf_op jit(solution)/shard_map/ppermute | solution.py:76
  55.8 4.0 %collective-permute-start.7 = (f32[4]{0:T(128)S(1)}, f32[4]{0:T(128)S(1)}, u32[]{:S(2)}, u32[]{:S(2)}) collective-permute-start(f32[4]{0:T(128)S(1)} %pad_maximum_fusion), channel_id=1, source_target_pairs={{0,1},{1,2},{2,3},{4,5},{5,6},{6,7},{8,9},{9,10},{10,11},{12,13},{... | collective-permute-start | bytes 56 | tf_op jit(solution)/shard_map/ppermute | solution.py:76
  59.8 4.3 %collective-permute-start.6 = (f32[4]{0:T(128)S(1)}, f32[4]{0:T(128)S(1)}, u32[]{:S(2)}, u32[]{:S(2)}) collective-permute-start(f32[4]{0:T(128)S(1)} %pad_maximum_fusion), channel_id=1, source_target_pairs={{0,4},{4,8},{8,12},{12,16},{16,20},{20,24},{24,28},{1,5},{5,9},{9,... | collective-permute-start | bytes 56 | tf_op jit(solution)/shard_map/ppermute | solution.py:76
  64.1 1.3 %collective-permute-start.5 = (f32[4]{0:T(128)S(1)}, f32[4]{0:T(128)S(1)}, u32[]{:S(2)}, u32[]{:S(2)}) collective-permute-start(f32[4]{0:T(128)S(1)} %pad_maximum_fusion), channel_id=1, source_target_pairs={{1,0},{2,1},{3,2},{5,4},{6,5},{7,6},{9,8},{10,9},{11,10},{13,12},{... | collective-permute-start | bytes 56 | tf_op jit(solution)/shard_map/ppermute | solution.py:76
  65.4 1.3 %collective-permute-start.4 = (f32[4]{0:T(128)S(1)}, f32[4]{0:T(128)S(1)}, u32[]{:S(2)}, u32[]{:S(2)}) collective-permute-start(f32[4]{0:T(128)S(1)} %pad_maximum_fusion), channel_id=1, source_target_pairs={{4,0},{8,4},{12,8},{16,12},{20,16},{24,20},{28,24},{5,1},{9,5},{13... | collective-permute-start | bytes 56 | tf_op jit(solution)/shard_map/ppermute | solution.py:76
  67.1 4.1 %collective-permute-done.4 = f32[4]{0:T(128)S(1)} collective-permute-done((f32[4]{0:T(128)S(1)}, f32[4]{0:T(128)S(1)}, u32[]{:S(2)}, u32[]{:S(2)}) %collective-permute-start.4) | collective-permute-done | bytes 48 | tf_op jit(solution)/shard_map/ppermute | solution.py:76
  71.4 4.4 %collective-permute-start.10 = (f32[4]{0:T(128)S(1)}, f32[4]{0:T(128)S(1)}, u32[]{:S(2)}, u32[]{:S(2)}) collective-permute-start(f32[4]{0:T(128)S(1)} %pad_maximum_fusion.1), channel_id=1, source_target_pairs={{0,5},{4,9},{8,13},{12,17},{16,21},{20,25},{24,29},{1,6},{5,10},{9... | collective-permute-start | bytes 56 | tf_op jit(solution)/shard_map/ppermute | solution.py:164
  75.8 3.9 %collective-permute-start.9 = (f32[4]{0:T(128)S(1)}, f32[4]{0:T(128)S(1)}, u32[]{:S(2)}, u32[]{:S(2)}) collective-permute-start(f32[4]{0:T(128)S(1)} %pad_maximum_fusion.1), channel_id=1, source_target_pairs={{0,1},{1,2},{2,3},{4,5},{5,6},{6,7},{8,9},{9,10},{10,11},{12,13},{... | collective-permute-start | bytes 56 | tf_op jit(solution)/shard_map/ppermute | solution.py:76
  79.7 2.0 %collective-permute-start.8 = (f32[4]{0:T(128)S(1)}, f32[4]{0:T(128)S(1)}, u32[]{:S(2)}, u32[]{:S(2)}) collective-permute-start(f32[4]{0:T(128)S(1)} %pad_maximum_fusion.1), channel_id=1, source_target_pairs={{0,4},{4,8},{8,12},{12,16},{16,20},{20,24},{24,28},{1,5},{5,9},{9,... | collective-permute-start | bytes 56 | tf_op jit(solution)/shard_map/ppermute | solution.py:76
  81.8 5.3 %add_multiply_fusion = f32[2,1024,1024]{2,1,0:T(8,128)S(1)} fusion(s32[]{:T(128)S(6)} %select_n.196, s32[]{:T(128)S(6)} %select_n.197, bf16[2,1024,1024]{2,1,0:T(8,128)(2,1)} %param.16, f32[1024,1024]{1,0:T(8,128)} %broadcast_multiply_fusion, f32[2]{0:T(128)S(1)} %divide_add_fusion, f32[2]{0:T(128)S(1)} %get-tuple-element.100), kind=kLoop, calls=%fused_computation | loop fusion | flops 8388608 | bytes 16777240 | tf_op jit(solution)/shard_map/mul | solution.py:65
  87.1 2.7 %fusion.21 = (f32[1024,1024]{1,0:T(8,128)}, f32[1024,128]{1,0:T(8,128)S(1)}) fusion(f32[1024,1024]{1,0:T(8,128)} %broadcast_multiply_fusion, pred[]{:T(512)} %compare_reduce_fusion, f32[128]{0:T(128)S(1)} %get-tuple-element.145, f32[1024]{0:T(1024)S(1)} %fusion.35), kind=kLoop, calls=%fused_computation.37 | loop fusion | flops 393216 | bytes 1577984 | tf_op jit(solution)/shard_map/scatter-add | solution.py:219
  89.8 2.0 %constant_dynamic-update-slice_fusion = (f32[1024,1024]{1,0:T(8,128)}, f32[128,1024]{1,0:T(8,128)S(1)}, f32[128,1024]{1,0:T(8,128)S(1)}) fusion(f32[1024,1024]{1,0:T(8,128)} %get-tuple-element.104, f32[1024]{0:T(1024)S(1)} %fusion.39, f32[128]{0:T(128)S(1)} %get-tuple-element.146), kind=kLoop, calls=%fused_computation.54 | loop fusion | flops 262144 | bytes 2101760 | tf_op jit(solution)/shard_map/scatter-add | solution.py:220
  94.2 3.4 %copy-done = f32[2,1024,1024]{2,1,0:T(8,128)} copy-done((f32[2,1024,1024]{2,1,0:T(8,128)}, f32[2,1024,1024]{2,1,0:T(8,128)S(1)}, u32[]{:S(2)}) %copy-start) | copy-done | bytes 8388632
  (55 shorter events, 17.3 us)
Async XLA Ops:
  1.5 92.5 %collective-permute-start.11 = (bf16[2,128,128]{2,1,0:T(8,128)(2,1)S(1)}, bf16[2,128,128]{2,1,0:T(8,128)(2,1)S(1)}, u32[]{:S(2)}, u32[]{:S(2)}) collective-permute-start(bf16[2,128,128]{2,1,0:T(8,128)(2,1)S(1)} %slice.216), channel_id=1, source_target_pairs={{0,5},{4,9},{8,13},{12,17},{16,21},{20,25},{24,29},{1,6},{5,10},{9... | collective-permute-start | bytes 196616 | tf_op jit(solution)/shard_map/ppermute | solution.py:108
  6.9 36.5 %collective-permute-start = (bf16[2,1024,128]{2,1,0:T(8,128)(2,1)S(1)}, bf16[2,1024,128]{2,1,0:T(8,128)(2,1)S(1)}, u32[]{:S(2)}, u32[]{:S(2)}) collective-permute-start(bf16[2,1024,128]{2,1,0:T(8,128)(2,1)S(1)} %slice.196), channel_id=1, source_target_pairs={{0,4},{4,8},{8,12},{12,16},{16,20},{20,24},{24,28},{1,5},{5,9},{9,... | collective-permute-start | bytes 1572872 | tf_op jit(solution)/shard_map/ppermute | solution.py:76
  11.5 37.0 %collective-permute-start.2 = (bf16[2,128,1024]{2,1,0:T(8,128)(2,1)S(1)}, bf16[2,128,1024]{2,1,0:T(8,128)(2,1)S(1)}, u32[]{:S(2)}, u32[]{:S(2)}) collective-permute-start(bf16[2,128,1024]{2,1,0:T(8,128)(2,1)S(1)} %slice.198), channel_id=1, source_target_pairs={{0,1},{1,2},{2,3},{4,5},{5,6},{6,7},{8,9},{9,10},{10,11},{12,13},{... | collective-permute-start | bytes 1572872 | tf_op jit(solution)/shard_map/ppermute | solution.py:76
  47.2 6.5 %collective-permute-start.1 = (f32[5,2]{0,1:T(2,128)S(1)}, f32[5,2]{0,1:T(2,128)S(1)}, u32[]{:S(2)}, u32[]{:S(2)}) collective-permute-start(f32[5,2]{0,1:T(2,128)S(1)} %stack.4), channel_id=1, source_target_pairs={{4,0},{8,4},{12,8},{16,12},{20,16},{24,20},{28,24},{5,1},{9,5},{13... | collective-permute-start | bytes 128 | tf_op jit(solution)/shard_map/ppermute | solution.py:76
  52.4 3.0 %collective-permute-start.3 = (f32[5,2]{0,1:T(2,128)S(1)}, f32[5,2]{0,1:T(2,128)S(1)}, u32[]{:S(2)}, u32[]{:S(2)}) collective-permute-start(f32[5,2]{0,1:T(2,128)S(1)} %stack.5), channel_id=1, source_target_pairs={{1,0},{2,1},{3,2},{5,4},{6,5},{7,6},{9,8},{10,9},{11,10},{13,12},{... | collective-permute-start | bytes 128 | tf_op jit(solution)/shard_map/ppermute | solution.py:76
  55.8 10.9 %collective-permute-start.7 = (f32[4]{0:T(128)S(1)}, f32[4]{0:T(128)S(1)}, u32[]{:S(2)}, u32[]{:S(2)}) collective-permute-start(f32[4]{0:T(128)S(1)} %pad_maximum_fusion), channel_id=1, source_target_pairs={{0,1},{1,2},{2,3},{4,5},{5,6},{6,7},{8,9},{9,10},{10,11},{12,13},{... | collective-permute-start | bytes 56 | tf_op jit(solution)/shard_map/ppermute | solution.py:76
  59.8 6.9 %collective-permute-start.6 = (f32[4]{0:T(128)S(1)}, f32[4]{0:T(128)S(1)}, u32[]{:S(2)}, u32[]{:S(2)}) collective-permute-start(f32[4]{0:T(128)S(1)} %pad_maximum_fusion), channel_id=1, source_target_pairs={{0,4},{4,8},{8,12},{12,16},{16,20},{20,24},{24,28},{1,5},{5,9},{9,... | collective-permute-start | bytes 56 | tf_op jit(solution)/shard_map/ppermute | solution.py:76
  64.1 3.1 %collective-permute-start.5 = (f32[4]{0:T(128)S(1)}, f32[4]{0:T(128)S(1)}, u32[]{:S(2)}, u32[]{:S(2)}) collective-permute-start(f32[4]{0:T(128)S(1)} %pad_maximum_fusion), channel_id=1, source_target_pairs={{1,0},{2,1},{3,2},{5,4},{6,5},{7,6},{9,8},{10,9},{11,10},{13,12},{... | collective-permute-start | bytes 56 | tf_op jit(solution)/shard_map/ppermute | solution.py:76
  65.4 5.8 %collective-permute-start.4 = (f32[4]{0:T(128)S(1)}, f32[4]{0:T(128)S(1)}, u32[]{:S(2)}, u32[]{:S(2)}) collective-permute-start(f32[4]{0:T(128)S(1)} %pad_maximum_fusion), channel_id=1, source_target_pairs={{4,0},{8,4},{12,8},{16,12},{20,16},{24,20},{28,24},{5,1},{9,5},{13... | collective-permute-start | bytes 56 | tf_op jit(solution)/shard_map/ppermute | solution.py:76
  71.4 22.5 %collective-permute-start.10 = (f32[4]{0:T(128)S(1)}, f32[4]{0:T(128)S(1)}, u32[]{:S(2)}, u32[]{:S(2)}) collective-permute-start(f32[4]{0:T(128)S(1)} %pad_maximum_fusion.1), channel_id=1, source_target_pairs={{0,5},{4,9},{8,13},{12,17},{16,21},{20,25},{24,29},{1,6},{5,10},{9... | collective-permute-start | bytes 56 | tf_op jit(solution)/shard_map/ppermute | solution.py:164
  75.8 16.7 %collective-permute-start.9 = (f32[4]{0:T(128)S(1)}, f32[4]{0:T(128)S(1)}, u32[]{:S(2)}, u32[]{:S(2)}) collective-permute-start(f32[4]{0:T(128)S(1)} %pad_maximum_fusion.1), channel_id=1, source_target_pairs={{0,1},{1,2},{2,3},{4,5},{5,6},{6,7},{8,9},{9,10},{10,11},{12,13},{... | collective-permute-start | bytes 56 | tf_op jit(solution)/shard_map/ppermute | solution.py:76
  79.7 12.9 %collective-permute-start.8 = (f32[4]{0:T(128)S(1)}, f32[4]{0:T(128)S(1)}, u32[]{:S(2)}, u32[]{:S(2)}) collective-permute-start(f32[4]{0:T(128)S(1)} %pad_maximum_fusion.1), channel_id=1, source_target_pairs={{0,4},{4,8},{8,12},{12,16},{16,20},{20,24},{24,28},{1,5},{5,9},{9,... | collective-permute-start | bytes 56 | tf_op jit(solution)/shard_map/ppermute | solution.py:76
  94.2 3.4 %copy-start = (f32[2,1024,1024]{2,1,0:T(8,128)}, f32[2,1024,1024]{2,1,0:T(8,128)S(1)}, u32[]{:S(2)}) copy-start(f32[2,1024,1024]{2,1,0:T(8,128)S(1)} %fusion.22) | copy-start | bytes 25165828

commit v6 on v4

--- a/solution.py
+++ b/solution.py
@@ -48,9 +48,29 @@
     )
 
 
+def pick(rows_out, rows_in, shift):
+    a = lax.broadcasted_iota(jnp.int32, (rows_out, rows_in), 0)
+    b = lax.broadcasted_iota(jnp.int32, (rows_out, rows_in), 1)
+    return jnp.where(b == a + shift, 1.0, 0.0).astype(jnp.bfloat16)
+
+
+def move_lanes(rows, left, lanes, emit):
+    width = STRIP
+    same = pick(width, width, -left).T
+    carry = pick(width, width, width - left).T
+    for k in range(lanes // width):
+        part = rows[:, k * width : (k + 1) * width]
+        block = jnp.dot(part, same, preferred_element_type=jnp.float32)
+        if k > 0:
+            before = rows[:, (k - 1) * width : k * width]
+            block = block + jnp.dot(before, carry, preferred_element_type=jnp.float32)
+        emit(k, block)
+
+
 def blend_kernel(idx_ref, off_ref, band_ref, terms_ref, cur_ref, prev_ref, lcur_ref, lprev_ref,
                  up_ref, corner_ref, out_ref, w_ref, *, n_row, n_col):
     f32 = jnp.float32
+    bf16 = jnp.bfloat16
     step = pl.program_id(0)
     planes, rows, tile_px = cur_ref.shape
     width = lcur_ref.shape[2]
@@ -90,17 +110,22 @@
     w_left = band_rows(y - top_l, r, lc, has_left) * jnp.where(j_l < tile_px, fade(j_l), 0.0)
     w_ref[...] = w_own
     w_ref[:, :width] += w_left
+    down_own = pick(rows, 2 * rows, rows - top)
+    down_left = pick(rows, 2 * rows, rows - top_l)
+    carry_left = pick(width, width, width - left_l).T
     for p in range(planes):
-        cur = cur_ref[p].astype(f32)
-        prev = prev_ref[p].astype(f32)
-        shifted_rows = jnp.where(t >= top, pltpu.roll(cur, top, 0), pltpu.roll(prev, top, 0))
-        window = pltpu.roll(shifted_rows, left, 1)
+        src = jnp.concatenate([prev_ref[p], cur_ref[p]], axis=0)
+        shifted_rows = jnp.dot(down_own, src, preferred_element_type=f32).astype(bf16)
         scale, level = gain(0, p)
-        out_ref[p] = (scale * window + level) * w_own
-        lcur = lcur_ref[p].astype(f32)
-        lprev = lprev_ref[p].astype(f32)
-        shifted_rows = jnp.where(t >= top_l, pltpu.roll(lcur, top_l, 0), pltpu.roll(lprev, top_l, 0))
-        window = pltpu.roll(shifted_rows, left_l, 1)
+
+        def emit(k, block, p=p, scale=scale, level=level):
+            span = slice(k * width, (k + 1) * width)
+            out_ref[p, :, span] = (scale * block + level) * w_own[:, span]
+
+        move_lanes(shifted_rows, left, tile_px, emit)
+        lsrc = jnp.concatenate([lprev_ref[p], lcur_ref[p]], axis=0)
+        lrows = jnp.dot(down_left, lsrc, preferred_element_type=f32).astype(bf16)
+        window = jnp.dot(lrows, carry_left, preferred_element_type=f32)
         scale, level = gain(1, p)
         out_ref[p, :, :width] += (scale * window + level) * w_left
 
@@ -119,11 +144,20 @@
         )
         w_ref[:width, :] += w_up
         w_ref[:width, :width] += w_corner
+        down_up = pick(width, width, width - top_u)
+        down_corner = pick(width, width, width - top_c)
+        carry_corner = pick(width, width, width - left_c).T
         for p in range(planes):
-            window = pltpu.roll(pltpu.roll(up_ref[p].astype(f32), top_u, 0), left_u, 1)
+            urows = jnp.dot(down_up, up_ref[p], preferred_element_type=f32).astype(bf16)
             scale, level = gain(2, p)
-            out_ref[p, :width, :] += (scale * window + level) * w_up
-            window = pltpu.roll(pltpu.roll(corner_ref[p].astype(f32), top_c, 0), left_c, 1)
+
+            def emit(k, block, p=p, scale=scale, level=level):
+                span = slice(k * width, (k + 1) * width)
+                out_ref[p, :width, span] += (scale * block + level) * w_up[:, span]
+
+            move_lanes(urows, left_u, tile_px, emit)
+            crows = jnp.dot(down_corner, corner_ref[p], preferred_element_type=f32).astype(bf16)
+            window = jnp.dot(crows, carry_corner, preferred_element_type=f32)
             scale, level = gain(3, p)
             out_ref[p, :width, :width] += (scale * window + level) * w_corner
 
@@ -212,8 +246,6 @@
     corner = tiles[:, tile_px - width :, tile_px - width :]
     from_left = shifted(right_strip, "col", n_col, 1)
     from_up = shifted(down_strip, "row", n_row, 1)
-    from_right = shifted(left_strip, "col", n_col, -1)
-    from_down = shifted(up_strip, "row", n_row, -1)
     diagonal = [
         (j * n_row + i, (j + 1) * n_row + i + 1) for i in range(n_row - 1) for j in range(n_col - 1)
     ]
@@ -230,18 +262,14 @@
         return (strip_ids < extent).astype(jnp.float32)[None, :, None]
 
     f32 = jnp.float32
-    right_stats = strip_stats(
-        right_strip.astype(f32), from_right.astype(f32), across(extents[0, row_index, col_index])
-    )
-    down_stats = strip_stats(
-        down_strip.astype(f32), from_down.astype(f32), along(extents[1, row_index, col_index])
-    )
     left_stats = strip_stats(
         from_left.astype(f32), left_strip.astype(f32), across(extents[0, row_index, left_col])
     )
     up_stats = strip_stats(
         from_up.astype(f32), up_strip.astype(f32), along(extents[1, upper_row, col_index])
     )
+    right_stats = shifted(left_stats, "col", n_col, -1)
+    down_stats = shifted(up_stats, "row", n_row, -1)
     has_right = col_index < n_col - 1
     has_down = row_index < n_row - 1
     has_left_pair = col_index > 0

time: 96 us -> 78 us (0.81)
  waiting for transfers between devices: 20 us -> 7.45 us
  Pallas kernels: 22.2 us -> 13.6 us
  starting transfers between devices: 32.7 us -> 36.1 us
  other arithmetic: 11.5 us -> 9.05 us
  local copies, waits for them, and re-layouts: 7.76 us -> 10 us
    ppermute x10, waiting for transfers between devices: 20 us -> 7.44 us  [shifted(): return lax.ppermute(block, axis, route)]
    pallas_call x1, Pallas kernels: 22.2 us -> 13.6 us  [blend(): pl.pallas_call(functools.partial(blend_kernel, n_row=n_row, n_col=n_col),...]
    ppermute x1, starting transfers between devices: 2.39 us -> 4.39 us  [local(): final_corner = lax.ppermute(final, ('col', 'row'), diagonal)]
    ppermute x10, starting transfers between devices: 27.5 us -> 29.1 us  [shifted(): return lax.ppermute(block, axis, route)]
    slice x2, local copies, waits for them, and re-layouts: 3.53 us -> 2.16 us  [the longest x1 1.08 us: local(): down_strip = tiles[:, tile_px - width:, :]]
    reduce_sum x4 -> x2, other arithmetic: 4.43 us -> 3.52 us  [strip_stats(): covariance = jnp.sum(dev_former * dev_latter, axis=(-2, -1)) / number]
  transfers between devices with their start and end apart: 12 -> 12, of which waited for: 3 -> 3; matrix products, arithmetic and copies ran while one was open for 19% -> 23% of each run, Pallas kernels for 0% -> 0%
where the time goes in v6:
time: 78 us; the launch traced here: 77.1 us
  starting transfers between devices  36.1 us (46%)
  Pallas kernels  13.6 us (17%)
  local copies, waits for them, and re-layouts  10 us (13%)
  other arithmetic  9.05 us (12%)
  waiting for transfers between devices  7.45 us (10%)
  between operations  0.88 us (1%)
    ppermute x10, starting transfers between devices, shifted(): return lax.ppermute(block, axis, route)  29.1 us
    pallas_call x1, Pallas kernels, blend(): pl.pallas_call(functools.partial(blend_kernel, n_row=n_row, n_col=n_col),...  13.6 us
    ppermute x10, waiting for transfers between devices, shifted(): return lax.ppermute(block, axis, route)  7.44 us
    ppermute x1, starting transfers between devices, local(): final_corner = lax.ppermute(final, ('col', 'row'), diagonal)  4.39 us
    reduce_sum x2, other arithmetic, strip_stats(): covariance = jnp.sum(dev_former * dev_latter, axis=(-2, -1)) / number  3.52 us
    reduce_sum x2, other arithmetic, strip_stats(): mean_former = jnp.sum(former * full, axis=(-2, -1)) / number  3.31 us
    ppermute x1, starting transfers between devices, local(): from_corner = lax.ppermute(corner, ('col', 'row'), diagonal)  2.57 us
  transfers between devices with their start and end apart: 12, of which 3 were waited for; matrix products, arithmetic and copies ran while one was open for 23% of the time, Pallas kernels for 0%

profile of v6, /device:TPU:16, one launch (start us, length us, event | category | flops | bytes accessed | tf_op | source)
XLA Modules:
  0.0 77.1 jit_solution(8245904305778233706)
XLA Ops:
  1.7 3.4 %collective-permute-start = (bf16[2,1024,128]{2,1,0:T(8,128)(2,1)S(1)}, bf16[2,1024,128]{2,1,0:T(8,128)(2,1)S(1)}, u32[]{:S(2)}, u32[]{:S(2)}) collective-permute-start(bf16[2,1024,128]{2,1,0:T(8,128)(2,1)S(1)} %slice.57), channel_id=1, source_target_pairs={{0,4},{4,8},{8,12},{12,16},{16,20},{20,24},{24,28},{1,5},{5,9},{9,... | collective-permute-start | bytes 1572872 | tf_op jit(solution)/shard_map/ppermute | solution.py:220
  6.0 2.6 %collective-permute-start.11 = (bf16[2,128,128]{2,1,0:T(8,128)(2,1)S(1)}, bf16[2,128,128]{2,1,0:T(8,128)(2,1)S(1)}, u32[]{:S(2)}, u32[]{:S(2)}) collective-permute-start(bf16[2,128,128]{2,1,0:T(8,128)(2,1)S(1)} %slice.75), channel_id=1, source_target_pairs={{0,5},{4,9},{8,13},{12,17},{16,21},{20,25},{24,29},{1,6},{5,10},{9... | collective-permute-start | bytes 196616 | tf_op jit(solution)/shard_map/ppermute | solution.py:252
  8.6 1.1 %slice.59 = bf16[2,128,1024]{2,1,0:T(8,128)(2,1)S(1)} slice(bf16[2,1024,1024]{2,1,0:T(8,128)(2,1)} %prev_ref.1), slice={[0:2], [896:1024], [0:1024]} | slice | bytes 1048576 | tf_op jit(solution)/shard_map/slice | solution.py:243
  9.7 3.8 %collective-permute-start.2 = (bf16[2,128,1024]{2,1,0:T(8,128)(2,1)S(1)}, bf16[2,128,1024]{2,1,0:T(8,128)(2,1)S(1)}, u32[]{:S(2)}, u32[]{:S(2)}) collective-permute-start(bf16[2,128,1024]{2,1,0:T(8,128)(2,1)S(1)} %slice.59), channel_id=1, source_target_pairs={{0,1},{1,2},{2,3},{4,5},{5,6},{6,7},{8,9},{9,10},{10,11},{12,13},{... | collective-permute-start | bytes 1572872 | tf_op jit(solution)/shard_map/ppermute | solution.py:220
  13.5 1.3 %reshape.160.off_ref = s32[64]{0:T(128)} reshape(s32[2,4,8]{2,1,0:T(4,128)} %param.6) | data formatting | bytes 512 | tf_op jit(solution)/shard_map/reshape | solution.py:211
  14.8 1.4 %reshape.161.band_ref = s32[64]{0:T(128)} reshape(s32[2,4,8]{2,1,0:T(4,128)} %param.7) | data formatting | bytes 512 | tf_op jit(solution)/shard_map/reshape | solution.py:211
  16.1 1.4 %constant_dynamic-slice_fusion.1 = (s32[1,1,1]{2,1,0:T(1,128)}, s32[1,1,1]{2,1,0:T(1,128)}) fusion(s32[2,4,8]{2,1,0:T(4,128)} %param.5, s32[]{:T(128)S(6)} %select_n.115, s32[]{:T(128)S(6)} %max.6, s32[]{:T(128)S(6)} %max.7, s32[]{:T(128)S(6)} %select_n.118), kind=kLoop, calls=%fused_computation.117 | loop fusion | bytes 32 | tf_op jit(solution)/shard_map/dynamic_slice | solution.py:266
  19.4 1.6 %fusion = (f32[2]{0:T(128)S(1)}, f32[2]{0:T(128)S(1)}, f32[2]{0:T(128)S(1)}) fusion(bf16[2,1024,128]{2,1,0:T(8,128)(2,1)S(1)} %collective-permute-done.lcur_ref.lprev_ref, f32[128]{0:T(128)S(1)} %compare_convert_fusion.1, bf16[2,1024,1024]{2,1,0:T(8,128)(2,1)} %prev_ref.1), kind=kLoop, calls=%fused_computation.8 | loop fusion | flops 1835002 | bytes 1049112 | tf_op jit(solution)/shard_map/reduce_sum | solution.py:22
  21.2 1.7 %fusion.5 = (f32[2]{0:T(128)S(1)}, f32[2]{0:T(128)S(1)}, f32[2]{0:T(128)S(1)}) fusion(bf16[2,1024,128]{2,1,0:T(8,128)(2,1)S(1)} %collective-permute-done.lcur_ref.lprev_ref, f32[2]{0:T(128)S(1)} %get-tuple-element.43, f32[2]{0:T(128)S(1)} %get-tuple-element.42, f32[128]{0:T(128)S(1)} %compare_convert_fusion.1, bf16[2,1024,1024]{2,1,0:T(8,128)(2,1)} %prev_ref.1), kind=kLoop, calls=%fused_computation.13 | loop fusion | flops 3145722 | bytes 1049128 | tf_op jit(solution)/shard_map/reduce_sum | solution.py:28
  23.3 3.3 %collective-permute-start.1 = (f32[5,2]{0,1:T(2,128)S(1)}, f32[5,2]{0,1:T(2,128)S(1)}, u32[]{:S(2)}, u32[]{:S(2)}) collective-permute-start(f32[5,2]{0,1:T(2,128)S(1)} %stack.13), channel_id=1, source_target_pairs={{4,0},{8,4},{12,8},{16,12},{20,16},{24,20},{28,24},{5,1},{9,5},{13... | collective-permute-start | bytes 128 | tf_op jit(solution)/shard_map/ppermute | solution.py:220
  26.7 1.7 %fusion.10 = (f32[2]{0:T(128)S(1)}, f32[2]{0:T(128)S(1)}, f32[2]{0:T(128)S(1)}) fusion(bf16[2,128,1024]{2,1,0:T(8,128)(2,1)S(1)} %collective-permute-done.2.up_ref, f32[128]{0:T(128)S(1)} %compare_convert_fusion, bf16[2,1024,1024]{2,1,0:T(8,128)(2,1)} %prev_ref.1), kind=kLoop, calls=%fused_computation.18 | loop fusion | flops 1835002 | bytes 1049112 | tf_op jit(solution)/shard_map/reduce_sum | solution.py:22
  28.6 1.8 %fusion.15 = (f32[2]{0:T(128)S(1)}, f32[2]{0:T(128)S(1)}, f32[2]{0:T(128)S(1)}) fusion(bf16[2,128,1024]{2,1,0:T(8,128)(2,1)S(1)} %collective-permute-done.2.up_ref, f32[2]{0:T(128)S(1)} %get-tuple-element.45, f32[2]{0:T(128)S(1)} %get-tuple-element.44, f32[128]{0:T(128)S(1)} %compare_convert_fusion, bf16[2,1024,1024]{2,1,0:T(8,128)(2,1)} %prev_ref.1), kind=kLoop, calls=%fused_computation.23 | loop fusion | flops 3145722 | bytes 1049128 | tf_op jit(solution)/shard_map/reduce_sum | solution.py:28
  30.7 1.3 %collective-permute-start.3 = (f32[5,2]{0,1:T(2,128)S(1)}, f32[5,2]{0,1:T(2,128)S(1)}, u32[]{:S(2)}, u32[]{:S(2)}) collective-permute-start(f32[5,2]{0,1:T(2,128)S(1)} %stack.14), channel_id=1, source_target_pairs={{1,0},{2,1},{3,2},{5,4},{6,5},{7,6},{9,8},{10,9},{11,10},{13,12},{... | collective-permute-start | bytes 128 | tf_op jit(solution)/shard_map/ppermute | solution.py:220
  32.3 1.5 %collective-permute-done.3 = f32[5,2]{0,1:T(2,128)S(1)} collective-permute-done((f32[5,2]{0,1:T(2,128)S(1)}, f32[5,2]{0,1:T(2,128)S(1)}, u32[]{:S(2)}, u32[]{:S(2)}) %collective-permute-start.3) | collective-permute-done | bytes 72 | tf_op jit(solution)/shard_map/ppermute | solution.py:220
  34.2 3.4 %collective-permute-start.7 = (f32[4]{0:T(128)S(1)}, f32[4]{0:T(128)S(1)}, u32[]{:S(2)}, u32[]{:S(2)}) collective-permute-start(f32[4]{0:T(128)S(1)} %pad_maximum_fusion), channel_id=1, source_target_pairs={{0,1},{1,2},{2,3},{4,5},{5,6},{6,7},{8,9},{9,10},{10,11},{12,13},{... | collective-permute-start | bytes 56 | tf_op jit(solution)/shard_map/ppermute | solution.py:220
  37.6 2.5 %collective-permute-start.6 = (f32[4]{0:T(128)S(1)}, f32[4]{0:T(128)S(1)}, u32[]{:S(2)}, u32[]{:S(2)}) collective-permute-start(f32[4]{0:T(128)S(1)} %pad_maximum_fusion), channel_id=1, source_target_pairs={{0,4},{4,8},{8,12},{12,16},{16,20},{20,24},{24,28},{1,5},{5,9},{9,... | collective-permute-start | bytes 56 | tf_op jit(solution)/shard_map/ppermute | solution.py:220
  40.1 1.3 %collective-permute-start.5 = (f32[4]{0:T(128)S(1)}, f32[4]{0:T(128)S(1)}, u32[]{:S(2)}, u32[]{:S(2)}) collective-permute-start(f32[4]{0:T(128)S(1)} %pad_maximum_fusion), channel_id=1, source_target_pairs={{1,0},{2,1},{3,2},{5,4},{6,5},{7,6},{9,8},{10,9},{11,10},{13,12},{... | collective-permute-start | bytes 56 | tf_op jit(solution)/shard_map/ppermute | solution.py:220
  41.4 4.2 %collective-permute-start.4 = (f32[4]{0:T(128)S(1)}, f32[4]{0:T(128)S(1)}, u32[]{:S(2)}, u32[]{:S(2)}) collective-permute-start(f32[4]{0:T(128)S(1)} %pad_maximum_fusion), channel_id=1, source_target_pairs={{4,0},{8,4},{12,8},{16,12},{20,16},{24,20},{28,24},{5,1},{9,5},{13... | collective-permute-start | bytes 56 | tf_op jit(solution)/shard_map/ppermute | solution.py:220
  45.7 1.6 %collective-permute-done.4 = f32[4]{0:T(128)S(1)} collective-permute-done((f32[4]{0:T(128)S(1)}, f32[4]{0:T(128)S(1)}, u32[]{:S(2)}, u32[]{:S(2)}) %collective-permute-start.4) | collective-permute-done | bytes 48 | tf_op jit(solution)/shard_map/ppermute | solution.py:220
  47.5 4.4 %collective-permute-start.10 = (f32[4]{0:T(128)S(1)}, f32[4]{0:T(128)S(1)}, u32[]{:S(2)}, u32[]{:S(2)}) collective-permute-start(f32[4]{0:T(128)S(1)} %pad_maximum_fusion.1), channel_id=1, source_target_pairs={{0,5},{4,9},{8,13},{12,17},{16,21},{20,25},{24,29},{1,6},{5,10},{9... | collective-permute-start | bytes 56 | tf_op jit(solution)/shard_map/ppermute | solution.py:308
  51.9 3.9 %collective-permute-start.9 = (f32[4]{0:T(128)S(1)}, f32[4]{0:T(128)S(1)}, u32[]{:S(2)}, u32[]{:S(2)}) collective-permute-start(f32[4]{0:T(128)S(1)} %pad_maximum_fusion.1), channel_id=1, source_target_pairs={{0,1},{1,2},{2,3},{4,5},{5,6},{6,7},{8,9},{9,10},{10,11},{12,13},{... | collective-permute-start | bytes 56 | tf_op jit(solution)/shard_map/ppermute | solution.py:220
  55.8 1.9 %collective-permute-start.8 = (f32[4]{0:T(128)S(1)}, f32[4]{0:T(128)S(1)}, u32[]{:S(2)}, u32[]{:S(2)}) collective-permute-start(f32[4]{0:T(128)S(1)} %pad_maximum_fusion.1), channel_id=1, source_target_pairs={{0,4},{4,8},{8,12},{12,16},{16,20},{20,24},{24,28},{1,5},{5,9},{9,... | collective-permute-start | bytes 56 | tf_op jit(solution)/shard_map/ppermute | solution.py:220
  57.9 4.3 %collective-permute-done.8 = f32[4]{0:T(128)S(1)} collective-permute-done((f32[4]{0:T(128)S(1)}, f32[4]{0:T(128)S(1)}, u32[]{:S(2)}, u32[]{:S(2)}) %collective-permute-start.8) | collective-permute-done | bytes 48 | tf_op jit(solution)/shard_map/ppermute | solution.py:220
  63.5 13.6 %shard_map.59 = (f32[2,1024,1024]{2,1,0:T(8,128)}, f32[1024,1024]{1,0:T(8,128)}) custom-call(s32[2]{0:T(128)} %pad_add_fusion.idx_ref, s32[64]{0:T(128)} %reshape.160.off_ref, s32[64]{0:T(128)} %reshape.161.band_ref, f32[16]{0:T(128)} %concatenate.11.terms_ref, bf16[2,1024,1024]{2,1,0:T(8,128)(2,1)} %prev_ref.1, bf16[2,1024,1024]{2,1,0:T(8,128)(2,1)} %prev_ref.1, ...), custom_call_target="tpu_custom_call" | custom-call | flops 25165824 | bytes 22020096 | tf_op jit(solution)/shard_map/pallas_call | solution.py:199
  (48 shorter events, 7.2 us)
Async XLA Ops:
  1.7 17.7 %collective-permute-start = (bf16[2,1024,128]{2,1,0:T(8,128)(2,1)S(1)}, bf16[2,1024,128]{2,1,0:T(8,128)(2,1)S(1)}, u32[]{:S(2)}, u32[]{:S(2)}) collective-permute-start(bf16[2,1024,128]{2,1,0:T(8,128)(2,1)S(1)} %slice.57), channel_id=1, source_target_pairs={{0,4},{4,8},{8,12},{12,16},{16,20},{20,24},{24,28},{1,5},{5,9},{9,... | collective-permute-start | bytes 1572872 | tf_op jit(solution)/shard_map/ppermute | solution.py:220
  6.0 56.8 %collective-permute-start.11 = (bf16[2,128,128]{2,1,0:T(8,128)(2,1)S(1)}, bf16[2,128,128]{2,1,0:T(8,128)(2,1)S(1)}, u32[]{:S(2)}, u32[]{:S(2)}) collective-permute-start(bf16[2,128,128]{2,1,0:T(8,128)(2,1)S(1)} %slice.75), channel_id=1, source_target_pairs={{0,5},{4,9},{8,13},{12,17},{16,21},{20,25},{24,29},{1,6},{5,10},{9... | collective-permute-start | bytes 196616 | tf_op jit(solution)/shard_map/ppermute | solution.py:252
  9.7 17.0 %collective-permute-start.2 = (bf16[2,128,1024]{2,1,0:T(8,128)(2,1)S(1)}, bf16[2,128,1024]{2,1,0:T(8,128)(2,1)S(1)}, u32[]{:S(2)}, u32[]{:S(2)}) collective-permute-start(bf16[2,128,1024]{2,1,0:T(8,128)(2,1)S(1)} %slice.59), channel_id=1, source_target_pairs={{0,1},{1,2},{2,3},{4,5},{5,6},{6,7},{8,9},{9,10},{10,11},{12,13},{... | collective-permute-start | bytes 1572872 | tf_op jit(solution)/shard_map/ppermute | solution.py:220
  19.4 43.4 %copy-start = (bf16[2,1024,128]{2,1,0:T(8,128)(2,1)}, bf16[2,1024,128]{2,1,0:T(8,128)(2,1)S(1)}, u32[]{:S(2)}) copy-start(bf16[2,1024,128]{2,1,0:T(8,128)(2,1)S(1)} %collective-permute-done.lcur_ref.lprev_ref) | copy-start | bytes 1572868
  23.3 8.7 %collective-permute-start.1 = (f32[5,2]{0,1:T(2,128)S(1)}, f32[5,2]{0,1:T(2,128)S(1)}, u32[]{:S(2)}, u32[]{:S(2)}) collective-permute-start(f32[5,2]{0,1:T(2,128)S(1)} %stack.13), channel_id=1, source_target_pairs={{4,0},{8,4},{12,8},{16,12},{20,16},{24,20},{28,24},{5,1},{9,5},{13... | collective-permute-start | bytes 128 | tf_op jit(solution)/shard_map/ppermute | solution.py:220
  26.7 36.2 %copy-start.1 = (bf16[2,128,1024]{2,1,0:T(8,128)(2,1)}, bf16[2,128,1024]{2,1,0:T(8,128)(2,1)S(1)}, u32[]{:S(2)}) copy-start(bf16[2,128,1024]{2,1,0:T(8,128)(2,1)S(1)} %collective-permute-done.2.up_ref) | copy-start | bytes 1572868
  30.7 3.0 %collective-permute-start.3 = (f32[5,2]{0,1:T(2,128)S(1)}, f32[5,2]{0,1:T(2,128)S(1)}, u32[]{:S(2)}, u32[]{:S(2)}) collective-permute-start(f32[5,2]{0,1:T(2,128)S(1)} %stack.14), channel_id=1, source_target_pairs={{1,0},{2,1},{3,2},{5,4},{6,5},{7,6},{9,8},{10,9},{11,10},{13,12},{... | collective-permute-start | bytes 128 | tf_op jit(solution)/shard_map/ppermute | solution.py:220
  34.2 11.5 %collective-permute-start.7 = (f32[4]{0:T(128)S(1)}, f32[4]{0:T(128)S(1)}, u32[]{:S(2)}, u32[]{:S(2)}) collective-permute-start(f32[4]{0:T(128)S(1)} %pad_maximum_fusion), channel_id=1, source_target_pairs={{0,1},{1,2},{2,3},{4,5},{5,6},{6,7},{8,9},{9,10},{10,11},{12,13},{... | collective-permute-start | bytes 56 | tf_op jit(solution)/shard_map/ppermute | solution.py:220
  37.6 8.1 %collective-permute-start.6 = (f32[4]{0:T(128)S(1)}, f32[4]{0:T(128)S(1)}, u32[]{:S(2)}, u32[]{:S(2)}) collective-permute-start(f32[4]{0:T(128)S(1)} %pad_maximum_fusion), channel_id=1, source_target_pairs={{0,4},{4,8},{8,12},{12,16},{16,20},{20,24},{24,28},{1,5},{5,9},{9,... | collective-permute-start | bytes 56 | tf_op jit(solution)/shard_map/ppermute | solution.py:220
  40.1 5.5 %collective-permute-start.5 = (f32[4]{0:T(128)S(1)}, f32[4]{0:T(128)S(1)}, u32[]{:S(2)}, u32[]{:S(2)}) collective-permute-start(f32[4]{0:T(128)S(1)} %pad_maximum_fusion), channel_id=1, source_target_pairs={{1,0},{2,1},{3,2},{5,4},{6,5},{7,6},{9,8},{10,9},{11,10},{13,12},{... | collective-permute-start | bytes 56 | tf_op jit(solution)/shard_map/ppermute | solution.py:220
  41.4 5.9 %collective-permute-start.4 = (f32[4]{0:T(128)S(1)}, f32[4]{0:T(128)S(1)}, u32[]{:S(2)}, u32[]{:S(2)}) collective-permute-start(f32[4]{0:T(128)S(1)} %pad_maximum_fusion), channel_id=1, source_target_pairs={{4,0},{8,4},{12,8},{16,12},{20,16},{24,20},{28,24},{5,1},{9,5},{13... | collective-permute-start | bytes 56 | tf_op jit(solution)/shard_map/ppermute | solution.py:220
  47.5 10.2 %collective-permute-start.10 = (f32[4]{0:T(128)S(1)}, f32[4]{0:T(128)S(1)}, u32[]{:S(2)}, u32[]{:S(2)}) collective-permute-start(f32[4]{0:T(128)S(1)} %pad_maximum_fusion.1), channel_id=1, source_target_pairs={{0,5},{4,9},{8,13},{12,17},{16,21},{20,25},{24,29},{1,6},{5,10},{9... | collective-permute-start | bytes 56 | tf_op jit(solution)/shard_map/ppermute | solution.py:308
  51.9 5.9 %collective-permute-start.9 = (f32[4]{0:T(128)S(1)}, f32[4]{0:T(128)S(1)}, u32[]{:S(2)}, u32[]{:S(2)}) collective-permute-start(f32[4]{0:T(128)S(1)} %pad_maximum_fusion.1), channel_id=1, source_target_pairs={{0,1},{1,2},{2,3},{4,5},{5,6},{6,7},{8,9},{9,10},{10,11},{12,13},{... | collective-permute-start | bytes 56 | tf_op jit(solution)/shard_map/ppermute | solution.py:220
  55.8 6.4 %collective-permute-start.8 = (f32[4]{0:T(128)S(1)}, f32[4]{0:T(128)S(1)}, u32[]{:S(2)}, u32[]{:S(2)}) collective-permute-start(f32[4]{0:T(128)S(1)} %pad_maximum_fusion.1), channel_id=1, source_target_pairs={{0,4},{4,8},{8,12},{12,16},{16,20},{20,24},{24,28},{1,5},{5,9},{9,... | collective-permute-start | bytes 56 | tf_op jit(solution)/shard_map/ppermute | solution.py:220
  62.8 0.6 copy-start.2

commit v7 on v6

--- a/solution.py
+++ b/solution.py
@@ -57,13 +57,13 @@
 def move_lanes(rows, left, lanes, emit):
     width = STRIP
     same = pick(width, width, -left).T
-    carry = pick(width, width, width - left).T
+    both = pick(width, 2 * width, width - left).T
     for k in range(lanes // width):
-        part = rows[:, k * width : (k + 1) * width]
-        block = jnp.dot(part, same, preferred_element_type=jnp.float32)
-        if k > 0:
-            before = rows[:, (k - 1) * width : k * width]
-            block = block + jnp.dot(before, carry, preferred_element_type=jnp.float32)
+        if k == 0:
+            block = jnp.dot(rows[:, :width], same, preferred_element_type=jnp.float32)
+        else:
+            pair = rows[:, (k - 1) * width : (k + 1) * width]
+            block = jnp.dot(pair, both, preferred_element_type=jnp.float32)
         emit(k, block)
 
 
@@ -110,11 +110,12 @@
     w_left = band_rows(y - top_l, r, lc, has_left) * jnp.where(j_l < tile_px, fade(j_l), 0.0)
     w_ref[...] = w_own
     w_ref[:, :width] += w_left
-    down_own = pick(rows, 2 * rows, rows - top)
-    down_left = pick(rows, 2 * rows, rows - top_l)
+    reach = SPILL
+    down_own = pick(rows, reach + rows, reach - top)
+    down_left = pick(rows, reach + rows, reach - top_l)
     carry_left = pick(width, width, width - left_l).T
     for p in range(planes):
-        src = jnp.concatenate([prev_ref[p], cur_ref[p]], axis=0)
+        src = jnp.concatenate([prev_ref[p, rows - reach :], cur_ref[p]], axis=0)
         shifted_rows = jnp.dot(down_own, src, preferred_element_type=f32).astype(bf16)
         scale, level = gain(0, p)
 
@@ -123,7 +124,7 @@
             out_ref[p, :, span] = (scale * block + level) * w_own[:, span]
 
         move_lanes(shifted_rows, left, tile_px, emit)
-        lsrc = jnp.concatenate([lprev_ref[p], lcur_ref[p]], axis=0)
+        lsrc = jnp.concatenate([lprev_ref[p, rows - reach :], lcur_ref[p]], axis=0)
         lrows = jnp.dot(down_left, lsrc, preferred_element_type=f32).astype(bf16)
         window = jnp.dot(lrows, carry_left, preferred_element_type=f32)
         scale, level = gain(1, p)

time: 78 us -> 77.5 us (level)
  no operation moved by 1% of the time
where the time goes in v7:
time: 77.5 us; the launch traced here: 76.7 us
  starting transfers between devices  36.1 us (47%)
  Pallas kernels  13.2 us (17%)
  local copies, waits for them, and re-layouts  10 us (13%)
  other arithmetic  9.05 us (12%)
  waiting for transfers between devices  7.45 us (10%)
  between operations  0.88 us (1%)
    ppermute x10, starting transfers between devices, shifted(): return lax.ppermute(block, axis, route)  29.1 us
    pallas_call x1, Pallas kernels, blend(): pl.pallas_call(functools.partial(blend_kernel, n_row=n_row, n_col=n_col),...  13.2 us
    ppermute x10, waiting for transfers between devices, shifted(): return lax.ppermute(block, axis, route)  7.44 us
    ppermute x1, starting transfers between devices, local(): final_corner = lax.ppermute(final, ('col', 'row'), diagonal)  4.39 us
    reduce_sum x2, other arithmetic, strip_stats(): covariance = jnp.sum(dev_former * dev_latter, axis=(-2, -1)) / number  3.52 us
    reduce_sum x2, other arithmetic, strip_stats(): mean_former = jnp.sum(former * full, axis=(-2, -1)) / number  3.31 us
    ppermute x1, starting transfers between devices, local(): from_corner = lax.ppermute(corner, ('col', 'row'), diagonal)  2.57 us
  transfers between devices with their start and end apart: 12, of which 3 were waited for; matrix products, arithmetic and copies ran while one was open for 23% of the time, Pallas kernels for 0%

profile of v7, /device:TPU:16, one launch (start us, length us, event | category | flops | bytes accessed | tf_op | source)
XLA Modules:
  0.0 76.7 jit_solution(13962785620054048541)
XLA Ops:
  1.7 3.4 %collective-permute-start = (bf16[2,1024,128]{2,1,0:T(8,128)(2,1)S(1)}, bf16[2,1024,128]{2,1,0:T(8,128)(2,1)S(1)}, u32[]{:S(2)}, u32[]{:S(2)}) collective-permute-start(bf16[2,1024,128]{2,1,0:T(8,128)(2,1)S(1)} %slice.57), channel_id=1, source_target_pairs={{0,4},{4,8},{8,12},{12,16},{16,20},{20,24},{24,28},{1,5},{5,9},{9,... | collective-permute-start | bytes 1572872 | tf_op jit(solution)/shard_map/ppermute | solution.py:221
  6.0 2.6 %collective-permute-start.11 = (bf16[2,128,128]{2,1,0:T(8,128)(2,1)S(1)}, bf16[2,128,128]{2,1,0:T(8,128)(2,1)S(1)}, u32[]{:S(2)}, u32[]{:S(2)}) collective-permute-start(bf16[2,128,128]{2,1,0:T(8,128)(2,1)S(1)} %slice.75), channel_id=1, source_target_pairs={{0,5},{4,9},{8,13},{12,17},{16,21},{20,25},{24,29},{1,6},{5,10},{9... | collective-permute-start | bytes 196616 | tf_op jit(solution)/shard_map/ppermute | solution.py:253
  8.6 1.1 %slice.59 = bf16[2,128,1024]{2,1,0:T(8,128)(2,1)S(1)} slice(bf16[2,1024,1024]{2,1,0:T(8,128)(2,1)} %prev_ref.1), slice={[0:2], [896:1024], [0:1024]} | slice | bytes 1048576 | tf_op jit(solution)/shard_map/slice | solution.py:244
  9.7 3.8 %collective-permute-start.2 = (bf16[2,128,1024]{2,1,0:T(8,128)(2,1)S(1)}, bf16[2,128,1024]{2,1,0:T(8,128)(2,1)S(1)}, u32[]{:S(2)}, u32[]{:S(2)}) collective-permute-start(bf16[2,128,1024]{2,1,0:T(8,128)(2,1)S(1)} %slice.59), channel_id=1, source_target_pairs={{0,1},{1,2},{2,3},{4,5},{5,6},{6,7},{8,9},{9,10},{10,11},{12,13},{... | collective-permute-start | bytes 1572872 | tf_op jit(solution)/shard_map/ppermute | solution.py:221
  13.5 1.3 %reshape.160.off_ref = s32[64]{0:T(128)} reshape(s32[2,4,8]{2,1,0:T(4,128)} %param.6) | data formatting | bytes 512 | tf_op jit(solution)/shard_map/reshape | solution.py:212
  14.8 1.4 %reshape.161.band_ref = s32[64]{0:T(128)} reshape(s32[2,4,8]{2,1,0:T(4,128)} %param.7) | data formatting | bytes 512 | tf_op jit(solution)/shard_map/reshape | solution.py:212
  16.1 1.4 %constant_dynamic-slice_fusion.1 = (s32[1,1,1]{2,1,0:T(1,128)}, s32[1,1,1]{2,1,0:T(1,128)}) fusion(s32[2,4,8]{2,1,0:T(4,128)} %param.5, s32[]{:T(128)S(6)} %select_n.115, s32[]{:T(128)S(6)} %max.6, s32[]{:T(128)S(6)} %max.7, s32[]{:T(128)S(6)} %select_n.118), kind=kLoop, calls=%fused_computation.117 | loop fusion | bytes 32 | tf_op jit(solution)/shard_map/dynamic_slice | solution.py:267
  19.4 1.6 %fusion = (f32[2]{0:T(128)S(1)}, f32[2]{0:T(128)S(1)}, f32[2]{0:T(128)S(1)}) fusion(bf16[2,1024,128]{2,1,0:T(8,128)(2,1)S(1)} %collective-permute-done.lcur_ref.lprev_ref, f32[128]{0:T(128)S(1)} %compare_convert_fusion.1, bf16[2,1024,1024]{2,1,0:T(8,128)(2,1)} %prev_ref.1), kind=kLoop, calls=%fused_computation.8 | loop fusion | flops 1835002 | bytes 1049112 | tf_op jit(solution)/shard_map/reduce_sum | solution.py:22
  21.2 1.7 %fusion.5 = (f32[2]{0:T(128)S(1)}, f32[2]{0:T(128)S(1)}, f32[2]{0:T(128)S(1)}) fusion(bf16[2,1024,128]{2,1,0:T(8,128)(2,1)S(1)} %collective-permute-done.lcur_ref.lprev_ref, f32[2]{0:T(128)S(1)} %get-tuple-element.43, f32[2]{0:T(128)S(1)} %get-tuple-element.42, f32[128]{0:T(128)S(1)} %compare_convert_fusion.1, bf16[2,1024,1024]{2,1,0:T(8,128)(2,1)} %prev_ref.1), kind=kLoop, calls=%fused_computation.13 | loop fusion | flops 3145722 | bytes 1049128 | tf_op jit(solution)/shard_map/reduce_sum | solution.py:28
  23.3 3.3 %collective-permute-start.1 = (f32[5,2]{0,1:T(2,128)S(1)}, f32[5,2]{0,1:T(2,128)S(1)}, u32[]{:S(2)}, u32[]{:S(2)}) collective-permute-start(f32[5,2]{0,1:T(2,128)S(1)} %stack.13), channel_id=1, source_target_pairs={{4,0},{8,4},{12,8},{16,12},{20,16},{24,20},{28,24},{5,1},{9,5},{13... | collective-permute-start | bytes 128 | tf_op jit(solution)/shard_map/ppermute | solution.py:221
  26.7 1.7 %fusion.10 = (f32[2]{0:T(128)S(1)}, f32[2]{0:T(128)S(1)}, f32[2]{0:T(128)S(1)}) fusion(bf16[2,128,1024]{2,1,0:T(8,128)(2,1)S(1)} %collective-permute-done.2.up_ref, f32[128]{0:T(128)S(1)} %compare_convert_fusion, bf16[2,1024,1024]{2,1,0:T(8,128)(2,1)} %prev_ref.1), kind=kLoop, calls=%fused_computation.18 | loop fusion | flops 1835002 | bytes 1049112 | tf_op jit(solution)/shard_map/reduce_sum | solution.py:22
  28.6 1.8 %fusion.15 = (f32[2]{0:T(128)S(1)}, f32[2]{0:T(128)S(1)}, f32[2]{0:T(128)S(1)}) fusion(bf16[2,128,1024]{2,1,0:T(8,128)(2,1)S(1)} %collective-permute-done.2.up_ref, f32[2]{0:T(128)S(1)} %get-tuple-element.45, f32[2]{0:T(128)S(1)} %get-tuple-element.44, f32[128]{0:T(128)S(1)} %compare_convert_fusion, bf16[2,1024,1024]{2,1,0:T(8,128)(2,1)} %prev_ref.1), kind=kLoop, calls=%fused_computation.23 | loop fusion | flops 3145722 | bytes 1049128 | tf_op jit(solution)/shard_map/reduce_sum | solution.py:28
  30.7 1.3 %collective-permute-start.3 = (f32[5,2]{0,1:T(2,128)S(1)}, f32[5,2]{0,1:T(2,128)S(1)}, u32[]{:S(2)}, u32[]{:S(2)}) collective-permute-start(f32[5,2]{0,1:T(2,128)S(1)} %stack.14), channel_id=1, source_target_pairs={{1,0},{2,1},{3,2},{5,4},{6,5},{7,6},{9,8},{10,9},{11,10},{13,12},{... | collective-permute-start | bytes 128 | tf_op jit(solution)/shard_map/ppermute | solution.py:221
  32.3 1.5 %collective-permute-done.3 = f32[5,2]{0,1:T(2,128)S(1)} collective-permute-done((f32[5,2]{0,1:T(2,128)S(1)}, f32[5,2]{0,1:T(2,128)S(1)}, u32[]{:S(2)}, u32[]{:S(2)}) %collective-permute-start.3) | collective-permute-done | bytes 72 | tf_op jit(solution)/shard_map/ppermute | solution.py:221
  34.2 3.4 %collective-permute-start.7 = (f32[4]{0:T(128)S(1)}, f32[4]{0:T(128)S(1)}, u32[]{:S(2)}, u32[]{:S(2)}) collective-permute-start(f32[4]{0:T(128)S(1)} %pad_maximum_fusion), channel_id=1, source_target_pairs={{0,1},{1,2},{2,3},{4,5},{5,6},{6,7},{8,9},{9,10},{10,11},{12,13},{... | collective-permute-start | bytes 56 | tf_op jit(solution)/shard_map/ppermute | solution.py:221
  37.6 2.5 %collective-permute-start.6 = (f32[4]{0:T(128)S(1)}, f32[4]{0:T(128)S(1)}, u32[]{:S(2)}, u32[]{:S(2)}) collective-permute-start(f32[4]{0:T(128)S(1)} %pad_maximum_fusion), channel_id=1, source_target_pairs={{0,4},{4,8},{8,12},{12,16},{16,20},{20,24},{24,28},{1,5},{5,9},{9,... | collective-permute-start | bytes 56 | tf_op jit(solution)/shard_map/ppermute | solution.py:221
  40.1 1.3 %collective-permute-start.5 = (f32[4]{0:T(128)S(1)}, f32[4]{0:T(128)S(1)}, u32[]{:S(2)}, u32[]{:S(2)}) collective-permute-start(f32[4]{0:T(128)S(1)} %pad_maximum_fusion), channel_id=1, source_target_pairs={{1,0},{2,1},{3,2},{5,4},{6,5},{7,6},{9,8},{10,9},{11,10},{13,12},{... | collective-permute-start | bytes 56 | tf_op jit(solution)/shard_map/ppermute | solution.py:221
  41.4 4.2 %collective-permute-start.4 = (f32[4]{0:T(128)S(1)}, f32[4]{0:T(128)S(1)}, u32[]{:S(2)}, u32[]{:S(2)}) collective-permute-start(f32[4]{0:T(128)S(1)} %pad_maximum_fusion), channel_id=1, source_target_pairs={{4,0},{8,4},{12,8},{16,12},{20,16},{24,20},{28,24},{5,1},{9,5},{13... | collective-permute-start | bytes 56 | tf_op jit(solution)/shard_map/ppermute | solution.py:221
  45.7 1.6 %collective-permute-done.4 = f32[4]{0:T(128)S(1)} collective-permute-done((f32[4]{0:T(128)S(1)}, f32[4]{0:T(128)S(1)}, u32[]{:S(2)}, u32[]{:S(2)}) %collective-permute-start.4) | collective-permute-done | bytes 48 | tf_op jit(solution)/shard_map/ppermute | solution.py:221
  47.5 4.4 %collective-permute-start.10 = (f32[4]{0:T(128)S(1)}, f32[4]{0:T(128)S(1)}, u32[]{:S(2)}, u32[]{:S(2)}) collective-permute-start(f32[4]{0:T(128)S(1)} %pad_maximum_fusion.1), channel_id=1, source_target_pairs={{0,5},{4,9},{8,13},{12,17},{16,21},{20,25},{24,29},{1,6},{5,10},{9... | collective-permute-start | bytes 56 | tf_op jit(solution)/shard_map/ppermute | solution.py:309
  51.9 3.9 %collective-permute-start.9 = (f32[4]{0:T(128)S(1)}, f32[4]{0:T(128)S(1)}, u32[]{:S(2)}, u32[]{:S(2)}) collective-permute-start(f32[4]{0:T(128)S(1)} %pad_maximum_fusion.1), channel_id=1, source_target_pairs={{0,1},{1,2},{2,3},{4,5},{5,6},{6,7},{8,9},{9,10},{10,11},{12,13},{... | collective-permute-start | bytes 56 | tf_op jit(solution)/shard_map/ppermute | solution.py:221
  55.8 1.9 %collective-permute-start.8 = (f32[4]{0:T(128)S(1)}, f32[4]{0:T(128)S(1)}, u32[]{:S(2)}, u32[]{:S(2)}) collective-permute-start(f32[4]{0:T(128)S(1)} %pad_maximum_fusion.1), channel_id=1, source_target_pairs={{0,4},{4,8},{8,12},{12,16},{16,20},{20,24},{24,28},{1,5},{5,9},{9,... | collective-permute-start | bytes 56 | tf_op jit(solution)/shard_map/ppermute | solution.py:221
  57.9 4.3 %collective-permute-done.8 = f32[4]{0:T(128)S(1)} collective-permute-done((f32[4]{0:T(128)S(1)}, f32[4]{0:T(128)S(1)}, u32[]{:S(2)}, u32[]{:S(2)}) %collective-permute-start.8) | collective-permute-done | bytes 48 | tf_op jit(solution)/shard_map/ppermute | solution.py:221
  63.5 13.2 %shard_map.59 = (f32[2,1024,1024]{2,1,0:T(8,128)}, f32[1024,1024]{1,0:T(8,128)}) custom-call(s32[2]{0:T(128)} %pad_add_fusion.idx_ref, s32[64]{0:T(128)} %reshape.160.off_ref, s32[64]{0:T(128)} %reshape.161.band_ref, f32[16]{0:T(128)} %concatenate.11.terms_ref, bf16[2,1024,1024]{2,1,0:T(8,128)(2,1)} %prev_ref.1, bf16[2,1024,1024]{2,1,0:T(8,128)(2,1)} %prev_ref.1, ...), custom_call_target="tpu_custom_call" | custom-call | flops 25165824 | bytes 22020096 | tf_op jit(solution)/shard_map/pallas_call | solution.py:200
  (48 shorter events, 7.2 us)
Async XLA Ops:
  1.7 17.7 %collective-permute-start = (bf16[2,1024,128]{2,1,0:T(8,128)(2,1)S(1)}, bf16[2,1024,128]{2,1,0:T(8,128)(2,1)S(1)}, u32[]{:S(2)}, u32[]{:S(2)}) collective-permute-start(bf16[2,1024,128]{2,1,0:T(8,128)(2,1)S(1)} %slice.57), channel_id=1, source_target_pairs={{0,4},{4,8},{8,12},{12,16},{16,20},{20,24},{24,28},{1,5},{5,9},{9,... | collective-permute-start | bytes 1572872 | tf_op jit(solution)/shard_map/ppermute | solution.py:221
  6.0 56.8 %collective-permute-start.11 = (bf16[2,128,128]{2,1,0:T(8,128)(2,1)S(1)}, bf16[2,128,128]{2,1,0:T(8,128)(2,1)S(1)}, u32[]{:S(2)}, u32[]{:S(2)}) collective-permute-start(bf16[2,128,128]{2,1,0:T(8,128)(2,1)S(1)} %slice.75), channel_id=1, source_target_pairs={{0,5},{4,9},{8,13},{12,17},{16,21},{20,25},{24,29},{1,6},{5,10},{9... | collective-permute-start | bytes 196616 | tf_op jit(solution)/shard_map/ppermute | solution.py:253
  9.7 17.0 %collective-permute-start.2 = (bf16[2,128,1024]{2,1,0:T(8,128)(2,1)S(1)}, bf16[2,128,1024]{2,1,0:T(8,128)(2,1)S(1)}, u32[]{:S(2)}, u32[]{:S(2)}) collective-permute-start(bf16[2,128,1024]{2,1,0:T(8,128)(2,1)S(1)} %slice.59), channel_id=1, source_target_pairs={{0,1},{1,2},{2,3},{4,5},{5,6},{6,7},{8,9},{9,10},{10,11},{12,13},{... | collective-permute-start | bytes 1572872 | tf_op jit(solution)/shard_map/ppermute | solution.py:221
  19.4 43.4 %copy-start = (bf16[2,1024,128]{2,1,0:T(8,128)(2,1)}, bf16[2,1024,128]{2,1,0:T(8,128)(2,1)S(1)}, u32[]{:S(2)}) copy-start(bf16[2,1024,128]{2,1,0:T(8,128)(2,1)S(1)} %collective-permute-done.lcur_ref.lprev_ref) | copy-start | bytes 1572868
  23.3 8.7 %collective-permute-start.1 = (f32[5,2]{0,1:T(2,128)S(1)}, f32[5,2]{0,1:T(2,128)S(1)}, u32[]{:S(2)}, u32[]{:S(2)}) collective-permute-start(f32[5,2]{0,1:T(2,128)S(1)} %stack.13), channel_id=1, source_target_pairs={{4,0},{8,4},{12,8},{16,12},{20,16},{24,20},{28,24},{5,1},{9,5},{13... | collective-permute-start | bytes 128 | tf_op jit(solution)/shard_map/ppermute | solution.py:221
  26.7 36.2 %copy-start.1 = (bf16[2,128,1024]{2,1,0:T(8,128)(2,1)}, bf16[2,128,1024]{2,1,0:T(8,128)(2,1)S(1)}, u32[]{:S(2)}) copy-start(bf16[2,128,1024]{2,1,0:T(8,128)(2,1)S(1)} %collective-permute-done.2.up_ref) | copy-start | bytes 1572868
  30.7 3.0 %collective-permute-start.3 = (f32[5,2]{0,1:T(2,128)S(1)}, f32[5,2]{0,1:T(2,128)S(1)}, u32[]{:S(2)}, u32[]{:S(2)}) collective-permute-start(f32[5,2]{0,1:T(2,128)S(1)} %stack.14), channel_id=1, source_target_pairs={{1,0},{2,1},{3,2},{5,4},{6,5},{7,6},{9,8},{10,9},{11,10},{13,12},{... | collective-permute-start | bytes 128 | tf_op jit(solution)/shard_map/ppermute | solution.py:221
  34.2 11.5 %collective-permute-start.7 = (f32[4]{0:T(128)S(1)}, f32[4]{0:T(128)S(1)}, u32[]{:S(2)}, u32[]{:S(2)}) collective-permute-start(f32[4]{0:T(128)S(1)} %pad_maximum_fusion), channel_id=1, source_target_pairs={{0,1},{1,2},{2,3},{4,5},{5,6},{6,7},{8,9},{9,10},{10,11},{12,13},{... | collective-permute-start | bytes 56 | tf_op jit(solution)/shard_map/ppermute | solution.py:221
  37.6 8.1 %collective-permute-start.6 = (f32[4]{0:T(128)S(1)}, f32[4]{0:T(128)S(1)}, u32[]{:S(2)}, u32[]{:S(2)}) collective-permute-start(f32[4]{0:T(128)S(1)} %pad_maximum_fusion), channel_id=1, source_target_pairs={{0,4},{4,8},{8,12},{12,16},{16,20},{20,24},{24,28},{1,5},{5,9},{9,... | collective-permute-start | bytes 56 | tf_op jit(solution)/shard_map/ppermute | solution.py:221
  40.1 5.5 %collective-permute-start.5 = (f32[4]{0:T(128)S(1)}, f32[4]{0:T(128)S(1)}, u32[]{:S(2)}, u32[]{:S(2)}) collective-permute-start(f32[4]{0:T(128)S(1)} %pad_maximum_fusion), channel_id=1, source_target_pairs={{1,0},{2,1},{3,2},{5,4},{6,5},{7,6},{9,8},{10,9},{11,10},{13,12},{... | collective-permute-start | bytes 56 | tf_op jit(solution)/shard_map/ppermute | solution.py:221
  41.4 5.9 %collective-permute-start.4 = (f32[4]{0:T(128)S(1)}, f32[4]{0:T(128)S(1)}, u32[]{:S(2)}, u32[]{:S(2)}) collective-permute-start(f32[4]{0:T(128)S(1)} %pad_maximum_fusion), channel_id=1, source_target_pairs={{4,0},{8,4},{12,8},{16,12},{20,16},{24,20},{28,24},{5,1},{9,5},{13... | collective-permute-start | bytes 56 | tf_op jit(solution)/shard_map/ppermute | solution.py:221
  47.5 10.2 %collective-permute-start.10 = (f32[4]{0:T(128)S(1)}, f32[4]{0:T(128)S(1)}, u32[]{:S(2)}, u32[]{:S(2)}) collective-permute-start(f32[4]{0:T(128)S(1)} %pad_maximum_fusion.1), channel_id=1, source_target_pairs={{0,5},{4,9},{8,13},{12,17},{16,21},{20,25},{24,29},{1,6},{5,10},{9... | collective-permute-start | bytes 56 | tf_op jit(solution)/shard_map/ppermute | solution.py:309
  51.9 5.9 %collective-permute-start.9 = (f32[4]{0:T(128)S(1)}, f32[4]{0:T(128)S(1)}, u32[]{:S(2)}, u32[]{:S(2)}) collective-permute-start(f32[4]{0:T(128)S(1)} %pad_maximum_fusion.1), channel_id=1, source_target_pairs={{0,1},{1,2},{2,3},{4,5},{5,6},{6,7},{8,9},{9,10},{10,11},{12,13},{... | collective-permute-start | bytes 56 | tf_op jit(solution)/shard_map/ppermute | solution.py:221
  55.8 6.4 %collective-permute-start.8 = (f32[4]{0:T(128)S(1)}, f32[4]{0:T(128)S(1)}, u32[]{:S(2)}, u32[]{:S(2)}) collective-permute-start(f32[4]{0:T(128)S(1)} %pad_maximum_fusion.1), channel_id=1, source_target_pairs={{0,4},{4,8},{8,12},{12,16},{16,20},{20,24},{24,28},{1,5},{5,9},{9,... | collective-permute-start | bytes 56 | tf_op jit(solution)/shard_map/ppermute | solution.py:221
  62.8 0.6 copy-start.2

commit v8 on v7

--- a/solution.py
+++ b/solution.py
@@ -56,14 +56,12 @@
 
 def move_lanes(rows, left, lanes, emit):
     width = STRIP
-    same = pick(width, width, -left).T
-    both = pick(width, 2 * width, width - left).T
+    lane = lax.broadcasted_iota(jnp.int32, (1, width), 1)
+    before = None
     for k in range(lanes // width):
-        if k == 0:
-            block = jnp.dot(rows[:, :width], same, preferred_element_type=jnp.float32)
-        else:
-            pair = rows[:, (k - 1) * width : (k + 1) * width]
-            block = jnp.dot(pair, both, preferred_element_type=jnp.float32)
+        turned = pltpu.roll(rows[:, k * width : (k + 1) * width], left, 1)
+        block = turned if before is None else jnp.where(lane >= left, turned, before)
+        before = turned
         emit(k, block)
 
 
@@ -113,10 +111,9 @@
     reach = SPILL
     down_own = pick(rows, reach + rows, reach - top)
     down_left = pick(rows, reach + rows, reach - top_l)
-    carry_left = pick(width, width, width - left_l).T
     for p in range(planes):
         src = jnp.concatenate([prev_ref[p, rows - reach :], cur_ref[p]], axis=0)
-        shifted_rows = jnp.dot(down_own, src, preferred_element_type=f32).astype(bf16)
+        shifted_rows = jnp.dot(down_own, src, preferred_element_type=f32)
         scale, level = gain(0, p)
 
         def emit(k, block, p=p, scale=scale, level=level):
@@ -125,8 +122,8 @@
 
         move_lanes(shifted_rows, left, tile_px, emit)
         lsrc = jnp.concatenate([lprev_ref[p, rows - reach :], lcur_ref[p]], axis=0)
-        lrows = jnp.dot(down_left, lsrc, preferred_element_type=f32).astype(bf16)
-        window = jnp.dot(lrows, carry_left, preferred_element_type=f32)
+        lrows = jnp.dot(down_left, lsrc, preferred_element_type=f32)
+        window = pltpu.roll(lrows, left_l, 1)
         scale, level = gain(1, p)
         out_ref[p, :, :width] += (scale * window + level) * w_left
 
@@ -147,9 +144,8 @@
         w_ref[:width, :width] += w_corner
         down_up = pick(width, width, width - top_u)
         down_corner = pick(width, width, width - top_c)
-        carry_corner = pick(width, width, width - left_c).T
         for p in range(planes):
-            urows = jnp.dot(down_up, up_ref[p], preferred_element_type=f32).astype(bf16)
+            urows = jnp.dot(down_up, up_ref[p], preferred_element_type=f32)
             scale, level = gain(2, p)
 
             def emit(k, block, p=p, scale=scale, level=level):
@@ -157,8 +153,8 @@
                 out_ref[p, :width, span] += (scale * block + level) * w_up[:, span]
 
             move_lanes(urows, left_u, tile_px, emit)
-            crows = jnp.dot(down_corner, corner_ref[p], preferred_element_type=f32).astype(bf16)
-            window = jnp.dot(crows, carry_corner, preferred_element_type=f32)
+            crows = jnp.dot(down_corner, corner_ref[p], preferred_element_type=f32)
+            window = pltpu.roll(crows, left_c, 1)
             scale, level = gain(3, p)
             out_ref[p, :width, :width] += (scale * window + level) * w_corner
 

time: 77.5 us -> 75.9 us (0.979)
  Pallas kernels: 13.2 us -> 11.5 us
    pallas_call x1, Pallas kernels: 13.2 us -> 11.5 us  [blend(): pl.pallas_call(functools.partial(blend_kernel, n_row=n_row, n_col=n_col),...]
where the time goes in v8:
time: 75.9 us; the launch traced here: 75 us
  starting transfers between devices  36.1 us (48%)
  Pallas kernels  11.5 us (15%)
  local copies, waits for them, and re-layouts  10 us (13%)
  other arithmetic  9.05 us (12%)
  waiting for transfers between devices  7.45 us (10%)
  between operations  0.88 us (1%)
    ppermute x10, starting transfers between devices, shifted(): return lax.ppermute(block, axis, route)  29.1 us
    pallas_call x1, Pallas kernels, blend(): pl.pallas_call(functools.partial(blend_kernel, n_row=n_row, n_col=n_col),...  11.5 us
    ppermute x10, waiting for transfers between devices, shifted(): return lax.ppermute(block, axis, route)  7.44 us
    ppermute x1, starting transfers between devices, local(): final_corner = lax.ppermute(final, ('col', 'row'), diagonal)  4.39 us
    reduce_sum x2, other arithmetic, strip_stats(): covariance = jnp.sum(dev_former * dev_latter, axis=(-2, -1)) / number  3.52 us
    reduce_sum x2, other arithmetic, strip_stats(): mean_former = jnp.sum(former * full, axis=(-2, -1)) / number  3.31 us
    ppermute x1, starting transfers between devices, local(): from_corner = lax.ppermute(corner, ('col', 'row'), diagonal)  2.57 us
  transfers between devices with their start and end apart: 12, of which 3 were waited for; matrix products, arithmetic and copies ran while one was open for 23% of the time, Pallas kernels for 0%

profile of v8, /device:TPU:16, one launch (start us, length us, event | category | flops | bytes accessed | tf_op | source)
XLA Modules:
  0.0 75.0 jit_solution(719753735294193729)
XLA Ops:
  1.7 3.4 %collective-permute-start = (bf16[2,1024,128]{2,1,0:T(8,128)(2,1)S(1)}, bf16[2,1024,128]{2,1,0:T(8,128)(2,1)S(1)}, u32[]{:S(2)}, u32[]{:S(2)}) collective-permute-start(bf16[2,1024,128]{2,1,0:T(8,128)(2,1)S(1)} %slice.57), channel_id=1, source_target_pairs={{0,4},{4,8},{8,12},{12,16},{16,20},{20,24},{24,28},{1,5},{5,9},{9,... | collective-permute-start | bytes 1572872 | tf_op jit(solution)/shard_map/ppermute | solution.py:217
  6.0 2.6 %collective-permute-start.11 = (bf16[2,128,128]{2,1,0:T(8,128)(2,1)S(1)}, bf16[2,128,128]{2,1,0:T(8,128)(2,1)S(1)}, u32[]{:S(2)}, u32[]{:S(2)}) collective-permute-start(bf16[2,128,128]{2,1,0:T(8,128)(2,1)S(1)} %slice.75), channel_id=1, source_target_pairs={{0,5},{4,9},{8,13},{12,17},{16,21},{20,25},{24,29},{1,6},{5,10},{9... | collective-permute-start | bytes 196616 | tf_op jit(solution)/shard_map/ppermute | solution.py:249
  8.6 1.1 %slice.59 = bf16[2,128,1024]{2,1,0:T(8,128)(2,1)S(1)} slice(bf16[2,1024,1024]{2,1,0:T(8,128)(2,1)} %prev_ref.1), slice={[0:2], [896:1024], [0:1024]} | slice | bytes 1048576 | tf_op jit(solution)/shard_map/slice | solution.py:240
  9.7 3.8 %collective-permute-start.2 = (bf16[2,128,1024]{2,1,0:T(8,128)(2,1)S(1)}, bf16[2,128,1024]{2,1,0:T(8,128)(2,1)S(1)}, u32[]{:S(2)}, u32[]{:S(2)}) collective-permute-start(bf16[2,128,1024]{2,1,0:T(8,128)(2,1)S(1)} %slice.59), channel_id=1, source_target_pairs={{0,1},{1,2},{2,3},{4,5},{5,6},{6,7},{8,9},{9,10},{10,11},{12,13},{... | collective-permute-start | bytes 1572872 | tf_op jit(solution)/shard_map/ppermute | solution.py:217
  13.5 1.3 %reshape.160.off_ref = s32[64]{0:T(128)} reshape(s32[2,4,8]{2,1,0:T(4,128)} %param.6) | data formatting | bytes 512 | tf_op jit(solution)/shard_map/reshape | solution.py:208
  14.8 1.4 %reshape.161.band_ref = s32[64]{0:T(128)} reshape(s32[2,4,8]{2,1,0:T(4,128)} %param.7) | data formatting | bytes 512 | tf_op jit(solution)/shard_map/reshape | solution.py:208
  16.1 1.4 %constant_dynamic-slice_fusion.1 = (s32[1,1,1]{2,1,0:T(1,128)}, s32[1,1,1]{2,1,0:T(1,128)}) fusion(s32[2,4,8]{2,1,0:T(4,128)} %param.5, s32[]{:T(128)S(6)} %select_n.115, s32[]{:T(128)S(6)} %max.6, s32[]{:T(128)S(6)} %max.7, s32[]{:T(128)S(6)} %select_n.118), kind=kLoop, calls=%fused_computation.117 | loop fusion | bytes 32 | tf_op jit(solution)/shard_map/dynamic_slice | solution.py:263
  19.4 1.6 %fusion = (f32[2]{0:T(128)S(1)}, f32[2]{0:T(128)S(1)}, f32[2]{0:T(128)S(1)}) fusion(bf16[2,1024,128]{2,1,0:T(8,128)(2,1)S(1)} %collective-permute-done.lcur_ref.lprev_ref, f32[128]{0:T(128)S(1)} %compare_convert_fusion.1, bf16[2,1024,1024]{2,1,0:T(8,128)(2,1)} %prev_ref.1), kind=kLoop, calls=%fused_computation.8 | loop fusion | flops 1835002 | bytes 1049112 | tf_op jit(solution)/shard_map/reduce_sum | solution.py:22
  21.2 1.7 %fusion.5 = (f32[2]{0:T(128)S(1)}, f32[2]{0:T(128)S(1)}, f32[2]{0:T(128)S(1)}) fusion(bf16[2,1024,128]{2,1,0:T(8,128)(2,1)S(1)} %collective-permute-done.lcur_ref.lprev_ref, f32[2]{0:T(128)S(1)} %get-tuple-element.43, f32[2]{0:T(128)S(1)} %get-tuple-element.42, f32[128]{0:T(128)S(1)} %compare_convert_fusion.1, bf16[2,1024,1024]{2,1,0:T(8,128)(2,1)} %prev_ref.1), kind=kLoop, calls=%fused_computation.13 | loop fusion | flops 3145722 | bytes 1049128 | tf_op jit(solution)/shard_map/reduce_sum | solution.py:28
  23.3 3.3 %collective-permute-start.1 = (f32[5,2]{0,1:T(2,128)S(1)}, f32[5,2]{0,1:T(2,128)S(1)}, u32[]{:S(2)}, u32[]{:S(2)}) collective-permute-start(f32[5,2]{0,1:T(2,128)S(1)} %stack.13), channel_id=1, source_target_pairs={{4,0},{8,4},{12,8},{16,12},{20,16},{24,20},{28,24},{5,1},{9,5},{13... | collective-permute-start | bytes 128 | tf_op jit(solution)/shard_map/ppermute | solution.py:217
  26.7 1.7 %fusion.10 = (f32[2]{0:T(128)S(1)}, f32[2]{0:T(128)S(1)}, f32[2]{0:T(128)S(1)}) fusion(bf16[2,128,1024]{2,1,0:T(8,128)(2,1)S(1)} %collective-permute-done.2.up_ref, f32[128]{0:T(128)S(1)} %compare_convert_fusion, bf16[2,1024,1024]{2,1,0:T(8,128)(2,1)} %prev_ref.1), kind=kLoop, calls=%fused_computation.18 | loop fusion | flops 1835002 | bytes 1049112 | tf_op jit(solution)/shard_map/reduce_sum | solution.py:22
  28.6 1.8 %fusion.15 = (f32[2]{0:T(128)S(1)}, f32[2]{0:T(128)S(1)}, f32[2]{0:T(128)S(1)}) fusion(bf16[2,128,1024]{2,1,0:T(8,128)(2,1)S(1)} %collective-permute-done.2.up_ref, f32[2]{0:T(128)S(1)} %get-tuple-element.45, f32[2]{0:T(128)S(1)} %get-tuple-element.44, f32[128]{0:T(128)S(1)} %compare_convert_fusion, bf16[2,1024,1024]{2,1,0:T(8,128)(2,1)} %prev_ref.1), kind=kLoop, calls=%fused_computation.23 | loop fusion | flops 3145722 | bytes 1049128 | tf_op jit(solution)/shard_map/reduce_sum | solution.py:28
  30.7 1.3 %collective-permute-start.3 = (f32[5,2]{0,1:T(2,128)S(1)}, f32[5,2]{0,1:T(2,128)S(1)}, u32[]{:S(2)}, u32[]{:S(2)}) collective-permute-start(f32[5,2]{0,1:T(2,128)S(1)} %stack.14), channel_id=1, source_target_pairs={{1,0},{2,1},{3,2},{5,4},{6,5},{7,6},{9,8},{10,9},{11,10},{13,12},{... | collective-permute-start | bytes 128 | tf_op jit(solution)/shard_map/ppermute | solution.py:217
  32.3 1.5 %collective-permute-done.3 = f32[5,2]{0,1:T(2,128)S(1)} collective-permute-done((f32[5,2]{0,1:T(2,128)S(1)}, f32[5,2]{0,1:T(2,128)S(1)}, u32[]{:S(2)}, u32[]{:S(2)}) %collective-permute-start.3) | collective-permute-done | bytes 72 | tf_op jit(solution)/shard_map/ppermute | solution.py:217
  34.2 3.4 %collective-permute-start.7 = (f32[4]{0:T(128)S(1)}, f32[4]{0:T(128)S(1)}, u32[]{:S(2)}, u32[]{:S(2)}) collective-permute-start(f32[4]{0:T(128)S(1)} %pad_maximum_fusion), channel_id=1, source_target_pairs={{0,1},{1,2},{2,3},{4,5},{5,6},{6,7},{8,9},{9,10},{10,11},{12,13},{... | collective-permute-start | bytes 56 | tf_op jit(solution)/shard_map/ppermute | solution.py:217
  37.6 2.5 %collective-permute-start.6 = (f32[4]{0:T(128)S(1)}, f32[4]{0:T(128)S(1)}, u32[]{:S(2)}, u32[]{:S(2)}) collective-permute-start(f32[4]{0:T(128)S(1)} %pad_maximum_fusion), channel_id=1, source_target_pairs={{0,4},{4,8},{8,12},{12,16},{16,20},{20,24},{24,28},{1,5},{5,9},{9,... | collective-permute-start | bytes 56 | tf_op jit(solution)/shard_map/ppermute | solution.py:217
  40.1 1.3 %collective-permute-start.5 = (f32[4]{0:T(128)S(1)}, f32[4]{0:T(128)S(1)}, u32[]{:S(2)}, u32[]{:S(2)}) collective-permute-start(f32[4]{0:T(128)S(1)} %pad_maximum_fusion), channel_id=1, source_target_pairs={{1,0},{2,1},{3,2},{5,4},{6,5},{7,6},{9,8},{10,9},{11,10},{13,12},{... | collective-permute-start | bytes 56 | tf_op jit(solution)/shard_map/ppermute | solution.py:217
  41.4 4.2 %collective-permute-start.4 = (f32[4]{0:T(128)S(1)}, f32[4]{0:T(128)S(1)}, u32[]{:S(2)}, u32[]{:S(2)}) collective-permute-start(f32[4]{0:T(128)S(1)} %pad_maximum_fusion), channel_id=1, source_target_pairs={{4,0},{8,4},{12,8},{16,12},{20,16},{24,20},{28,24},{5,1},{9,5},{13... | collective-permute-start | bytes 56 | tf_op jit(solution)/shard_map/ppermute | solution.py:217
  45.7 1.6 %collective-permute-done.4 = f32[4]{0:T(128)S(1)} collective-permute-done((f32[4]{0:T(128)S(1)}, f32[4]{0:T(128)S(1)}, u32[]{:S(2)}, u32[]{:S(2)}) %collective-permute-start.4) | collective-permute-done | bytes 48 | tf_op jit(solution)/shard_map/ppermute | solution.py:217
  47.5 4.4 %collective-permute-start.10 = (f32[4]{0:T(128)S(1)}, f32[4]{0:T(128)S(1)}, u32[]{:S(2)}, u32[]{:S(2)}) collective-permute-start(f32[4]{0:T(128)S(1)} %pad_maximum_fusion.1), channel_id=1, source_target_pairs={{0,5},{4,9},{8,13},{12,17},{16,21},{20,25},{24,29},{1,6},{5,10},{9... | collective-permute-start | bytes 56 | tf_op jit(solution)/shard_map/ppermute | solution.py:305
  51.9 3.9 %collective-permute-start.9 = (f32[4]{0:T(128)S(1)}, f32[4]{0:T(128)S(1)}, u32[]{:S(2)}, u32[]{:S(2)}) collective-permute-start(f32[4]{0:T(128)S(1)} %pad_maximum_fusion.1), channel_id=1, source_target_pairs={{0,1},{1,2},{2,3},{4,5},{5,6},{6,7},{8,9},{9,10},{10,11},{12,13},{... | collective-permute-start | bytes 56 | tf_op jit(solution)/shard_map/ppermute | solution.py:217
  55.8 1.9 %collective-permute-start.8 = (f32[4]{0:T(128)S(1)}, f32[4]{0:T(128)S(1)}, u32[]{:S(2)}, u32[]{:S(2)}) collective-permute-start(f32[4]{0:T(128)S(1)} %pad_maximum_fusion.1), channel_id=1, source_target_pairs={{0,4},{4,8},{8,12},{12,16},{16,20},{20,24},{24,28},{1,5},{5,9},{9,... | collective-permute-start | bytes 56 | tf_op jit(solution)/shard_map/ppermute | solution.py:217
  57.9 4.3 %collective-permute-done.8 = f32[4]{0:T(128)S(1)} collective-permute-done((f32[4]{0:T(128)S(1)}, f32[4]{0:T(128)S(1)}, u32[]{:S(2)}, u32[]{:S(2)}) %collective-permute-start.8) | collective-permute-done | bytes 48 | tf_op jit(solution)/shard_map/ppermute | solution.py:217
  63.5 11.5 %shard_map.59 = (f32[2,1024,1024]{2,1,0:T(8,128)}, f32[1024,1024]{1,0:T(8,128)}) custom-call(s32[2]{0:T(128)} %pad_add_fusion.idx_ref, s32[64]{0:T(128)} %reshape.160.off_ref, s32[64]{0:T(128)} %reshape.161.band_ref, f32[16]{0:T(128)} %concatenate.11.terms_ref, bf16[2,1024,1024]{2,1,0:T(8,128)(2,1)} %prev_ref.1, bf16[2,1024,1024]{2,1,0:T(8,128)(2,1)} %prev_ref.1, ...), custom_call_target="tpu_custom_call" | custom-call | flops 25165824 | bytes 22020096 | tf_op jit(solution)/shard_map/pallas_call | solution.py:196
  (48 shorter events, 7.2 us)
Async XLA Ops:
  1.7 17.7 %collective-permute-start = (bf16[2,1024,128]{2,1,0:T(8,128)(2,1)S(1)}, bf16[2,1024,128]{2,1,0:T(8,128)(2,1)S(1)}, u32[]{:S(2)}, u32[]{:S(2)}) collective-permute-start(bf16[2,1024,128]{2,1,0:T(8,128)(2,1)S(1)} %slice.57), channel_id=1, source_target_pairs={{0,4},{4,8},{8,12},{12,16},{16,20},{20,24},{24,28},{1,5},{5,9},{9,... | collective-permute-start | bytes 1572872 | tf_op jit(solution)/shard_map/ppermute | solution.py:217
  6.0 56.8 %collective-permute-start.11 = (bf16[2,128,128]{2,1,0:T(8,128)(2,1)S(1)}, bf16[2,128,128]{2,1,0:T(8,128)(2,1)S(1)}, u32[]{:S(2)}, u32[]{:S(2)}) collective-permute-start(bf16[2,128,128]{2,1,0:T(8,128)(2,1)S(1)} %slice.75), channel_id=1, source_target_pairs={{0,5},{4,9},{8,13},{12,17},{16,21},{20,25},{24,29},{1,6},{5,10},{9... | collective-permute-start | bytes 196616 | tf_op jit(solution)/shard_map/ppermute | solution.py:249
  9.7 17.0 %collective-permute-start.2 = (bf16[2,128,1024]{2,1,0:T(8,128)(2,1)S(1)}, bf16[2,128,1024]{2,1,0:T(8,128)(2,1)S(1)}, u32[]{:S(2)}, u32[]{:S(2)}) collective-permute-start(bf16[2,128,1024]{2,1,0:T(8,128)(2,1)S(1)} %slice.59), channel_id=1, source_target_pairs={{0,1},{1,2},{2,3},{4,5},{5,6},{6,7},{8,9},{9,10},{10,11},{12,13},{... | collective-permute-start | bytes 1572872 | tf_op jit(solution)/shard_map/ppermute | solution.py:217
  19.4 43.4 %copy-start = (bf16[2,1024,128]{2,1,0:T(8,128)(2,1)}, bf16[2,1024,128]{2,1,0:T(8,128)(2,1)S(1)}, u32[]{:S(2)}) copy-start(bf16[2,1024,128]{2,1,0:T(8,128)(2,1)S(1)} %collective-permute-done.lcur_ref.lprev_ref) | copy-start | bytes 1572868
  23.3 8.7 %collective-permute-start.1 = (f32[5,2]{0,1:T(2,128)S(1)}, f32[5,2]{0,1:T(2,128)S(1)}, u32[]{:S(2)}, u32[]{:S(2)}) collective-permute-start(f32[5,2]{0,1:T(2,128)S(1)} %stack.13), channel_id=1, source_target_pairs={{4,0},{8,4},{12,8},{16,12},{20,16},{24,20},{28,24},{5,1},{9,5},{13... | collective-permute-start | bytes 128 | tf_op jit(solution)/shard_map/ppermute | solution.py:217
  26.7 36.2 %copy-start.1 = (bf16[2,128,1024]{2,1,0:T(8,128)(2,1)}, bf16[2,128,1024]{2,1,0:T(8,128)(2,1)S(1)}, u32[]{:S(2)}) copy-start(bf16[2,128,1024]{2,1,0:T(8,128)(2,1)S(1)} %collective-permute-done.2.up_ref) | copy-start | bytes 1572868
  30.7 3.0 %collective-permute-start.3 = (f32[5,2]{0,1:T(2,128)S(1)}, f32[5,2]{0,1:T(2,128)S(1)}, u32[]{:S(2)}, u32[]{:S(2)}) collective-permute-start(f32[5,2]{0,1:T(2,128)S(1)} %stack.14), channel_id=1, source_target_pairs={{1,0},{2,1},{3,2},{5,4},{6,5},{7,6},{9,8},{10,9},{11,10},{13,12},{... | collective-permute-start | bytes 128 | tf_op jit(solution)/shard_map/ppermute | solution.py:217
  34.2 11.5 %collective-permute-start.7 = (f32[4]{0:T(128)S(1)}, f32[4]{0:T(128)S(1)}, u32[]{:S(2)}, u32[]{:S(2)}) collective-permute-start(f32[4]{0:T(128)S(1)} %pad_maximum_fusion), channel_id=1, source_target_pairs={{0,1},{1,2},{2,3},{4,5},{5,6},{6,7},{8,9},{9,10},{10,11},{12,13},{... | collective-permute-start | bytes 56 | tf_op jit(solution)/shard_map/ppermute | solution.py:217
  37.6 8.1 %collective-permute-start.6 = (f32[4]{0:T(128)S(1)}, f32[4]{0:T(128)S(1)}, u32[]{:S(2)}, u32[]{:S(2)}) collective-permute-start(f32[4]{0:T(128)S(1)} %pad_maximum_fusion), channel_id=1, source_target_pairs={{0,4},{4,8},{8,12},{12,16},{16,20},{20,24},{24,28},{1,5},{5,9},{9,... | collective-permute-start | bytes 56 | tf_op jit(solution)/shard_map/ppermute | solution.py:217
  40.1 5.5 %collective-permute-start.5 = (f32[4]{0:T(128)S(1)}, f32[4]{0:T(128)S(1)}, u32[]{:S(2)}, u32[]{:S(2)}) collective-permute-start(f32[4]{0:T(128)S(1)} %pad_maximum_fusion), channel_id=1, source_target_pairs={{1,0},{2,1},{3,2},{5,4},{6,5},{7,6},{9,8},{10,9},{11,10},{13,12},{... | collective-permute-start | bytes 56 | tf_op jit(solution)/shard_map/ppermute | solution.py:217
  41.4 5.9 %collective-permute-start.4 = (f32[4]{0:T(128)S(1)}, f32[4]{0:T(128)S(1)}, u32[]{:S(2)}, u32[]{:S(2)}) collective-permute-start(f32[4]{0:T(128)S(1)} %pad_maximum_fusion), channel_id=1, source_target_pairs={{4,0},{8,4},{12,8},{16,12},{20,16},{24,20},{28,24},{5,1},{9,5},{13... | collective-permute-start | bytes 56 | tf_op jit(solution)/shard_map/ppermute | solution.py:217
  47.5 10.2 %collective-permute-start.10 = (f32[4]{0:T(128)S(1)}, f32[4]{0:T(128)S(1)}, u32[]{:S(2)}, u32[]{:S(2)}) collective-permute-start(f32[4]{0:T(128)S(1)} %pad_maximum_fusion.1), channel_id=1, source_target_pairs={{0,5},{4,9},{8,13},{12,17},{16,21},{20,25},{24,29},{1,6},{5,10},{9... | collective-permute-start | bytes 56 | tf_op jit(solution)/shard_map/ppermute | solution.py:305
  51.9 5.9 %collective-permute-start.9 = (f32[4]{0:T(128)S(1)}, f32[4]{0:T(128)S(1)}, u32[]{:S(2)}, u32[]{:S(2)}) collective-permute-start(f32[4]{0:T(128)S(1)} %pad_maximum_fusion.1), channel_id=1, source_target_pairs={{0,1},{1,2},{2,3},{4,5},{5,6},{6,7},{8,9},{9,10},{10,11},{12,13},{... | collective-permute-start | bytes 56 | tf_op jit(solution)/shard_map/ppermute | solution.py:217
  55.8 6.4 %collective-permute-start.8 = (f32[4]{0:T(128)S(1)}, f32[4]{0:T(128)S(1)}, u32[]{:S(2)}, u32[]{:S(2)}) collective-permute-start(f32[4]{0:T(128)S(1)} %pad_maximum_fusion.1), channel_id=1, source_target_pairs={{0,4},{4,8},{8,12},{12,16},{16,20},{20,24},{24,28},{1,5},{5,9},{9,... | collective-permute-start | bytes 56 | tf_op jit(solution)/shard_map/ppermute | solution.py:217
  62.8 0.6 copy-start.2

commit v9 on v8

--- a/solution.py
+++ b/solution.py
@@ -65,7 +65,7 @@
         emit(k, block)
 
 
-def blend_kernel(idx_ref, off_ref, band_ref, terms_ref, cur_ref, prev_ref, lcur_ref, lprev_ref,
+def blend_kernel(off_ref, band_ref, terms_ref, cur_ref, prev_ref, lcur_ref, lprev_ref,
                  up_ref, corner_ref, out_ref, w_ref, *, n_row, n_col):
     f32 = jnp.float32
     bf16 = jnp.bfloat16
@@ -73,15 +73,15 @@
     planes, rows, tile_px = cur_ref.shape
     width = lcur_ref.shape[2]
     cells = n_row * n_col
-    r = idx_ref[0]
-    c = idx_ref[1]
+    r = lax.axis_index("row")
+    c = lax.axis_index("col")
     lc = jnp.maximum(c - 1, 0)
     ur = jnp.maximum(r - 1, 0)
     has_left = c > 0
     has_up = r > 0
 
     def table(ref, k, rr, cc):
-        return ref[k * cells + rr * n_col + cc]
+        return ref[k, rr, cc]
 
     def fade(ids):
         return (jnp.minimum(ids, tile_px - 1 - ids) + 1).astype(f32) / (tile_px / 2.0)
@@ -159,7 +159,7 @@
             out_ref[p, :width, :width] += (scale * window + level) * w_corner
 
 
-def blend(idx, offsets, bands, terms, tiles, from_left, from_up, from_corner, n_row, n_col):
+def blend(offsets, bands, terms, tiles, from_left, from_up, from_corner, n_row, n_col):
     planes, tile_px, _ = tiles.shape
     width = from_left.shape[2]
     rows = min(ROWS, tile_px)
@@ -175,7 +175,7 @@
         return (0, 0, 0)
 
     grid_spec = pltpu.PrefetchScalarGridSpec(
-        num_scalar_prefetch=3,
+        num_scalar_prefetch=2,
         grid=(steps,),
         in_specs=[
             pl.BlockSpec(memory_space=pltpu.SMEM),
@@ -205,7 +205,7 @@
             flops=12 * planes * tile_px * tile_px, transcendentals=0,
             bytes_accessed=out_bytes + in_bytes,
         ),
-    )(idx, offsets.reshape(-1), bands.reshape(-1), terms, tiles, tiles, from_left, from_left,
+    )(offsets, bands, terms, tiles, tiles, from_left, from_left,
       from_up, from_corner)
 
 
@@ -309,8 +309,7 @@
         jnp.exp(final_up[:planes]), final_up[planes:],
         jnp.exp(final_corner[:planes]), final_corner[planes:],
     ])
-    idx = jnp.stack([row_index, col_index]).astype(jnp.int32)
-    return blend(idx, offsets, bands, terms, tiles, from_left, from_up, from_corner, n_row, n_col)
+    return blend(offsets, bands, terms, tiles, from_left, from_up, from_corner, n_row, n_col)
 
 
 def solution(mesh):

time: 75.9 us -> 74.6 us (0.983)
  local copies, waits for them, and re-layouts: 10 us -> 7.28 us
  waiting for transfers between devices: 7.45 us -> 10.1 us
    ppermute x10, waiting for transfers between devices: 7.44 us -> 10.1 us  [shifted(): return lax.ppermute(block, axis, route)]
    reshape x2 -> x0, local copies, waits for them, and re-layouts: 2.61 us -> none  [the longest x1 1.35 us: blend(): bands.reshape(-1)]
  transfers between devices with their start and end apart: 12 -> 12, of which waited for: 3 -> 4; matrix products, arithmetic and copies ran while one was open for 23% -> 19% of each run, Pallas kernels for 0% -> 0%
where the time goes in v9:
time: 74.6 us; the launch traced here: 73.7 us
  starting transfers between devices  35.5 us (48%)
  Pallas kernels  11.6 us (16%)
  waiting for transfers between devices  10.1 us (14%)
  other arithmetic  8.45 us (11%)
  local copies, waits for them, and re-layouts  7.28 us (10%)
  between operations  0.87 us (1%)
    ppermute x10, starting transfers between devices, shifted(): return lax.ppermute(block, axis, route)  28.9 us
    pallas_call x1, Pallas kernels, blend(): pl.pallas_call(functools.partial(blend_kernel, n_row=n_row, n_col=n_col),...  11.6 us
    ppermute x10, waiting for transfers between devices, shifted(): return lax.ppermute(block, axis, route)  10.1 us
    ppermute x1, starting transfers between devices, local(): final_corner = lax.ppermute(final, ('col', 'row'), diagonal)  4 us
    reduce_sum x2, other arithmetic, strip_stats(): covariance = jnp.sum(dev_former * dev_latter, axis=(-2, -1)) / number  3.52 us
    reduce_sum x2, other arithmetic, strip_stats(): mean_former = jnp.sum(former * full, axis=(-2, -1)) / number  3.31 us
    ppermute x1, starting transfers between devices, local(): from_corner = lax.ppermute(corner, ('col', 'row'), diagonal)  2.57 us
  transfers between devices with their start and end apart: 12, of which 4 were waited for; matrix products, arithmetic and copies ran while one was open for 19% of the time, Pallas kernels for 0%

profile of v9, /device:TPU:16, one launch (start us, length us, event | category | flops | bytes accessed | tf_op | source)
XLA Modules:
  0.0 73.7 jit_solution(6669423929337496975)
XLA Ops:
  0.6 1.1 %slice.57 = bf16[2,1024,128]{2,1,0:T(8,128)(2,1)S(1)} slice(bf16[2,1024,1024]{2,1,0:T(8,128)(2,1)} %prev_ref.1), slice={[0:2], [0:1024], [896:1024]} | slice | bytes 1048576 | tf_op jit(solution)/shard_map/slice | solution.py:239
  1.7 3.4 %collective-permute-start = (bf16[2,1024,128]{2,1,0:T(8,128)(2,1)S(1)}, bf16[2,1024,128]{2,1,0:T(8,128)(2,1)S(1)}, u32[]{:S(2)}, u32[]{:S(2)}) collective-permute-start(bf16[2,1024,128]{2,1,0:T(8,128)(2,1)S(1)} %slice.57), channel_id=1, source_target_pairs={{0,4},{4,8},{8,12},{12,16},{16,20},{20,24},{24,28},{1,5},{5,9},{9,... | collective-permute-start | bytes 1572872 | tf_op jit(solution)/shard_map/ppermute | solution.py:217
  6.0 2.6 %collective-permute-start.11 = (bf16[2,128,128]{2,1,0:T(8,128)(2,1)S(1)}, bf16[2,128,128]{2,1,0:T(8,128)(2,1)S(1)}, u32[]{:S(2)}, u32[]{:S(2)}) collective-permute-start(bf16[2,128,128]{2,1,0:T(8,128)(2,1)S(1)} %slice.75), channel_id=1, source_target_pairs={{0,5},{4,9},{8,13},{12,17},{16,21},{20,25},{24,29},{1,6},{5,10},{9... | collective-permute-start | bytes 196616 | tf_op jit(solution)/shard_map/ppermute | solution.py:249
  8.6 1.1 %slice.59 = bf16[2,128,1024]{2,1,0:T(8,128)(2,1)S(1)} slice(bf16[2,1024,1024]{2,1,0:T(8,128)(2,1)} %prev_ref.1), slice={[0:2], [896:1024], [0:1024]} | slice | bytes 1048576 | tf_op jit(solution)/shard_map/slice | solution.py:240
  9.7 3.8 %collective-permute-start.2 = (bf16[2,128,1024]{2,1,0:T(8,128)(2,1)S(1)}, bf16[2,128,1024]{2,1,0:T(8,128)(2,1)S(1)}, u32[]{:S(2)}, u32[]{:S(2)}) collective-permute-start(bf16[2,128,1024]{2,1,0:T(8,128)(2,1)S(1)} %slice.59), channel_id=1, source_target_pairs={{0,1},{1,2},{2,3},{4,5},{5,6},{6,7},{8,9},{9,10},{10,11},{12,13},{... | collective-permute-start | bytes 1572872 | tf_op jit(solution)/shard_map/ppermute | solution.py:217
  13.5 1.3 %constant_dynamic-slice_fusion.1 = (s32[1,1,1]{2,1,0:T(1,128)}, s32[1,1,1]{2,1,0:T(1,128)}) fusion(s32[2,4,8]{2,1,0:T(4,128)} %param.5, s32[]{:T(128)S(6)} %select_n.115, s32[]{:T(128)S(6)} %max.6, s32[]{:T(128)S(6)} %max.7, s32[]{:T(128)S(6)} %select_n.118), kind=kLoop, calls=%fused_computation.116 | loop fusion | bytes 32 | tf_op jit(solution)/shard_map/dynamic_slice | solution.py:263
  16.1 2.7 %collective-permute-done.lcur_ref.lprev_ref = bf16[2,1024,128]{2,1,0:T(8,128)(2,1)S(1)} collective-permute-done((bf16[2,1024,128]{2,1,0:T(8,128)(2,1)S(1)}, bf16[2,1024,128]{2,1,0:T(8,128)(2,1)S(1)}, u32[]{:S(2)}, u32[]{:S(2)}) %collective-permute-start) | collective-permute-done | bytes 524320 | tf_op jit(solution)/shard_map/ppermute | solution.py:217
  18.9 1.6 %fusion = (f32[2]{0:T(128)S(1)}, f32[2]{0:T(128)S(1)}, f32[2]{0:T(128)S(1)}) fusion(bf16[2,1024,128]{2,1,0:T(8,128)(2,1)S(1)} %collective-permute-done.lcur_ref.lprev_ref, f32[128]{0:T(128)S(1)} %compare_convert_fusion.1, bf16[2,1024,1024]{2,1,0:T(8,128)(2,1)} %prev_ref.1), kind=kLoop, calls=%fused_computation.8 | loop fusion | flops 1835002 | bytes 1049112 | tf_op jit(solution)/shard_map/reduce_sum | solution.py:22
  20.7 1.7 %fusion.5 = (f32[2]{0:T(128)S(1)}, f32[2]{0:T(128)S(1)}, f32[2]{0:T(128)S(1)}) fusion(bf16[2,1024,128]{2,1,0:T(8,128)(2,1)S(1)} %collective-permute-done.lcur_ref.lprev_ref, f32[2]{0:T(128)S(1)} %get-tuple-element.43, f32[2]{0:T(128)S(1)} %get-tuple-element.42, f32[128]{0:T(128)S(1)} %compare_convert_fusion.1, bf16[2,1024,1024]{2,1,0:T(8,128)(2,1)} %prev_ref.1), kind=kLoop, calls=%fused_computation.13 | loop fusion | flops 3145722 | bytes 1049128 | tf_op jit(solution)/shard_map/reduce_sum | solution.py:28
  22.8 1.9 %collective-permute-start.1 = (f32[5,2]{0,1:T(2,128)S(1)}, f32[5,2]{0,1:T(2,128)S(1)}, u32[]{:S(2)}, u32[]{:S(2)}) collective-permute-start(f32[5,2]{0,1:T(2,128)S(1)} %stack.4), channel_id=1, source_target_pairs={{4,0},{8,4},{12,8},{16,12},{20,16},{24,20},{28,24},{5,1},{9,5},{13... | collective-permute-start | bytes 128 | tf_op jit(solution)/shard_map/ppermute | solution.py:217
  24.7 1.7 %fusion.10 = (f32[2]{0:T(128)S(1)}, f32[2]{0:T(128)S(1)}, f32[2]{0:T(128)S(1)}) fusion(bf16[2,128,1024]{2,1,0:T(8,128)(2,1)S(1)} %collective-permute-done.2.up_ref, f32[128]{0:T(128)S(1)} %compare_convert_fusion, bf16[2,1024,1024]{2,1,0:T(8,128)(2,1)} %prev_ref.1), kind=kLoop, calls=%fused_computation.18 | loop fusion | flops 1835002 | bytes 1049112 | tf_op jit(solution)/shard_map/reduce_sum | solution.py:22
  26.6 1.8 %fusion.15 = (f32[2]{0:T(128)S(1)}, f32[2]{0:T(128)S(1)}, f32[2]{0:T(128)S(1)}) fusion(bf16[2,128,1024]{2,1,0:T(8,128)(2,1)S(1)} %collective-permute-done.2.up_ref, f32[2]{0:T(128)S(1)} %get-tuple-element.45, f32[2]{0:T(128)S(1)} %get-tuple-element.44, f32[128]{0:T(128)S(1)} %compare_convert_fusion, bf16[2,1024,1024]{2,1,0:T(8,128)(2,1)} %prev_ref.1), kind=kLoop, calls=%fused_computation.23 | loop fusion | flops 3145722 | bytes 1049128 | tf_op jit(solution)/shard_map/reduce_sum | solution.py:28
  28.8 1.3 %collective-permute-start.3 = (f32[5,2]{0,1:T(2,128)S(1)}, f32[5,2]{0,1:T(2,128)S(1)}, u32[]{:S(2)}, u32[]{:S(2)}) collective-permute-start(f32[5,2]{0,1:T(2,128)S(1)} %stack.5), channel_id=1, source_target_pairs={{1,0},{2,1},{3,2},{5,4},{6,5},{7,6},{9,8},{10,9},{11,10},{13,12},{... | collective-permute-start | bytes 128 | tf_op jit(solution)/shard_map/ppermute | solution.py:217
  30.3 1.5 %collective-permute-done.3 = f32[5,2]{0,1:T(2,128)S(1)} collective-permute-done((f32[5,2]{0,1:T(2,128)S(1)}, f32[5,2]{0,1:T(2,128)S(1)}, u32[]{:S(2)}, u32[]{:S(2)}) %collective-permute-start.3) | collective-permute-done | bytes 72 | tf_op jit(solution)/shard_map/ppermute | solution.py:217
  32.2 4.1 %collective-permute-start.7 = (f32[4]{0:T(128)S(1)}, f32[4]{0:T(128)S(1)}, u32[]{:S(2)}, u32[]{:S(2)}) collective-permute-start(f32[4]{0:T(128)S(1)} %pad_maximum_fusion), channel_id=1, source_target_pairs={{0,1},{1,2},{2,3},{4,5},{5,6},{6,7},{8,9},{9,10},{10,11},{12,13},{... | collective-permute-start | bytes 56 | tf_op jit(solution)/shard_map/ppermute | solution.py:217
  36.3 3.3 %collective-permute-start.6 = (f32[4]{0:T(128)S(1)}, f32[4]{0:T(128)S(1)}, u32[]{:S(2)}, u32[]{:S(2)}) collective-permute-start(f32[4]{0:T(128)S(1)} %pad_maximum_fusion), channel_id=1, source_target_pairs={{0,4},{4,8},{8,12},{12,16},{16,20},{20,24},{24,28},{1,5},{5,9},{9,... | collective-permute-start | bytes 56 | tf_op jit(solution)/shard_map/ppermute | solution.py:217
  39.7 1.3 %collective-permute-start.5 = (f32[4]{0:T(128)S(1)}, f32[4]{0:T(128)S(1)}, u32[]{:S(2)}, u32[]{:S(2)}) collective-permute-start(f32[4]{0:T(128)S(1)} %pad_maximum_fusion), channel_id=1, source_target_pairs={{1,0},{2,1},{3,2},{5,4},{6,5},{7,6},{9,8},{10,9},{11,10},{13,12},{... | collective-permute-start | bytes 56 | tf_op jit(solution)/shard_map/ppermute | solution.py:217
  41.0 3.4 %collective-permute-start.4 = (f32[4]{0:T(128)S(1)}, f32[4]{0:T(128)S(1)}, u32[]{:S(2)}, u32[]{:S(2)}) collective-permute-start(f32[4]{0:T(128)S(1)} %pad_maximum_fusion), channel_id=1, source_target_pairs={{4,0},{8,4},{12,8},{16,12},{20,16},{24,20},{28,24},{5,1},{9,5},{13... | collective-permute-start | bytes 56 | tf_op jit(solution)/shard_map/ppermute | solution.py:217
  44.4 2.0 %collective-permute-done.4 = f32[4]{0:T(128)S(1)} collective-permute-done((f32[4]{0:T(128)S(1)}, f32[4]{0:T(128)S(1)}, u32[]{:S(2)}, u32[]{:S(2)}) %collective-permute-start.4) | collective-permute-done | bytes 48 | tf_op jit(solution)/shard_map/ppermute | solution.py:217
  46.6 4.0 %collective-permute-start.10 = (f32[4]{0:T(128)S(1)}, f32[4]{0:T(128)S(1)}, u32[]{:S(2)}, u32[]{:S(2)}) collective-permute-start(f32[4]{0:T(128)S(1)} %pad_maximum_fusion.1), channel_id=1, source_target_pairs={{0,5},{4,9},{8,13},{12,17},{16,21},{20,25},{24,29},{1,6},{5,10},{9... | collective-permute-start | bytes 56 | tf_op jit(solution)/shard_map/ppermute | solution.py:305
  50.6 3.9 %collective-permute-start.9 = (f32[4]{0:T(128)S(1)}, f32[4]{0:T(128)S(1)}, u32[]{:S(2)}, u32[]{:S(2)}) collective-permute-start(f32[4]{0:T(128)S(1)} %pad_maximum_fusion.1), channel_id=1, source_target_pairs={{0,1},{1,2},{2,3},{4,5},{5,6},{6,7},{8,9},{9,10},{10,11},{12,13},{... | collective-permute-start | bytes 56 | tf_op jit(solution)/shard_map/ppermute | solution.py:217
  54.5 2.4 %collective-permute-start.8 = (f32[4]{0:T(128)S(1)}, f32[4]{0:T(128)S(1)}, u32[]{:S(2)}, u32[]{:S(2)}) collective-permute-start(f32[4]{0:T(128)S(1)} %pad_maximum_fusion.1), channel_id=1, source_target_pairs={{0,4},{4,8},{8,12},{12,16},{16,20},{20,24},{24,28},{1,5},{5,9},{9,... | collective-permute-start | bytes 56 | tf_op jit(solution)/shard_map/ppermute | solution.py:217
  57.1 3.8 %collective-permute-done.8 = f32[4]{0:T(128)S(1)} collective-permute-done((f32[4]{0:T(128)S(1)}, f32[4]{0:T(128)S(1)}, u32[]{:S(2)}, u32[]{:S(2)}) %collective-permute-start.8) | collective-permute-done | bytes 48 | tf_op jit(solution)/shard_map/ppermute | solution.py:217
  62.1 11.6 %shard_map.59 = (f32[2,1024,1024]{2,1,0:T(8,128)}, f32[1024,1024]{1,0:T(8,128)}) custom-call(s32[2,4,8]{2,1,0:T(4,128)} %off_ref.1, s32[2,4,8]{2,1,0:T(4,128)} %band_ref.1, f32[16]{0:T(128)} %concatenate.11.terms_ref, bf16[2,1024,1024]{2,1,0:T(8,128)(2,1)} %prev_ref.1, bf16[2,1024,1024]{2,1,0:T(8,128)(2,1)} %prev_ref.1, bf16[2,1024,128]{2,1,0:T(8,128)(2,1)} %copy-done, ...), custom_call_target="tpu_custom_call" | custom-call | flops 25165824 | bytes 22020096 | tf_op jit(solution)/shard_map/pallas_call | solution.py:196
  (45 shorter events, 5.5 us)
Async XLA Ops:
  1.7 17.2 %collective-permute-start = (bf16[2,1024,128]{2,1,0:T(8,128)(2,1)S(1)}, bf16[2,1024,128]{2,1,0:T(8,128)(2,1)S(1)}, u32[]{:S(2)}, u32[]{:S(2)}) collective-permute-start(bf16[2,1024,128]{2,1,0:T(8,128)(2,1)S(1)} %slice.57), channel_id=1, source_target_pairs={{0,4},{4,8},{8,12},{12,16},{16,20},{20,24},{24,28},{1,5},{5,9},{9,... | collective-permute-start | bytes 1572872 | tf_op jit(solution)/shard_map/ppermute | solution.py:217
  6.0 55.5 %collective-permute-start.11 = (bf16[2,128,128]{2,1,0:T(8,128)(2,1)S(1)}, bf16[2,128,128]{2,1,0:T(8,128)(2,1)S(1)}, u32[]{:S(2)}, u32[]{:S(2)}) collective-permute-start(bf16[2,128,128]{2,1,0:T(8,128)(2,1)S(1)} %slice.75), channel_id=1, source_target_pairs={{0,5},{4,9},{8,13},{12,17},{16,21},{20,25},{24,29},{1,6},{5,10},{9... | collective-permute-start | bytes 196616 | tf_op jit(solution)/shard_map/ppermute | solution.py:249
  9.7 15.0 %collective-permute-start.2 = (bf16[2,128,1024]{2,1,0:T(8,128)(2,1)S(1)}, bf16[2,128,1024]{2,1,0:T(8,128)(2,1)S(1)}, u32[]{:S(2)}, u32[]{:S(2)}) collective-permute-start(bf16[2,128,1024]{2,1,0:T(8,128)(2,1)S(1)} %slice.59), channel_id=1, source_target_pairs={{0,1},{1,2},{2,3},{4,5},{5,6},{6,7},{8,9},{9,10},{10,11},{12,13},{... | collective-permute-start | bytes 1572872 | tf_op jit(solution)/shard_map/ppermute | solution.py:217
  18.9 42.6 %copy-start = (bf16[2,1024,128]{2,1,0:T(8,128)(2,1)}, bf16[2,1024,128]{2,1,0:T(8,128)(2,1)S(1)}, u32[]{:S(2)}) copy-start(bf16[2,1024,128]{2,1,0:T(8,128)(2,1)S(1)} %collective-permute-done.lcur_ref.lprev_ref) | copy-start | bytes 1572868
  22.8 7.3 %collective-permute-start.1 = (f32[5,2]{0,1:T(2,128)S(1)}, f32[5,2]{0,1:T(2,128)S(1)}, u32[]{:S(2)}, u32[]{:S(2)}) collective-permute-start(f32[5,2]{0,1:T(2,128)S(1)} %stack.4), channel_id=1, source_target_pairs={{4,0},{8,4},{12,8},{16,12},{20,16},{24,20},{28,24},{5,1},{9,5},{13... | collective-permute-start | bytes 128 | tf_op jit(solution)/shard_map/ppermute | solution.py:217
  24.7 36.8 %copy-start.1 = (bf16[2,128,1024]{2,1,0:T(8,128)(2,1)}, bf16[2,128,1024]{2,1,0:T(8,128)(2,1)S(1)}, u32[]{:S(2)}) copy-start(bf16[2,128,1024]{2,1,0:T(8,128)(2,1)S(1)} %collective-permute-done.2.up_ref) | copy-start | bytes 1572868
  28.8 3.0 %collective-permute-start.3 = (f32[5,2]{0,1:T(2,128)S(1)}, f32[5,2]{0,1:T(2,128)S(1)}, u32[]{:S(2)}, u32[]{:S(2)}) collective-permute-start(f32[5,2]{0,1:T(2,128)S(1)} %stack.5), channel_id=1, source_target_pairs={{1,0},{2,1},{3,2},{5,4},{6,5},{7,6},{9,8},{10,9},{11,10},{13,12},{... | collective-permute-start | bytes 128 | tf_op jit(solution)/shard_map/ppermute | solution.py:217
  32.2 12.2 %collective-permute-start.7 = (f32[4]{0:T(128)S(1)}, f32[4]{0:T(128)S(1)}, u32[]{:S(2)}, u32[]{:S(2)}) collective-permute-start(f32[4]{0:T(128)S(1)} %pad_maximum_fusion), channel_id=1, source_target_pairs={{0,1},{1,2},{2,3},{4,5},{5,6},{6,7},{8,9},{9,10},{10,11},{12,13},{... | collective-permute-start | bytes 56 | tf_op jit(solution)/shard_map/ppermute | solution.py:217
  36.3 8.1 %collective-permute-start.6 = (f32[4]{0:T(128)S(1)}, f32[4]{0:T(128)S(1)}, u32[]{:S(2)}, u32[]{:S(2)}) collective-permute-start(f32[4]{0:T(128)S(1)} %pad_maximum_fusion), channel_id=1, source_target_pairs={{0,4},{4,8},{8,12},{12,16},{16,20},{20,24},{24,28},{1,5},{5,9},{9,... | collective-permute-start | bytes 56 | tf_op jit(solution)/shard_map/ppermute | solution.py:217
  39.7 4.7 %collective-permute-start.5 = (f32[4]{0:T(128)S(1)}, f32[4]{0:T(128)S(1)}, u32[]{:S(2)}, u32[]{:S(2)}) collective-permute-start(f32[4]{0:T(128)S(1)} %pad_maximum_fusion), channel_id=1, source_target_pairs={{1,0},{2,1},{3,2},{5,4},{6,5},{7,6},{9,8},{10,9},{11,10},{13,12},{... | collective-permute-start | bytes 56 | tf_op jit(solution)/shard_map/ppermute | solution.py:217
  41.0 5.5 %collective-permute-start.4 = (f32[4]{0:T(128)S(1)}, f32[4]{0:T(128)S(1)}, u32[]{:S(2)}, u32[]{:S(2)}) collective-permute-start(f32[4]{0:T(128)S(1)} %pad_maximum_fusion), channel_id=1, source_target_pairs={{4,0},{8,4},{12,8},{16,12},{20,16},{24,20},{28,24},{5,1},{9,5},{13... | collective-permute-start | bytes 56 | tf_op jit(solution)/shard_map/ppermute | solution.py:217
  46.6 10.3 %collective-permute-start.10 = (f32[4]{0:T(128)S(1)}, f32[4]{0:T(128)S(1)}, u32[]{:S(2)}, u32[]{:S(2)}) collective-permute-start(f32[4]{0:T(128)S(1)} %pad_maximum_fusion.1), channel_id=1, source_target_pairs={{0,5},{4,9},{8,13},{12,17},{16,21},{20,25},{24,29},{1,6},{5,10},{9... | collective-permute-start | bytes 56 | tf_op jit(solution)/shard_map/ppermute | solution.py:305
  50.6 6.4 %collective-permute-start.9 = (f32[4]{0:T(128)S(1)}, f32[4]{0:T(128)S(1)}, u32[]{:S(2)}, u32[]{:S(2)}) collective-permute-start(f32[4]{0:T(128)S(1)} %pad_maximum_fusion.1), channel_id=1, source_target_pairs={{0,1},{1,2},{2,3},{4,5},{5,6},{6,7},{8,9},{9,10},{10,11},{12,13},{... | collective-permute-start | bytes 56 | tf_op jit(solution)/shard_map/ppermute | solution.py:217
  54.5 6.4 %collective-permute-start.8 = (f32[4]{0:T(128)S(1)}, f32[4]{0:T(128)S(1)}, u32[]{:S(2)}, u32[]{:S(2)}) collective-permute-start(f32[4]{0:T(128)S(1)} %pad_maximum_fusion.1), channel_id=1, source_target_pairs={{0,4},{4,8},{8,12},{12,16},{16,20},{20,24},{24,28},{1,5},{5,9},{9,... | collective-permute-start | bytes 56 | tf_op jit(solution)/shard_map/ppermute | solution.py:217
  61.5 0.6 copy-start.2

commit v10 on v9

--- a/solution.py
+++ b/solution.py
@@ -14,19 +14,6 @@
 
 
 eps = 1e-06
-
-
-def strip_stats(former, latter, window):
-    full = jnp.broadcast_to(window, former.shape)
-    number = jnp.sum(full, axis=(-2, -1))
-    mean_former = jnp.sum(former * full, axis=(-2, -1)) / number
-    mean_latter = jnp.sum(latter * full, axis=(-2, -1)) / number
-    dev_former = (former - mean_former[:, None, None]) * full
-    dev_latter = (latter - mean_latter[:, None, None]) * full
-    var_former = jnp.sum(dev_former * dev_former, axis=(-2, -1)) / number
-    var_latter = jnp.sum(dev_latter * dev_latter, axis=(-2, -1)) / number
-    covariance = jnp.sum(dev_former * dev_latter, axis=(-2, -1)) / number
-    return jnp.stack([mean_former, mean_latter, var_former, var_latter, covariance])
 
 
 def pair_terms(stats):
@@ -159,6 +146,79 @@
             out_ref[p, :width, :width] += (scale * window + level) * w_corner
 
 
+def stats_kernel(ext_ref, far_left_ref, own_left_ref, far_up_ref, own_up_ref, left_ref, up_ref):
+    f32 = jnp.float32
+    r = lax.axis_index("row")
+    c = lax.axis_index("col")
+    planes = far_left_ref.shape[0]
+    width = left_ref.shape[1]
+    extent_h = ext_ref[0, r, jnp.maximum(c - 1, 0)]
+    extent_v = ext_ref[1, jnp.maximum(r - 1, 0), c]
+
+    def measure(former_ref, latter_ref, window, out_ref):
+        full = jnp.broadcast_to(window.astype(f32), former_ref.shape[1:])
+        number = jnp.sum(full)
+        out_ref[...] = jnp.zeros(out_ref.shape, f32)
+        for p in range(planes):
+            former = former_ref[p].astype(f32)
+            latter = latter_ref[p].astype(f32)
+            mean_former = jnp.sum(former * full) / number
+            mean_latter = jnp.sum(latter * full) / number
+            dev_former = (former - mean_former) * full
+            dev_latter = (latter - mean_latter) * full
+            values = (
+                mean_former,
+                mean_latter,
+                jnp.sum(dev_former * dev_former) / number,
+                jnp.sum(dev_latter * dev_latter) / number,
+                jnp.sum(dev_former * dev_latter) / number,
+            )
+            for k, value in enumerate(values):
+                out_ref[pl.ds(k * planes + p, 1), :] = jnp.broadcast_to(value, (1, width))
+
+    lane = lax.broadcasted_iota(jnp.int32, (1, width), 1)
+    line = lax.broadcasted_iota(jnp.int32, (width, 1), 0)
+    measure(far_left_ref, own_left_ref, lane < extent_h, left_ref)
+    measure(far_up_ref, own_up_ref, line < extent_v, up_ref)
+
+
+def pair_stats(extents, from_left, from_up, tiles):
+    planes, tile_px, _ = tiles.shape
+    width = from_left.shape[2]
+    rows_out = 16
+
+    def first(*_):
+        return (0, 0, 0)
+
+    grid_spec = pltpu.PrefetchScalarGridSpec(
+        num_scalar_prefetch=1,
+        grid=(1,),
+        in_specs=[
+            pl.BlockSpec((planes, tile_px, width), first),
+            pl.BlockSpec((planes, tile_px, width), first),
+            pl.BlockSpec((planes, width, tile_px), first),
+            pl.BlockSpec((planes, width, tile_px), first),
+        ],
+        out_specs=[
+            pl.BlockSpec((rows_out, width), lambda *_: (0, 0)),
+            pl.BlockSpec((rows_out, width), lambda *_: (0, 0)),
+        ],
+    )
+    return pl.pallas_call(
+        stats_kernel,
+        grid_spec=grid_spec,
+        out_shape=[jax.ShapeDtypeStruct((rows_out, width), jnp.float32)] * 2,
+        cost_estimate=pl.CostEstimate(
+            flops=24 * planes * tile_px * width, transcendentals=0,
+            bytes_accessed=2 * 4 * planes * tile_px * width,
+        ),
+    )(extents, from_left, tiles, from_up, tiles)
+
+
+def unpack_stats(block, planes):
+    return block[: 5 * planes, 0].reshape(5, planes)
+
+
 def blend(offsets, bands, terms, tiles, from_left, from_up, from_corner, n_row, n_col):
     planes, tile_px, _ = tiles.shape
     width = from_left.shape[2]
@@ -238,8 +298,6 @@
 
     right_strip = tiles[:, :, tile_px - width :]
     down_strip = tiles[:, tile_px - width :, :]
-    left_strip = tiles[:, :, :width]
-    up_strip = tiles[:, :width, :]
     corner = tiles[:, tile_px - width :, tile_px - width :]
     from_left = shifted(right_strip, "col", n_col, 1)
     from_up = shifted(down_strip, "row", n_row, 1)
@@ -250,23 +308,14 @@
 
     left_col = jnp.maximum(col_index - 1, 0)
     upper_row = jnp.maximum(row_index - 1, 0)
-    strip_ids = jnp.arange(width, dtype=jnp.int32)
-
-    def across(extent):
-        return (strip_ids < extent).astype(jnp.float32)[None, None, :]
-
-    def along(extent):
-        return (strip_ids < extent).astype(jnp.float32)[None, :, None]
-
     f32 = jnp.float32
-    left_stats = strip_stats(
-        from_left.astype(f32), left_strip.astype(f32), across(extents[0, row_index, left_col])
-    )
-    up_stats = strip_stats(
-        from_up.astype(f32), up_strip.astype(f32), along(extents[1, upper_row, col_index])
-    )
-    right_stats = shifted(left_stats, "col", n_col, -1)
-    down_stats = shifted(up_stats, "row", n_row, -1)
+    left_block, up_block = pair_stats(extents, from_left, from_up, tiles)
+    right_block = shifted(left_block, "col", n_col, -1)
+    down_block = shifted(up_block, "row", n_row, -1)
+    left_stats = unpack_stats(left_block, planes)
+    up_stats = unpack_stats(up_block, planes)
+    right_stats = unpack_stats(right_block, planes)
+    down_stats = unpack_stats(down_block, planes)
     has_right = col_index < n_col - 1
     has_down = row_index < n_row - 1
     has_left_pair = col_index > 0

time: 74.6 us -> 74.4 us (level)
  other arithmetic: 8.45 us -> 0.29 us
  Pallas kernels: 11.6 us -> 16.6 us
  waiting for transfers between devices: 10.1 us -> 12.8 us
    reduce_sum x4 -> x0, other arithmetic: 6.83 us -> none  [the longest x2 3.52 us: strip_stats(): covariance = jnp.sum(dev_former * dev_latter, axis=(-2, -1)) / number]
    pallas_call x0 -> x1, Pallas kernels: none -> 4.97 us  [pair_stats(): pl.pallas_call(stats_kernel, grid_spec=grid_spec, out_shape=[jax.ShapeDty...]
    ppermute x10, waiting for transfers between devices: 10.1 us -> 12.8 us  [shifted(): return lax.ppermute(block, axis, route)]
    ppermute x1, starting transfers between devices: 2.57 us -> 5.04 us  [local(): from_corner = lax.ppermute(corner, ('col', 'row'), diagonal)]
    ppermute x10, starting transfers between devices: 28.9 us -> 26.6 us  [shifted(): return lax.ppermute(block, axis, route)]
    unnamed x6, local copies, waits for them, and re-layouts: 0.62 us -> 2.21 us
    convert_element_type x2 -> x0, other arithmetic: 1.3 us -> none  [the longest x1 0.65 us: along(): return (strip_ids < extent).astype(jnp.float32)[None, :, None]]
    dynamic_slice x1 -> x0, local copies, waits for them, and re-layouts: 1.29 us -> none  [local(): extents[0, row_index, left_col]]
  transfers between devices with their start and end apart: 12 -> 12, of which waited for: 4 -> 5; matrix products, arithmetic and copies ran while one was open for 19% -> 6% of each run, Pallas kernels for 0% -> 7%
where the time goes in v10:
time: 74.4 us; the launch traced here: 73.7 us
  starting transfers between devices  35.7 us (48%)
  Pallas kernels  16.6 us (22%)
  waiting for transfers between devices  12.8 us (17%)
  local copies, waits for them, and re-layouts  7.51 us (10%)
  between operations  0.81 us (1%)
    ppermute x10, starting transfers between devices, shifted(): return lax.ppermute(block, axis, route)  26.6 us
    ppermute x10, waiting for transfers between devices, shifted(): return lax.ppermute(block, axis, route)  12.8 us
    pallas_call x1, Pallas kernels, blend(): pl.pallas_call(functools.partial(blend_kernel, n_row=n_row, n_col=n_col),...  11.6 us
    ppermute x1, starting transfers between devices, local(): from_corner = lax.ppermute(corner, ('col', 'row'), diagonal)  5.04 us
    pallas_call x1, Pallas kernels, pair_stats(): pl.pallas_call(stats_kernel, grid_spec=grid_spec, out_shape=[jax.ShapeDty...  4.97 us
    ppermute x1, starting transfers between devices, local(): final_corner = lax.ppermute(final, ('col', 'row'), diagonal)  4 us
    unnamed x6, local copies, waits for them, and re-layouts  2.21 us
    another operation x3, local copies, waits for them, and re-layouts, pair_terms(): mean_former, mean_latter, var_former, var_latter, covariance = stats  1.5 us
  transfers between devices with their start and end apart: 12, of which 5 were waited for; matrix products, arithmetic and copies ran while one was open for 6% of the time, Pallas kernels for 7%

profile of v10, /device:TPU:16, one launch (start us, length us, event | category | flops | bytes accessed | tf_op | source)
XLA Modules:
  0.0 73.7 jit_solution(16786576374646979900)
XLA Ops:
  0.6 1.1 %slice.95 = bf16[2,1024,128]{2,1,0:T(8,128)(2,1)S(1)} slice(bf16[2,1024,1024]{2,1,0:T(8,128)(2,1)} %prev_ref.1), slice={[0:2], [0:1024], [896:1024]} | slice | bytes 1048576 | tf_op jit(solution)/shard_map/slice | solution.py:299
  1.7 3.4 %collective-permute-start = (bf16[2,1024,128]{2,1,0:T(8,128)(2,1)S(1)}, bf16[2,1024,128]{2,1,0:T(8,128)(2,1)S(1)}, u32[]{:S(2)}, u32[]{:S(2)}) collective-permute-start(bf16[2,1024,128]{2,1,0:T(8,128)(2,1)S(1)} %slice.95), channel_id=1, source_target_pairs={{0,4},{4,8},{8,12},{12,16},{16,20},{20,24},{24,28},{1,5},{5,9},{9,... | collective-permute-start | bytes 1572872 | tf_op jit(solution)/shard_map/ppermute | solution.py:277
  5.1 1.1 %slice.96 = bf16[2,128,1024]{2,1,0:T(8,128)(2,1)S(1)} slice(bf16[2,1024,1024]{2,1,0:T(8,128)(2,1)} %prev_ref.1), slice={[0:2], [896:1024], [0:1024]} | slice | bytes 1048576 | tf_op jit(solution)/shard_map/slice | solution.py:300
  6.2 1.5 %collective-permute-start.1 = (bf16[2,128,1024]{2,1,0:T(8,128)(2,1)S(1)}, bf16[2,128,1024]{2,1,0:T(8,128)(2,1)S(1)}, u32[]{:S(2)}, u32[]{:S(2)}) collective-permute-start(bf16[2,128,1024]{2,1,0:T(8,128)(2,1)S(1)} %slice.96), channel_id=1, source_target_pairs={{0,1},{1,2},{2,3},{4,5},{5,6},{6,7},{8,9},{9,10},{10,11},{12,13},{... | collective-permute-start | bytes 1572872 | tf_op jit(solution)/shard_map/ppermute | solution.py:277
  7.7 0.9 %slice.111 = bf16[2,128,128]{2,1,0:T(8,128)(2,1)S(1)} slice(bf16[2,1024,1024]{2,1,0:T(8,128)(2,1)} %prev_ref.1), slice={[0:2], [896:1024], [896:1024]} | slice | bytes 131072 | tf_op jit(solution)/shard_map/slice | solution.py:301
  8.6 5.0 %collective-permute-start.11 = (bf16[2,128,128]{2,1,0:T(8,128)(2,1)S(1)}, bf16[2,128,128]{2,1,0:T(8,128)(2,1)S(1)}, u32[]{:S(2)}, u32[]{:S(2)}) collective-permute-start(bf16[2,128,128]{2,1,0:T(8,128)(2,1)S(1)} %slice.111), channel_id=1, source_target_pairs={{0,5},{4,9},{8,13},{12,17},{16,21},{20,25},{24,29},{1,6},{5,10},{9... | collective-permute-start | bytes 196616 | tf_op jit(solution)/shard_map/ppermute | solution.py:307
  13.7 5.2 %collective-permute-done.far_left_ref.lcur_ref.lprev_ref = bf16[2,1024,128]{2,1,0:T(8,128)(2,1)S(1)} collective-permute-done((bf16[2,1024,128]{2,1,0:T(8,128)(2,1)S(1)}, bf16[2,1024,128]{2,1,0:T(8,128)(2,1)S(1)}, u32[]{:S(2)}, u32[]{:S(2)}) %collective-permute-start) | collective-permute-done | bytes 524320 | tf_op jit(solution)/shard_map/ppermute | solution.py:277
  18.9 0.8 %copy-done = bf16[2,1024,128]{2,1,0:T(8,128)(2,1)} copy-done((bf16[2,1024,128]{2,1,0:T(8,128)(2,1)}, bf16[2,1024,128]{2,1,0:T(8,128)(2,1)S(1)}, u32[]{:S(2)}) %copy-start) | copy-done | bytes 524312
  19.7 0.8 %copy-done.1 = bf16[2,128,1024]{2,1,0:T(8,128)(2,1)} copy-done((bf16[2,128,1024]{2,1,0:T(8,128)(2,1)}, bf16[2,128,1024]{2,1,0:T(8,128)(2,1)S(1)}, u32[]{:S(2)}) %copy-start.1) | copy-done | bytes 524312
  20.5 5.0 %shard_map.59 = (f32[16,128]{1,0:T(8,128)}, f32[16,128]{1,0:T(8,128)}) custom-call(s32[2,4,8]{2,1,0:T(4,128)} %ext_ref.1, bf16[2,1024,128]{2,1,0:T(8,128)(2,1)} %copy-done, bf16[2,1024,1024]{2,1,0:T(8,128)(2,1)} %prev_ref.1, bf16[2,128,1024]{2,1,0:T(8,128)(2,1)} %copy-done.1, bf16[2,1024,1024]{2,1,0:T(8,128)(2,1)} %prev_ref.1), custom_call_target="tpu_custom_call" | custom-call | flops 6291456 | bytes 2097152 | tf_op jit(solution)/shard_map/pallas_call | solution.py:207
  25.4 1.9 %collective-permute-start.2 = (f32[16,128]{1,0:T(8,128)}, f32[16,128]{1,0:T(8,128)S(1)}, u32[]{:S(2)}, u32[]{:S(2)}) collective-permute-start(f32[16,128]{1,0:T(8,128)} %get-tuple-element.4), channel_id=1, source_target_pairs={{4,0},{8,4},{12,8},{16,12},{20,16},{24,20},{28,24},{5,1},{9,5},{13... | collective-permute-start | bytes 24584 | tf_op jit(solution)/shard_map/ppermute | solution.py:277
  27.4 1.1 %slice_reduce_fusion.10 = (f32[2]{0:T(128)S(1)}, f32[2]{0:T(128)S(1)}, f32[2]{0:T(128)S(1)}, f32[2]{0:T(128)S(1)}, f32[2]{0:T(128)S(1)}, /*index=5*/f32[2]{0:T(1...) fusion(f32[16,128]{1,0:T(8,128)} %get-tuple-element.5, f32[16,128]{1,0:T(8,128)} %get-tuple-element.4), kind=kLoop, calls=%fused_computation.10 | loop fusion | bytes 160 | tf_op jit(solution)/shard_map/unstack | solution.py:20
  28.5 1.3 %collective-permute-start.3 = (f32[16,128]{1,0:T(8,128)}, f32[16,128]{1,0:T(8,128)S(1)}, u32[]{:S(2)}, u32[]{:S(2)}) collective-permute-start(f32[16,128]{1,0:T(8,128)} %get-tuple-element.5), channel_id=1, source_target_pairs={{1,0},{2,1},{3,2},{5,4},{6,5},{7,6},{9,8},{10,9},{11,10},{13,12},{... | collective-permute-start | bytes 24584 | tf_op jit(solution)/shard_map/ppermute | solution.py:277
  29.8 1.4 %collective-permute-done.2 = f32[16,128]{1,0:T(8,128)S(1)} collective-permute-done((f32[16,128]{1,0:T(8,128)}, f32[16,128]{1,0:T(8,128)S(1)}, u32[]{:S(2)}, u32[]{:S(2)}) %collective-permute-start.2) | collective-permute-done | bytes 8224 | tf_op jit(solution)/shard_map/ppermute | solution.py:277
  32.1 4.2 %collective-permute-start.7 = (f32[4]{0:T(128)S(1)}, f32[4]{0:T(128)S(1)}, u32[]{:S(2)}, u32[]{:S(2)}) collective-permute-start(f32[4]{0:T(128)S(1)} %pad_maximum_fusion), channel_id=1, source_target_pairs={{0,1},{1,2},{2,3},{4,5},{5,6},{6,7},{8,9},{9,10},{10,11},{12,13},{... | collective-permute-start | bytes 56 | tf_op jit(solution)/shard_map/ppermute | solution.py:277
  36.3 3.3 %collective-permute-start.6 = (f32[4]{0:T(128)S(1)}, f32[4]{0:T(128)S(1)}, u32[]{:S(2)}, u32[]{:S(2)}) collective-permute-start(f32[4]{0:T(128)S(1)} %pad_maximum_fusion), channel_id=1, source_target_pairs={{0,4},{4,8},{8,12},{12,16},{16,20},{20,24},{24,28},{1,5},{5,9},{9,... | collective-permute-start | bytes 56 | tf_op jit(solution)/shard_map/ppermute | solution.py:277
  39.6 1.3 %collective-permute-start.5 = (f32[4]{0:T(128)S(1)}, f32[4]{0:T(128)S(1)}, u32[]{:S(2)}, u32[]{:S(2)}) collective-permute-start(f32[4]{0:T(128)S(1)} %pad_maximum_fusion), channel_id=1, source_target_pairs={{1,0},{2,1},{3,2},{5,4},{6,5},{7,6},{9,8},{10,9},{11,10},{13,12},{... | collective-permute-start | bytes 56 | tf_op jit(solution)/shard_map/ppermute | solution.py:277
  40.9 3.4 %collective-permute-start.4 = (f32[4]{0:T(128)S(1)}, f32[4]{0:T(128)S(1)}, u32[]{:S(2)}, u32[]{:S(2)}) collective-permute-start(f32[4]{0:T(128)S(1)} %pad_maximum_fusion), channel_id=1, source_target_pairs={{4,0},{8,4},{12,8},{16,12},{20,16},{24,20},{28,24},{5,1},{9,5},{13... | collective-permute-start | bytes 56 | tf_op jit(solution)/shard_map/ppermute | solution.py:277
  44.4 2.0 %collective-permute-done.4 = f32[4]{0:T(128)S(1)} collective-permute-done((f32[4]{0:T(128)S(1)}, f32[4]{0:T(128)S(1)}, u32[]{:S(2)}, u32[]{:S(2)}) %collective-permute-start.4) | collective-permute-done | bytes 48 | tf_op jit(solution)/shard_map/ppermute | solution.py:277
  46.5 4.0 %collective-permute-start.10 = (f32[4]{0:T(128)S(1)}, f32[4]{0:T(128)S(1)}, u32[]{:S(2)}, u32[]{:S(2)}) collective-permute-start(f32[4]{0:T(128)S(1)} %pad_maximum_fusion.1), channel_id=1, source_target_pairs={{0,5},{4,9},{8,13},{12,17},{16,21},{20,25},{24,29},{1,6},{5,10},{9... | collective-permute-start | bytes 56 | tf_op jit(solution)/shard_map/ppermute | solution.py:354
  50.5 3.9 %collective-permute-start.9 = (f32[4]{0:T(128)S(1)}, f32[4]{0:T(128)S(1)}, u32[]{:S(2)}, u32[]{:S(2)}) collective-permute-start(f32[4]{0:T(128)S(1)} %pad_maximum_fusion.1), channel_id=1, source_target_pairs={{0,1},{1,2},{2,3},{4,5},{5,6},{6,7},{8,9},{9,10},{10,11},{12,13},{... | collective-permute-start | bytes 56 | tf_op jit(solution)/shard_map/ppermute | solution.py:277
  54.4 2.4 %collective-permute-start.8 = (f32[4]{0:T(128)S(1)}, f32[4]{0:T(128)S(1)}, u32[]{:S(2)}, u32[]{:S(2)}) collective-permute-start(f32[4]{0:T(128)S(1)} %pad_maximum_fusion.1), channel_id=1, source_target_pairs={{0,4},{4,8},{8,12},{12,16},{16,20},{20,24},{24,28},{1,5},{5,9},{9,... | collective-permute-start | bytes 56 | tf_op jit(solution)/shard_map/ppermute | solution.py:277
  57.0 3.8 %collective-permute-done.8 = f32[4]{0:T(128)S(1)} collective-permute-done((f32[4]{0:T(128)S(1)}, f32[4]{0:T(128)S(1)}, u32[]{:S(2)}, u32[]{:S(2)}) %collective-permute-start.8) | collective-permute-done | bytes 48 | tf_op jit(solution)/shard_map/ppermute | solution.py:277
  62.1 11.6 %shard_map.60 = (f32[2,1024,1024]{2,1,0:T(8,128)}, f32[1024,1024]{1,0:T(8,128)}) custom-call(s32[2,4,8]{2,1,0:T(4,128)} %off_ref.1, s32[2,4,8]{2,1,0:T(4,128)} %band_ref.1, f32[16]{0:T(128)} %concatenate.11.terms_ref, bf16[2,1024,1024]{2,1,0:T(8,128)(2,1)} %prev_ref.1, bf16[2,1024,1024]{2,1,0:T(8,128)(2,1)} %prev_ref.1, bf16[2,1024,128]{2,1,0:T(8,128)(2,1)} %copy-done, ...), custom_call_target="tpu_custom_call" | custom-call | flops 25165824 | bytes 22020096 | tf_op jit(solution)/shard_map/pallas_call | solution.py:256
  (24 shorter events, 2.5 us)
Async XLA Ops:
  1.7 17.2 %collective-permute-start = (bf16[2,1024,128]{2,1,0:T(8,128)(2,1)S(1)}, bf16[2,1024,128]{2,1,0:T(8,128)(2,1)S(1)}, u32[]{:S(2)}, u32[]{:S(2)}) collective-permute-start(bf16[2,1024,128]{2,1,0:T(8,128)(2,1)S(1)} %slice.95), channel_id=1, source_target_pairs={{0,4},{4,8},{8,12},{12,16},{16,20},{20,24},{24,28},{1,5},{5,9},{9,... | collective-permute-start | bytes 1572872 | tf_op jit(solution)/shard_map/ppermute | solution.py:277
  6.2 12.6 %collective-permute-start.1 = (bf16[2,128,1024]{2,1,0:T(8,128)(2,1)S(1)}, bf16[2,128,1024]{2,1,0:T(8,128)(2,1)S(1)}, u32[]{:S(2)}, u32[]{:S(2)}) collective-permute-start(bf16[2,128,1024]{2,1,0:T(8,128)(2,1)S(1)} %slice.96), channel_id=1, source_target_pairs={{0,1},{1,2},{2,3},{4,5},{5,6},{6,7},{8,9},{9,10},{10,11},{12,13},{... | collective-permute-start | bytes 1572872 | tf_op jit(solution)/shard_map/ppermute | solution.py:277
  8.6 52.9 %collective-permute-start.11 = (bf16[2,128,128]{2,1,0:T(8,128)(2,1)S(1)}, bf16[2,128,128]{2,1,0:T(8,128)(2,1)S(1)}, u32[]{:S(2)}, u32[]{:S(2)}) collective-permute-start(bf16[2,128,128]{2,1,0:T(8,128)(2,1)S(1)} %slice.111), channel_id=1, source_target_pairs={{0,5},{4,9},{8,13},{12,17},{16,21},{20,25},{24,29},{1,6},{5,10},{9... | collective-permute-start | bytes 196616 | tf_op jit(solution)/shard_map/ppermute | solution.py:307
  18.9 0.8 %copy-start = (bf16[2,1024,128]{2,1,0:T(8,128)(2,1)}, bf16[2,1024,128]{2,1,0:T(8,128)(2,1)S(1)}, u32[]{:S(2)}) copy-start(bf16[2,1024,128]{2,1,0:T(8,128)(2,1)S(1)} %collective-permute-done.far_left_ref.lcur_ref.lprev_ref) | copy-start | bytes 1572868
  19.7 0.8 %copy-start.1 = (bf16[2,128,1024]{2,1,0:T(8,128)(2,1)}, bf16[2,128,1024]{2,1,0:T(8,128)(2,1)S(1)}, u32[]{:S(2)}) copy-start(bf16[2,128,1024]{2,1,0:T(8,128)(2,1)S(1)} %collective-permute-done.1.far_up_ref.up_ref) | copy-start | bytes 1572868
  25.4 5.7 %collective-permute-start.2 = (f32[16,128]{1,0:T(8,128)}, f32[16,128]{1,0:T(8,128)S(1)}, u32[]{:S(2)}, u32[]{:S(2)}) collective-permute-start(f32[16,128]{1,0:T(8,128)} %get-tuple-element.4), channel_id=1, source_target_pairs={{4,0},{8,4},{12,8},{16,12},{20,16},{24,20},{28,24},{5,1},{9,5},{13... | collective-permute-start | bytes 24584 | tf_op jit(solution)/shard_map/ppermute | solution.py:277
  28.5 3.3 %collective-permute-start.3 = (f32[16,128]{1,0:T(8,128)}, f32[16,128]{1,0:T(8,128)S(1)}, u32[]{:S(2)}, u32[]{:S(2)}) collective-permute-start(f32[16,128]{1,0:T(8,128)} %get-tuple-element.5), channel_id=1, source_target_pairs={{1,0},{2,1},{3,2},{5,4},{6,5},{7,6},{9,8},{10,9},{11,10},{13,12},{... | collective-permute-start | bytes 24584 | tf_op jit(solution)/shard_map/ppermute | solution.py:277
  32.1 12.2 %collective-permute-start.7 = (f32[4]{0:T(128)S(1)}, f32[4]{0:T(128)S(1)}, u32[]{:S(2)}, u32[]{:S(2)}) collective-permute-start(f32[4]{0:T(128)S(1)} %pad_maximum_fusion), channel_id=1, source_target_pairs={{0,1},{1,2},{2,3},{4,5},{5,6},{6,7},{8,9},{9,10},{10,11},{12,13},{... | collective-permute-start | bytes 56 | tf_op jit(solution)/shard_map/ppermute | solution.py:277
  36.3 8.1 %collective-permute-start.6 = (f32[4]{0:T(128)S(1)}, f32[4]{0:T(128)S(1)}, u32[]{:S(2)}, u32[]{:S(2)}) collective-permute-start(f32[4]{0:T(128)S(1)} %pad_maximum_fusion), channel_id=1, source_target_pairs={{0,4},{4,8},{8,12},{12,16},{16,20},{20,24},{24,28},{1,5},{5,9},{9,... | collective-permute-start | bytes 56 | tf_op jit(solution)/shard_map/ppermute | solution.py:277
  39.6 4.7 %collective-permute-start.5 = (f32[4]{0:T(128)S(1)}, f32[4]{0:T(128)S(1)}, u32[]{:S(2)}, u32[]{:S(2)}) collective-permute-start(f32[4]{0:T(128)S(1)} %pad_maximum_fusion), channel_id=1, source_target_pairs={{1,0},{2,1},{3,2},{5,4},{6,5},{7,6},{9,8},{10,9},{11,10},{13,12},{... | collective-permute-start | bytes 56 | tf_op jit(solution)/shard_map/ppermute | solution.py:277
  40.9 5.5 %collective-permute-start.4 = (f32[4]{0:T(128)S(1)}, f32[4]{0:T(128)S(1)}, u32[]{:S(2)}, u32[]{:S(2)}) collective-permute-start(f32[4]{0:T(128)S(1)} %pad_maximum_fusion), channel_id=1, source_target_pairs={{4,0},{8,4},{12,8},{16,12},{20,16},{24,20},{28,24},{5,1},{9,5},{13... | collective-permute-start | bytes 56 | tf_op jit(solution)/shard_map/ppermute | solution.py:277
  46.5 10.3 %collective-permute-start.10 = (f32[4]{0:T(128)S(1)}, f32[4]{0:T(128)S(1)}, u32[]{:S(2)}, u32[]{:S(2)}) collective-permute-start(f32[4]{0:T(128)S(1)} %pad_maximum_fusion.1), channel_id=1, source_target_pairs={{0,5},{4,9},{8,13},{12,17},{16,21},{20,25},{24,29},{1,6},{5,10},{9... | collective-permute-start | bytes 56 | tf_op jit(solution)/shard_map/ppermute | solution.py:354
  50.5 6.4 %collective-permute-start.9 = (f32[4]{0:T(128)S(1)}, f32[4]{0:T(128)S(1)}, u32[]{:S(2)}, u32[]{:S(2)}) collective-permute-start(f32[4]{0:T(128)S(1)} %pad_maximum_fusion.1), channel_id=1, source_target_pairs={{0,1},{1,2},{2,3},{4,5},{5,6},{6,7},{8,9},{9,10},{10,11},{12,13},{... | collective-permute-start | bytes 56 | tf_op jit(solution)/shard_map/ppermute | solution.py:277
  54.4 6.4 %collective-permute-start.8 = (f32[4]{0:T(128)S(1)}, f32[4]{0:T(128)S(1)}, u32[]{:S(2)}, u32[]{:S(2)}) collective-permute-start(f32[4]{0:T(128)S(1)} %pad_maximum_fusion.1), channel_id=1, source_target_pairs={{0,4},{4,8},{8,12},{12,16},{16,20},{20,24},{24,28},{1,5},{5,9},{9,... | collective-permute-start | bytes 56 | tf_op jit(solution)/shard_map/ppermute | solution.py:277
  61.4 0.6 copy-start.2

commit v11 on v10

--- a/solution.py
+++ b/solution.py
@@ -304,7 +304,6 @@
     diagonal = [
         (j * n_row + i, (j + 1) * n_row + i + 1) for i in range(n_row - 1) for j in range(n_col - 1)
     ]
-    from_corner = lax.ppermute(corner, ("col", "row"), diagonal)
 
     left_col = jnp.maximum(col_index - 1, 0)
     upper_row = jnp.maximum(row_index - 1, 0)
@@ -351,7 +350,16 @@
     final = jnp.concatenate([own_gain, own_level])
     final_left = shifted(final, "col", n_col, 1)
     final_up = shifted(final, "row", n_row, 1)
-    final_corner = lax.ppermute(final, ("col", "row"), diagonal)
+    lanes = corner.shape[2]
+    packet = jnp.concatenate(
+        [
+            corner.astype(jnp.float32).reshape(planes * width, lanes),
+            jnp.pad(final[None, :], ((0, 7), (0, lanes - final.shape[0]))),
+        ]
+    )
+    packet = lax.ppermute(packet, ("col", "row"), diagonal)
+    final_corner = packet[planes * width, : final.shape[0]]
+    from_corner = packet[: planes * width].reshape(planes, width, lanes).astype(jnp.bfloat16)
     terms = jnp.concatenate([
         jnp.exp(own_gain), own_level,
         jnp.exp(final_left[:planes]), final_left[planes:],

time: 74.4 us -> 76 us (1.022)
  the two profiles are of different devices: /device:TPU:16 before, /device:TPU:17 now
where the time goes in v11:
time: 76 us; the launch traced here: 75.3 us
  starting transfers between devices  34.1 us (45%)
  Pallas kernels  16.6 us (22%)
  waiting for transfers between devices  15.9 us (21%)
  local copies, waits for them, and re-layouts  7.52 us (10%)
  between operations  0.81 us (1%)
    ppermute x10, starting transfers between devices, shifted(): return lax.ppermute(block, axis, route)  31.8 us
    pallas_call x1, Pallas kernels, blend(): pl.pallas_call(functools.partial(blend_kernel, n_row=n_row, n_col=n_col),...  11.6 us
    ppermute x10, waiting for transfers between devices, shifted(): return lax.ppermute(block, axis, route)  10.2 us
    ppermute x1, waiting for transfers between devices, local(): packet = lax.ppermute(packet, ('col', 'row'), diagonal)  5.69 us
    pallas_call x1, Pallas kernels, pair_stats(): pl.pallas_call(stats_kernel, grid_spec=grid_spec, out_shape=[jax.ShapeDty...  4.97 us
    ppermute x1, starting transfers between devices, local(): packet = lax.ppermute(packet, ('col', 'row'), diagonal)  2.26 us
    unnamed x4, local copies, waits for them, and re-layouts  1.59 us
  transfers between devices with their start and end apart: 11, of which 4 were waited for; matrix products, arithmetic and copies ran while one was open for 5% of the time, Pallas kernels for 0%

profile of v11, /device:TPU:17, one launch (start us, length us, event | category | flops | bytes accessed | tf_op | source)
XLA Modules:
  0.0 75.3 jit_solution(11543155608188935360)
XLA Ops:
  0.6 1.1 %slice.106 = bf16[2,1024,128]{2,1,0:T(8,128)(2,1)S(1)} slice(bf16[2,1024,1024]{2,1,0:T(8,128)(2,1)} %prev_ref.1), slice={[0:2], [0:1024], [896:1024]} | slice | bytes 1048576 | tf_op jit(solution)/shard_map/slice | solution.py:299
  1.7 3.1 %collective-permute-start = (bf16[2,1024,128]{2,1,0:T(8,128)(2,1)S(1)}, bf16[2,1024,128]{2,1,0:T(8,128)(2,1)S(1)}, u32[]{:S(2)}, u32[]{:S(2)}) collective-permute-start(bf16[2,1024,128]{2,1,0:T(8,128)(2,1)S(1)} %slice.106), channel_id=1, source_target_pairs={{0,4},{4,8},{8,12},{12,16},{16,20},{20,24},{24,28},{1,5},{5,9},{9,... | collective-permute-start | bytes 1572872 | tf_op jit(solution)/shard_map/ppermute | solution.py:277
  4.9 1.1 %slice.107 = bf16[2,128,1024]{2,1,0:T(8,128)(2,1)S(1)} slice(bf16[2,1024,1024]{2,1,0:T(8,128)(2,1)} %prev_ref.1), slice={[0:2], [896:1024], [0:1024]} | slice | bytes 1048576 | tf_op jit(solution)/shard_map/slice | solution.py:300
  6.0 4.0 %collective-permute-start.1 = (bf16[2,128,1024]{2,1,0:T(8,128)(2,1)S(1)}, bf16[2,128,1024]{2,1,0:T(8,128)(2,1)S(1)}, u32[]{:S(2)}, u32[]{:S(2)}) collective-permute-start(bf16[2,128,1024]{2,1,0:T(8,128)(2,1)S(1)} %slice.107), channel_id=1, source_target_pairs={{0,1},{1,2},{2,3},{4,5},{5,6},{6,7},{8,9},{9,10},{10,11},{12,13},{... | collective-permute-start | bytes 1572872 | tf_op jit(solution)/shard_map/ppermute | solution.py:277
  9.9 0.9 %slice.120 = bf16[2,128,128]{2,1,0:T(8,128)(2,1)S(1)} slice(bf16[2,1024,1024]{2,1,0:T(8,128)(2,1)} %prev_ref.1), slice={[0:2], [896:1024], [896:1024]} | slice | bytes 131072 | tf_op jit(solution)/shard_map/slice | solution.py:301
  10.8 6.5 %collective-permute-done.far_left_ref.lcur_ref.lprev_ref = bf16[2,1024,128]{2,1,0:T(8,128)(2,1)S(1)} collective-permute-done((bf16[2,1024,128]{2,1,0:T(8,128)(2,1)S(1)}, bf16[2,1024,128]{2,1,0:T(8,128)(2,1)S(1)}, u32[]{:S(2)}, u32[]{:S(2)}) %collective-permute-start) | collective-permute-done | bytes 524320 | tf_op jit(solution)/shard_map/ppermute | solution.py:277
  17.3 0.8 %copy-done = bf16[2,1024,128]{2,1,0:T(8,128)(2,1)} copy-done((bf16[2,1024,128]{2,1,0:T(8,128)(2,1)}, bf16[2,1024,128]{2,1,0:T(8,128)(2,1)S(1)}, u32[]{:S(2)}) %copy-start) | copy-done | bytes 524312
  18.1 0.8 %copy-done.1 = bf16[2,128,1024]{2,1,0:T(8,128)(2,1)} copy-done((bf16[2,128,1024]{2,1,0:T(8,128)(2,1)}, bf16[2,128,1024]{2,1,0:T(8,128)(2,1)S(1)}, u32[]{:S(2)}) %copy-start.1) | copy-done | bytes 524312
  18.9 5.0 %shard_map.59 = (f32[16,128]{1,0:T(8,128)}, f32[16,128]{1,0:T(8,128)}) custom-call(s32[2,4,8]{2,1,0:T(4,128)} %ext_ref.1, bf16[2,1024,128]{2,1,0:T(8,128)(2,1)} %copy-done, bf16[2,1024,1024]{2,1,0:T(8,128)(2,1)} %prev_ref.1, bf16[2,128,1024]{2,1,0:T(8,128)(2,1)} %copy-done.1, bf16[2,1024,1024]{2,1,0:T(8,128)(2,1)} %prev_ref.1), custom_call_target="tpu_custom_call" | custom-call | flops 6291456 | bytes 2097152 | tf_op jit(solution)/shard_map/pallas_call | solution.py:207
  23.9 2.1 %collective-permute-start.2 = (f32[16,128]{1,0:T(8,128)}, f32[16,128]{1,0:T(8,128)S(1)}, u32[]{:S(2)}, u32[]{:S(2)}) collective-permute-start(f32[16,128]{1,0:T(8,128)} %get-tuple-element.4), channel_id=1, source_target_pairs={{4,0},{8,4},{12,8},{16,12},{20,16},{24,20},{28,24},{5,1},{9,5},{13... | collective-permute-start | bytes 24584 | tf_op jit(solution)/shard_map/ppermute | solution.py:277
  26.0 1.1 %slice_reduce_fusion.10 = (f32[2]{0:T(128)S(1)}, f32[2]{0:T(128)S(1)}, f32[2]{0:T(128)S(1)}, f32[2]{0:T(128)S(1)}, f32[2]{0:T(128)S(1)}, /*index=5*/f32[2]{0:T(1...) fusion(f32[16,128]{1,0:T(8,128)} %get-tuple-element.5, f32[16,128]{1,0:T(8,128)} %get-tuple-element.4), kind=kLoop, calls=%fused_computation.14 | loop fusion | bytes 160 | tf_op jit(solution)/shard_map/unstack | solution.py:20
  27.2 3.7 %collective-permute-start.3 = (f32[16,128]{1,0:T(8,128)}, f32[16,128]{1,0:T(8,128)S(1)}, u32[]{:S(2)}, u32[]{:S(2)}) collective-permute-start(f32[16,128]{1,0:T(8,128)} %get-tuple-element.5), channel_id=1, source_target_pairs={{1,0},{2,1},{3,2},{5,4},{6,5},{7,6},{9,8},{10,9},{11,10},{13,12},{... | collective-permute-start | bytes 24584 | tf_op jit(solution)/shard_map/ppermute | solution.py:277
  31.1 2.4 %collective-permute-done.3 = f32[16,128]{1,0:T(8,128)S(1)} collective-permute-done((f32[16,128]{1,0:T(8,128)}, f32[16,128]{1,0:T(8,128)S(1)}, u32[]{:S(2)}, u32[]{:S(2)}) %collective-permute-start.3) | collective-permute-done | bytes 8224 | tf_op jit(solution)/shard_map/ppermute | solution.py:277
  33.8 1.9 %collective-permute-start.7 = (f32[4]{0:T(128)S(1)}, f32[4]{0:T(128)S(1)}, u32[]{:S(2)}, u32[]{:S(2)}) collective-permute-start(f32[4]{0:T(128)S(1)} %pad_maximum_fusion), channel_id=1, source_target_pairs={{0,1},{1,2},{2,3},{4,5},{5,6},{6,7},{8,9},{9,10},{10,11},{12,13},{... | collective-permute-start | bytes 56 | tf_op jit(solution)/shard_map/ppermute | solution.py:277
  35.8 3.1 %collective-permute-start.6 = (f32[4]{0:T(128)S(1)}, f32[4]{0:T(128)S(1)}, u32[]{:S(2)}, u32[]{:S(2)}) collective-permute-start(f32[4]{0:T(128)S(1)} %pad_maximum_fusion), channel_id=1, source_target_pairs={{0,4},{4,8},{8,12},{12,16},{16,20},{20,24},{24,28},{1,5},{5,9},{9,... | collective-permute-start | bytes 56 | tf_op jit(solution)/shard_map/ppermute | solution.py:277
  38.9 2.7 %collective-permute-start.5 = (f32[4]{0:T(128)S(1)}, f32[4]{0:T(128)S(1)}, u32[]{:S(2)}, u32[]{:S(2)}) collective-permute-start(f32[4]{0:T(128)S(1)} %pad_maximum_fusion), channel_id=1, source_target_pairs={{1,0},{2,1},{3,2},{5,4},{6,5},{7,6},{9,8},{10,9},{11,10},{13,12},{... | collective-permute-start | bytes 56 | tf_op jit(solution)/shard_map/ppermute | solution.py:277
  41.6 3.0 %collective-permute-start.4 = (f32[4]{0:T(128)S(1)}, f32[4]{0:T(128)S(1)}, u32[]{:S(2)}, u32[]{:S(2)}) collective-permute-start(f32[4]{0:T(128)S(1)} %pad_maximum_fusion), channel_id=1, source_target_pairs={{4,0},{8,4},{12,8},{16,12},{20,16},{24,20},{28,24},{5,1},{9,5},{13... | collective-permute-start | bytes 56 | tf_op jit(solution)/shard_map/ppermute | solution.py:277
  44.7 1.2 %collective-permute-done.4 = f32[4]{0:T(128)S(1)} collective-permute-done((f32[4]{0:T(128)S(1)}, f32[4]{0:T(128)S(1)}, u32[]{:S(2)}, u32[]{:S(2)}) %collective-permute-start.4) | collective-permute-done | bytes 48 | tf_op jit(solution)/shard_map/ppermute | solution.py:277
  46.2 4.0 %collective-permute-start.9 = (f32[4]{0:T(128)S(1)}, f32[4]{0:T(128)S(1)}, u32[]{:S(2)}, u32[]{:S(2)}) collective-permute-start(f32[4]{0:T(128)S(1)} %pad_maximum_fusion.1), channel_id=1, source_target_pairs={{0,1},{1,2},{2,3},{4,5},{5,6},{6,7},{8,9},{9,10},{10,11},{12,13},{... | collective-permute-start | bytes 56 | tf_op jit(solution)/shard_map/ppermute | solution.py:277
  50.2 4.0 %collective-permute-start.8 = (f32[4]{0:T(128)S(1)}, f32[4]{0:T(128)S(1)}, u32[]{:S(2)}, u32[]{:S(2)}) collective-permute-start(f32[4]{0:T(128)S(1)} %pad_maximum_fusion.1), channel_id=1, source_target_pairs={{0,4},{4,8},{8,12},{12,16},{16,20},{20,24},{24,28},{1,5},{5,9},{9,... | collective-permute-start | bytes 56 | tf_op jit(solution)/shard_map/ppermute | solution.py:277
  54.3 2.3 %collective-permute-start.10 = (f32[264,128]{1,0:T(8,128)S(1)}, f32[264,128]{1,0:T(8,128)S(1)}, u32[]{:S(2)}, u32[]{:S(2)}) collective-permute-start(f32[264,128]{1,0:T(8,128)S(1)} %select_maximum_fusion), channel_id=1, source_target_pairs={{0,5},{4,9},{8,13},{12,17},{16,21},{20,25},{24,29},{1,6},{5,10},{9... | collective-permute-start | bytes 405512 | tf_op jit(solution)/shard_map/ppermute | solution.py:360
  56.7 5.7 %collective-permute-done.10 = f32[264,128]{1,0:T(8,128)S(1)} collective-permute-done((f32[264,128]{1,0:T(8,128)S(1)}, f32[264,128]{1,0:T(8,128)S(1)}, u32[]{:S(2)}, u32[]{:S(2)}) %collective-permute-start.10) | collective-permute-done | bytes 135200 | tf_op jit(solution)/shard_map/ppermute | solution.py:360
  63.0 0.6 slice.191
  63.7 11.6 %shard_map.60 = (f32[2,1024,1024]{2,1,0:T(8,128)}, f32[1024,1024]{1,0:T(8,128)}) custom-call(s32[2,4,8]{2,1,0:T(4,128)} %off_ref.1, s32[2,4,8]{2,1,0:T(4,128)} %band_ref.1, f32[16]{0:T(128)} %concatenate.15.terms_ref, bf16[2,1024,1024]{2,1,0:T(8,128)(2,1)} %prev_ref.1, bf16[2,1024,1024]{2,1,0:T(8,128)(2,1)} %prev_ref.1, bf16[2,1024,128]{2,1,0:T(8,128)(2,1)} %copy-done, ...), custom_call_target="tpu_custom_call" | custom-call | flops 25165824 | bytes 22020096 | tf_op jit(solution)/shard_map/pallas_call | solution.py:256
  (24 shorter events, 1.6 us)
Async XLA Ops:
  1.7 15.6 %collective-permute-start = (bf16[2,1024,128]{2,1,0:T(8,128)(2,1)S(1)}, bf16[2,1024,128]{2,1,0:T(8,128)(2,1)S(1)}, u32[]{:S(2)}, u32[]{:S(2)}) collective-permute-start(bf16[2,1024,128]{2,1,0:T(8,128)(2,1)S(1)} %slice.106), channel_id=1, source_target_pairs={{0,4},{4,8},{8,12},{12,16},{16,20},{20,24},{24,28},{1,5},{5,9},{9,... | collective-permute-start | bytes 1572872 | tf_op jit(solution)/shard_map/ppermute | solution.py:277
  6.0 11.4 %collective-permute-start.1 = (bf16[2,128,1024]{2,1,0:T(8,128)(2,1)S(1)}, bf16[2,128,1024]{2,1,0:T(8,128)(2,1)S(1)}, u32[]{:S(2)}, u32[]{:S(2)}) collective-permute-start(bf16[2,128,1024]{2,1,0:T(8,128)(2,1)S(1)} %slice.107), channel_id=1, source_target_pairs={{0,1},{1,2},{2,3},{4,5},{5,6},{6,7},{8,9},{9,10},{10,11},{12,13},{... | collective-permute-start | bytes 1572872 | tf_op jit(solution)/shard_map/ppermute | solution.py:277
  17.3 0.8 %copy-start = (bf16[2,1024,128]{2,1,0:T(8,128)(2,1)}, bf16[2,1024,128]{2,1,0:T(8,128)(2,1)S(1)}, u32[]{:S(2)}) copy-start(bf16[2,1024,128]{2,1,0:T(8,128)(2,1)S(1)} %collective-permute-done.far_left_ref.lcur_ref.lprev_ref) | copy-start | bytes 1572868
  18.1 0.8 %copy-start.1 = (bf16[2,128,1024]{2,1,0:T(8,128)(2,1)}, bf16[2,128,1024]{2,1,0:T(8,128)(2,1)S(1)}, u32[]{:S(2)}) copy-start(bf16[2,128,1024]{2,1,0:T(8,128)(2,1)S(1)} %collective-permute-done.1.far_up_ref.up_ref) | copy-start | bytes 1572868
  23.9 7.0 %collective-permute-start.2 = (f32[16,128]{1,0:T(8,128)}, f32[16,128]{1,0:T(8,128)S(1)}, u32[]{:S(2)}, u32[]{:S(2)}) collective-permute-start(f32[16,128]{1,0:T(8,128)} %get-tuple-element.4), channel_id=1, source_target_pairs={{4,0},{8,4},{12,8},{16,12},{20,16},{24,20},{28,24},{5,1},{9,5},{13... | collective-permute-start | bytes 24584 | tf_op jit(solution)/shard_map/ppermute | solution.py:277
  27.2 6.4 %collective-permute-start.3 = (f32[16,128]{1,0:T(8,128)}, f32[16,128]{1,0:T(8,128)S(1)}, u32[]{:S(2)}, u32[]{:S(2)}) collective-permute-start(f32[16,128]{1,0:T(8,128)} %get-tuple-element.5), channel_id=1, source_target_pairs={{1,0},{2,1},{3,2},{5,4},{6,5},{7,6},{9,8},{10,9},{11,10},{13,12},{... | collective-permute-start | bytes 24584 | tf_op jit(solution)/shard_map/ppermute | solution.py:277
  33.8 10.8 %collective-permute-start.7 = (f32[4]{0:T(128)S(1)}, f32[4]{0:T(128)S(1)}, u32[]{:S(2)}, u32[]{:S(2)}) collective-permute-start(f32[4]{0:T(128)S(1)} %pad_maximum_fusion), channel_id=1, source_target_pairs={{0,1},{1,2},{2,3},{4,5},{5,6},{6,7},{8,9},{9,10},{10,11},{12,13},{... | collective-permute-start | bytes 56 | tf_op jit(solution)/shard_map/ppermute | solution.py:277
  35.8 8.9 %collective-permute-start.6 = (f32[4]{0:T(128)S(1)}, f32[4]{0:T(128)S(1)}, u32[]{:S(2)}, u32[]{:S(2)}) collective-permute-start(f32[4]{0:T(128)S(1)} %pad_maximum_fusion), channel_id=1, source_target_pairs={{0,4},{4,8},{8,12},{12,16},{16,20},{20,24},{24,28},{1,5},{5,9},{9,... | collective-permute-start | bytes 56 | tf_op jit(solution)/shard_map/ppermute | solution.py:277
  38.9 5.7 %collective-permute-start.5 = (f32[4]{0:T(128)S(1)}, f32[4]{0:T(128)S(1)}, u32[]{:S(2)}, u32[]{:S(2)}) collective-permute-start(f32[4]{0:T(128)S(1)} %pad_maximum_fusion), channel_id=1, source_target_pairs={{1,0},{2,1},{3,2},{5,4},{6,5},{7,6},{9,8},{10,9},{11,10},{13,12},{... | collective-permute-start | bytes 56 | tf_op jit(solution)/shard_map/ppermute | solution.py:277
  41.6 4.3 %collective-permute-start.4 = (f32[4]{0:T(128)S(1)}, f32[4]{0:T(128)S(1)}, u32[]{:S(2)}, u32[]{:S(2)}) collective-permute-start(f32[4]{0:T(128)S(1)} %pad_maximum_fusion), channel_id=1, source_target_pairs={{4,0},{8,4},{12,8},{16,12},{20,16},{24,20},{28,24},{5,1},{9,5},{13... | collective-permute-start | bytes 56 | tf_op jit(solution)/shard_map/ppermute | solution.py:277
  46.2 10.4 %collective-permute-start.9 = (f32[4]{0:T(128)S(1)}, f32[4]{0:T(128)S(1)}, u32[]{:S(2)}, u32[]{:S(2)}) collective-permute-start(f32[4]{0:T(128)S(1)} %pad_maximum_fusion.1), channel_id=1, source_target_pairs={{0,1},{1,2},{2,3},{4,5},{5,6},{6,7},{8,9},{9,10},{10,11},{12,13},{... | collective-permute-start | bytes 56 | tf_op jit(solution)/shard_map/ppermute | solution.py:277
  50.2 6.4 %collective-permute-start.8 = (f32[4]{0:T(128)S(1)}, f32[4]{0:T(128)S(1)}, u32[]{:S(2)}, u32[]{:S(2)}) collective-permute-start(f32[4]{0:T(128)S(1)} %pad_maximum_fusion.1), channel_id=1, source_target_pairs={{0,4},{4,8},{8,12},{12,16},{16,20},{20,24},{24,28},{1,5},{5,9},{9,... | collective-permute-start | bytes 56 | tf_op jit(solution)/shard_map/ppermute | solution.py:277
  54.3 8.1 %collective-permute-start.10 = (f32[264,128]{1,0:T(8,128)S(1)}, f32[264,128]{1,0:T(8,128)S(1)}, u32[]{:S(2)}, u32[]{:S(2)}) collective-permute-start(f32[264,128]{1,0:T(8,128)S(1)} %select_maximum_fusion), channel_id=1, source_target_pairs={{0,5},{4,9},{8,13},{12,17},{16,21},{20,25},{24,29},{1,6},{5,10},{9... | collective-permute-start | bytes 405512 | tf_op jit(solution)/shard_map/ppermute | solution.py:360

commit v12 on v10

--- a/solution.py
+++ b/solution.py
@@ -52,13 +52,12 @@
         emit(k, block)
 
 
-def blend_kernel(off_ref, band_ref, terms_ref, cur_ref, prev_ref, lcur_ref, lprev_ref,
-                 up_ref, corner_ref, out_ref, w_ref, *, n_row, n_col):
+def shift_kernel(off_ref, band_ref, cur_ref, prev_ref, moved_ref, w_ref, *, n_row, n_col):
     f32 = jnp.float32
     bf16 = jnp.bfloat16
     step = pl.program_id(0)
     planes, rows, tile_px = cur_ref.shape
-    width = lcur_ref.shape[2]
+    width = STRIP
     cells = n_row * n_col
     r = lax.axis_index("row")
     c = lax.axis_index("col")
@@ -101,18 +100,12 @@
     for p in range(planes):
         src = jnp.concatenate([prev_ref[p, rows - reach :], cur_ref[p]], axis=0)
         shifted_rows = jnp.dot(down_own, src, preferred_element_type=f32)
-        scale, level = gain(0, p)
-
-        def emit(k, block, p=p, scale=scale, level=level):
+
+        def emit(k, block, p=p):
             span = slice(k * width, (k + 1) * width)
-            out_ref[p, :, span] = (scale * block + level) * w_own[:, span]
+            moved_ref[p, :, span] = block.astype(moved_ref.dtype)
 
         move_lanes(shifted_rows, left, tile_px, emit)
-        lsrc = jnp.concatenate([lprev_ref[p, rows - reach :], lcur_ref[p]], axis=0)
-        lrows = jnp.dot(down_left, lsrc, preferred_element_type=f32)
-        window = pltpu.roll(lrows, left_l, 1)
-        scale, level = gain(1, p)
-        out_ref[p, :, :width] += (scale * window + level) * w_left
 
     @pl.when(step == 0)
     def _():
@@ -129,6 +122,73 @@
         )
         w_ref[:width, :] += w_up
         w_ref[:width, :width] += w_corner
+
+
+def blend_kernel(off_ref, band_ref, terms_ref, moved_ref, lcur_ref, lprev_ref,
+                 up_ref, corner_ref, out_ref, *, n_row, n_col):
+    f32 = jnp.float32
+    bf16 = jnp.bfloat16
+    step = pl.program_id(0)
+    planes, rows, tile_px = moved_ref.shape
+    width = lcur_ref.shape[2]
+    cells = n_row * n_col
+    r = lax.axis_index("row")
+    c = lax.axis_index("col")
+    lc = jnp.maximum(c - 1, 0)
+    ur = jnp.maximum(r - 1, 0)
+    has_left = c > 0
+    has_up = r > 0
+
+    def table(ref, k, rr, cc):
+        return ref[k, rr, cc]
+
+    def fade(ids):
+        return (jnp.minimum(ids, tile_px - 1 - ids) + 1).astype(f32) / (tile_px / 2.0)
+
+    def band_rows(ids, rr, cc, extra):
+        live = (ids >= table(band_ref, 0, rr, cc) * BLOCK) & (ids < table(band_ref, 1, rr, cc) * BLOCK)
+        live = live & (ids >= 0) & (ids < tile_px) & extra
+        return jnp.where(live, fade(ids), 0.0)
+
+    def gain(k, p):
+        return terms_ref[k * 2 * planes + p], terms_ref[k * 2 * planes + planes + p]
+
+    t = lax.broadcasted_iota(jnp.int32, (rows, 1), 0)
+    x = lax.broadcasted_iota(jnp.int32, (1, tile_px), 1)
+    xs = lax.broadcasted_iota(jnp.int32, (1, width), 1)
+    y = step * rows + t
+    top = table(off_ref, 0, r, c)
+    left = table(off_ref, 1, r, c)
+    top_l = table(off_ref, 0, r, lc)
+    left_l = table(off_ref, 1, r, lc)
+    j = x - left
+    w_own = band_rows(y - top, r, c, True) * jnp.where(j >= 0, fade(j), 0.0)
+    j_l = xs + tile_px - left_l
+    w_left = band_rows(y - top_l, r, lc, has_left) * jnp.where(j_l < tile_px, fade(j_l), 0.0)
+    reach = SPILL
+    down_left = pick(rows, reach + rows, reach - top_l)
+    for p in range(planes):
+        scale, level = gain(0, p)
+        out_ref[p] = (scale * moved_ref[p].astype(f32) + level) * w_own
+        lsrc = jnp.concatenate([lprev_ref[p, rows - reach :], lcur_ref[p]], axis=0)
+        lrows = jnp.dot(down_left, lsrc, preferred_element_type=f32)
+        window = pltpu.roll(lrows, left_l, 1)
+        scale, level = gain(1, p)
+        out_ref[p, :, :width] += (scale * window + level) * w_left
+
+    @pl.when(step == 0)
+    def _():
+        te = lax.broadcasted_iota(jnp.int32, (width, 1), 0)
+        top_u = table(off_ref, 0, ur, c)
+        left_u = table(off_ref, 1, ur, c)
+        top_c = table(off_ref, 0, ur, lc)
+        left_c = table(off_ref, 1, ur, lc)
+        j_u = x - left_u
+        w_up = band_rows(te + tile_px - top_u, ur, c, has_up) * jnp.where(j_u >= 0, fade(j_u), 0.0)
+        j_c = xs + tile_px - left_c
+        w_corner = band_rows(te + tile_px - top_c, ur, lc, has_up & has_left) * jnp.where(
+            j_c < tile_px, fade(j_c), 0.0
+        )
         down_up = pick(width, width, width - top_u)
         down_corner = pick(width, width, width - top_c)
         for p in range(planes):
@@ -219,11 +279,47 @@
     return block[: 5 * planes, 0].reshape(5, planes)
 
 
-def blend(offsets, bands, terms, tiles, from_left, from_up, from_corner, n_row, n_col):
+def shift_tile(offsets, bands, tiles, n_row, n_col):
     planes, tile_px, _ = tiles.shape
+    rows = min(ROWS, tile_px)
+
+    def cur(b, *_):
+        return (0, b, 0)
+
+    def prev(b, *_):
+        return (0, jnp.maximum(b - 1, 0), 0)
+
+    grid_spec = pltpu.PrefetchScalarGridSpec(
+        num_scalar_prefetch=2,
+        grid=(tile_px // rows,),
+        in_specs=[
+            pl.BlockSpec((planes, rows, tile_px), cur),
+            pl.BlockSpec((planes, rows, tile_px), prev),
+        ],
+        out_specs=[
+            pl.BlockSpec((planes, rows, tile_px), cur),
+            pl.BlockSpec((rows, tile_px), lambda b, *_: (b, 0)),
+        ],
+    )
+    return pl.pallas_call(
+        functools.partial(shift_kernel, n_row=n_row, n_col=n_col),
+        grid_spec=grid_spec,
+        out_shape=[
+            jax.ShapeDtypeStruct((planes, tile_px, tile_px), tiles.dtype),
+            jax.ShapeDtypeStruct((tile_px, tile_px), jnp.float32),
+        ],
+        compiler_params=pltpu.CompilerParams(dimension_semantics=("arbitrary",)),
+        cost_estimate=pl.CostEstimate(
+            flops=2 * planes * tile_px * tile_px * 2 * rows, transcendentals=0,
+            bytes_accessed=2 * 2 * planes * tile_px * tile_px + 4 * tile_px * tile_px,
+        ),
+    )(offsets, bands, tiles, tiles)
+
+
+def blend(offsets, bands, terms, moved, from_left, from_up, from_corner, n_row, n_col):
+    planes, tile_px, _ = moved.shape
     width = from_left.shape[2]
     rows = min(ROWS, tile_px)
-    steps = tile_px // rows
 
     def cur(b, *_):
         return (0, b, 0)
@@ -236,37 +332,27 @@
 
     grid_spec = pltpu.PrefetchScalarGridSpec(
         num_scalar_prefetch=2,
-        grid=(steps,),
+        grid=(tile_px // rows,),
         in_specs=[
             pl.BlockSpec(memory_space=pltpu.SMEM),
             pl.BlockSpec((planes, rows, tile_px), cur),
-            pl.BlockSpec((planes, rows, tile_px), prev),
             pl.BlockSpec((planes, rows, width), cur),
             pl.BlockSpec((planes, rows, width), prev),
             pl.BlockSpec((planes, width, tile_px), fixed),
             pl.BlockSpec((planes, width, width), fixed),
         ],
-        out_specs=[
-            pl.BlockSpec((planes, rows, tile_px), cur),
-            pl.BlockSpec((rows, tile_px), lambda b, *_: (b, 0)),
-        ],
-    )
-    out_bytes = 4 * (planes + 1) * tile_px * tile_px
-    in_bytes = 2 * 2 * planes * tile_px * (tile_px + width)
+        out_specs=pl.BlockSpec((planes, rows, tile_px), cur),
+    )
     return pl.pallas_call(
         functools.partial(blend_kernel, n_row=n_row, n_col=n_col),
         grid_spec=grid_spec,
-        out_shape=[
-            jax.ShapeDtypeStruct((planes, tile_px, tile_px), jnp.float32),
-            jax.ShapeDtypeStruct((tile_px, tile_px), jnp.float32),
-        ],
+        out_shape=jax.ShapeDtypeStruct((planes, tile_px, tile_px), jnp.float32),
         compiler_params=pltpu.CompilerParams(dimension_semantics=("arbitrary",)),
         cost_estimate=pl.CostEstimate(
-            flops=12 * planes * tile_px * tile_px, transcendentals=0,
-            bytes_accessed=out_bytes + in_bytes,
+            flops=4 * planes * tile_px * tile_px, transcendentals=0,
+            bytes_accessed=(2 + 4) * planes * tile_px * tile_px,
         ),
-    )(offsets, bands, terms, tiles, tiles, from_left, from_left,
-      from_up, from_corner)
+    )(offsets, bands, terms, moved, from_left, from_left, from_up, from_corner)
 
 
 def shifted(block, axis, count, step):
@@ -309,6 +395,7 @@
     left_col = jnp.maximum(col_index - 1, 0)
     upper_row = jnp.maximum(row_index - 1, 0)
     f32 = jnp.float32
+    moved, weight = shift_tile(offsets, bands, tiles, n_row, n_col)
     left_block, up_block = pair_stats(extents, from_left, from_up, tiles)
     right_block = shifted(left_block, "col", n_col, -1)
     down_block = shifted(up_block, "row", n_row, -1)
@@ -358,7 +445,8 @@
         jnp.exp(final_up[:planes]), final_up[planes:],
         jnp.exp(final_corner[:planes]), final_corner[planes:],
     ])
-    return blend(offsets, bands, terms, tiles, from_left, from_up, from_corner, n_row, n_col)
+    blended = blend(offsets, bands, terms, moved, from_left, from_up, from_corner, n_row, n_col)
+    return blended, weight
 
 
 def solution(mesh):

time: 74.4 us -> 76.8 us (1.032)
  Pallas kernels: 16.6 us -> 23.4 us
  waiting for transfers between devices: 12.8 us -> 7.71 us
    pallas_call x0 -> x1, Pallas kernels: none -> 9.78 us  [shift_tile(): pl.pallas_call(functools.partial(shift_kernel, n_row=n_row, n_col=n_col),...]
    ppermute x10, waiting for transfers between devices: 12.8 us -> 7.71 us  [shifted(): return lax.ppermute(block, axis, route)]
    pallas_call x1, Pallas kernels: 11.6 us -> 8.71 us  [blend(): pl.pallas_call(functools.partial(blend_kernel, n_row=n_row, n_col=n_col),...]
  transfers between devices with their start and end apart: 12 -> 12, of which waited for: 5 -> 3; matrix products, arithmetic and copies ran while one was open for 6% -> 6% of each run, Pallas kernels for 7% -> 19%
where the time goes in v12:
time: 76.8 us; the launch traced here: 75.9 us
  starting transfers between devices  36.1 us (47%)
  Pallas kernels  23.4 us (30%)
  waiting for transfers between devices  7.71 us (10%)
  local copies, waits for them, and re-layouts  7.53 us (10%)
  between operations  0.82 us (1%)
    ppermute x10, starting transfers between devices, shifted(): return lax.ppermute(block, axis, route)  26.7 us
    pallas_call x1, Pallas kernels, shift_tile(): pl.pallas_call(functools.partial(shift_kernel, n_row=n_row, n_col=n_col),...  9.78 us
    pallas_call x1, Pallas kernels, blend(): pl.pallas_call(functools.partial(blend_kernel, n_row=n_row, n_col=n_col),...  8.71 us
    ppermute x10, waiting for transfers between devices, shifted(): return lax.ppermute(block, axis, route)  7.71 us
    ppermute x1, starting transfers between devices, local(): from_corner = lax.ppermute(corner, ('col', 'row'), diagonal)  5.04 us
    pallas_call x1, Pallas kernels, pair_stats(): pl.pallas_call(stats_kernel, grid_spec=grid_spec, out_shape=[jax.ShapeDty...  4.96 us
    ppermute x1, starting transfers between devices, local(): final_corner = lax.ppermute(final, ('col', 'row'), diagonal)  4.39 us
    unnamed x6, local copies, waits for them, and re-layouts  2.22 us
  transfers between devices with their start and end apart: 12, of which 3 were waited for; matrix products, arithmetic and copies ran while one was open for 6% of the time, Pallas kernels for 19%

profile of v12, /device:TPU:16, one launch (start us, length us, event | category | flops | bytes accessed | tf_op | source)
XLA Modules:
  0.0 75.9 jit_solution(6515146331310503071)
XLA Ops:
  0.6 1.1 %slice.95 = bf16[2,1024,128]{2,1,0:T(8,128)(2,1)S(1)} slice(bf16[2,1024,1024]{2,1,0:T(8,128)(2,1)} %prev_ref.1), slice={[0:2], [0:1024], [896:1024]} | slice | bytes 1048576 | tf_op jit(solution)/shard_map/slice | solution.py:385
  1.7 3.4 %collective-permute-start = (bf16[2,1024,128]{2,1,0:T(8,128)(2,1)S(1)}, bf16[2,1024,128]{2,1,0:T(8,128)(2,1)S(1)}, u32[]{:S(2)}, u32[]{:S(2)}) collective-permute-start(bf16[2,1024,128]{2,1,0:T(8,128)(2,1)S(1)} %slice.95), channel_id=1, source_target_pairs={{0,4},{4,8},{8,12},{12,16},{16,20},{20,24},{24,28},{1,5},{5,9},{9,... | collective-permute-start | bytes 1572872 | tf_op jit(solution)/shard_map/ppermute | solution.py:363
  5.1 1.1 %slice.96 = bf16[2,128,1024]{2,1,0:T(8,128)(2,1)S(1)} slice(bf16[2,1024,1024]{2,1,0:T(8,128)(2,1)} %prev_ref.1), slice={[0:2], [896:1024], [0:1024]} | slice | bytes 1048576 | tf_op jit(solution)/shard_map/slice | solution.py:386
  6.2 1.5 %collective-permute-start.1 = (bf16[2,128,1024]{2,1,0:T(8,128)(2,1)S(1)}, bf16[2,128,1024]{2,1,0:T(8,128)(2,1)S(1)}, u32[]{:S(2)}, u32[]{:S(2)}) collective-permute-start(bf16[2,128,1024]{2,1,0:T(8,128)(2,1)S(1)} %slice.96), channel_id=1, source_target_pairs={{0,1},{1,2},{2,3},{4,5},{5,6},{6,7},{8,9},{9,10},{10,11},{12,13},{... | collective-permute-start | bytes 1572872 | tf_op jit(solution)/shard_map/ppermute | solution.py:363
  7.7 0.9 %slice.111 = bf16[2,128,128]{2,1,0:T(8,128)(2,1)S(1)} slice(bf16[2,1024,1024]{2,1,0:T(8,128)(2,1)} %prev_ref.1), slice={[0:2], [896:1024], [896:1024]} | slice | bytes 131072 | tf_op jit(solution)/shard_map/slice | solution.py:387
  8.6 5.0 %collective-permute-start.11 = (bf16[2,128,128]{2,1,0:T(8,128)(2,1)S(1)}, bf16[2,128,128]{2,1,0:T(8,128)(2,1)S(1)}, u32[]{:S(2)}, u32[]{:S(2)}) collective-permute-start(bf16[2,128,128]{2,1,0:T(8,128)(2,1)S(1)} %slice.111), channel_id=1, source_target_pairs={{0,5},{4,9},{8,13},{12,17},{16,21},{20,25},{24,29},{1,6},{5,10},{9... | collective-permute-start | bytes 196616 | tf_op jit(solution)/shard_map/ppermute | solution.py:393
  13.7 9.8 %shard_map.60 = (bf16[2,1024,1024]{2,1,0:T(8,128)(2,1)}, f32[1024,1024]{1,0:T(8,128)}) custom-call(s32[2,4,8]{2,1,0:T(4,128)} %off_ref.3, s32[2,4,8]{2,1,0:T(4,128)} %band_ref.3, bf16[2,1024,1024]{2,1,0:T(8,128)(2,1)} %prev_ref.1, bf16[2,1024,1024]{2,1,0:T(8,128)(2,1)} %prev_ref.1), custom_call_target="tpu_custom_call" | custom-call | flops 2147483648 | bytes 12582912 | tf_op jit(solution)/shard_map/pallas_call | solution.py:304
  23.5 0.8 %copy-done = bf16[2,1024,128]{2,1,0:T(8,128)(2,1)} copy-done((bf16[2,1024,128]{2,1,0:T(8,128)(2,1)}, bf16[2,1024,128]{2,1,0:T(8,128)(2,1)S(1)}, u32[]{:S(2)}) %copy-start) | copy-done | bytes 524312
  24.2 0.8 %copy-done.1 = bf16[2,128,1024]{2,1,0:T(8,128)(2,1)} copy-done((bf16[2,128,1024]{2,1,0:T(8,128)(2,1)}, bf16[2,128,1024]{2,1,0:T(8,128)(2,1)S(1)}, u32[]{:S(2)}) %copy-start.1) | copy-done | bytes 524312
  25.1 5.0 %shard_map.59 = (f32[16,128]{1,0:T(8,128)}, f32[16,128]{1,0:T(8,128)}) custom-call(s32[2,4,8]{2,1,0:T(4,128)} %ext_ref.1, bf16[2,1024,128]{2,1,0:T(8,128)(2,1)} %copy-done, bf16[2,1024,1024]{2,1,0:T(8,128)(2,1)} %prev_ref.1, bf16[2,128,1024]{2,1,0:T(8,128)(2,1)} %copy-done.1, bf16[2,1024,1024]{2,1,0:T(8,128)(2,1)} %prev_ref.1), custom_call_target="tpu_custom_call" | custom-call | flops 6291456 | bytes 2097152 | tf_op jit(solution)/shard_map/pallas_call | solution.py:267
  30.0 3.3 %collective-permute-start.2 = (f32[16,128]{1,0:T(8,128)}, f32[16,128]{1,0:T(8,128)S(1)}, u32[]{:S(2)}, u32[]{:S(2)}) collective-permute-start(f32[16,128]{1,0:T(8,128)} %get-tuple-element.6), channel_id=1, source_target_pairs={{4,0},{8,4},{12,8},{16,12},{20,16},{24,20},{28,24},{5,1},{9,5},{13... | collective-permute-start | bytes 24584 | tf_op jit(solution)/shard_map/ppermute | solution.py:363
  33.3 1.1 %slice_reduce_fusion.10 = (f32[2]{0:T(128)S(1)}, f32[2]{0:T(128)S(1)}, f32[2]{0:T(128)S(1)}, f32[2]{0:T(128)S(1)}, f32[2]{0:T(128)S(1)}, /*index=5*/f32[2]{0:T(1...) fusion(f32[16,128]{1,0:T(8,128)} %get-tuple-element.7, f32[16,128]{1,0:T(8,128)} %get-tuple-element.6), kind=kLoop, calls=%fused_computation.10 | loop fusion | bytes 160 | tf_op jit(solution)/shard_map/unstack | solution.py:20
  34.4 1.3 %collective-permute-start.3 = (f32[16,128]{1,0:T(8,128)}, f32[16,128]{1,0:T(8,128)S(1)}, u32[]{:S(2)}, u32[]{:S(2)}) collective-permute-start(f32[16,128]{1,0:T(8,128)} %get-tuple-element.7), channel_id=1, source_target_pairs={{1,0},{2,1},{3,2},{5,4},{6,5},{7,6},{9,8},{10,9},{11,10},{13,12},{... | collective-permute-start | bytes 24584 | tf_op jit(solution)/shard_map/ppermute | solution.py:363
  35.9 1.8 %collective-permute-done.3 = f32[16,128]{1,0:T(8,128)S(1)} collective-permute-done((f32[16,128]{1,0:T(8,128)}, f32[16,128]{1,0:T(8,128)S(1)}, u32[]{:S(2)}, u32[]{:S(2)}) %collective-permute-start.3) | collective-permute-done | bytes 8224 | tf_op jit(solution)/shard_map/ppermute | solution.py:363
  38.0 3.4 %collective-permute-start.7 = (f32[4]{0:T(128)S(1)}, f32[4]{0:T(128)S(1)}, u32[]{:S(2)}, u32[]{:S(2)}) collective-permute-start(f32[4]{0:T(128)S(1)} %pad_maximum_fusion), channel_id=1, source_target_pairs={{0,1},{1,2},{2,3},{4,5},{5,6},{6,7},{8,9},{9,10},{10,11},{12,13},{... | collective-permute-start | bytes 56 | tf_op jit(solution)/shard_map/ppermute | solution.py:363
  41.4 2.5 %collective-permute-start.6 = (f32[4]{0:T(128)S(1)}, f32[4]{0:T(128)S(1)}, u32[]{:S(2)}, u32[]{:S(2)}) collective-permute-start(f32[4]{0:T(128)S(1)} %pad_maximum_fusion), channel_id=1, source_target_pairs={{0,4},{4,8},{8,12},{12,16},{16,20},{20,24},{24,28},{1,5},{5,9},{9,... | collective-permute-start | bytes 56 | tf_op jit(solution)/shard_map/ppermute | solution.py:363
  43.9 1.3 %collective-permute-start.5 = (f32[4]{0:T(128)S(1)}, f32[4]{0:T(128)S(1)}, u32[]{:S(2)}, u32[]{:S(2)}) collective-permute-start(f32[4]{0:T(128)S(1)} %pad_maximum_fusion), channel_id=1, source_target_pairs={{1,0},{2,1},{3,2},{5,4},{6,5},{7,6},{9,8},{10,9},{11,10},{13,12},{... | collective-permute-start | bytes 56 | tf_op jit(solution)/shard_map/ppermute | solution.py:363
  45.2 4.2 %collective-permute-start.4 = (f32[4]{0:T(128)S(1)}, f32[4]{0:T(128)S(1)}, u32[]{:S(2)}, u32[]{:S(2)}) collective-permute-start(f32[4]{0:T(128)S(1)} %pad_maximum_fusion), channel_id=1, source_target_pairs={{4,0},{8,4},{12,8},{16,12},{20,16},{24,20},{28,24},{5,1},{9,5},{13... | collective-permute-start | bytes 56 | tf_op jit(solution)/shard_map/ppermute | solution.py:363
  49.5 1.6 %collective-permute-done.4 = f32[4]{0:T(128)S(1)} collective-permute-done((f32[4]{0:T(128)S(1)}, f32[4]{0:T(128)S(1)}, u32[]{:S(2)}, u32[]{:S(2)}) %collective-permute-start.4) | collective-permute-done | bytes 48 | tf_op jit(solution)/shard_map/ppermute | solution.py:363
  51.3 4.4 %collective-permute-start.10 = (f32[4]{0:T(128)S(1)}, f32[4]{0:T(128)S(1)}, u32[]{:S(2)}, u32[]{:S(2)}) collective-permute-start(f32[4]{0:T(128)S(1)} %pad_maximum_fusion.1), channel_id=1, source_target_pairs={{0,5},{4,9},{8,13},{12,17},{16,21},{20,25},{24,29},{1,6},{5,10},{9... | collective-permute-start | bytes 56 | tf_op jit(solution)/shard_map/ppermute | solution.py:441
  55.7 3.9 %collective-permute-start.9 = (f32[4]{0:T(128)S(1)}, f32[4]{0:T(128)S(1)}, u32[]{:S(2)}, u32[]{:S(2)}) collective-permute-start(f32[4]{0:T(128)S(1)} %pad_maximum_fusion.1), channel_id=1, source_target_pairs={{0,1},{1,2},{2,3},{4,5},{5,6},{6,7},{8,9},{9,10},{10,11},{12,13},{... | collective-permute-start | bytes 56 | tf_op jit(solution)/shard_map/ppermute | solution.py:363
  59.6 1.9 %collective-permute-start.8 = (f32[4]{0:T(128)S(1)}, f32[4]{0:T(128)S(1)}, u32[]{:S(2)}, u32[]{:S(2)}) collective-permute-start(f32[4]{0:T(128)S(1)} %pad_maximum_fusion.1), channel_id=1, source_target_pairs={{0,4},{4,8},{8,12},{12,16},{16,20},{20,24},{24,28},{1,5},{5,9},{9,... | collective-permute-start | bytes 56 | tf_op jit(solution)/shard_map/ppermute | solution.py:363
  61.6 4.3 %collective-permute-done.8 = f32[4]{0:T(128)S(1)} collective-permute-done((f32[4]{0:T(128)S(1)}, f32[4]{0:T(128)S(1)}, u32[]{:S(2)}, u32[]{:S(2)}) %collective-permute-start.8) | collective-permute-done | bytes 48 | tf_op jit(solution)/shard_map/ppermute | solution.py:363
  67.2 8.7 %shard_map.61 = f32[2,1024,1024]{2,1,0:T(8,128)} custom-call(s32[2,4,8]{2,1,0:T(4,128)} %off_ref.3, s32[2,4,8]{2,1,0:T(4,128)} %band_ref.3, f32[16]{0:T(128)} %concatenate.11.terms_ref, bf16[2,1024,1024]{2,1,0:T(8,128)(2,1)} %get-tuple-element.8.moved_ref, bf16[2,1024,128]{2,1,0:T(8,128)(2,1)} %copy-done, bf16[2,1024,128]{2,1,0:T(8,128)(2,1)} %copy-done, ...), custom_call_target="tpu_custom_call" | custom-call | flops 8388608 | bytes 12582912 | tf_op jit(solution)/shard_map/pallas_call | solution.py:346
  (25 shorter events, 2.2 us)
Async XLA Ops:
  1.7 21.7 %collective-permute-start = (bf16[2,1024,128]{2,1,0:T(8,128)(2,1)S(1)}, bf16[2,1024,128]{2,1,0:T(8,128)(2,1)S(1)}, u32[]{:S(2)}, u32[]{:S(2)}) collective-permute-start(bf16[2,1024,128]{2,1,0:T(8,128)(2,1)S(1)} %slice.95), channel_id=1, source_target_pairs={{0,4},{4,8},{8,12},{12,16},{16,20},{20,24},{24,28},{1,5},{5,9},{9,... | collective-permute-start | bytes 1572872 | tf_op jit(solution)/shard_map/ppermute | solution.py:363
  6.2 17.2 %collective-permute-start.1 = (bf16[2,128,1024]{2,1,0:T(8,128)(2,1)S(1)}, bf16[2,128,1024]{2,1,0:T(8,128)(2,1)S(1)}, u32[]{:S(2)}, u32[]{:S(2)}) collective-permute-start(bf16[2,128,1024]{2,1,0:T(8,128)(2,1)S(1)} %slice.96), channel_id=1, source_target_pairs={{0,1},{1,2},{2,3},{4,5},{5,6},{6,7},{8,9},{9,10},{10,11},{12,13},{... | collective-permute-start | bytes 1572872 | tf_op jit(solution)/shard_map/ppermute | solution.py:363
  8.6 58.0 %collective-permute-start.11 = (bf16[2,128,128]{2,1,0:T(8,128)(2,1)S(1)}, bf16[2,128,128]{2,1,0:T(8,128)(2,1)S(1)}, u32[]{:S(2)}, u32[]{:S(2)}) collective-permute-start(bf16[2,128,128]{2,1,0:T(8,128)(2,1)S(1)} %slice.111), channel_id=1, source_target_pairs={{0,5},{4,9},{8,13},{12,17},{16,21},{20,25},{24,29},{1,6},{5,10},{9... | collective-permute-start | bytes 196616 | tf_op jit(solution)/shard_map/ppermute | solution.py:393
  23.4 0.8 %copy-start = (bf16[2,1024,128]{2,1,0:T(8,128)(2,1)}, bf16[2,1024,128]{2,1,0:T(8,128)(2,1)S(1)}, u32[]{:S(2)}) copy-start(bf16[2,1024,128]{2,1,0:T(8,128)(2,1)S(1)} %collective-permute-done.far_left_ref.lcur_ref.lprev_ref) | copy-start | bytes 1572868
  24.2 0.8 %copy-start.1 = (bf16[2,128,1024]{2,1,0:T(8,128)(2,1)}, bf16[2,128,1024]{2,1,0:T(8,128)(2,1)S(1)}, u32[]{:S(2)}) copy-start(bf16[2,128,1024]{2,1,0:T(8,128)(2,1)S(1)} %collective-permute-done.1.far_up_ref.up_ref) | copy-start | bytes 1572868
  30.0 5.7 %collective-permute-start.2 = (f32[16,128]{1,0:T(8,128)}, f32[16,128]{1,0:T(8,128)S(1)}, u32[]{:S(2)}, u32[]{:S(2)}) collective-permute-start(f32[16,128]{1,0:T(8,128)} %get-tuple-element.6), channel_id=1, source_target_pairs={{4,0},{8,4},{12,8},{16,12},{20,16},{24,20},{28,24},{5,1},{9,5},{13... | collective-permute-start | bytes 24584 | tf_op jit(solution)/shard_map/ppermute | solution.py:363
  34.4 3.3 %collective-permute-start.3 = (f32[16,128]{1,0:T(8,128)}, f32[16,128]{1,0:T(8,128)S(1)}, u32[]{:S(2)}, u32[]{:S(2)}) collective-permute-start(f32[16,128]{1,0:T(8,128)} %get-tuple-element.7), channel_id=1, source_target_pairs={{1,0},{2,1},{3,2},{5,4},{6,5},{7,6},{9,8},{10,9},{11,10},{13,12},{... | collective-permute-start | bytes 24584 | tf_op jit(solution)/shard_map/ppermute | solution.py:363
  38.0 11.4 %collective-permute-start.7 = (f32[4]{0:T(128)S(1)}, f32[4]{0:T(128)S(1)}, u32[]{:S(2)}, u32[]{:S(2)}) collective-permute-start(f32[4]{0:T(128)S(1)} %pad_maximum_fusion), channel_id=1, source_target_pairs={{0,1},{1,2},{2,3},{4,5},{5,6},{6,7},{8,9},{9,10},{10,11},{12,13},{... | collective-permute-start | bytes 56 | tf_op jit(solution)/shard_map/ppermute | solution.py:363
  41.4 8.1 %collective-permute-start.6 = (f32[4]{0:T(128)S(1)}, f32[4]{0:T(128)S(1)}, u32[]{:S(2)}, u32[]{:S(2)}) collective-permute-start(f32[4]{0:T(128)S(1)} %pad_maximum_fusion), channel_id=1, source_target_pairs={{0,4},{4,8},{8,12},{12,16},{16,20},{20,24},{24,28},{1,5},{5,9},{9,... | collective-permute-start | bytes 56 | tf_op jit(solution)/shard_map/ppermute | solution.py:363
  43.9 5.5 %collective-permute-start.5 = (f32[4]{0:T(128)S(1)}, f32[4]{0:T(128)S(1)}, u32[]{:S(2)}, u32[]{:S(2)}) collective-permute-start(f32[4]{0:T(128)S(1)} %pad_maximum_fusion), channel_id=1, source_target_pairs={{1,0},{2,1},{3,2},{5,4},{6,5},{7,6},{9,8},{10,9},{11,10},{13,12},{... | collective-permute-start | bytes 56 | tf_op jit(solution)/shard_map/ppermute | solution.py:363
  45.2 5.9 %collective-permute-start.4 = (f32[4]{0:T(128)S(1)}, f32[4]{0:T(128)S(1)}, u32[]{:S(2)}, u32[]{:S(2)}) collective-permute-start(f32[4]{0:T(128)S(1)} %pad_maximum_fusion), channel_id=1, source_target_pairs={{4,0},{8,4},{12,8},{16,12},{20,16},{24,20},{28,24},{5,1},{9,5},{13... | collective-permute-start | bytes 56 | tf_op jit(solution)/shard_map/ppermute | solution.py:363
  51.3 10.2 %collective-permute-start.10 = (f32[4]{0:T(128)S(1)}, f32[4]{0:T(128)S(1)}, u32[]{:S(2)}, u32[]{:S(2)}) collective-permute-start(f32[4]{0:T(128)S(1)} %pad_maximum_fusion.1), channel_id=1, source_target_pairs={{0,5},{4,9},{8,13},{12,17},{16,21},{20,25},{24,29},{1,6},{5,10},{9... | collective-permute-start | bytes 56 | tf_op jit(solution)/shard_map/ppermute | solution.py:441
  55.7 5.9 %collective-permute-start.9 = (f32[4]{0:T(128)S(1)}, f32[4]{0:T(128)S(1)}, u32[]{:S(2)}, u32[]{:S(2)}) collective-permute-start(f32[4]{0:T(128)S(1)} %pad_maximum_fusion.1), channel_id=1, source_target_pairs={{0,1},{1,2},{2,3},{4,5},{5,6},{6,7},{8,9},{9,10},{10,11},{12,13},{... | collective-permute-start | bytes 56 | tf_op jit(solution)/shard_map/ppermute | solution.py:363
  59.6 6.4 %collective-permute-start.8 = (f32[4]{0:T(128)S(1)}, f32[4]{0:T(128)S(1)}, u32[]{:S(2)}, u32[]{:S(2)}) collective-permute-start(f32[4]{0:T(128)S(1)} %pad_maximum_fusion.1), channel_id=1, source_target_pairs={{0,4},{4,8},{8,12},{12,16},{16,20},{20,24},{24,28},{1,5},{5,9},{9,... | collective-permute-start | bytes 56 | tf_op jit(solution)/shard_map/ppermute | solution.py:363
  66.6 0.6 copy-start.2

commit v13 on v9

--- a/solution.py
+++ b/solution.py
@@ -65,7 +65,7 @@
         emit(k, block)
 
 
-def blend_kernel(off_ref, band_ref, terms_ref, cur_ref, prev_ref, lcur_ref, lprev_ref,
+def blend_kernel(off_ref, band_ref, own_ref, left_terms_ref, up_terms_ref, corner_terms_ref, cur_ref, prev_ref, lcur_ref, lprev_ref,
                  up_ref, corner_ref, out_ref, w_ref, *, n_row, n_col):
     f32 = jnp.float32
     bf16 = jnp.bfloat16
@@ -92,7 +92,8 @@
         return jnp.where(live, fade(ids), 0.0)
 
     def gain(k, p):
-        return terms_ref[k * 2 * planes + p], terms_ref[k * 2 * planes + planes + p]
+        ref = (own_ref, left_terms_ref, up_terms_ref, corner_terms_ref)[k]
+        return ref[p], ref[planes + p]
 
     t = lax.broadcasted_iota(jnp.int32, (rows, 1), 0)
     x = lax.broadcasted_iota(jnp.int32, (1, tile_px), 1)
@@ -179,6 +180,9 @@
         grid=(steps,),
         in_specs=[
             pl.BlockSpec(memory_space=pltpu.SMEM),
+            pl.BlockSpec(memory_space=pltpu.SMEM),
+            pl.BlockSpec(memory_space=pltpu.SMEM),
+            pl.BlockSpec(memory_space=pltpu.SMEM),
             pl.BlockSpec((planes, rows, tile_px), cur),
             pl.BlockSpec((planes, rows, tile_px), prev),
             pl.BlockSpec((planes, rows, width), cur),
@@ -205,7 +209,7 @@
             flops=12 * planes * tile_px * tile_px, transcendentals=0,
             bytes_accessed=out_bytes + in_bytes,
         ),
-    )(offsets, bands, terms, tiles, tiles, from_left, from_left,
+    )(offsets, bands, *terms, tiles, tiles, from_left, from_left,
       from_up, from_corner)
 
 
@@ -299,16 +303,11 @@
     )
     own_gain = gain_one + gain_two
     own_level = jnp.exp(gain_two) * level_one + level_two
-    final = jnp.concatenate([own_gain, own_level])
+    final = jnp.concatenate([jnp.exp(own_gain), own_level])
     final_left = shifted(final, "col", n_col, 1)
     final_up = shifted(final, "row", n_row, 1)
     final_corner = lax.ppermute(final, ("col", "row"), diagonal)
-    terms = jnp.concatenate([
-        jnp.exp(own_gain), own_level,
-        jnp.exp(final_left[:planes]), final_left[planes:],
-        jnp.exp(final_up[:planes]), final_up[planes:],
-        jnp.exp(final_corner[:planes]), final_corner[planes:],
-    ])
+    terms = (final, final_left, final_up, final_corner)
     return blend(offsets, bands, terms, tiles, from_left, from_up, from_corner, n_row, n_col)
 
 

time: 74.6 us -> 74 us (level)
  transfers between devices with their start and end apart: 12 -> 12, of which waited for: 4 -> 4; matrix products, arithmetic and copies ran while one was open for 19% -> 18% of each run, Pallas kernels for 0% -> 0%
where the time goes in v13:
time: 74 us; the launch traced here: 73.2 us
  starting transfers between devices  35.5 us (48%)
  Pallas kernels  11.6 us (16%)
  waiting for transfers between devices  10.1 us (14%)
  other arithmetic  8.5 us (11%)
  local copies, waits for them, and re-layouts  6.54 us (9%)
  between operations  0.93 us (1%)
    ppermute x10, starting transfers between devices, shifted(): return lax.ppermute(block, axis, route)  28.9 us
    pallas_call x1, Pallas kernels, blend(): pl.pallas_call(functools.partial(blend_kernel, n_row=n_row, n_col=n_col),...  11.6 us
    ppermute x10, waiting for transfers between devices, shifted(): return lax.ppermute(block, axis, route)  10.1 us
    ppermute x1, starting transfers between devices, local(): final_corner = lax.ppermute(final, ('col', 'row'), diagonal)  4 us
    reduce_sum x2, other arithmetic, strip_stats(): covariance = jnp.sum(dev_former * dev_latter, axis=(-2, -1)) / number  3.52 us
    reduce_sum x2, other arithmetic, strip_stats(): mean_former = jnp.sum(former * full, axis=(-2, -1)) / number  3.31 us
    ppermute x1, starting transfers between devices, local(): from_corner = lax.ppermute(corner, ('col', 'row'), diagonal)  2.57 us
  transfers between devices with their start and end apart: 12, of which 4 were waited for; matrix products, arithmetic and copies ran while one was open for 18% of the time, Pallas kernels for 0%

profile of v13, /device:TPU:16, one launch (start us, length us, event | category | flops | bytes accessed | tf_op | source)
XLA Modules:
  0.0 73.2 jit_solution(14926020349006503214)
XLA Ops:
  0.6 1.1 %slice.39 = bf16[2,1024,128]{2,1,0:T(8,128)(2,1)S(1)} slice(bf16[2,1024,1024]{2,1,0:T(8,128)(2,1)} %prev_ref.1), slice={[0:2], [0:1024], [896:1024]} | slice | bytes 1048576 | tf_op jit(solution)/shard_map/slice | solution.py:243
  1.7 3.4 %collective-permute-start = (bf16[2,1024,128]{2,1,0:T(8,128)(2,1)S(1)}, bf16[2,1024,128]{2,1,0:T(8,128)(2,1)S(1)}, u32[]{:S(2)}, u32[]{:S(2)}) collective-permute-start(bf16[2,1024,128]{2,1,0:T(8,128)(2,1)S(1)} %slice.39), channel_id=1, source_target_pairs={{0,4},{4,8},{8,12},{12,16},{16,20},{20,24},{24,28},{1,5},{5,9},{9,... | collective-permute-start | bytes 1572872 | tf_op jit(solution)/shard_map/ppermute | solution.py:221
  6.0 2.6 %collective-permute-start.11 = (bf16[2,128,128]{2,1,0:T(8,128)(2,1)S(1)}, bf16[2,128,128]{2,1,0:T(8,128)(2,1)S(1)}, u32[]{:S(2)}, u32[]{:S(2)}) collective-permute-start(bf16[2,128,128]{2,1,0:T(8,128)(2,1)S(1)} %slice.51), channel_id=1, source_target_pairs={{0,5},{4,9},{8,13},{12,17},{16,21},{20,25},{24,29},{1,6},{5,10},{9... | collective-permute-start | bytes 196616 | tf_op jit(solution)/shard_map/ppermute | solution.py:253
  8.6 1.1 %slice.41 = bf16[2,128,1024]{2,1,0:T(8,128)(2,1)S(1)} slice(bf16[2,1024,1024]{2,1,0:T(8,128)(2,1)} %prev_ref.1), slice={[0:2], [896:1024], [0:1024]} | slice | bytes 1048576 | tf_op jit(solution)/shard_map/slice | solution.py:244
  9.7 3.8 %collective-permute-start.2 = (bf16[2,128,1024]{2,1,0:T(8,128)(2,1)S(1)}, bf16[2,128,1024]{2,1,0:T(8,128)(2,1)S(1)}, u32[]{:S(2)}, u32[]{:S(2)}) collective-permute-start(bf16[2,128,1024]{2,1,0:T(8,128)(2,1)S(1)} %slice.41), channel_id=1, source_target_pairs={{0,1},{1,2},{2,3},{4,5},{5,6},{6,7},{8,9},{9,10},{10,11},{12,13},{... | collective-permute-start | bytes 1572872 | tf_op jit(solution)/shard_map/ppermute | solution.py:221
  13.5 1.3 %constant_dynamic-slice_fusion.1 = (s32[1,1,1]{2,1,0:T(1,128)}, s32[1,1,1]{2,1,0:T(1,128)}) fusion(s32[2,4,8]{2,1,0:T(4,128)} %param.5, s32[]{:T(128)S(6)} %select_n.115, s32[]{:T(128)S(6)} %max.6, s32[]{:T(128)S(6)} %max.7, s32[]{:T(128)S(6)} %select_n.118), kind=kLoop, calls=%fused_computation.114 | loop fusion | bytes 32 | tf_op jit(solution)/shard_map/dynamic_slice | solution.py:267
  16.1 2.7 %collective-permute-done.lcur_ref.lprev_ref = bf16[2,1024,128]{2,1,0:T(8,128)(2,1)S(1)} collective-permute-done((bf16[2,1024,128]{2,1,0:T(8,128)(2,1)S(1)}, bf16[2,1024,128]{2,1,0:T(8,128)(2,1)S(1)}, u32[]{:S(2)}, u32[]{:S(2)}) %collective-permute-start) | collective-permute-done | bytes 524320 | tf_op jit(solution)/shard_map/ppermute | solution.py:221
  18.9 1.6 %fusion = (f32[2]{0:T(128)S(1)}, f32[2]{0:T(128)S(1)}, f32[2]{0:T(128)S(1)}) fusion(bf16[2,1024,128]{2,1,0:T(8,128)(2,1)S(1)} %collective-permute-done.lcur_ref.lprev_ref, f32[128]{0:T(128)S(1)} %compare_convert_fusion.1, bf16[2,1024,1024]{2,1,0:T(8,128)(2,1)} %prev_ref.1), kind=kLoop, calls=%fused_computation.8 | loop fusion | flops 1835002 | bytes 1049112 | tf_op jit(solution)/shard_map/reduce_sum | solution.py:22
  20.7 1.7 %fusion.5 = (f32[2]{0:T(128)S(1)}, f32[2]{0:T(128)S(1)}, f32[2]{0:T(128)S(1)}) fusion(bf16[2,1024,128]{2,1,0:T(8,128)(2,1)S(1)} %collective-permute-done.lcur_ref.lprev_ref, f32[2]{0:T(128)S(1)} %get-tuple-element.35, f32[2]{0:T(128)S(1)} %get-tuple-element.34, f32[128]{0:T(128)S(1)} %compare_convert_fusion.1, bf16[2,1024,1024]{2,1,0:T(8,128)(2,1)} %prev_ref.1), kind=kLoop, calls=%fused_computation.13 | loop fusion | flops 3145722 | bytes 1049128 | tf_op jit(solution)/shard_map/reduce_sum | solution.py:28
  22.8 1.9 %collective-permute-start.1 = (f32[5,2]{0,1:T(2,128)S(1)}, f32[5,2]{0,1:T(2,128)S(1)}, u32[]{:S(2)}, u32[]{:S(2)}) collective-permute-start(f32[5,2]{0,1:T(2,128)S(1)} %stack.4), channel_id=1, source_target_pairs={{4,0},{8,4},{12,8},{16,12},{20,16},{24,20},{28,24},{5,1},{9,5},{13... | collective-permute-start | bytes 128 | tf_op jit(solution)/shard_map/ppermute | solution.py:221
  24.7 1.7 %fusion.10 = (f32[2]{0:T(128)S(1)}, f32[2]{0:T(128)S(1)}, f32[2]{0:T(128)S(1)}) fusion(bf16[2,128,1024]{2,1,0:T(8,128)(2,1)S(1)} %collective-permute-done.2.up_ref, f32[128]{0:T(128)S(1)} %compare_convert_fusion, bf16[2,1024,1024]{2,1,0:T(8,128)(2,1)} %prev_ref.1), kind=kLoop, calls=%fused_computation.18 | loop fusion | flops 1835002 | bytes 1049112 | tf_op jit(solution)/shard_map/reduce_sum | solution.py:22
  26.6 1.8 %fusion.15 = (f32[2]{0:T(128)S(1)}, f32[2]{0:T(128)S(1)}, f32[2]{0:T(128)S(1)}) fusion(bf16[2,128,1024]{2,1,0:T(8,128)(2,1)S(1)} %collective-permute-done.2.up_ref, f32[2]{0:T(128)S(1)} %get-tuple-element.37, f32[2]{0:T(128)S(1)} %get-tuple-element.36, f32[128]{0:T(128)S(1)} %compare_convert_fusion, bf16[2,1024,1024]{2,1,0:T(8,128)(2,1)} %prev_ref.1), kind=kLoop, calls=%fused_computation.23 | loop fusion | flops 3145722 | bytes 1049128 | tf_op jit(solution)/shard_map/reduce_sum | solution.py:28
  28.8 1.3 %collective-permute-start.3 = (f32[5,2]{0,1:T(2,128)S(1)}, f32[5,2]{0,1:T(2,128)S(1)}, u32[]{:S(2)}, u32[]{:S(2)}) collective-permute-start(f32[5,2]{0,1:T(2,128)S(1)} %stack.5), channel_id=1, source_target_pairs={{1,0},{2,1},{3,2},{5,4},{6,5},{7,6},{9,8},{10,9},{11,10},{13,12},{... | collective-permute-start | bytes 128 | tf_op jit(solution)/shard_map/ppermute | solution.py:221
  30.4 1.5 %collective-permute-done.3 = f32[5,2]{0,1:T(2,128)S(1)} collective-permute-done((f32[5,2]{0,1:T(2,128)S(1)}, f32[5,2]{0,1:T(2,128)S(1)}, u32[]{:S(2)}, u32[]{:S(2)}) %collective-permute-start.3) | collective-permute-done | bytes 72 | tf_op jit(solution)/shard_map/ppermute | solution.py:221
  32.3 4.1 %collective-permute-start.7 = (f32[4]{0:T(128)S(1)}, f32[4]{0:T(128)S(1)}, u32[]{:S(2)}, u32[]{:S(2)}) collective-permute-start(f32[4]{0:T(128)S(1)} %pad_maximum_fusion), channel_id=1, source_target_pairs={{0,1},{1,2},{2,3},{4,5},{5,6},{6,7},{8,9},{9,10},{10,11},{12,13},{... | collective-permute-start | bytes 56 | tf_op jit(solution)/shard_map/ppermute | solution.py:221
  36.4 3.3 %collective-permute-start.6 = (f32[4]{0:T(128)S(1)}, f32[4]{0:T(128)S(1)}, u32[]{:S(2)}, u32[]{:S(2)}) collective-permute-start(f32[4]{0:T(128)S(1)} %pad_maximum_fusion), channel_id=1, source_target_pairs={{0,4},{4,8},{8,12},{12,16},{16,20},{20,24},{24,28},{1,5},{5,9},{9,... | collective-permute-start | bytes 56 | tf_op jit(solution)/shard_map/ppermute | solution.py:221
  39.7 1.3 %collective-permute-start.5 = (f32[4]{0:T(128)S(1)}, f32[4]{0:T(128)S(1)}, u32[]{:S(2)}, u32[]{:S(2)}) collective-permute-start(f32[4]{0:T(128)S(1)} %pad_maximum_fusion), channel_id=1, source_target_pairs={{1,0},{2,1},{3,2},{5,4},{6,5},{7,6},{9,8},{10,9},{11,10},{13,12},{... | collective-permute-start | bytes 56 | tf_op jit(solution)/shard_map/ppermute | solution.py:221
  41.0 3.4 %collective-permute-start.4 = (f32[4]{0:T(128)S(1)}, f32[4]{0:T(128)S(1)}, u32[]{:S(2)}, u32[]{:S(2)}) collective-permute-start(f32[4]{0:T(128)S(1)} %pad_maximum_fusion), channel_id=1, source_target_pairs={{4,0},{8,4},{12,8},{16,12},{20,16},{24,20},{28,24},{5,1},{9,5},{13... | collective-permute-start | bytes 56 | tf_op jit(solution)/shard_map/ppermute | solution.py:221
  44.4 2.0 %collective-permute-done.4 = f32[4]{0:T(128)S(1)} collective-permute-done((f32[4]{0:T(128)S(1)}, f32[4]{0:T(128)S(1)}, u32[]{:S(2)}, u32[]{:S(2)}) %collective-permute-start.4) | collective-permute-done | bytes 48 | tf_op jit(solution)/shard_map/ppermute | solution.py:221
  46.7 4.0 %collective-permute-start.10 = (f32[4]{0:T(128)S(1)}, f32[4]{0:T(128)S(1)}, u32[]{:S(2)}, u32[]{:S(2)}) collective-permute-start(f32[4]{0:T(128)S(1)} %pad_maximum_fusion.1.own_ref), channel_id=1, source_target_pairs={{0,5},{4,9},{8,13},{12,17},{16,21},{20,25},{24,29},{1,6},{5,10},{9... | collective-permute-start | bytes 56 | tf_op jit(solution)/shard_map/ppermute | solution.py:309
  50.7 3.9 %collective-permute-start.9 = (f32[4]{0:T(128)S(1)}, f32[4]{0:T(128)S(1)}, u32[]{:S(2)}, u32[]{:S(2)}) collective-permute-start(f32[4]{0:T(128)S(1)} %pad_maximum_fusion.1.own_ref), channel_id=1, source_target_pairs={{0,1},{1,2},{2,3},{4,5},{5,6},{6,7},{8,9},{9,10},{10,11},{12,13},{... | collective-permute-start | bytes 56 | tf_op jit(solution)/shard_map/ppermute | solution.py:221
  54.6 2.4 %collective-permute-start.8 = (f32[4]{0:T(128)S(1)}, f32[4]{0:T(128)S(1)}, u32[]{:S(2)}, u32[]{:S(2)}) collective-permute-start(f32[4]{0:T(128)S(1)} %pad_maximum_fusion.1.own_ref), channel_id=1, source_target_pairs={{0,4},{4,8},{8,12},{12,16},{16,20},{20,24},{24,28},{1,5},{5,9},{9,... | collective-permute-start | bytes 56 | tf_op jit(solution)/shard_map/ppermute | solution.py:221
  57.1 3.9 %collective-permute-done.8.left_terms_ref = f32[4]{0:T(128)S(1)} collective-permute-done((f32[4]{0:T(128)S(1)}, f32[4]{0:T(128)S(1)}, u32[]{:S(2)}, u32[]{:S(2)}) %collective-permute-start.8) | collective-permute-done | bytes 48 | tf_op jit(solution)/shard_map/ppermute | solution.py:221
  61.6 11.6 %shard_map.59 = (f32[2,1024,1024]{2,1,0:T(8,128)}, f32[1024,1024]{1,0:T(8,128)}) custom-call(s32[2,4,8]{2,1,0:T(4,128)} %off_ref.1, s32[2,4,8]{2,1,0:T(4,128)} %band_ref.1, f32[4]{0:T(128)} %copy-done.3, f32[4]{0:T(128)} %copy-done.6, f32[4]{0:T(128)} %copy-done.5, f32[4]{0:T(128)} %copy-done.4, bf16[2,1024,1024]{2,1,0:T(8,128)(2,1)} %prev_ref.1, ...), custom_call_target="tpu_custom_call" | custom-call | flops 25165824 | bytes 22020096 | tf_op jit(solution)/shard_map/pallas_call | solution.py:200
  (49 shorter events, 4.8 us)
Async XLA Ops:
  1.7 17.2 %collective-permute-start = (bf16[2,1024,128]{2,1,0:T(8,128)(2,1)S(1)}, bf16[2,1024,128]{2,1,0:T(8,128)(2,1)S(1)}, u32[]{:S(2)}, u32[]{:S(2)}) collective-permute-start(bf16[2,1024,128]{2,1,0:T(8,128)(2,1)S(1)} %slice.39), channel_id=1, source_target_pairs={{0,4},{4,8},{8,12},{12,16},{16,20},{20,24},{24,28},{1,5},{5,9},{9,... | collective-permute-start | bytes 1572872 | tf_op jit(solution)/shard_map/ppermute | solution.py:221
  6.0 51.0 %collective-permute-start.11 = (bf16[2,128,128]{2,1,0:T(8,128)(2,1)S(1)}, bf16[2,128,128]{2,1,0:T(8,128)(2,1)S(1)}, u32[]{:S(2)}, u32[]{:S(2)}) collective-permute-start(bf16[2,128,128]{2,1,0:T(8,128)(2,1)S(1)} %slice.51), channel_id=1, source_target_pairs={{0,5},{4,9},{8,13},{12,17},{16,21},{20,25},{24,29},{1,6},{5,10},{9... | collective-permute-start | bytes 196616 | tf_op jit(solution)/shard_map/ppermute | solution.py:253
  9.7 15.0 %collective-permute-start.2 = (bf16[2,128,1024]{2,1,0:T(8,128)(2,1)S(1)}, bf16[2,128,1024]{2,1,0:T(8,128)(2,1)S(1)}, u32[]{:S(2)}, u32[]{:S(2)}) collective-permute-start(bf16[2,128,1024]{2,1,0:T(8,128)(2,1)S(1)} %slice.41), channel_id=1, source_target_pairs={{0,1},{1,2},{2,3},{4,5},{5,6},{6,7},{8,9},{9,10},{10,11},{12,13},{... | collective-permute-start | bytes 1572872 | tf_op jit(solution)/shard_map/ppermute | solution.py:221
  18.9 42.1 %copy-start = (bf16[2,1024,128]{2,1,0:T(8,128)(2,1)}, bf16[2,1024,128]{2,1,0:T(8,128)(2,1)S(1)}, u32[]{:S(2)}) copy-start(bf16[2,1024,128]{2,1,0:T(8,128)(2,1)S(1)} %collective-permute-done.lcur_ref.lprev_ref) | copy-start | bytes 1572868
  22.8 7.3 %collective-permute-start.1 = (f32[5,2]{0,1:T(2,128)S(1)}, f32[5,2]{0,1:T(2,128)S(1)}, u32[]{:S(2)}, u32[]{:S(2)}) collective-permute-start(f32[5,2]{0,1:T(2,128)S(1)} %stack.4), channel_id=1, source_target_pairs={{4,0},{8,4},{12,8},{16,12},{20,16},{24,20},{28,24},{5,1},{9,5},{13... | collective-permute-start | bytes 128 | tf_op jit(solution)/shard_map/ppermute | solution.py:221
  24.7 36.2 %copy-start.1 = (bf16[2,128,1024]{2,1,0:T(8,128)(2,1)}, bf16[2,128,1024]{2,1,0:T(8,128)(2,1)S(1)}, u32[]{:S(2)}) copy-start(bf16[2,128,1024]{2,1,0:T(8,128)(2,1)S(1)} %collective-permute-done.2.up_ref) | copy-start | bytes 1572868
  28.8 3.0 %collective-permute-start.3 = (f32[5,2]{0,1:T(2,128)S(1)}, f32[5,2]{0,1:T(2,128)S(1)}, u32[]{:S(2)}, u32[]{:S(2)}) collective-permute-start(f32[5,2]{0,1:T(2,128)S(1)} %stack.5), channel_id=1, source_target_pairs={{1,0},{2,1},{3,2},{5,4},{6,5},{7,6},{9,8},{10,9},{11,10},{13,12},{... | collective-permute-start | bytes 128 | tf_op jit(solution)/shard_map/ppermute | solution.py:221
  32.3 12.2 %collective-permute-start.7 = (f32[4]{0:T(128)S(1)}, f32[4]{0:T(128)S(1)}, u32[]{:S(2)}, u32[]{:S(2)}) collective-permute-start(f32[4]{0:T(128)S(1)} %pad_maximum_fusion), channel_id=1, source_target_pairs={{0,1},{1,2},{2,3},{4,5},{5,6},{6,7},{8,9},{9,10},{10,11},{12,13},{... | collective-permute-start | bytes 56 | tf_op jit(solution)/shard_map/ppermute | solution.py:221
  36.4 8.1 %collective-permute-start.6 = (f32[4]{0:T(128)S(1)}, f32[4]{0:T(128)S(1)}, u32[]{:S(2)}, u32[]{:S(2)}) collective-permute-start(f32[4]{0:T(128)S(1)} %pad_maximum_fusion), channel_id=1, source_target_pairs={{0,4},{4,8},{8,12},{12,16},{16,20},{20,24},{24,28},{1,5},{5,9},{9,... | collective-permute-start | bytes 56 | tf_op jit(solution)/shard_map/ppermute | solution.py:221
  39.7 4.7 %collective-permute-start.5 = (f32[4]{0:T(128)S(1)}, f32[4]{0:T(128)S(1)}, u32[]{:S(2)}, u32[]{:S(2)}) collective-permute-start(f32[4]{0:T(128)S(1)} %pad_maximum_fusion), channel_id=1, source_target_pairs={{1,0},{2,1},{3,2},{5,4},{6,5},{7,6},{9,8},{10,9},{11,10},{13,12},{... | collective-permute-start | bytes 56 | tf_op jit(solution)/shard_map/ppermute | solution.py:221
  41.0 5.5 %collective-permute-start.4 = (f32[4]{0:T(128)S(1)}, f32[4]{0:T(128)S(1)}, u32[]{:S(2)}, u32[]{:S(2)}) collective-permute-start(f32[4]{0:T(128)S(1)} %pad_maximum_fusion), channel_id=1, source_target_pairs={{4,0},{8,4},{12,8},{16,12},{20,16},{24,20},{28,24},{5,1},{9,5},{13... | collective-permute-start | bytes 56 | tf_op jit(solution)/shard_map/ppermute | solution.py:221
  46.7 14.3 %copy-start.3 = (f32[4]{0:T(128)}, f32[4]{0:T(128)S(1)}, u32[]{:S(2)}) copy-start(f32[4]{0:T(128)S(1)} %pad_maximum_fusion.1.own_ref) | copy-start | bytes 52
  46.7 10.4 %collective-permute-start.10 = (f32[4]{0:T(128)S(1)}, f32[4]{0:T(128)S(1)}, u32[]{:S(2)}, u32[]{:S(2)}) collective-permute-start(f32[4]{0:T(128)S(1)} %pad_maximum_fusion.1.own_ref), channel_id=1, source_target_pairs={{0,5},{4,9},{8,13},{12,17},{16,21},{20,25},{24,29},{1,6},{5,10},{9... | collective-permute-start | bytes 56 | tf_op jit(solution)/shard_map/ppermute | solution.py:309
  50.7 6.4 %collective-permute-start.9 = (f32[4]{0:T(128)S(1)}, f32[4]{0:T(128)S(1)}, u32[]{:S(2)}, u32[]{:S(2)}) collective-permute-start(f32[4]{0:T(128)S(1)} %pad_maximum_fusion.1.own_ref), channel_id=1, source_target_pairs={{0,1},{1,2},{2,3},{4,5},{5,6},{6,7},{8,9},{9,10},{10,11},{12,13},{... | collective-permute-start | bytes 56 | tf_op jit(solution)/shard_map/ppermute | solution.py:221
  54.6 6.4 %collective-permute-start.8 = (f32[4]{0:T(128)S(1)}, f32[4]{0:T(128)S(1)}, u32[]{:S(2)}, u32[]{:S(2)}) collective-permute-start(f32[4]{0:T(128)S(1)} %pad_maximum_fusion.1.own_ref), channel_id=1, source_target_pairs={{0,4},{4,8},{8,12},{12,16},{16,20},{20,24},{24,28},{1,5},{5,9},{9,... | collective-permute-start | bytes 56 | tf_op jit(solution)/shard_map/ppermute | solution.py:221
  57.0 3.9 %copy-start.2 = (bf16[2,128,128]{2,1,0:T(8,128)(2,1)}, bf16[2,128,128]{2,1,0:T(8,128)(2,1)S(1)}, u32[]{:S(2)}) copy-start(bf16[2,128,128]{2,1,0:T(8,128)(2,1)S(1)} %collective-permute-done.11.corner_ref) | copy-start | bytes 196612
  57.0 3.9 %copy-start.4 = (f32[4]{0:T(128)}, f32[4]{0:T(128)S(1)}, u32[]{:S(2)}) copy-start(f32[4]{0:T(128)S(1)} %collective-permute-done.10.corner_terms_ref) | copy-start | bytes 52
  57.1 3.9 %copy-start.5 = (f32[4]{0:T(128)}, f32[4]{0:T(128)S(1)}, u32[]{:S(2)}) copy-start(f32[4]{0:T(128)S(1)} %collective-permute-done.9.up_terms_ref) | copy-start | bytes 52
  61.0 0.6 copy-start.6

commit v14 on v13

--- a/solution.py
+++ b/solution.py
@@ -281,15 +281,15 @@
         masked_terms(left_stats, has_left_pair),
         masked_terms(up_stats, has_up_pair),
     )
-    first = jnp.concatenate([gain_one, level_one])
+    scale = jnp.exp(gain_one)
+    first = jnp.concatenate([scale, level_one])
     near = [
         shifted(first, "col", n_col, -1),
         shifted(first, "row", n_row, -1),
         shifted(first, "col", n_col, 1),
         shifted(first, "row", n_row, 1),
     ]
-    scale = jnp.exp(gain_one)
-    near_scale = [jnp.exp(item[:planes]) for item in near]
+    near_scale = [item[:planes] for item in near]
     near_level = [item[planes:] for item in near]
     right_two = corrected_stats(right_stats, scale, level_one, near_scale[0], near_level[0])
     down_two = corrected_stats(down_stats, scale, level_one, near_scale[1], near_level[1])

time: 74 us -> 74 us (level)
  no operation moved by 1% of the time
where the time goes in v14:
time: 74 us; the launch traced here: 73.2 us
  starting transfers between devices  35.5 us (48%)
  Pallas kernels  11.6 us (16%)
  waiting for transfers between devices  10.1 us (14%)
  other arithmetic  8.5 us (11%)
  local copies, waits for them, and re-layouts  6.54 us (9%)
  between operations  0.93 us (1%)
    ppermute x10, starting transfers between devices, shifted(): return lax.ppermute(block, axis, route)  28.9 us
    pallas_call x1, Pallas kernels, blend(): pl.pallas_call(functools.partial(blend_kernel, n_row=n_row, n_col=n_col),...  11.6 us
    ppermute x10, waiting for transfers between devices, shifted(): return lax.ppermute(block, axis, route)  10.1 us
    ppermute x1, starting transfers between devices, local(): final_corner = lax.ppermute(final, ('col', 'row'), diagonal)  4 us
    reduce_sum x2, other arithmetic, strip_stats(): covariance = jnp.sum(dev_former * dev_latter, axis=(-2, -1)) / number  3.52 us
    reduce_sum x2, other arithmetic, strip_stats(): mean_former = jnp.sum(former * full, axis=(-2, -1)) / number  3.31 us
    ppermute x1, starting transfers between devices, local(): from_corner = lax.ppermute(corner, ('col', 'row'), diagonal)  2.57 us
  transfers between devices with their start and end apart: 12, of which 4 were waited for; matrix products, arithmetic and copies ran while one was open for 18% of the time, Pallas kernels for 0%

profile of v14, /device:TPU:16, one launch (start us, length us, event | category | flops | bytes accessed | tf_op | source)
XLA Modules:
  0.0 73.2 jit_solution(9391879425977762103)
XLA Ops:
  0.6 1.1 %slice.39 = bf16[2,1024,128]{2,1,0:T(8,128)(2,1)S(1)} slice(bf16[2,1024,1024]{2,1,0:T(8,128)(2,1)} %prev_ref.1), slice={[0:2], [0:1024], [896:1024]} | slice | bytes 1048576 | tf_op jit(solution)/shard_map/slice | solution.py:243
  1.7 3.4 %collective-permute-start = (bf16[2,1024,128]{2,1,0:T(8,128)(2,1)S(1)}, bf16[2,1024,128]{2,1,0:T(8,128)(2,1)S(1)}, u32[]{:S(2)}, u32[]{:S(2)}) collective-permute-start(bf16[2,1024,128]{2,1,0:T(8,128)(2,1)S(1)} %slice.39), channel_id=1, source_target_pairs={{0,4},{4,8},{8,12},{12,16},{16,20},{20,24},{24,28},{1,5},{5,9},{9,... | collective-permute-start | bytes 1572872 | tf_op jit(solution)/shard_map/ppermute | solution.py:221
  6.0 2.6 %collective-permute-start.11 = (bf16[2,128,128]{2,1,0:T(8,128)(2,1)S(1)}, bf16[2,128,128]{2,1,0:T(8,128)(2,1)S(1)}, u32[]{:S(2)}, u32[]{:S(2)}) collective-permute-start(bf16[2,128,128]{2,1,0:T(8,128)(2,1)S(1)} %slice.51), channel_id=1, source_target_pairs={{0,5},{4,9},{8,13},{12,17},{16,21},{20,25},{24,29},{1,6},{5,10},{9... | collective-permute-start | bytes 196616 | tf_op jit(solution)/shard_map/ppermute | solution.py:253
  8.6 1.1 %slice.41 = bf16[2,128,1024]{2,1,0:T(8,128)(2,1)S(1)} slice(bf16[2,1024,1024]{2,1,0:T(8,128)(2,1)} %prev_ref.1), slice={[0:2], [896:1024], [0:1024]} | slice | bytes 1048576 | tf_op jit(solution)/shard_map/slice | solution.py:244
  9.7 3.8 %collective-permute-start.2 = (bf16[2,128,1024]{2,1,0:T(8,128)(2,1)S(1)}, bf16[2,128,1024]{2,1,0:T(8,128)(2,1)S(1)}, u32[]{:S(2)}, u32[]{:S(2)}) collective-permute-start(bf16[2,128,1024]{2,1,0:T(8,128)(2,1)S(1)} %slice.41), channel_id=1, source_target_pairs={{0,1},{1,2},{2,3},{4,5},{5,6},{6,7},{8,9},{9,10},{10,11},{12,13},{... | collective-permute-start | bytes 1572872 | tf_op jit(solution)/shard_map/ppermute | solution.py:221
  13.5 1.3 %constant_dynamic-slice_fusion.1 = (s32[1,1,1]{2,1,0:T(1,128)}, s32[1,1,1]{2,1,0:T(1,128)}) fusion(s32[2,4,8]{2,1,0:T(4,128)} %param.5, s32[]{:T(128)S(6)} %select_n.115, s32[]{:T(128)S(6)} %max.6, s32[]{:T(128)S(6)} %max.7, s32[]{:T(128)S(6)} %select_n.118), kind=kLoop, calls=%fused_computation.110 | loop fusion | bytes 32 | tf_op jit(solution)/shard_map/dynamic_slice | solution.py:267
  16.1 2.7 %collective-permute-done.lcur_ref.lprev_ref = bf16[2,1024,128]{2,1,0:T(8,128)(2,1)S(1)} collective-permute-done((bf16[2,1024,128]{2,1,0:T(8,128)(2,1)S(1)}, bf16[2,1024,128]{2,1,0:T(8,128)(2,1)S(1)}, u32[]{:S(2)}, u32[]{:S(2)}) %collective-permute-start) | collective-permute-done | bytes 524320 | tf_op jit(solution)/shard_map/ppermute | solution.py:221
  18.9 1.6 %fusion = (f32[2]{0:T(128)S(1)}, f32[2]{0:T(128)S(1)}, f32[2]{0:T(128)S(1)}) fusion(bf16[2,1024,128]{2,1,0:T(8,128)(2,1)S(1)} %collective-permute-done.lcur_ref.lprev_ref, f32[128]{0:T(128)S(1)} %compare_convert_fusion.1, bf16[2,1024,1024]{2,1,0:T(8,128)(2,1)} %prev_ref.1), kind=kLoop, calls=%fused_computation.8 | loop fusion | flops 1835002 | bytes 1049112 | tf_op jit(solution)/shard_map/reduce_sum | solution.py:22
  20.7 1.7 %fusion.5 = (f32[2]{0:T(128)S(1)}, f32[2]{0:T(128)S(1)}, f32[2]{0:T(128)S(1)}) fusion(bf16[2,1024,128]{2,1,0:T(8,128)(2,1)S(1)} %collective-permute-done.lcur_ref.lprev_ref, f32[2]{0:T(128)S(1)} %get-tuple-element.37, f32[2]{0:T(128)S(1)} %get-tuple-element.36, f32[128]{0:T(128)S(1)} %compare_convert_fusion.1, bf16[2,1024,1024]{2,1,0:T(8,128)(2,1)} %prev_ref.1), kind=kLoop, calls=%fused_computation.13 | loop fusion | flops 3145722 | bytes 1049128 | tf_op jit(solution)/shard_map/reduce_sum | solution.py:28
  22.8 1.9 %collective-permute-start.1 = (f32[5,2]{0,1:T(2,128)S(1)}, f32[5,2]{0,1:T(2,128)S(1)}, u32[]{:S(2)}, u32[]{:S(2)}) collective-permute-start(f32[5,2]{0,1:T(2,128)S(1)} %stack.4), channel_id=1, source_target_pairs={{4,0},{8,4},{12,8},{16,12},{20,16},{24,20},{28,24},{5,1},{9,5},{13... | collective-permute-start | bytes 128 | tf_op jit(solution)/shard_map/ppermute | solution.py:221
  24.7 1.7 %fusion.10 = (f32[2]{0:T(128)S(1)}, f32[2]{0:T(128)S(1)}, f32[2]{0:T(128)S(1)}) fusion(bf16[2,128,1024]{2,1,0:T(8,128)(2,1)S(1)} %collective-permute-done.2.up_ref, f32[128]{0:T(128)S(1)} %compare_convert_fusion, bf16[2,1024,1024]{2,1,0:T(8,128)(2,1)} %prev_ref.1), kind=kLoop, calls=%fused_computation.18 | loop fusion | flops 1835002 | bytes 1049112 | tf_op jit(solution)/shard_map/reduce_sum | solution.py:22
  26.6 1.8 %fusion.15 = (f32[2]{0:T(128)S(1)}, f32[2]{0:T(128)S(1)}, f32[2]{0:T(128)S(1)}) fusion(bf16[2,128,1024]{2,1,0:T(8,128)(2,1)S(1)} %collective-permute-done.2.up_ref, f32[2]{0:T(128)S(1)} %get-tuple-element.39, f32[2]{0:T(128)S(1)} %get-tuple-element.38, f32[128]{0:T(128)S(1)} %compare_convert_fusion, bf16[2,1024,1024]{2,1,0:T(8,128)(2,1)} %prev_ref.1), kind=kLoop, calls=%fused_computation.23 | loop fusion | flops 3145722 | bytes 1049128 | tf_op jit(solution)/shard_map/reduce_sum | solution.py:28
  28.8 1.3 %collective-permute-start.3 = (f32[5,2]{0,1:T(2,128)S(1)}, f32[5,2]{0,1:T(2,128)S(1)}, u32[]{:S(2)}, u32[]{:S(2)}) collective-permute-start(f32[5,2]{0,1:T(2,128)S(1)} %stack.5), channel_id=1, source_target_pairs={{1,0},{2,1},{3,2},{5,4},{6,5},{7,6},{9,8},{10,9},{11,10},{13,12},{... | collective-permute-start | bytes 128 | tf_op jit(solution)/shard_map/ppermute | solution.py:221
  30.4 1.5 %collective-permute-done.3 = f32[5,2]{0,1:T(2,128)S(1)} collective-permute-done((f32[5,2]{0,1:T(2,128)S(1)}, f32[5,2]{0,1:T(2,128)S(1)}, u32[]{:S(2)}, u32[]{:S(2)}) %collective-permute-start.3) | collective-permute-done | bytes 72 | tf_op jit(solution)/shard_map/ppermute | solution.py:221
  32.3 4.1 %collective-permute-start.7 = (f32[4]{0:T(128)S(1)}, f32[4]{0:T(128)S(1)}, u32[]{:S(2)}, u32[]{:S(2)}) collective-permute-start(f32[4]{0:T(128)S(1)} %pad_maximum_fusion), channel_id=1, source_target_pairs={{0,1},{1,2},{2,3},{4,5},{5,6},{6,7},{8,9},{9,10},{10,11},{12,13},{... | collective-permute-start | bytes 56 | tf_op jit(solution)/shard_map/ppermute | solution.py:221
  36.4 3.3 %collective-permute-start.6 = (f32[4]{0:T(128)S(1)}, f32[4]{0:T(128)S(1)}, u32[]{:S(2)}, u32[]{:S(2)}) collective-permute-start(f32[4]{0:T(128)S(1)} %pad_maximum_fusion), channel_id=1, source_target_pairs={{0,4},{4,8},{8,12},{12,16},{16,20},{20,24},{24,28},{1,5},{5,9},{9,... | collective-permute-start | bytes 56 | tf_op jit(solution)/shard_map/ppermute | solution.py:221
  39.7 1.3 %collective-permute-start.5 = (f32[4]{0:T(128)S(1)}, f32[4]{0:T(128)S(1)}, u32[]{:S(2)}, u32[]{:S(2)}) collective-permute-start(f32[4]{0:T(128)S(1)} %pad_maximum_fusion), channel_id=1, source_target_pairs={{1,0},{2,1},{3,2},{5,4},{6,5},{7,6},{9,8},{10,9},{11,10},{13,12},{... | collective-permute-start | bytes 56 | tf_op jit(solution)/shard_map/ppermute | solution.py:221
  41.0 3.4 %collective-permute-start.4 = (f32[4]{0:T(128)S(1)}, f32[4]{0:T(128)S(1)}, u32[]{:S(2)}, u32[]{:S(2)}) collective-permute-start(f32[4]{0:T(128)S(1)} %pad_maximum_fusion), channel_id=1, source_target_pairs={{4,0},{8,4},{12,8},{16,12},{20,16},{24,20},{28,24},{5,1},{9,5},{13... | collective-permute-start | bytes 56 | tf_op jit(solution)/shard_map/ppermute | solution.py:221
  44.5 2.0 %collective-permute-done.4 = f32[4]{0:T(128)S(1)} collective-permute-done((f32[4]{0:T(128)S(1)}, f32[4]{0:T(128)S(1)}, u32[]{:S(2)}, u32[]{:S(2)}) %collective-permute-start.4) | collective-permute-done | bytes 48 | tf_op jit(solution)/shard_map/ppermute | solution.py:221
  46.7 4.0 %collective-permute-start.10 = (f32[4]{0:T(128)S(1)}, f32[4]{0:T(128)S(1)}, u32[]{:S(2)}, u32[]{:S(2)}) collective-permute-start(f32[4]{0:T(128)S(1)} %pad_maximum_fusion.1.own_ref), channel_id=1, source_target_pairs={{0,5},{4,9},{8,13},{12,17},{16,21},{20,25},{24,29},{1,6},{5,10},{9... | collective-permute-start | bytes 56 | tf_op jit(solution)/shard_map/ppermute | solution.py:309
  50.7 3.9 %collective-permute-start.9 = (f32[4]{0:T(128)S(1)}, f32[4]{0:T(128)S(1)}, u32[]{:S(2)}, u32[]{:S(2)}) collective-permute-start(f32[4]{0:T(128)S(1)} %pad_maximum_fusion.1.own_ref), channel_id=1, source_target_pairs={{0,1},{1,2},{2,3},{4,5},{5,6},{6,7},{8,9},{9,10},{10,11},{12,13},{... | collective-permute-start | bytes 56 | tf_op jit(solution)/shard_map/ppermute | solution.py:221
  54.6 2.4 %collective-permute-start.8 = (f32[4]{0:T(128)S(1)}, f32[4]{0:T(128)S(1)}, u32[]{:S(2)}, u32[]{:S(2)}) collective-permute-start(f32[4]{0:T(128)S(1)} %pad_maximum_fusion.1.own_ref), channel_id=1, source_target_pairs={{0,4},{4,8},{8,12},{12,16},{16,20},{20,24},{24,28},{1,5},{5,9},{9,... | collective-permute-start | bytes 56 | tf_op jit(solution)/shard_map/ppermute | solution.py:221
  57.1 3.9 %collective-permute-done.8.left_terms_ref = f32[4]{0:T(128)S(1)} collective-permute-done((f32[4]{0:T(128)S(1)}, f32[4]{0:T(128)S(1)}, u32[]{:S(2)}, u32[]{:S(2)}) %collective-permute-start.8) | collective-permute-done | bytes 48 | tf_op jit(solution)/shard_map/ppermute | solution.py:221
  61.6 11.6 %shard_map.59 = (f32[2,1024,1024]{2,1,0:T(8,128)}, f32[1024,1024]{1,0:T(8,128)}) custom-call(s32[2,4,8]{2,1,0:T(4,128)} %off_ref.1, s32[2,4,8]{2,1,0:T(4,128)} %band_ref.1, f32[4]{0:T(128)} %copy-done.3, f32[4]{0:T(128)} %copy-done.6, f32[4]{0:T(128)} %copy-done.5, f32[4]{0:T(128)} %copy-done.4, bf16[2,1024,1024]{2,1,0:T(8,128)(2,1)} %prev_ref.1, ...), custom_call_target="tpu_custom_call" | custom-call | flops 25165824 | bytes 22020096 | tf_op jit(solution)/shard_map/pallas_call | solution.py:200
  (49 shorter events, 4.8 us)
Async XLA Ops:
  1.7 17.2 %collective-permute-start = (bf16[2,1024,128]{2,1,0:T(8,128)(2,1)S(1)}, bf16[2,1024,128]{2,1,0:T(8,128)(2,1)S(1)}, u32[]{:S(2)}, u32[]{:S(2)}) collective-permute-start(bf16[2,1024,128]{2,1,0:T(8,128)(2,1)S(1)} %slice.39), channel_id=1, source_target_pairs={{0,4},{4,8},{8,12},{12,16},{16,20},{20,24},{24,28},{1,5},{5,9},{9,... | collective-permute-start | bytes 1572872 | tf_op jit(solution)/shard_map/ppermute | solution.py:221
  6.0 51.0 %collective-permute-start.11 = (bf16[2,128,128]{2,1,0:T(8,128)(2,1)S(1)}, bf16[2,128,128]{2,1,0:T(8,128)(2,1)S(1)}, u32[]{:S(2)}, u32[]{:S(2)}) collective-permute-start(bf16[2,128,128]{2,1,0:T(8,128)(2,1)S(1)} %slice.51), channel_id=1, source_target_pairs={{0,5},{4,9},{8,13},{12,17},{16,21},{20,25},{24,29},{1,6},{5,10},{9... | collective-permute-start | bytes 196616 | tf_op jit(solution)/shard_map/ppermute | solution.py:253
  9.7 15.0 %collective-permute-start.2 = (bf16[2,128,1024]{2,1,0:T(8,128)(2,1)S(1)}, bf16[2,128,1024]{2,1,0:T(8,128)(2,1)S(1)}, u32[]{:S(2)}, u32[]{:S(2)}) collective-permute-start(bf16[2,128,1024]{2,1,0:T(8,128)(2,1)S(1)} %slice.41), channel_id=1, source_target_pairs={{0,1},{1,2},{2,3},{4,5},{5,6},{6,7},{8,9},{9,10},{10,11},{12,13},{... | collective-permute-start | bytes 1572872 | tf_op jit(solution)/shard_map/ppermute | solution.py:221
  18.9 42.1 %copy-start = (bf16[2,1024,128]{2,1,0:T(8,128)(2,1)}, bf16[2,1024,128]{2,1,0:T(8,128)(2,1)S(1)}, u32[]{:S(2)}) copy-start(bf16[2,1024,128]{2,1,0:T(8,128)(2,1)S(1)} %collective-permute-done.lcur_ref.lprev_ref) | copy-start | bytes 1572868
  22.8 7.3 %collective-permute-start.1 = (f32[5,2]{0,1:T(2,128)S(1)}, f32[5,2]{0,1:T(2,128)S(1)}, u32[]{:S(2)}, u32[]{:S(2)}) collective-permute-start(f32[5,2]{0,1:T(2,128)S(1)} %stack.4), channel_id=1, source_target_pairs={{4,0},{8,4},{12,8},{16,12},{20,16},{24,20},{28,24},{5,1},{9,5},{13... | collective-permute-start | bytes 128 | tf_op jit(solution)/shard_map/ppermute | solution.py:221
  24.7 36.2 %copy-start.1 = (bf16[2,128,1024]{2,1,0:T(8,128)(2,1)}, bf16[2,128,1024]{2,1,0:T(8,128)(2,1)S(1)}, u32[]{:S(2)}) copy-start(bf16[2,128,1024]{2,1,0:T(8,128)(2,1)S(1)} %collective-permute-done.2.up_ref) | copy-start | bytes 1572868
  28.8 3.0 %collective-permute-start.3 = (f32[5,2]{0,1:T(2,128)S(1)}, f32[5,2]{0,1:T(2,128)S(1)}, u32[]{:S(2)}, u32[]{:S(2)}) collective-permute-start(f32[5,2]{0,1:T(2,128)S(1)} %stack.5), channel_id=1, source_target_pairs={{1,0},{2,1},{3,2},{5,4},{6,5},{7,6},{9,8},{10,9},{11,10},{13,12},{... | collective-permute-start | bytes 128 | tf_op jit(solution)/shard_map/ppermute | solution.py:221
  32.3 12.2 %collective-permute-start.7 = (f32[4]{0:T(128)S(1)}, f32[4]{0:T(128)S(1)}, u32[]{:S(2)}, u32[]{:S(2)}) collective-permute-start(f32[4]{0:T(128)S(1)} %pad_maximum_fusion), channel_id=1, source_target_pairs={{0,1},{1,2},{2,3},{4,5},{5,6},{6,7},{8,9},{9,10},{10,11},{12,13},{... | collective-permute-start | bytes 56 | tf_op jit(solution)/shard_map/ppermute | solution.py:221
  36.4 8.1 %collective-permute-start.6 = (f32[4]{0:T(128)S(1)}, f32[4]{0:T(128)S(1)}, u32[]{:S(2)}, u32[]{:S(2)}) collective-permute-start(f32[4]{0:T(128)S(1)} %pad_maximum_fusion), channel_id=1, source_target_pairs={{0,4},{4,8},{8,12},{12,16},{16,20},{20,24},{24,28},{1,5},{5,9},{9,... | collective-permute-start | bytes 56 | tf_op jit(solution)/shard_map/ppermute | solution.py:221
  39.7 4.7 %collective-permute-start.5 = (f32[4]{0:T(128)S(1)}, f32[4]{0:T(128)S(1)}, u32[]{:S(2)}, u32[]{:S(2)}) collective-permute-start(f32[4]{0:T(128)S(1)} %pad_maximum_fusion), channel_id=1, source_target_pairs={{1,0},{2,1},{3,2},{5,4},{6,5},{7,6},{9,8},{10,9},{11,10},{13,12},{... | collective-permute-start | bytes 56 | tf_op jit(solution)/shard_map/ppermute | solution.py:221
  41.0 5.5 %collective-permute-start.4 = (f32[4]{0:T(128)S(1)}, f32[4]{0:T(128)S(1)}, u32[]{:S(2)}, u32[]{:S(2)}) collective-permute-start(f32[4]{0:T(128)S(1)} %pad_maximum_fusion), channel_id=1, source_target_pairs={{4,0},{8,4},{12,8},{16,12},{20,16},{24,20},{28,24},{5,1},{9,5},{13... | collective-permute-start | bytes 56 | tf_op jit(solution)/shard_map/ppermute | solution.py:221
  46.7 14.3 %copy-start.3 = (f32[4]{0:T(128)}, f32[4]{0:T(128)S(1)}, u32[]{:S(2)}) copy-start(f32[4]{0:T(128)S(1)} %pad_maximum_fusion.1.own_ref) | copy-start | bytes 52
  46.7 10.4 %collective-permute-start.10 = (f32[4]{0:T(128)S(1)}, f32[4]{0:T(128)S(1)}, u32[]{:S(2)}, u32[]{:S(2)}) collective-permute-start(f32[4]{0:T(128)S(1)} %pad_maximum_fusion.1.own_ref), channel_id=1, source_target_pairs={{0,5},{4,9},{8,13},{12,17},{16,21},{20,25},{24,29},{1,6},{5,10},{9... | collective-permute-start | bytes 56 | tf_op jit(solution)/shard_map/ppermute | solution.py:309
  50.7 6.4 %collective-permute-start.9 = (f32[4]{0:T(128)S(1)}, f32[4]{0:T(128)S(1)}, u32[]{:S(2)}, u32[]{:S(2)}) collective-permute-start(f32[4]{0:T(128)S(1)} %pad_maximum_fusion.1.own_ref), channel_id=1, source_target_pairs={{0,1},{1,2},{2,3},{4,5},{5,6},{6,7},{8,9},{9,10},{10,11},{12,13},{... | collective-permute-start | bytes 56 | tf_op jit(solution)/shard_map/ppermute | solution.py:221
  54.6 6.4 %collective-permute-start.8 = (f32[4]{0:T(128)S(1)}, f32[4]{0:T(128)S(1)}, u32[]{:S(2)}, u32[]{:S(2)}) collective-permute-start(f32[4]{0:T(128)S(1)} %pad_maximum_fusion.1.own_ref), channel_id=1, source_target_pairs={{0,4},{4,8},{8,12},{12,16},{16,20},{20,24},{24,28},{1,5},{5,9},{9,... | collective-permute-start | bytes 56 | tf_op jit(solution)/shard_map/ppermute | solution.py:221
  57.0 3.9 %copy-start.2 = (bf16[2,128,128]{2,1,0:T(8,128)(2,1)}, bf16[2,128,128]{2,1,0:T(8,128)(2,1)S(1)}, u32[]{:S(2)}) copy-start(bf16[2,128,128]{2,1,0:T(8,128)(2,1)S(1)} %collective-permute-done.11.corner_ref) | copy-start | bytes 196612
  57.0 3.9 %copy-start.4 = (f32[4]{0:T(128)}, f32[4]{0:T(128)S(1)}, u32[]{:S(2)}) copy-start(f32[4]{0:T(128)S(1)} %collective-permute-done.10.corner_terms_ref) | copy-start | bytes 52
  57.1 3.9 %copy-start.5 = (f32[4]{0:T(128)}, f32[4]{0:T(128)S(1)}, u32[]{:S(2)}) copy-start(f32[4]{0:T(128)S(1)} %collective-permute-done.9.up_terms_ref) | copy-start | bytes 52
  61.0 0.6 copy-start.6

commit v15 on v13

--- a/solution.py
+++ b/solution.py
@@ -19,14 +19,14 @@
 def strip_stats(former, latter, window):
     full = jnp.broadcast_to(window, former.shape)
     number = jnp.sum(full, axis=(-2, -1))
-    mean_former = jnp.sum(former * full, axis=(-2, -1)) / number
-    mean_latter = jnp.sum(latter * full, axis=(-2, -1)) / number
-    dev_former = (former - mean_former[:, None, None]) * full
-    dev_latter = (latter - mean_latter[:, None, None]) * full
-    var_former = jnp.sum(dev_former * dev_former, axis=(-2, -1)) / number
-    var_latter = jnp.sum(dev_latter * dev_latter, axis=(-2, -1)) / number
-    covariance = jnp.sum(dev_former * dev_latter, axis=(-2, -1)) / number
-    return jnp.stack([mean_former, mean_latter, var_former, var_latter, covariance])
+    means = jnp.sum(jnp.stack([former * full, latter * full]), axis=(-2, -1)) / number
+    dev_former = (former - means[0][:, None, None]) * full
+    dev_latter = (latter - means[1][:, None, None]) * full
+    spreads = jnp.sum(
+        jnp.stack([dev_former * dev_former, dev_latter * dev_latter, dev_former * dev_latter]),
+        axis=(-2, -1),
+    ) / number
+    return jnp.concatenate([means, spreads])
 
 
 def pair_terms(stats):

time: 74 us -> 78.5 us (1.061)
  waiting for transfers between devices: 10.1 us -> 15.7 us
  starting transfers between devices: 35.5 us -> 34.4 us
    ppermute x10, waiting for transfers between devices: 10.1 us -> 15.7 us  [shifted(): return lax.ppermute(block, axis, route)]
    ppermute x10, starting transfers between devices: 28.9 us -> 25.8 us  [shifted(): return lax.ppermute(block, axis, route)]
    another operation x0 -> x2, other arithmetic: none -> 2.99 us  [strip_stats(): jnp.stack([dev_former * dev_former, dev_latter * dev_latter, dev_former *...]
    reduce_sum x4 -> x6, other arithmetic: 6.83 us -> 4.4 us  [the longest x2 3.19 us: strip_stats(): number = jnp.sum(full, axis=(-2, -1))]
    ppermute x1, starting transfers between devices: 2.57 us -> 4.76 us  [local(): from_corner = lax.ppermute(corner, ('col', 'row'), diagonal)]
  transfers between devices with their start and end apart: 12 -> 12, of which waited for: 4 -> 4; matrix products, arithmetic and copies ran while one was open for 18% -> 17% of each run, Pallas kernels for 0% -> 0%
where the time goes in v15:
time: 78.5 us; the launch traced here: 77.7 us
  starting transfers between devices  34.4 us (44%)
  waiting for transfers between devices  15.7 us (20%)
  Pallas kernels  11.6 us (15%)
  other arithmetic  9.2 us (12%)
  local copies, waits for them, and re-layouts  5.8 us (7%)
  between operations  0.94 us (1%)
    ppermute x10, starting transfers between devices, shifted(): return lax.ppermute(block, axis, route)  25.8 us
    ppermute x10, waiting for transfers between devices, shifted(): return lax.ppermute(block, axis, route)  15.7 us
    pallas_call x1, Pallas kernels, blend(): pl.pallas_call(functools.partial(blend_kernel, n_row=n_row, n_col=n_col),...  11.6 us
    ppermute x1, starting transfers between devices, local(): from_corner = lax.ppermute(corner, ('col', 'row'), diagonal)  4.76 us
    ppermute x1, starting transfers between devices, local(): final_corner = lax.ppermute(final, ('col', 'row'), diagonal)  3.9 us
    reduce_sum x2, other arithmetic, strip_stats(): number = jnp.sum(full, axis=(-2, -1))  3.19 us
    another operation x2, other arithmetic, strip_stats(): jnp.stack([dev_former * dev_former, dev_latter * dev_latter, dev_former *...  2.99 us
  transfers between devices with their start and end apart: 12, of which 4 were waited for; matrix products, arithmetic and copies ran while one was open for 17% of the time, Pallas kernels for 0%

profile of v15, /device:TPU:16, one launch (start us, length us, event | category | flops | bytes accessed | tf_op | source)
XLA Modules:
  0.0 77.7 jit_solution(4019950627601406126)
XLA Ops:
  0.6 1.1 %slice.55 = bf16[2,128,1024]{2,1,0:T(8,128)(2,1)S(1)} slice(bf16[2,1024,1024]{2,1,0:T(8,128)(2,1)} %prev_ref.1), slice={[0:2], [896:1024], [0:1024]} | slice | bytes 1048576 | tf_op jit(solution)/shard_map/slice | solution.py:244
  1.7 1.8 %collective-permute-start.2 = (bf16[2,128,1024]{2,1,0:T(8,128)(2,1)S(1)}, bf16[2,128,1024]{2,1,0:T(8,128)(2,1)S(1)}, u32[]{:S(2)}, u32[]{:S(2)}) collective-permute-start(bf16[2,128,1024]{2,1,0:T(8,128)(2,1)S(1)} %slice.55), channel_id=1, source_target_pairs={{0,1},{1,2},{2,3},{4,5},{5,6},{6,7},{8,9},{9,10},{10,11},{12,13},{... | collective-permute-start | bytes 1572872 | tf_op jit(solution)/shard_map/ppermute | solution.py:221
  4.4 4.8 %collective-permute-start.11 = (bf16[2,128,128]{2,1,0:T(8,128)(2,1)S(1)}, bf16[2,128,128]{2,1,0:T(8,128)(2,1)S(1)}, u32[]{:S(2)}, u32[]{:S(2)}) collective-permute-start(bf16[2,128,128]{2,1,0:T(8,128)(2,1)S(1)} %slice.67), channel_id=1, source_target_pairs={{0,5},{4,9},{8,13},{12,17},{16,21},{20,25},{24,29},{1,6},{5,10},{9... | collective-permute-start | bytes 196616 | tf_op jit(solution)/shard_map/ppermute | solution.py:253
  9.1 1.1 %slice.51 = bf16[2,1024,128]{2,1,0:T(8,128)(2,1)S(1)} slice(bf16[2,1024,1024]{2,1,0:T(8,128)(2,1)} %prev_ref.1), slice={[0:2], [0:1024], [896:1024]} | slice | bytes 1048576 | tf_op jit(solution)/shard_map/slice | solution.py:243
  10.2 3.4 %collective-permute-start = (bf16[2,1024,128]{2,1,0:T(8,128)(2,1)S(1)}, bf16[2,1024,128]{2,1,0:T(8,128)(2,1)S(1)}, u32[]{:S(2)}, u32[]{:S(2)}) collective-permute-start(bf16[2,1024,128]{2,1,0:T(8,128)(2,1)S(1)} %slice.51), channel_id=1, source_target_pairs={{0,4},{4,8},{8,12},{12,16},{16,20},{20,24},{24,28},{1,5},{5,9},{9,... | collective-permute-start | bytes 1572872 | tf_op jit(solution)/shard_map/ppermute | solution.py:221
  13.7 1.3 %constant_dynamic-slice_fusion.1 = (s32[1,1,1]{2,1,0:T(1,128)}, s32[1,1,1]{2,1,0:T(1,128)}) fusion(s32[2,4,8]{2,1,0:T(4,128)} %param.5, s32[]{:T(128)S(6)} %select_n.115, s32[]{:T(128)S(6)} %max.6, s32[]{:T(128)S(6)} %max.7, s32[]{:T(128)S(6)} %select_n.118), kind=kLoop, calls=%fused_computation.142 | loop fusion | bytes 32 | tf_op jit(solution)/shard_map/dynamic_slice | solution.py:267
  16.3 1.7 %broadcast_reduce_fusion.1 = (f32[2]{0:T(128)S(1)}, f32[1,2,128,1024]{3,2,1,0:T(8,128)S(1)}, f32[1,2,128,1024]{3,2,1,0:T(8,128)S(1)}) fusion(f32[128]{0:T(128)S(1)} %compare_convert_fusion, bf16[2,1024,1024]{2,1,0:T(8,128)(2,1)} %prev_ref.1, bf16[2,128,1024]{2,1,0:T(8,128)(2,1)S(1)} %collective-permute-done.2.up_ref), kind=kLoop, calls=%fused_computation.33 | loop fusion | flops 1310718 | bytes 3146248 | tf_op jit(solution)/shard_map/reduce_sum | solution.py:21
  18.4 8.3 %collective-permute-done.lcur_ref.lprev_ref = bf16[2,1024,128]{2,1,0:T(8,128)(2,1)S(1)} collective-permute-done((bf16[2,1024,128]{2,1,0:T(8,128)(2,1)S(1)}, bf16[2,1024,128]{2,1,0:T(8,128)(2,1)S(1)}, u32[]{:S(2)}, u32[]{:S(2)}) %collective-permute-start) | collective-permute-done | bytes 524320 | tf_op jit(solution)/shard_map/ppermute | solution.py:221
  26.7 1.5 %broadcast_reduce_fusion = (f32[2]{0:T(128)S(1)}, f32[1,2,1024,128]{3,2,1,0:T(8,128)S(1)}, f32[1,2,1024,128]{3,2,1,0:T(8,128)S(1)}) fusion(f32[128]{0:T(128)S(1)} %compare_convert_fusion.1, bf16[2,1024,1024]{2,1,0:T(8,128)(2,1)} %prev_ref.1, bf16[2,1024,128]{2,1,0:T(8,128)(2,1)S(1)} %collective-permute-done.lcur_ref.lprev_ref), kind=kLoop, calls=%fused_computation.32 | loop fusion | flops 1310718 | bytes 3146248 | tf_op jit(solution)/shard_map/reduce_sum | solution.py:21
  28.6 1.4 %fusion.9 = (f32[1,2,1024,128]{3,2,1,0:T(8,128)S(1)}, f32[1,2,1024,128]{3,2,1,0:T(8,128)S(1)}, f32[1,2,1024,128]{3,2,1,0:T(8,128)S(1)}) fusion(f32[2]{0:T(128)S(1)} %get-tuple-element.23, f32[128]{0:T(128)S(1)} %compare_convert_fusion.1, bf16[2,1024,1024]{2,1,0:T(8,128)(2,1)} %prev_ref.1, f32[2]{0:T(128)S(1)} %get-tuple-element.22, ...), kind=kLoop, calls=%fused_computation.21 | loop fusion | flops 2359296 | bytes 4194832 | tf_op jit(solution)/shard_map/stack | solution.py:26
  30.5 2.4 %collective-permute-start.1 = (f32[5,2]{0,1:T(2,128)S(1)}, f32[5,2]{0,1:T(2,128)S(1)}, u32[]{:S(2)}, u32[]{:S(2)}) collective-permute-start(f32[5,2]{0,1:T(2,128)S(1)} %pad_maximum_fusion), channel_id=1, source_target_pairs={{4,0},{8,4},{12,8},{16,12},{20,16},{24,20},{28,24},{5,1},{9,5},{13... | collective-permute-start | bytes 128 | tf_op jit(solution)/shard_map/ppermute | solution.py:221
  32.9 1.6 %fusion.19 = (f32[1,2,128,1024]{3,2,1,0:T(8,128)S(1)}, f32[1,2,128,1024]{3,2,1,0:T(8,128)S(1)}, f32[1,2,128,1024]{3,2,1,0:T(8,128)S(1)}) fusion(f32[2]{0:T(128)S(1)} %get-tuple-element.25, f32[128]{0:T(128)S(1)} %compare_convert_fusion, bf16[2,1024,1024]{2,1,0:T(8,128)(2,1)} %prev_ref.1, f32[2]{0:T(128)S(1)} %get-tuple-element.24, ...), kind=kLoop, calls=%fused_computation.31 | loop fusion | flops 2359296 | bytes 4194832 | tf_op jit(solution)/shard_map/stack | solution.py:26
  35.0 1.3 %collective-permute-start.3 = (f32[5,2]{0,1:T(2,128)S(1)}, f32[5,2]{0,1:T(2,128)S(1)}, u32[]{:S(2)}, u32[]{:S(2)}) collective-permute-start(f32[5,2]{0,1:T(2,128)S(1)} %pad_maximum_fusion.1), channel_id=1, source_target_pairs={{1,0},{2,1},{3,2},{5,4},{6,5},{7,6},{9,8},{10,9},{11,10},{13,12},{... | collective-permute-start | bytes 128 | tf_op jit(solution)/shard_map/ppermute | solution.py:221
  36.6 1.5 %collective-permute-done.3 = f32[5,2]{0,1:T(2,128)S(1)} collective-permute-done((f32[5,2]{0,1:T(2,128)S(1)}, f32[5,2]{0,1:T(2,128)S(1)}, u32[]{:S(2)}, u32[]{:S(2)}) %collective-permute-start.3) | collective-permute-done | bytes 72 | tf_op jit(solution)/shard_map/ppermute | solution.py:221
  38.5 2.4 %collective-permute-start.7 = (f32[4]{0:T(128)S(1)}, f32[4]{0:T(128)S(1)}, u32[]{:S(2)}, u32[]{:S(2)}) collective-permute-start(f32[4]{0:T(128)S(1)} %pad_maximum_fusion.2), channel_id=1, source_target_pairs={{0,1},{1,2},{2,3},{4,5},{5,6},{6,7},{8,9},{9,10},{10,11},{12,13},{... | collective-permute-start | bytes 56 | tf_op jit(solution)/shard_map/ppermute | solution.py:221
  40.9 3.4 %collective-permute-start.6 = (f32[4]{0:T(128)S(1)}, f32[4]{0:T(128)S(1)}, u32[]{:S(2)}, u32[]{:S(2)}) collective-permute-start(f32[4]{0:T(128)S(1)} %pad_maximum_fusion.2), channel_id=1, source_target_pairs={{0,4},{4,8},{8,12},{12,16},{16,20},{20,24},{24,28},{1,5},{5,9},{9,... | collective-permute-start | bytes 56 | tf_op jit(solution)/shard_map/ppermute | solution.py:221
  44.3 1.3 %collective-permute-start.5 = (f32[4]{0:T(128)S(1)}, f32[4]{0:T(128)S(1)}, u32[]{:S(2)}, u32[]{:S(2)}) collective-permute-start(f32[4]{0:T(128)S(1)} %pad_maximum_fusion.2), channel_id=1, source_target_pairs={{1,0},{2,1},{3,2},{5,4},{6,5},{7,6},{9,8},{10,9},{11,10},{13,12},{... | collective-permute-start | bytes 56 | tf_op jit(solution)/shard_map/ppermute | solution.py:221
  45.6 3.3 %collective-permute-start.4 = (f32[4]{0:T(128)S(1)}, f32[4]{0:T(128)S(1)}, u32[]{:S(2)}, u32[]{:S(2)}) collective-permute-start(f32[4]{0:T(128)S(1)} %pad_maximum_fusion.2), channel_id=1, source_target_pairs={{4,0},{8,4},{12,8},{16,12},{20,16},{24,20},{28,24},{5,1},{9,5},{13... | collective-permute-start | bytes 56 | tf_op jit(solution)/shard_map/ppermute | solution.py:221
  49.0 2.1 %collective-permute-done.4 = f32[4]{0:T(128)S(1)} collective-permute-done((f32[4]{0:T(128)S(1)}, f32[4]{0:T(128)S(1)}, u32[]{:S(2)}, u32[]{:S(2)}) %collective-permute-start.4) | collective-permute-done | bytes 48 | tf_op jit(solution)/shard_map/ppermute | solution.py:221
  51.3 3.9 %collective-permute-start.10 = (f32[4]{0:T(128)S(1)}, f32[4]{0:T(128)S(1)}, u32[]{:S(2)}, u32[]{:S(2)}) collective-permute-start(f32[4]{0:T(128)S(1)} %pad_maximum_fusion.3.own_ref), channel_id=1, source_target_pairs={{0,5},{4,9},{8,13},{12,17},{16,21},{20,25},{24,29},{1,6},{5,10},{9... | collective-permute-start | bytes 56 | tf_op jit(solution)/shard_map/ppermute | solution.py:309
  55.2 3.9 %collective-permute-start.9 = (f32[4]{0:T(128)S(1)}, f32[4]{0:T(128)S(1)}, u32[]{:S(2)}, u32[]{:S(2)}) collective-permute-start(f32[4]{0:T(128)S(1)} %pad_maximum_fusion.3.own_ref), channel_id=1, source_target_pairs={{0,1},{1,2},{2,3},{4,5},{5,6},{6,7},{8,9},{9,10},{10,11},{12,13},{... | collective-permute-start | bytes 56 | tf_op jit(solution)/shard_map/ppermute | solution.py:221
  59.1 2.5 %collective-permute-start.8 = (f32[4]{0:T(128)S(1)}, f32[4]{0:T(128)S(1)}, u32[]{:S(2)}, u32[]{:S(2)}) collective-permute-start(f32[4]{0:T(128)S(1)} %pad_maximum_fusion.3.own_ref), channel_id=1, source_target_pairs={{0,4},{4,8},{8,12},{12,16},{16,20},{20,24},{24,28},{1,5},{5,9},{9,... | collective-permute-start | bytes 56 | tf_op jit(solution)/shard_map/ppermute | solution.py:221
  61.7 3.8 %collective-permute-done.8.left_terms_ref = f32[4]{0:T(128)S(1)} collective-permute-done((f32[4]{0:T(128)S(1)}, f32[4]{0:T(128)S(1)}, u32[]{:S(2)}, u32[]{:S(2)}) %collective-permute-start.8) | collective-permute-done | bytes 48 | tf_op jit(solution)/shard_map/ppermute | solution.py:221
  66.1 11.6 %shard_map.59 = (f32[2,1024,1024]{2,1,0:T(8,128)}, f32[1024,1024]{1,0:T(8,128)}) custom-call(s32[2,4,8]{2,1,0:T(4,128)} %off_ref.1, s32[2,4,8]{2,1,0:T(4,128)} %band_ref.1, f32[4]{0:T(128)} %copy-done.3, f32[4]{0:T(128)} %copy-done.6, f32[4]{0:T(128)} %copy-done.5, f32[4]{0:T(128)} %copy-done.4, bf16[2,1024,1024]{2,1,0:T(8,128)(2,1)} %prev_ref.1, ...), custom_call_target="tpu_custom_call" | custom-call | flops 25165824 | bytes 22020096 | tf_op jit(solution)/shard_map/pallas_call | solution.py:200
  (49 shorter events, 5.4 us)
Async XLA Ops:
  1.7 14.6 %collective-permute-start.2 = (bf16[2,128,1024]{2,1,0:T(8,128)(2,1)S(1)}, bf16[2,128,1024]{2,1,0:T(8,128)(2,1)S(1)}, u32[]{:S(2)}, u32[]{:S(2)}) collective-permute-start(bf16[2,128,1024]{2,1,0:T(8,128)(2,1)S(1)} %slice.55), channel_id=1, source_target_pairs={{0,1},{1,2},{2,3},{4,5},{5,6},{6,7},{8,9},{9,10},{10,11},{12,13},{... | collective-permute-start | bytes 1572872 | tf_op jit(solution)/shard_map/ppermute | solution.py:221
  4.4 57.3 %collective-permute-start.11 = (bf16[2,128,128]{2,1,0:T(8,128)(2,1)S(1)}, bf16[2,128,128]{2,1,0:T(8,128)(2,1)S(1)}, u32[]{:S(2)}, u32[]{:S(2)}) collective-permute-start(bf16[2,128,128]{2,1,0:T(8,128)(2,1)S(1)} %slice.67), channel_id=1, source_target_pairs={{0,5},{4,9},{8,13},{12,17},{16,21},{20,25},{24,29},{1,6},{5,10},{9... | collective-permute-start | bytes 196616 | tf_op jit(solution)/shard_map/ppermute | solution.py:253
  10.2 16.5 %collective-permute-start = (bf16[2,1024,128]{2,1,0:T(8,128)(2,1)S(1)}, bf16[2,1024,128]{2,1,0:T(8,128)(2,1)S(1)}, u32[]{:S(2)}, u32[]{:S(2)}) collective-permute-start(bf16[2,1024,128]{2,1,0:T(8,128)(2,1)S(1)} %slice.51), channel_id=1, source_target_pairs={{0,4},{4,8},{8,12},{12,16},{16,20},{20,24},{24,28},{1,5},{5,9},{9,... | collective-permute-start | bytes 1572872 | tf_op jit(solution)/shard_map/ppermute | solution.py:221
  16.3 16.6 %copy-start.1 = (bf16[2,128,1024]{2,1,0:T(8,128)(2,1)}, bf16[2,128,1024]{2,1,0:T(8,128)(2,1)S(1)}, u32[]{:S(2)}) copy-start(bf16[2,128,1024]{2,1,0:T(8,128)(2,1)S(1)} %collective-permute-done.2.up_ref) | copy-start | bytes 1572868
  26.7 3.3 %copy-start = (bf16[2,1024,128]{2,1,0:T(8,128)(2,1)}, bf16[2,1024,128]{2,1,0:T(8,128)(2,1)S(1)}, u32[]{:S(2)}) copy-start(bf16[2,1024,128]{2,1,0:T(8,128)(2,1)S(1)} %collective-permute-done.lcur_ref.lprev_ref) | copy-start | bytes 1572868
  30.5 5.8 %collective-permute-start.1 = (f32[5,2]{0,1:T(2,128)S(1)}, f32[5,2]{0,1:T(2,128)S(1)}, u32[]{:S(2)}, u32[]{:S(2)}) collective-permute-start(f32[5,2]{0,1:T(2,128)S(1)} %pad_maximum_fusion), channel_id=1, source_target_pairs={{4,0},{8,4},{12,8},{16,12},{20,16},{24,20},{28,24},{5,1},{9,5},{13... | collective-permute-start | bytes 128 | tf_op jit(solution)/shard_map/ppermute | solution.py:221
  35.0 3.0 %collective-permute-start.3 = (f32[5,2]{0,1:T(2,128)S(1)}, f32[5,2]{0,1:T(2,128)S(1)}, u32[]{:S(2)}, u32[]{:S(2)}) collective-permute-start(f32[5,2]{0,1:T(2,128)S(1)} %pad_maximum_fusion.1), channel_id=1, source_target_pairs={{1,0},{2,1},{3,2},{5,4},{6,5},{7,6},{9,8},{10,9},{11,10},{13,12},{... | collective-permute-start | bytes 128 | tf_op jit(solution)/shard_map/ppermute | solution.py:221
  38.5 10.5 %collective-permute-start.7 = (f32[4]{0:T(128)S(1)}, f32[4]{0:T(128)S(1)}, u32[]{:S(2)}, u32[]{:S(2)}) collective-permute-start(f32[4]{0:T(128)S(1)} %pad_maximum_fusion.2), channel_id=1, source_target_pairs={{0,1},{1,2},{2,3},{4,5},{5,6},{6,7},{8,9},{9,10},{10,11},{12,13},{... | collective-permute-start | bytes 56 | tf_op jit(solution)/shard_map/ppermute | solution.py:221
  40.9 8.1 %collective-permute-start.6 = (f32[4]{0:T(128)S(1)}, f32[4]{0:T(128)S(1)}, u32[]{:S(2)}, u32[]{:S(2)}) collective-permute-start(f32[4]{0:T(128)S(1)} %pad_maximum_fusion.2), channel_id=1, source_target_pairs={{0,4},{4,8},{8,12},{12,16},{16,20},{20,24},{24,28},{1,5},{5,9},{9,... | collective-permute-start | bytes 56 | tf_op jit(solution)/shard_map/ppermute | solution.py:221
  44.3 4.6 %collective-permute-start.5 = (f32[4]{0:T(128)S(1)}, f32[4]{0:T(128)S(1)}, u32[]{:S(2)}, u32[]{:S(2)}) collective-permute-start(f32[4]{0:T(128)S(1)} %pad_maximum_fusion.2), channel_id=1, source_target_pairs={{1,0},{2,1},{3,2},{5,4},{6,5},{7,6},{9,8},{10,9},{11,10},{13,12},{... | collective-permute-start | bytes 56 | tf_op jit(solution)/shard_map/ppermute | solution.py:221
  45.6 5.5 %collective-permute-start.4 = (f32[4]{0:T(128)S(1)}, f32[4]{0:T(128)S(1)}, u32[]{:S(2)}, u32[]{:S(2)}) collective-permute-start(f32[4]{0:T(128)S(1)} %pad_maximum_fusion.2), channel_id=1, source_target_pairs={{4,0},{8,4},{12,8},{16,12},{20,16},{24,20},{28,24},{5,1},{9,5},{13... | collective-permute-start | bytes 56 | tf_op jit(solution)/shard_map/ppermute | solution.py:221
  51.3 14.2 %copy-start.3 = (f32[4]{0:T(128)}, f32[4]{0:T(128)S(1)}, u32[]{:S(2)}) copy-start(f32[4]{0:T(128)S(1)} %pad_maximum_fusion.3.own_ref) | copy-start | bytes 52
  51.3 10.4 %collective-permute-start.10 = (f32[4]{0:T(128)S(1)}, f32[4]{0:T(128)S(1)}, u32[]{:S(2)}, u32[]{:S(2)}) collective-permute-start(f32[4]{0:T(128)S(1)} %pad_maximum_fusion.3.own_ref), channel_id=1, source_target_pairs={{0,5},{4,9},{8,13},{12,17},{16,21},{20,25},{24,29},{1,6},{5,10},{9... | collective-permute-start | bytes 56 | tf_op jit(solution)/shard_map/ppermute | solution.py:309
  55.2 6.5 %collective-permute-start.9 = (f32[4]{0:T(128)S(1)}, f32[4]{0:T(128)S(1)}, u32[]{:S(2)}, u32[]{:S(2)}) collective-permute-start(f32[4]{0:T(128)S(1)} %pad_maximum_fusion.3.own_ref), channel_id=1, source_target_pairs={{0,1},{1,2},{2,3},{4,5},{5,6},{6,7},{8,9},{9,10},{10,11},{12,13},{... | collective-permute-start | bytes 56 | tf_op jit(solution)/shard_map/ppermute | solution.py:221
  59.1 6.4 %collective-permute-start.8 = (f32[4]{0:T(128)S(1)}, f32[4]{0:T(128)S(1)}, u32[]{:S(2)}, u32[]{:S(2)}) collective-permute-start(f32[4]{0:T(128)S(1)} %pad_maximum_fusion.3.own_ref), channel_id=1, source_target_pairs={{0,4},{4,8},{8,12},{12,16},{16,20},{20,24},{24,28},{1,5},{5,9},{9,... | collective-permute-start | bytes 56 | tf_op jit(solution)/shard_map/ppermute | solution.py:221
  61.7 3.8 %copy-start.2 = (bf16[2,128,128]{2,1,0:T(8,128)(2,1)}, bf16[2,128,128]{2,1,0:T(8,128)(2,1)S(1)}, u32[]{:S(2)}) copy-start(bf16[2,128,128]{2,1,0:T(8,128)(2,1)S(1)} %collective-permute-done.11.corner_ref) | copy-start | bytes 196612
  61.7 3.8 %copy-start.4 = (f32[4]{0:T(128)}, f32[4]{0:T(128)S(1)}, u32[]{:S(2)}) copy-start(f32[4]{0:T(128)S(1)} %collective-permute-done.10.corner_terms_ref) | copy-start | bytes 52
  61.7 3.8 %copy-start.5 = (f32[4]{0:T(128)}, f32[4]{0:T(128)S(1)}, u32[]{:S(2)}) copy-start(f32[4]{0:T(128)S(1)} %collective-permute-done.9.up_terms_ref) | copy-start | bytes 52
  65.5 0.6 copy-start.6
